TPU v7x, 512 devices: a whole 4x8x8 slice. The times are simulated.
512 devices in a mesh: dp: 8 (over y_lo, core), gx: 64 (over y_hi, z, x).
Axes of the slice: x: 4, y: 8 (y_hi: 2, y_lo: 4; y = y_hi * 4 + y_lo), z: 8, core: 2. Of those that a mesh axis runs over, the one named last changes fastest.
Arguments:
- features: bfloat16 [8, 16, 128, 8, 256], P('dp', None, 'gx'), may hold values from -6 to 6
- offsets: int32 [8, 3], P('dp'), may hold values from 0 to 255, as said below
- flip_bits: int32 [8, 3], P('dp'), may hold values from 0 to 1
- weight: bfloat16 [27, 16, 16], replicated, may hold values from -0.3125 to 0.3125
- conv_bias: float32 [16], replicated, may hold values from -3 to 3
- cotangent: bfloat16 [8, 16, 128, 8, 256], P('dp', None, 'gx'), may hold values from -6 to 6
Outputs:
- hidden: bfloat16 [8, 16, 128, 8, 256], P('dp', None, 'gx')
- grad_input: bfloat16 [8, 16, 128, 8, 256], P('dp', None, 'gx')
- grad_weight: float32 [27, 16, 16], replicated
- grad_bias: float32 [16], replicated
Inputs may be any that keep to these rules, and one draw needn't show every extreme that they name: `offsets`: column 0 lies in 0 to 127, column 1 in 0 to 7, column 2 in 0 to 255.
All inputs are finite; a program needn't handle non-finite values.
Results may differ from a plain program's by a relative error of at most 0.0075.
Values may be sent and summed in bfloat16 or wider, within the bound.
No kernel may reach another device: no remote copies, remote signals or barrier semaphores. Data moves between devices by JAX's collectives and lax.ppermute only.
A program may use at most 64 MiB of HBM per device.

v0:
```python
import math

import jax
import jax.numpy as jnp
from jax import lax
from jax.sharding import PartitionSpec as P

tap_offsets = [
    (shift_x, shift_y, shift_z)
    for shift_x in range(3)
    for shift_y in range(3)
    for shift_z in range(3)
]


def shifted(value, axis, steps):
    count = lax.axis_size(axis)
    pairs = [(source, (source + steps) % count) for source in range(count)]
    return lax.ppermute(value, axis, pairs)


def butterfly_sum(value, axis):
    count = lax.axis_size(axis)
    step = 1
    while step < count:
        pairs = [(source, source ^ step) for source in range(count)]
        value = value + lax.ppermute(value, axis, pairs)
        step *= 2
    return value


def permute_axis(volume, offset, mirror_bit, dim_index):
    reverse = jnp.flip(volume, dim_index)
    return jnp.where(
        mirror_bit == 1,
        jnp.roll(reverse, -offset, axis=dim_index),
        jnp.roll(volume, offset, axis=dim_index),
    )


def augment_local(volume, offset, mirror_bits):
    volume = permute_axis(volume, offset[1], mirror_bits[1], 2)
    return permute_axis(volume, offset[2], mirror_bits[2], 3)


def gelu_parts(pre_act):
    normal_cdf = 0.5 * (1.0 + lax.erf(pre_act * 0.7071067811865476))
    density = jnp.exp(-0.5 * pre_act * pre_act) * 0.3989422804014327
    return (pre_act * normal_cdf, normal_cdf + pre_act * density)


def routed(value, axis, sign, constant):
    count = lax.axis_size(axis)
    here = lax.axis_index(axis)
    step = 1
    while step < count:
        low = jnp.mod(sign * (here - constant), step)
        source = here // (2 * step) * (2 * step) + here % (2 * step) // step * step + low
        target = jnp.mod(sign * source + constant, count)
        swap = (source // step % 2) != (target // step % 2)
        pairs = [(peer, peer ^ step) for peer in range(count)]
        value = jnp.where(swap, lax.ppermute(value, axis, pairs), value)
        step *= 2
    return value


def on_device(features, offsets, flip_bits, weight, conv_bias, cotangent):
    planes = features.shape[2]
    devices_x = lax.axis_size("gx")
    length_x = planes * devices_x
    local = jax.vmap(augment_local)(features, offsets, flip_bits)
    flip_x = flip_bits[0, 0] == 1
    block = jnp.where(flip_x, jnp.flip(local, 2), local)
    effective = jnp.where(flip_x, jnp.mod(-offsets[0, 0], length_x), offsets[0, 0])
    coarse_steps = effective // planes
    remain = effective % planes
    sign = jnp.where(flip_x, -1, 1)
    constant = jnp.where(flip_x, devices_x - 1 + coarse_steps, coarse_steps)
    coarse = routed(block, "gx", sign, constant)
    before = shifted(coarse, "gx", 1)
    after = shifted(coarse, "gx", -1)
    joined = jnp.concatenate([before, coarse, after], axis=2)
    padded = lax.dynamic_slice_in_dim(joined, planes - 1 - remain, planes + 2, axis=2)

    taps = len(tap_offsets)
    channels = features.shape[1]
    total = jnp.zeros(features.shape, jnp.float32) + conv_bias[None, :, None, None, None]
    for tap_index, (shift_x, shift_y, shift_z) in enumerate(tap_offsets):
        window = jnp.roll(
            padded[:, :, shift_x : shift_x + planes], (1 - shift_y, 1 - shift_z), axis=(3, 4)
        )
        total = total + jnp.einsum(
            "oi,bixyz->boxyz", weight[tap_index], window, preferred_element_type=jnp.float32
        )
    hidden, slope = gelu_parts(total)
    grad_pre = (cotangent.astype(jnp.float32) * slope).astype(jnp.bfloat16)
    grad_before = shifted(grad_pre[:, :, planes - 1 : planes], "gx", 1)
    grad_after = shifted(grad_pre[:, :, 0:1], "gx", -1)
    grad_list = []
    for tap_index, (shift_x, shift_y, shift_z) in enumerate(tap_offsets):
        window = jnp.roll(
            padded[:, :, shift_x : shift_x + planes], (1 - shift_y, 1 - shift_z), axis=(3, 4)
        )
        grad_list.append(
            jnp.einsum("boxyz,bixyz->oi", grad_pre, window, preferred_element_type=jnp.float32)
        )
    grad_b = jnp.sum(grad_pre.astype(jnp.float32), axis=(0, 2, 3, 4))
    stacked = jnp.concatenate([jnp.stack(grad_list).reshape(-1), grad_b])
    summed = butterfly_sum(butterfly_sum(stacked, "dp"), "gx")
    grad_pad = jnp.concatenate([grad_before, grad_pre, grad_after], axis=2)
    grad_in = jnp.zeros(features.shape, jnp.float32)
    for tap_index, (shift_x, shift_y, shift_z) in enumerate(tap_offsets):
        moved_grad = jnp.roll(
            grad_pad[:, :, 2 - shift_x : 2 - shift_x + planes],
            (shift_y - 1, shift_z - 1),
            axis=(3, 4),
        )
        grad_in = grad_in + jnp.einsum(
            "oi,boxyz->bixyz", weight[tap_index], moved_grad, preferred_element_type=jnp.float32
        )
    cell_count = (
        features.shape[0] * lax.axis_size("dp") * length_x * features.shape[3] * features.shape[4]
    )
    grad_scale = 1.0 / math.sqrt(cell_count)
    summed = summed * grad_scale
    weight_count = taps * channels * channels
    return (
        hidden.astype(jnp.bfloat16),
        grad_in.astype(jnp.bfloat16),
        summed[:weight_count].reshape(taps, channels, channels),
        summed[weight_count:],
    )


def solution(mesh):
    in_specs = (
        P("dp", None, "gx", None, None),
        P("dp", None),
        P("dp", None),
        P(),
        P(),
        P("dp", None, "gx", None, None),
    )
    out_specs = (P("dp", None, "gx", None, None), P("dp", None, "gx", None, None), P(), P())
    return jax.shard_map(
        on_device, mesh=mesh, in_specs=in_specs, out_specs=out_specs, check_vma=False
    )
```

profile of v0, /device:TPU:2, one launch (start us, length us, event | category | flops | bytes accessed | tf_op | source)
XLA Modules:
  0.0 188.6 jit_solution(8451011160800925356)
XLA Ops:
  11.4 7.8 %collective-permute-start = (bf16[1,16,2,8,256]{4,1,3,2,0:T(8,128)(2,1)S(1)}, bf16[1,16,2,8,256]{4,1,3,2,0:T(8,128)(2,1)S(1)}, u32[]{:S(2)}, u32[]{:S(2)}) collective-permute-start(bf16[1,16,2,8,256]{4,1,3,2,0:T(8,128)(2,1)S(1)} %reverse_select_fusion), channel_id=1, source_target_pairs={{0,1},{1,0},{2,3},{3,2},{4,5},{5,4},{6,7},{7,6},{8,9},{9,8},{10,11... | collective-permute-start | bytes 393224 | tf_op jit(solution)/shard_map/ppermute | solution.py:62
  22.2 1.9 %collective-permute-start.1 = (bf16[1,16,2,8,256]{4,1,3,2,0:T(8,128)(2,1)S(1)}, bf16[1,16,2,8,256]{4,1,3,2,0:T(8,128)(2,1)S(1)}, u32[]{:S(2)}, u32[]{:S(2)}) collective-permute-start(bf16[1,16,2,8,256]{4,1,3,2,0:T(8,128)(2,1)S(1)} %broadcast_select_fusion), channel_id=1, source_target_pairs={{0,2},{1,3},{2,0},{3,1},{4,6},{5,7},{6,4},{7,5},{8,10},{9,11},{10,... | collective-permute-start | bytes 393224 | tf_op jit(solution)/shard_map/ppermute | solution.py:62
  24.3 6.3 %collective-permute-done.1 = bf16[1,16,2,8,256]{4,1,3,2,0:T(8,128)(2,1)S(1)} collective-permute-done((bf16[1,16,2,8,256]{4,1,3,2,0:T(8,128)(2,1)S(1)}, bf16[1,16,2,8,256]{4,1,3,2,0:T(8,128)(2,1)S(1)}, u32[]{:S(2)}, u32[]{:S(2)}) %collective-permute-start.1) | collective-permute-done | bytes 131104 | tf_op jit(solution)/shard_map/ppermute | solution.py:62
  30.6 1.9 %collective-permute-start.2 = (bf16[1,16,2,8,256]{4,1,3,2,0:T(8,128)(2,1)S(1)}, bf16[1,16,2,8,256]{4,1,3,2,0:T(8,128)(2,1)S(1)}, u32[]{:S(2)}, u32[]{:S(2)}) collective-permute-start(bf16[1,16,2,8,256]{4,1,3,2,0:T(8,128)(2,1)S(1)} %broadcast_select_fusion.1), channel_id=1, source_target_pairs={{0,4},{1,5},{2,6},{3,7},{4,0},{5,1},{6,2},{7,3},{8,12},{9,13},{10,... | collective-permute-start | bytes 393224 | tf_op jit(solution)/shard_map/ppermute | solution.py:62
  32.6 4.8 %collective-permute-done.2 = bf16[1,16,2,8,256]{4,1,3,2,0:T(8,128)(2,1)S(1)} collective-permute-done((bf16[1,16,2,8,256]{4,1,3,2,0:T(8,128)(2,1)S(1)}, bf16[1,16,2,8,256]{4,1,3,2,0:T(8,128)(2,1)S(1)}, u32[]{:S(2)}, u32[]{:S(2)}) %collective-permute-start.2) | collective-permute-done | bytes 131104 | tf_op jit(solution)/shard_map/ppermute | solution.py:62
  37.4 2.8 %collective-permute-start.3 = (bf16[1,16,2,8,256]{4,1,3,2,0:T(8,128)(2,1)S(1)}, bf16[1,16,2,8,256]{4,1,3,2,0:T(8,128)(2,1)S(1)}, u32[]{:S(2)}, u32[]{:S(2)}) collective-permute-start(bf16[1,16,2,8,256]{4,1,3,2,0:T(8,128)(2,1)S(1)} %broadcast_select_fusion.2), channel_id=1, source_target_pairs={{0,8},{1,9},{2,10},{3,11},{4,12},{5,13},{6,14},{7,15},{8,0},{9,1},... | collective-permute-start | bytes 393224 | tf_op jit(solution)/shard_map/ppermute | solution.py:62
  40.4 5.6 %collective-permute-done.3 = bf16[1,16,2,8,256]{4,1,3,2,0:T(8,128)(2,1)S(1)} collective-permute-done((bf16[1,16,2,8,256]{4,1,3,2,0:T(8,128)(2,1)S(1)}, bf16[1,16,2,8,256]{4,1,3,2,0:T(8,128)(2,1)S(1)}, u32[]{:S(2)}, u32[]{:S(2)}) %collective-permute-start.3) | collective-permute-done | bytes 131104 | tf_op jit(solution)/shard_map/ppermute | solution.py:62
  46.1 7.9 %collective-permute-start.4 = (bf16[1,16,2,8,256]{4,1,3,2,0:T(8,128)(2,1)S(1)}, bf16[1,16,2,8,256]{4,1,3,2,0:T(8,128)(2,1)S(1)}, u32[]{:S(2)}, u32[]{:S(2)}) collective-permute-start(bf16[1,16,2,8,256]{4,1,3,2,0:T(8,128)(2,1)S(1)} %broadcast_select_fusion.3), channel_id=1, source_target_pairs={{0,16},{1,17},{2,18},{3,19},{4,20},{5,21},{6,22},{7,23},{8,24},{9,... | collective-permute-start | bytes 393224 | tf_op jit(solution)/shard_map/ppermute | solution.py:62
  54.3 2.7 %collective-permute-done.4 = bf16[1,16,2,8,256]{4,1,3,2,0:T(8,128)(2,1)S(1)} collective-permute-done((bf16[1,16,2,8,256]{4,1,3,2,0:T(8,128)(2,1)S(1)}, bf16[1,16,2,8,256]{4,1,3,2,0:T(8,128)(2,1)S(1)}, u32[]{:S(2)}, u32[]{:S(2)}) %collective-permute-start.4) | collective-permute-done | bytes 131104 | tf_op jit(solution)/shard_map/ppermute | solution.py:62
  57.0 7.7 %collective-permute-start.5 = (bf16[1,16,2,8,256]{4,1,3,2,0:T(8,128)(2,1)S(1)}, bf16[1,16,2,8,256]{4,1,3,2,0:T(8,128)(2,1)S(1)}, u32[]{:S(2)}, u32[]{:S(2)}) collective-permute-start(bf16[1,16,2,8,256]{4,1,3,2,0:T(8,128)(2,1)S(1)} %broadcast_select_fusion.4), channel_id=1, source_target_pairs={{0,32},{1,33},{2,34},{3,35},{4,36},{5,37},{6,38},{7,39},{8,40},{9,... | collective-permute-start | bytes 393224 | tf_op jit(solution)/shard_map/ppermute | solution.py:62
  66.4 2.2 %collective-permute-done.5 = bf16[1,16,2,8,256]{4,1,3,2,0:T(8,128)(2,1)S(1)} collective-permute-done((bf16[1,16,2,8,256]{4,1,3,2,0:T(8,128)(2,1)S(1)}, bf16[1,16,2,8,256]{4,1,3,2,0:T(8,128)(2,1)S(1)}, u32[]{:S(2)}, u32[]{:S(2)}) %collective-permute-start.5) | collective-permute-done | bytes 131104 | tf_op jit(solution)/shard_map/ppermute | solution.py:62
  68.6 3.7 %collective-permute-start.7 = (bf16[1,16,2,8,256]{4,1,3,2,0:T(8,128)(2,1)S(1)}, bf16[1,16,2,8,256]{4,1,3,2,0:T(8,128)(2,1)S(1)}, u32[]{:S(2)}, u32[]{:S(2)}) collective-permute-start(bf16[1,16,2,8,256]{4,1,3,2,0:T(8,128)(2,1)S(1)} %broadcast_select_fusion.5), channel_id=1, source_target_pairs={{0,63},{1,0},{2,1},{3,2},{4,3},{5,4},{6,5},{7,6},{8,7},{9,8},{10,9... | collective-permute-start | bytes 393224 | tf_op jit(solution)/shard_map/ppermute | solution.py:19
  72.3 2.1 %collective-permute-start.6 = (bf16[1,16,2,8,256]{4,1,3,2,0:T(8,128)(2,1)S(1)}, bf16[1,16,2,8,256]{4,1,3,2,0:T(8,128)(2,1)S(1)}, u32[]{:S(2)}, u32[]{:S(2)}) collective-permute-start(bf16[1,16,2,8,256]{4,1,3,2,0:T(8,128)(2,1)S(1)} %broadcast_select_fusion.5), channel_id=1, source_target_pairs={{0,1},{1,2},{2,3},{3,4},{4,5},{5,6},{6,7},{7,8},{8,9},{9,10},{10,1... | collective-permute-start | bytes 393224 | tf_op jit(solution)/shard_map/ppermute | solution.py:19
  78.4 12.9 %collective-permute-done.6 = bf16[1,16,2,8,256]{4,1,3,2,0:T(8,128)(2,1)S(1)} collective-permute-done((bf16[1,16,2,8,256]{4,1,3,2,0:T(8,128)(2,1)S(1)}, bf16[1,16,2,8,256]{4,1,3,2,0:T(8,128)(2,1)S(1)}, u32[]{:S(2)}, u32[]{:S(2)}) %collective-permute-start.6) | collective-permute-done | bytes 131104 | tf_op jit(solution)/shard_map/ppermute | solution.py:19
  105.9 1.9 %collective-permute-start.10 = (f32[6928]{0:T(1024)S(1)}, f32[6928]{0:T(1024)S(1)}, u32[]{:S(2)}, u32[]{:S(2)}) collective-permute-start(f32[6928]{0:T(1024)S(1)} %pad_maximum_fusion.12), channel_id=1, source_target_pairs={{0,64},{64,0},{128,192},{192,128},{256,320},{320,256},{384,448},{4... | collective-permute-start | bytes 83144 | tf_op jit(solution)/shard_map/ppermute | solution.py:27
  107.8 13.4 %collective-permute-start.8 = (bf16[1,16,1,8,256]{4,1,3,2,0:T(8,128)(2,1)S(1)}, bf16[1,16,1,8,256]{4,1,3,2,0:T(8,128)(2,1)S(1)}, u32[]{:S(2)}, u32[]{:S(2)}) collective-permute-start(bf16[1,16,1,8,256]{4,1,3,2,0:T(8,128)(2,1)S(1)} %get-tuple-element.114), channel_id=1, source_target_pairs={{0,63},{1,0},{2,1},{3,2},{4,3},{5,4},{6,5},{7,6},{8,7},{9,8},{10,9... | collective-permute-start | bytes 196616 | tf_op jit(solution)/shard_map/ppermute | solution.py:19
  121.3 1.9 %collective-permute-start.9 = (bf16[1,16,1,8,256]{4,1,3,2,0:T(8,128)(2,1)S(1)}, bf16[1,16,1,8,256]{4,1,3,2,0:T(8,128)(2,1)S(1)}, u32[]{:S(2)}, u32[]{:S(2)}) collective-permute-start(bf16[1,16,1,8,256]{4,1,3,2,0:T(8,128)(2,1)S(1)} %get-tuple-element.115), channel_id=1, source_target_pairs={{0,1},{1,2},{2,3},{3,4},{4,5},{5,6},{6,7},{7,8},{8,9},{9,10},{10,1... | collective-permute-start | bytes 196616 | tf_op jit(solution)/shard_map/ppermute | solution.py:19
  123.2 1.9 %collective-permute-start.11 = (f32[6928]{0:T(1024)S(1)}, f32[6928]{0:T(1024)S(1)}, u32[]{:S(2)}, u32[]{:S(2)}) collective-permute-start(f32[6928]{0:T(1024)S(1)} %fusion.383), channel_id=1, source_target_pairs={{0,128},{64,192},{128,0},{192,64},{256,384},{320,448},{384,256},{4... | collective-permute-start | bytes 83144 | tf_op jit(solution)/shard_map/ppermute | solution.py:27
  125.9 3.1 %collective-permute-done.11 = f32[6928]{0:T(1024)S(1)} collective-permute-done((f32[6928]{0:T(1024)S(1)}, f32[6928]{0:T(1024)S(1)}, u32[]{:S(2)}, u32[]{:S(2)}) %collective-permute-start.11) | collective-permute-done | bytes 27744 | tf_op jit(solution)/shard_map/ppermute | solution.py:27
  129.0 2.1 %collective-permute-start.12 = (f32[6928]{0:T(1024)S(1)}, f32[6928]{0:T(1024)S(1)}, u32[]{:S(2)}, u32[]{:S(2)}) collective-permute-start(f32[6928]{0:T(1024)S(1)} %add.521), channel_id=1, source_target_pairs={{0,256},{64,320},{128,384},{192,448},{256,0},{320,64},{384,128},{4... | collective-permute-start | bytes 83144 | tf_op jit(solution)/shard_map/ppermute | solution.py:27
  138.2 7.9 %collective-permute-start.13 = (f32[6928]{0:T(1024)S(1)}, f32[6928]{0:T(1024)S(1)}, u32[]{:S(2)}, u32[]{:S(2)}) collective-permute-start(f32[6928]{0:T(1024)S(1)} %add.522), channel_id=1, source_target_pairs={{0,1},{1,0},{2,3},{3,2},{4,5},{5,4},{6,7},{7,6},{8,9},{9,8},{10,11... | collective-permute-start | bytes 83144 | tf_op jit(solution)/shard_map/ppermute | solution.py:27
  146.2 1.7 collective-permute-done.13
  147.9 1.9 %collective-permute-start.14 = (f32[6928]{0:T(1024)S(1)}, f32[6928]{0:T(1024)S(1)}, u32[]{:S(2)}, u32[]{:S(2)}) collective-permute-start(f32[6928]{0:T(1024)S(1)} %add.523), channel_id=1, source_target_pairs={{0,2},{1,3},{2,0},{3,1},{4,6},{5,7},{6,4},{7,5},{8,10},{9,11},{10,... | collective-permute-start | bytes 83144 | tf_op jit(solution)/shard_map/ppermute | solution.py:27
  150.1 5.1 %collective-permute-done.14 = f32[6928]{0:T(1024)S(1)} collective-permute-done((f32[6928]{0:T(1024)S(1)}, f32[6928]{0:T(1024)S(1)}, u32[]{:S(2)}, u32[]{:S(2)}) %collective-permute-start.14) | collective-permute-done | bytes 27744 | tf_op jit(solution)/shard_map/ppermute | solution.py:27
  155.2 1.9 %collective-permute-start.15 = (f32[6928]{0:T(1024)S(1)}, f32[6928]{0:T(1024)S(1)}, u32[]{:S(2)}, u32[]{:S(2)}) collective-permute-start(f32[6928]{0:T(1024)S(1)} %add.524), channel_id=1, source_target_pairs={{0,4},{1,5},{2,6},{3,7},{4,0},{5,1},{6,2},{7,3},{8,12},{9,13},{10,... | collective-permute-start | bytes 83144 | tf_op jit(solution)/shard_map/ppermute | solution.py:27
  157.4 3.6 %collective-permute-done.15 = f32[6928]{0:T(1024)S(1)} collective-permute-done((f32[6928]{0:T(1024)S(1)}, f32[6928]{0:T(1024)S(1)}, u32[]{:S(2)}, u32[]{:S(2)}) %collective-permute-start.15) | collective-permute-done | bytes 27744 | tf_op jit(solution)/shard_map/ppermute | solution.py:27
  161.0 1.9 %collective-permute-start.16 = (f32[6928]{0:T(1024)S(1)}, f32[6928]{0:T(1024)S(1)}, u32[]{:S(2)}, u32[]{:S(2)}) collective-permute-start(f32[6928]{0:T(1024)S(1)} %add.525), channel_id=1, source_target_pairs={{0,8},{1,9},{2,10},{3,11},{4,12},{5,13},{6,14},{7,15},{8,0},{9,1},... | collective-permute-start | bytes 83144 | tf_op jit(solution)/shard_map/ppermute | solution.py:27
  163.1 4.6 %collective-permute-done.16 = f32[6928]{0:T(1024)S(1)} collective-permute-done((f32[6928]{0:T(1024)S(1)}, f32[6928]{0:T(1024)S(1)}, u32[]{:S(2)}, u32[]{:S(2)}) %collective-permute-start.16) | collective-permute-done | bytes 27744 | tf_op jit(solution)/shard_map/ppermute | solution.py:27
  167.8 1.9 %collective-permute-start.17 = (f32[6928]{0:T(1024)S(1)}, f32[6928]{0:T(1024)S(1)}, u32[]{:S(2)}, u32[]{:S(2)}) collective-permute-start(f32[6928]{0:T(1024)S(1)} %add.526), channel_id=1, source_target_pairs={{0,16},{1,17},{2,18},{3,19},{4,20},{5,21},{6,22},{7,23},{8,24},{9,... | collective-permute-start | bytes 83144 | tf_op jit(solution)/shard_map/ppermute | solution.py:27
  170.0 7.5 %collective-permute-done.17 = f32[6928]{0:T(1024)S(1)} collective-permute-done((f32[6928]{0:T(1024)S(1)}, f32[6928]{0:T(1024)S(1)}, u32[]{:S(2)}, u32[]{:S(2)}) %collective-permute-start.17) | collective-permute-done | bytes 27744 | tf_op jit(solution)/shard_map/ppermute | solution.py:27
  177.4 1.9 %collective-permute-start.18 = (f32[6928]{0:T(1024)S(1)}, f32[6928]{0:T(1024)S(1)}, u32[]{:S(2)}, u32[]{:S(2)}) collective-permute-start(f32[6928]{0:T(1024)S(1)} %add.527), channel_id=1, source_target_pairs={{0,32},{1,33},{2,34},{3,35},{4,36},{5,37},{6,38},{7,39},{8,40},{9,... | collective-permute-start | bytes 83144 | tf_op jit(solution)/shard_map/ppermute | solution.py:27
  180.3 6.8 %collective-permute-done.18 = f32[6928]{0:T(1024)S(1)} collective-permute-done((f32[6928]{0:T(1024)S(1)}, f32[6928]{0:T(1024)S(1)}, u32[]{:S(2)}, u32[]{:S(2)}) %collective-permute-start.18) | collective-permute-done | bytes 27744 | tf_op jit(solution)/shard_map/ppermute | solution.py:27
  (183 shorter events, 35.4 us)
Async XLA Ops:
  0.6 9.9 %copy-start.2 = (bf16[1,16,2,8,256]{4,3,2,1,0:T(8,128)(2,1)S(1)}, bf16[1,16,2,8,256]{4,3,2,1,0:T(8,128)(2,1)}, u32[]{:S(2)}) copy-start(bf16[1,16,2,8,256]{4,3,2,1,0:T(8,128)(2,1)} %param.10) | copy-start | bytes 393220
  11.4 10.8 %collective-permute-start = (bf16[1,16,2,8,256]{4,1,3,2,0:T(8,128)(2,1)S(1)}, bf16[1,16,2,8,256]{4,1,3,2,0:T(8,128)(2,1)S(1)}, u32[]{:S(2)}, u32[]{:S(2)}) collective-permute-start(bf16[1,16,2,8,256]{4,1,3,2,0:T(8,128)(2,1)S(1)} %reverse_select_fusion), channel_id=1, source_target_pairs={{0,1},{1,0},{2,3},{3,2},{4,5},{5,4},{6,7},{7,6},{8,9},{9,8},{10,11... | collective-permute-start | bytes 393224 | tf_op jit(solution)/shard_map/ppermute | solution.py:62
  22.2 8.4 %collective-permute-start.1 = (bf16[1,16,2,8,256]{4,1,3,2,0:T(8,128)(2,1)S(1)}, bf16[1,16,2,8,256]{4,1,3,2,0:T(8,128)(2,1)S(1)}, u32[]{:S(2)}, u32[]{:S(2)}) collective-permute-start(bf16[1,16,2,8,256]{4,1,3,2,0:T(8,128)(2,1)S(1)} %broadcast_select_fusion), channel_id=1, source_target_pairs={{0,2},{1,3},{2,0},{3,1},{4,6},{5,7},{6,4},{7,5},{8,10},{9,11},{10,... | collective-permute-start | bytes 393224 | tf_op jit(solution)/shard_map/ppermute | solution.py:62
  30.6 6.9 %collective-permute-start.2 = (bf16[1,16,2,8,256]{4,1,3,2,0:T(8,128)(2,1)S(1)}, bf16[1,16,2,8,256]{4,1,3,2,0:T(8,128)(2,1)S(1)}, u32[]{:S(2)}, u32[]{:S(2)}) collective-permute-start(bf16[1,16,2,8,256]{4,1,3,2,0:T(8,128)(2,1)S(1)} %broadcast_select_fusion.1), channel_id=1, source_target_pairs={{0,4},{1,5},{2,6},{3,7},{4,0},{5,1},{6,2},{7,3},{8,12},{9,13},{10,... | collective-permute-start | bytes 393224 | tf_op jit(solution)/shard_map/ppermute | solution.py:62
  37.4 8.6 %collective-permute-start.3 = (bf16[1,16,2,8,256]{4,1,3,2,0:T(8,128)(2,1)S(1)}, bf16[1,16,2,8,256]{4,1,3,2,0:T(8,128)(2,1)S(1)}, u32[]{:S(2)}, u32[]{:S(2)}) collective-permute-start(bf16[1,16,2,8,256]{4,1,3,2,0:T(8,128)(2,1)S(1)} %broadcast_select_fusion.2), channel_id=1, source_target_pairs={{0,8},{1,9},{2,10},{3,11},{4,12},{5,13},{6,14},{7,15},{8,0},{9,1},... | collective-permute-start | bytes 393224 | tf_op jit(solution)/shard_map/ppermute | solution.py:62
  46.1 10.9 %collective-permute-start.4 = (bf16[1,16,2,8,256]{4,1,3,2,0:T(8,128)(2,1)S(1)}, bf16[1,16,2,8,256]{4,1,3,2,0:T(8,128)(2,1)S(1)}, u32[]{:S(2)}, u32[]{:S(2)}) collective-permute-start(bf16[1,16,2,8,256]{4,1,3,2,0:T(8,128)(2,1)S(1)} %broadcast_select_fusion.3), channel_id=1, source_target_pairs={{0,16},{1,17},{2,18},{3,19},{4,20},{5,21},{6,22},{7,23},{8,24},{9,... | collective-permute-start | bytes 393224 | tf_op jit(solution)/shard_map/ppermute | solution.py:62
  57.0 7.8 %copy-start = (bf16[27,16,16]{0,2,1:T(8,128)(2,1)S(1)}, bf16[27,16,16]{0,2,1:T(8,128)(2,1)}, u32[]{:S(2)}) copy-start(bf16[27,16,16]{0,2,1:T(8,128)(2,1)} %param.13) | copy-start | bytes 41476
  57.0 11.6 %collective-permute-start.5 = (bf16[1,16,2,8,256]{4,1,3,2,0:T(8,128)(2,1)S(1)}, bf16[1,16,2,8,256]{4,1,3,2,0:T(8,128)(2,1)S(1)}, u32[]{:S(2)}, u32[]{:S(2)}) collective-permute-start(bf16[1,16,2,8,256]{4,1,3,2,0:T(8,128)(2,1)S(1)} %broadcast_select_fusion.4), channel_id=1, source_target_pairs={{0,32},{1,33},{2,34},{3,35},{4,36},{5,37},{6,38},{7,39},{8,40},{9,... | collective-permute-start | bytes 393224 | tf_op jit(solution)/shard_map/ppermute | solution.py:62
  68.6 9.7 %collective-permute-start.7 = (bf16[1,16,2,8,256]{4,1,3,2,0:T(8,128)(2,1)S(1)}, bf16[1,16,2,8,256]{4,1,3,2,0:T(8,128)(2,1)S(1)}, u32[]{:S(2)}, u32[]{:S(2)}) collective-permute-start(bf16[1,16,2,8,256]{4,1,3,2,0:T(8,128)(2,1)S(1)} %broadcast_select_fusion.5), channel_id=1, source_target_pairs={{0,63},{1,0},{2,1},{3,2},{4,3},{5,4},{6,5},{7,6},{8,7},{9,8},{10,9... | collective-permute-start | bytes 393224 | tf_op jit(solution)/shard_map/ppermute | solution.py:19
  72.3 18.9 %collective-permute-start.6 = (bf16[1,16,2,8,256]{4,1,3,2,0:T(8,128)(2,1)S(1)}, bf16[1,16,2,8,256]{4,1,3,2,0:T(8,128)(2,1)S(1)}, u32[]{:S(2)}, u32[]{:S(2)}) collective-permute-start(bf16[1,16,2,8,256]{4,1,3,2,0:T(8,128)(2,1)S(1)} %broadcast_select_fusion.5), channel_id=1, source_target_pairs={{0,1},{1,2},{2,3},{3,4},{4,5},{5,6},{6,7},{7,8},{8,9},{9,10},{10,1... | collective-permute-start | bytes 393224 | tf_op jit(solution)/shard_map/ppermute | solution.py:19
  97.8 0.9 copy-start.1
  98.1 0.7 copy-start.3
  105.9 17.3 %collective-permute-start.10 = (f32[6928]{0:T(1024)S(1)}, f32[6928]{0:T(1024)S(1)}, u32[]{:S(2)}, u32[]{:S(2)}) collective-permute-start(f32[6928]{0:T(1024)S(1)} %pad_maximum_fusion.12), channel_id=1, source_target_pairs={{0,64},{64,0},{128,192},{192,128},{256,320},{320,256},{384,448},{4... | collective-permute-start | bytes 83144 | tf_op jit(solution)/shard_map/ppermute | solution.py:27
  107.8 23.3 %collective-permute-start.8 = (bf16[1,16,1,8,256]{4,1,3,2,0:T(8,128)(2,1)S(1)}, bf16[1,16,1,8,256]{4,1,3,2,0:T(8,128)(2,1)S(1)}, u32[]{:S(2)}, u32[]{:S(2)}) collective-permute-start(bf16[1,16,1,8,256]{4,1,3,2,0:T(8,128)(2,1)S(1)} %get-tuple-element.114), channel_id=1, source_target_pairs={{0,63},{1,0},{2,1},{3,2},{4,3},{5,4},{6,5},{7,6},{8,7},{9,8},{10,9... | collective-permute-start | bytes 196616 | tf_op jit(solution)/shard_map/ppermute | solution.py:19
  121.3 9.8 %collective-permute-start.9 = (bf16[1,16,1,8,256]{4,1,3,2,0:T(8,128)(2,1)S(1)}, bf16[1,16,1,8,256]{4,1,3,2,0:T(8,128)(2,1)S(1)}, u32[]{:S(2)}, u32[]{:S(2)}) collective-permute-start(bf16[1,16,1,8,256]{4,1,3,2,0:T(8,128)(2,1)S(1)} %get-tuple-element.115), channel_id=1, source_target_pairs={{0,1},{1,2},{2,3},{3,4},{4,5},{5,6},{6,7},{7,8},{8,9},{9,10},{10,1... | collective-permute-start | bytes 196616 | tf_op jit(solution)/shard_map/ppermute | solution.py:19
  123.2 5.8 %collective-permute-start.11 = (f32[6928]{0:T(1024)S(1)}, f32[6928]{0:T(1024)S(1)}, u32[]{:S(2)}, u32[]{:S(2)}) collective-permute-start(f32[6928]{0:T(1024)S(1)} %fusion.383), channel_id=1, source_target_pairs={{0,128},{64,192},{128,0},{192,64},{256,384},{320,448},{384,256},{4... | collective-permute-start | bytes 83144 | tf_op jit(solution)/shard_map/ppermute | solution.py:27
  129.0 9.2 %collective-permute-start.12 = (f32[6928]{0:T(1024)S(1)}, f32[6928]{0:T(1024)S(1)}, u32[]{:S(2)}, u32[]{:S(2)}) collective-permute-start(f32[6928]{0:T(1024)S(1)} %add.521), channel_id=1, source_target_pairs={{0,256},{64,320},{128,384},{192,448},{256,0},{320,64},{384,128},{4... | collective-permute-start | bytes 83144 | tf_op jit(solution)/shard_map/ppermute | solution.py:27
  138.2 9.7 %collective-permute-start.13 = (f32[6928]{0:T(1024)S(1)}, f32[6928]{0:T(1024)S(1)}, u32[]{:S(2)}, u32[]{:S(2)}) collective-permute-start(f32[6928]{0:T(1024)S(1)} %add.522), channel_id=1, source_target_pairs={{0,1},{1,0},{2,3},{3,2},{4,5},{5,4},{6,7},{7,6},{8,9},{9,8},{10,11... | collective-permute-start | bytes 83144 | tf_op jit(solution)/shard_map/ppermute | solution.py:27
  147.9 7.3 %collective-permute-start.14 = (f32[6928]{0:T(1024)S(1)}, f32[6928]{0:T(1024)S(1)}, u32[]{:S(2)}, u32[]{:S(2)}) collective-permute-start(f32[6928]{0:T(1024)S(1)} %add.523), channel_id=1, source_target_pairs={{0,2},{1,3},{2,0},{3,1},{4,6},{5,7},{6,4},{7,5},{8,10},{9,11},{10,... | collective-permute-start | bytes 83144 | tf_op jit(solution)/shard_map/ppermute | solution.py:27
  155.2 5.8 %collective-permute-start.15 = (f32[6928]{0:T(1024)S(1)}, f32[6928]{0:T(1024)S(1)}, u32[]{:S(2)}, u32[]{:S(2)}) collective-permute-start(f32[6928]{0:T(1024)S(1)} %add.524), channel_id=1, source_target_pairs={{0,4},{1,5},{2,6},{3,7},{4,0},{5,1},{6,2},{7,3},{8,12},{9,13},{10,... | collective-permute-start | bytes 83144 | tf_op jit(solution)/shard_map/ppermute | solution.py:27
  161.0 6.8 %collective-permute-start.16 = (f32[6928]{0:T(1024)S(1)}, f32[6928]{0:T(1024)S(1)}, u32[]{:S(2)}, u32[]{:S(2)}) collective-permute-start(f32[6928]{0:T(1024)S(1)} %add.525), channel_id=1, source_target_pairs={{0,8},{1,9},{2,10},{3,11},{4,12},{5,13},{6,14},{7,15},{8,0},{9,1},... | collective-permute-start | bytes 83144 | tf_op jit(solution)/shard_map/ppermute | solution.py:27
  167.8 9.7 %collective-permute-start.17 = (f32[6928]{0:T(1024)S(1)}, f32[6928]{0:T(1024)S(1)}, u32[]{:S(2)}, u32[]{:S(2)}) collective-permute-start(f32[6928]{0:T(1024)S(1)} %add.526), channel_id=1, source_target_pairs={{0,16},{1,17},{2,18},{3,19},{4,20},{5,21},{6,22},{7,23},{8,24},{9,... | collective-permute-start | bytes 83144 | tf_op jit(solution)/shard_map/ppermute | solution.py:27
  177.4 9.7 %collective-permute-start.18 = (f32[6928]{0:T(1024)S(1)}, f32[6928]{0:T(1024)S(1)}, u32[]{:S(2)}, u32[]{:S(2)}) collective-permute-start(f32[6928]{0:T(1024)S(1)} %add.527), channel_id=1, source_target_pairs={{0,32},{1,33},{2,34},{3,35},{4,36},{5,37},{6,38},{7,39},{8,40},{9,... | collective-permute-start | bytes 83144 | tf_op jit(solution)/shard_map/ppermute | solution.py:27
where the time goes:
time: 189 us
  starting transfers between devices  74.7 us (40%)
  waiting for transfers between devices  67.8 us (36%)
  matrix products  18.9 us (10%)
  local copies, waits for them, and re-layouts  12.9 us (7%)
  between operations  11.6 us (6%)
  other arithmetic  2.67 us (1%)
    ppermute x9, waiting for transfers between devices, butterfly_sum(): value = value + lax.ppermute(value, axis, pairs)  32.5 us
    ppermute x6, starting transfers between devices, routed(): value = jnp.where(swap, lax.ppermute(value, axis, pairs), value)  30.2 us
    ppermute x9, starting transfers between devices, butterfly_sum(): value = value + lax.ppermute(value, axis, pairs)  23.3 us
    ppermute x6, waiting for transfers between devices, routed(): value = jnp.where(swap, lax.ppermute(value, axis, pairs), value)  22.4 us
    ppermute x4, starting transfers between devices, shifted(): return lax.ppermute(value, axis, pairs)  21.2 us
    ppermute x4, waiting for transfers between devices, shifted(): return lax.ppermute(value, axis, pairs)  12.9 us
    unnamed x39, local copies, waits for them, and re-layouts  7.82 us
    dot_general x27, matrix products, on_device(): jnp.einsum('oi,boxyz->bixyz', weight[tap_index], moved_grad, preferred_el...  6.58 us
  transfers between devices with their start and end apart: 19, of which 14 were waited for; matrix products, arithmetic and copies ran while one was open for 8% of the time, Pallas kernels for 0%

commit v1 on v0

--- a/solution.py
+++ b/solution.py
@@ -21,11 +21,23 @@
 
 def butterfly_sum(value, axis):
     count = lax.axis_size(axis)
+    here = lax.axis_index(axis)
     step = 1
     while step < count:
-        pairs = [(source, source ^ step) for source in range(count)]
-        value = value + lax.ppermute(value, axis, pairs)
-        step *= 2
+        if step * 4 <= count:
+            found = [value] + [
+                lax.ppermute(value, axis, [(peer, peer ^ (m * step)) for peer in range(count)])
+                for m in (1, 2, 3)
+            ]
+            stacked = jnp.stack(found)
+            place = here // step % 4
+            ordered = [stacked[jnp.bitwise_xor(j, place)] for j in range(4)]
+            value = (ordered[0] + ordered[1]) + (ordered[2] + ordered[3])
+            step *= 4
+        else:
+            pairs = [(peer, peer ^ step) for peer in range(count)]
+            value = value + lax.ppermute(value, axis, pairs)
+            step *= 2
     return value
 
 
@@ -49,19 +61,24 @@
     return (pre_act * normal_cdf, normal_cdf + pre_act * density)
 
 
-def routed(value, axis, sign, constant):
+def routed(pieces, axis, sign, constants):
     count = lax.axis_size(axis)
     here = lax.axis_index(axis)
     step = 1
     while step < count:
-        low = jnp.mod(sign * (here - constant), step)
-        source = here // (2 * step) * (2 * step) + here % (2 * step) // step * step + low
-        target = jnp.mod(sign * source + constant, count)
-        swap = (source // step % 2) != (target // step % 2)
         pairs = [(peer, peer ^ step) for peer in range(count)]
-        value = jnp.where(swap, lax.ppermute(value, axis, pairs), value)
+        sizes = [piece.shape[2] for piece in pieces]
+        arrived = lax.ppermute(jnp.concatenate(pieces, axis=2), axis, pairs)
+        updated = []
+        begin = 0
+        for piece, size, constant in zip(pieces, sizes, constants):
+            wanted = jnp.mod(sign * (here - constant), 2 * step)
+            take = (wanted // step % 2) != (here // step % 2)
+            updated.append(jnp.where(take, arrived[:, :, begin : begin + size], piece))
+            begin += size
+        pieces = updated
         step *= 2
-    return value
+    return pieces
 
 
 def on_device(features, offsets, flip_bits, weight, conv_bias, cotangent):
@@ -76,9 +93,9 @@
     remain = effective % planes
     sign = jnp.where(flip_x, -1, 1)
     constant = jnp.where(flip_x, devices_x - 1 + coarse_steps, coarse_steps)
-    coarse = routed(block, "gx", sign, constant)
-    before = shifted(coarse, "gx", 1)
-    after = shifted(coarse, "gx", -1)
+    before, coarse, after = routed(
+        [block, block, block[:, :, 0:1]], "gx", sign, [constant + 1, constant, constant - 1]
+    )
     joined = jnp.concatenate([before, coarse, after], axis=2)
     padded = lax.dynamic_slice_in_dim(joined, planes - 1 - remain, planes + 2, axis=2)
 

time: 189 us -> 217 us (1.15)
  the two profiles are of different devices: /device:TPU:2 before, /device:TPU:6 now
where the time goes in v1:
time: 217 us; the launch traced here: 216 us
  starting transfers between devices  102 us (47%)
  waiting for transfers between devices  64.7 us (30%)
  matrix products  18.9 us (9%)
  local copies, waits for them, and re-layouts  14.1 us (6%)
  between operations  12.3 us (6%)
  other arithmetic  4.03 us (2%)
    ppermute x12, starting transfers between devices, butterfly_sum(): lax.ppermute(value, axis, [(peer, peer ^ m * step) for peer in range(coun...  55.3 us
    ppermute x6, waiting for transfers between devices, routed(): arrived = lax.ppermute(jnp.concatenate(pieces, axis=2), axis, pairs)  50.7 us
    ppermute x6, starting transfers between devices, routed(): arrived = lax.ppermute(jnp.concatenate(pieces, axis=2), axis, pairs)  34.1 us
    ppermute x12, waiting for transfers between devices, butterfly_sum(): lax.ppermute(value, axis, [(peer, peer ^ m * step) for peer in range(coun...  12.6 us
    unnamed x39, local copies, waits for them, and re-layouts  9.38 us
    ppermute x2, starting transfers between devices, shifted(): return lax.ppermute(value, axis, pairs)  7.95 us
    dot_general x27, matrix products, on_device(): jnp.einsum('oi,boxyz->bixyz', weight[tap_index], moved_grad, preferred_el...  6.58 us
    dot_general x27, matrix products, on_device(): jnp.einsum('boxyz,bixyz->oi', grad_pre, window, preferred_element_type=jn...  6.18 us
  transfers between devices with their start and end apart: 21, of which 9 were waited for; matrix products, arithmetic and copies ran while one was open for 7% of the time, Pallas kernels for 0%

profile of v1, /device:TPU:6, one launch (start us, length us, event | category | flops | bytes accessed | tf_op | source)
XLA Modules:
  0.0 216.0 jit_solution(15310483297921648870)
XLA Ops:
  0.6 1.4 fusion.384
  9.8 0.9 copy.70
  12.2 2.7 %collective-permute-start = (bf16[1,16,5,8,256]{4,1,3,2,0:T(8,128)(2,1)S(1)}, bf16[1,16,5,8,256]{4,1,3,2,0:T(8,128)(2,1)S(1)}, u32[]{:S(2)}, u32[]{:S(2)}) collective-permute-start(bf16[1,16,5,8,256]{4,1,3,2,0:T(8,128)(2,1)S(1)} %pad_maximum_fusion), channel_id=1, source_target_pairs={{0,1},{1,0},{2,3},{3,2},{4,5},{5,4},{6,7},{7,6},{8,9},{9,8},{10,11... | collective-permute-start | bytes 983048 | tf_op jit(solution)/shard_map/ppermute | solution.py:71
  17.0 6.5 %collective-permute-done = bf16[1,16,5,8,256]{4,1,3,2,0:T(8,128)(2,1)S(1)} collective-permute-done((bf16[1,16,5,8,256]{4,1,3,2,0:T(8,128)(2,1)S(1)}, bf16[1,16,5,8,256]{4,1,3,2,0:T(8,128)(2,1)S(1)}, u32[]{:S(2)}, u32[]{:S(2)}) %collective-permute-start) | collective-permute-done | bytes 327712 | tf_op jit(solution)/shard_map/ppermute | solution.py:71
  23.7 4.8 %collective-permute-start.1 = (bf16[1,16,5,8,256]{4,1,3,2,0:T(8,128)(2,1)S(1)}, bf16[1,16,5,8,256]{4,1,3,2,0:T(8,128)(2,1)S(1)}, u32[]{:S(2)}, u32[]{:S(2)}) collective-permute-start(bf16[1,16,5,8,256]{4,1,3,2,0:T(8,128)(2,1)S(1)} %pad_maximum_fusion.1), channel_id=1, source_target_pairs={{0,2},{1,3},{2,0},{3,1},{4,6},{5,7},{6,4},{7,5},{8,10},{9,11},{10,... | collective-permute-start | bytes 983048 | tf_op jit(solution)/shard_map/ppermute | solution.py:71
  28.7 6.9 %collective-permute-done.1 = bf16[1,16,5,8,256]{4,1,3,2,0:T(8,128)(2,1)S(1)} collective-permute-done((bf16[1,16,5,8,256]{4,1,3,2,0:T(8,128)(2,1)S(1)}, bf16[1,16,5,8,256]{4,1,3,2,0:T(8,128)(2,1)S(1)}, u32[]{:S(2)}, u32[]{:S(2)}) %collective-permute-start.1) | collective-permute-done | bytes 327712 | tf_op jit(solution)/shard_map/ppermute | solution.py:71
  35.7 4.3 %collective-permute-start.2 = (bf16[1,16,5,8,256]{4,1,3,2,0:T(8,128)(2,1)S(1)}, bf16[1,16,5,8,256]{4,1,3,2,0:T(8,128)(2,1)S(1)}, u32[]{:S(2)}, u32[]{:S(2)}) collective-permute-start(bf16[1,16,5,8,256]{4,1,3,2,0:T(8,128)(2,1)S(1)} %pad_maximum_fusion.2), channel_id=1, source_target_pairs={{0,4},{1,5},{2,6},{3,7},{4,0},{5,1},{6,2},{7,3},{8,12},{9,13},{10,... | collective-permute-start | bytes 983048 | tf_op jit(solution)/shard_map/ppermute | solution.py:71
  40.2 5.7 %collective-permute-done.2 = bf16[1,16,5,8,256]{4,1,3,2,0:T(8,128)(2,1)S(1)} collective-permute-done((bf16[1,16,5,8,256]{4,1,3,2,0:T(8,128)(2,1)S(1)}, bf16[1,16,5,8,256]{4,1,3,2,0:T(8,128)(2,1)S(1)}, u32[]{:S(2)}, u32[]{:S(2)}) %collective-permute-start.2) | collective-permute-done | bytes 327712 | tf_op jit(solution)/shard_map/ppermute | solution.py:71
  46.0 6.1 %collective-permute-start.3 = (bf16[1,16,5,8,256]{4,1,3,2,0:T(8,128)(2,1)S(1)}, bf16[1,16,5,8,256]{4,1,3,2,0:T(8,128)(2,1)S(1)}, u32[]{:S(2)}, u32[]{:S(2)}) collective-permute-start(bf16[1,16,5,8,256]{4,1,3,2,0:T(8,128)(2,1)S(1)} %pad_maximum_fusion.3), channel_id=1, source_target_pairs={{0,8},{1,9},{2,10},{3,11},{4,12},{5,13},{6,14},{7,15},{8,0},{9,1},... | collective-permute-start | bytes 983048 | tf_op jit(solution)/shard_map/ppermute | solution.py:71
  52.3 12.1 %collective-permute-done.3 = bf16[1,16,5,8,256]{4,1,3,2,0:T(8,128)(2,1)S(1)} collective-permute-done((bf16[1,16,5,8,256]{4,1,3,2,0:T(8,128)(2,1)S(1)}, bf16[1,16,5,8,256]{4,1,3,2,0:T(8,128)(2,1)S(1)}, u32[]{:S(2)}, u32[]{:S(2)}) %collective-permute-start.3) | collective-permute-done | bytes 327712 | tf_op jit(solution)/shard_map/ppermute | solution.py:71
  64.5 8.4 %collective-permute-start.4 = (bf16[1,16,5,8,256]{4,1,3,2,0:T(8,128)(2,1)S(1)}, bf16[1,16,5,8,256]{4,1,3,2,0:T(8,128)(2,1)S(1)}, u32[]{:S(2)}, u32[]{:S(2)}) collective-permute-start(bf16[1,16,5,8,256]{4,1,3,2,0:T(8,128)(2,1)S(1)} %pad_maximum_fusion.4), channel_id=1, source_target_pairs={{0,16},{1,17},{2,18},{3,19},{4,20},{5,21},{6,22},{7,23},{8,24},{9,... | collective-permute-start | bytes 983048 | tf_op jit(solution)/shard_map/ppermute | solution.py:71
  73.2 13.8 %collective-permute-done.4 = bf16[1,16,5,8,256]{4,1,3,2,0:T(8,128)(2,1)S(1)} collective-permute-done((bf16[1,16,5,8,256]{4,1,3,2,0:T(8,128)(2,1)S(1)}, bf16[1,16,5,8,256]{4,1,3,2,0:T(8,128)(2,1)S(1)}, u32[]{:S(2)}, u32[]{:S(2)}) %collective-permute-start.4) | collective-permute-done | bytes 327712 | tf_op jit(solution)/shard_map/ppermute | solution.py:71
  87.1 7.7 %collective-permute-start.5 = (bf16[1,16,5,8,256]{4,1,3,2,0:T(8,128)(2,1)S(1)}, bf16[1,16,5,8,256]{4,1,3,2,0:T(8,128)(2,1)S(1)}, u32[]{:S(2)}, u32[]{:S(2)}) collective-permute-start(bf16[1,16,5,8,256]{4,1,3,2,0:T(8,128)(2,1)S(1)} %pad_maximum_fusion.5), channel_id=1, source_target_pairs={{0,32},{1,33},{2,34},{3,35},{4,36},{5,37},{6,38},{7,39},{8,40},{9,... | collective-permute-start | bytes 983048 | tf_op jit(solution)/shard_map/ppermute | solution.py:71
  100.6 5.6 %collective-permute-done.5 = bf16[1,16,5,8,256]{4,1,3,2,0:T(8,128)(2,1)S(1)} collective-permute-done((bf16[1,16,5,8,256]{4,1,3,2,0:T(8,128)(2,1)S(1)}, bf16[1,16,5,8,256]{4,1,3,2,0:T(8,128)(2,1)S(1)}, u32[]{:S(2)}, u32[]{:S(2)}) %collective-permute-start.5) | collective-permute-done | bytes 327712 | tf_op jit(solution)/shard_map/ppermute | solution.py:71
  120.9 1.9 collective-permute-start.8
  122.8 4.0 %collective-permute-start.9 = (f32[6928]{0:T(1024)S(1)}, f32[6928]{0:T(1024)S(1)}, u32[]{:S(2)}, u32[]{:S(2)}) collective-permute-start(f32[6928]{0:T(1024)S(1)} %pad_maximum_fusion.22), channel_id=1, source_target_pairs={{0,128},{64,192},{128,0},{192,64},{256,384},{320,448},{384,256},{4... | collective-permute-start | bytes 83144 | tf_op jit(solution)/shard_map/ppermute | solution.py:29
  126.9 2.0 collective-permute-start.10
  129.0 2.7 %collective-permute-start.6 = (bf16[1,16,1,8,256]{4,1,3,2,0:T(8,128)(2,1)S(1)}, bf16[1,16,1,8,256]{4,1,3,2,0:T(8,128)(2,1)S(1)}, u32[]{:S(2)}, u32[]{:S(2)}) collective-permute-start(bf16[1,16,1,8,256]{4,1,3,2,0:T(8,128)(2,1)S(1)} %get-tuple-element.130), channel_id=1, source_target_pairs={{0,63},{1,0},{2,1},{3,2},{4,3},{5,4},{6,5},{7,6},{8,7},{9,8},{10,9... | collective-permute-start | bytes 196616 | tf_op jit(solution)/shard_map/ppermute | solution.py:19
  131.7 5.2 %collective-permute-start.7 = (bf16[1,16,1,8,256]{4,1,3,2,0:T(8,128)(2,1)S(1)}, bf16[1,16,1,8,256]{4,1,3,2,0:T(8,128)(2,1)S(1)}, u32[]{:S(2)}, u32[]{:S(2)}) collective-permute-start(bf16[1,16,1,8,256]{4,1,3,2,0:T(8,128)(2,1)S(1)} %get-tuple-element.131), channel_id=1, source_target_pairs={{0,1},{1,2},{2,3},{3,4},{4,5},{5,6},{6,7},{7,8},{8,9},{9,10},{10,1... | collective-permute-start | bytes 196616 | tf_op jit(solution)/shard_map/ppermute | solution.py:19
  137.3 4.6 %collective-permute-start.11 = (f32[6928]{0:T(1024)S(1)}, f32[6928]{0:T(1024)S(1)}, u32[]{:S(2)}, u32[]{:S(2)}) collective-permute-start(f32[6928]{0:T(1024)S(1)} %add_reduce_fusion), channel_id=1, source_target_pairs={{0,256},{64,320},{128,384},{192,448},{256,0},{320,64},{384,128},{4... | collective-permute-start | bytes 83144 | tf_op jit(solution)/shard_map/ppermute | solution.py:39
  142.8 1.5 collective-permute-done.11
  144.2 1.9 collective-permute-start.12
  146.2 12.5 %collective-permute-start.13 = (f32[6928]{0:T(1024)S(1)}, f32[6928]{0:T(1024)S(1)}, u32[]{:S(2)}, u32[]{:S(2)}) collective-permute-start(f32[6928]{0:T(1024)S(1)} %add.625), channel_id=1, source_target_pairs={{0,2},{1,3},{2,0},{3,1},{4,6},{5,7},{6,4},{7,5},{8,10},{9,11},{10,... | collective-permute-start | bytes 83144 | tf_op jit(solution)/shard_map/ppermute | solution.py:29
  158.6 2.1 collective-permute-start.14
  169.1 1.9 collective-permute-start.15
  171.0 2.6 %collective-permute-start.16 = (f32[6928]{0:T(1024)S(1)}, f32[6928]{0:T(1024)S(1)}, u32[]{:S(2)}, u32[]{:S(2)}) collective-permute-start(f32[6928]{0:T(1024)S(1)} %get-tuple-element.38), channel_id=1, source_target_pairs={{0,8},{1,9},{2,10},{3,11},{4,12},{5,13},{6,14},{7,15},{8,0},{9,1},... | collective-permute-start | bytes 83144 | tf_op jit(solution)/shard_map/ppermute | solution.py:29
  173.6 5.6 %collective-permute-start.17 = (f32[6928]{0:T(1024)S(1)}, f32[6928]{0:T(1024)S(1)}, u32[]{:S(2)}, u32[]{:S(2)}) collective-permute-start(f32[6928]{0:T(1024)S(1)} %get-tuple-element.38), channel_id=1, source_target_pairs={{0,12},{1,13},{2,14},{3,15},{4,8},{5,9},{6,10},{7,11},{8,4},{9,5},... | collective-permute-start | bytes 83144 | tf_op jit(solution)/shard_map/ppermute | solution.py:29
  179.6 1.6 collective-permute-done.17
  181.5 11.5 %collective-permute-start.18 = (f32[6928]{0:T(1024)S(1)}, f32[6928]{0:T(1024)S(1)}, u32[]{:S(2)}, u32[]{:S(2)}) collective-permute-start(f32[6928]{0:T(1024)S(1)} %get-tuple-element.36), channel_id=1, source_target_pairs={{0,16},{1,17},{2,18},{3,19},{4,20},{5,21},{6,22},{7,23},{8,24},{9,... | collective-permute-start | bytes 83144 | tf_op jit(solution)/shard_map/ppermute | solution.py:29
  193.0 6.7 %collective-permute-start.19 = (f32[6928]{0:T(1024)S(1)}, f32[6928]{0:T(1024)S(1)}, u32[]{:S(2)}, u32[]{:S(2)}) collective-permute-start(f32[6928]{0:T(1024)S(1)} %get-tuple-element.36), channel_id=1, source_target_pairs={{0,32},{1,33},{2,34},{3,35},{4,36},{5,37},{6,38},{7,39},{8,40},{9,... | collective-permute-start | bytes 83144 | tf_op jit(solution)/shard_map/ppermute | solution.py:29
  199.7 2.5 %collective-permute-start.20 = (f32[6928]{0:T(1024)S(1)}, f32[6928]{0:T(1024)S(1)}, u32[]{:S(2)}, u32[]{:S(2)}) collective-permute-start(f32[6928]{0:T(1024)S(1)} %get-tuple-element.36), channel_id=1, source_target_pairs={{0,48},{1,49},{2,50},{3,51},{4,52},{5,53},{6,54},{7,55},{8,56},{9,... | collective-permute-start | bytes 83144 | tf_op jit(solution)/shard_map/ppermute | solution.py:29
  203.3 10.9 %collective-permute-done.20 = f32[6928]{0:T(1024)S(1)} collective-permute-done((f32[6928]{0:T(1024)S(1)}, f32[6928]{0:T(1024)S(1)}, u32[]{:S(2)}, u32[]{:S(2)}) %collective-permute-start.20) | collective-permute-done | bytes 27744 | tf_op jit(solution)/shard_map/ppermute | solution.py:29
  (215 shorter events, 34.7 us)
Async XLA Ops:
  7.2 0.7 copy-start.2
  12.2 11.3 %collective-permute-start = (bf16[1,16,5,8,256]{4,1,3,2,0:T(8,128)(2,1)S(1)}, bf16[1,16,5,8,256]{4,1,3,2,0:T(8,128)(2,1)S(1)}, u32[]{:S(2)}, u32[]{:S(2)}) collective-permute-start(bf16[1,16,5,8,256]{4,1,3,2,0:T(8,128)(2,1)S(1)} %pad_maximum_fusion), channel_id=1, source_target_pairs={{0,1},{1,0},{2,3},{3,2},{4,5},{5,4},{6,7},{7,6},{8,9},{9,8},{10,11... | collective-permute-start | bytes 983048 | tf_op jit(solution)/shard_map/ppermute | solution.py:71
  23.7 12.0 %collective-permute-start.1 = (bf16[1,16,5,8,256]{4,1,3,2,0:T(8,128)(2,1)S(1)}, bf16[1,16,5,8,256]{4,1,3,2,0:T(8,128)(2,1)S(1)}, u32[]{:S(2)}, u32[]{:S(2)}) collective-permute-start(bf16[1,16,5,8,256]{4,1,3,2,0:T(8,128)(2,1)S(1)} %pad_maximum_fusion.1), channel_id=1, source_target_pairs={{0,2},{1,3},{2,0},{3,1},{4,6},{5,7},{6,4},{7,5},{8,10},{9,11},{10,... | collective-permute-start | bytes 983048 | tf_op jit(solution)/shard_map/ppermute | solution.py:71
  35.7 10.2 %collective-permute-start.2 = (bf16[1,16,5,8,256]{4,1,3,2,0:T(8,128)(2,1)S(1)}, bf16[1,16,5,8,256]{4,1,3,2,0:T(8,128)(2,1)S(1)}, u32[]{:S(2)}, u32[]{:S(2)}) collective-permute-start(bf16[1,16,5,8,256]{4,1,3,2,0:T(8,128)(2,1)S(1)} %pad_maximum_fusion.2), channel_id=1, source_target_pairs={{0,4},{1,5},{2,6},{3,7},{4,0},{5,1},{6,2},{7,3},{8,12},{9,13},{10,... | collective-permute-start | bytes 983048 | tf_op jit(solution)/shard_map/ppermute | solution.py:71
  46.0 18.4 %collective-permute-start.3 = (bf16[1,16,5,8,256]{4,1,3,2,0:T(8,128)(2,1)S(1)}, bf16[1,16,5,8,256]{4,1,3,2,0:T(8,128)(2,1)S(1)}, u32[]{:S(2)}, u32[]{:S(2)}) collective-permute-start(bf16[1,16,5,8,256]{4,1,3,2,0:T(8,128)(2,1)S(1)} %pad_maximum_fusion.3), channel_id=1, source_target_pairs={{0,8},{1,9},{2,10},{3,11},{4,12},{5,13},{6,14},{7,15},{8,0},{9,1},... | collective-permute-start | bytes 983048 | tf_op jit(solution)/shard_map/ppermute | solution.py:71
  64.5 22.5 %collective-permute-start.4 = (bf16[1,16,5,8,256]{4,1,3,2,0:T(8,128)(2,1)S(1)}, bf16[1,16,5,8,256]{4,1,3,2,0:T(8,128)(2,1)S(1)}, u32[]{:S(2)}, u32[]{:S(2)}) collective-permute-start(bf16[1,16,5,8,256]{4,1,3,2,0:T(8,128)(2,1)S(1)} %pad_maximum_fusion.4), channel_id=1, source_target_pairs={{0,16},{1,17},{2,18},{3,19},{4,20},{5,21},{6,22},{7,23},{8,24},{9,... | collective-permute-start | bytes 983048 | tf_op jit(solution)/shard_map/ppermute | solution.py:71
  87.0 7.8 %copy-start = (bf16[27,16,16]{0,2,1:T(8,128)(2,1)S(1)}, bf16[27,16,16]{0,2,1:T(8,128)(2,1)}, u32[]{:S(2)}) copy-start(bf16[27,16,16]{0,2,1:T(8,128)(2,1)} %param.13) | copy-start | bytes 41476
  87.1 19.1 %collective-permute-start.5 = (bf16[1,16,5,8,256]{4,1,3,2,0:T(8,128)(2,1)S(1)}, bf16[1,16,5,8,256]{4,1,3,2,0:T(8,128)(2,1)S(1)}, u32[]{:S(2)}, u32[]{:S(2)}) collective-permute-start(bf16[1,16,5,8,256]{4,1,3,2,0:T(8,128)(2,1)S(1)} %pad_maximum_fusion.5), channel_id=1, source_target_pairs={{0,32},{1,33},{2,34},{3,35},{4,36},{5,37},{6,38},{7,39},{8,40},{9,... | collective-permute-start | bytes 983048 | tf_op jit(solution)/shard_map/ppermute | solution.py:71
  112.9 0.9 copy-start.1
  113.1 0.7 copy-start.3
  120.9 16.0 %collective-permute-start.8 = (f32[6928]{0:T(1024)S(1)}, f32[6928]{0:T(1024)S(1)}, u32[]{:S(2)}, u32[]{:S(2)}) collective-permute-start(f32[6928]{0:T(1024)S(1)} %pad_maximum_fusion.22), channel_id=1, source_target_pairs={{0,64},{64,0},{128,192},{192,128},{256,320},{320,256},{384,448},{4... | collective-permute-start | bytes 83144 | tf_op jit(solution)/shard_map/ppermute | solution.py:29
  122.8 14.1 %collective-permute-start.9 = (f32[6928]{0:T(1024)S(1)}, f32[6928]{0:T(1024)S(1)}, u32[]{:S(2)}, u32[]{:S(2)}) collective-permute-start(f32[6928]{0:T(1024)S(1)} %pad_maximum_fusion.22), channel_id=1, source_target_pairs={{0,128},{64,192},{128,0},{192,64},{256,384},{320,448},{384,256},{4... | collective-permute-start | bytes 83144 | tf_op jit(solution)/shard_map/ppermute | solution.py:29
  126.9 10.1 %collective-permute-start.10 = (f32[6928]{0:T(1024)S(1)}, f32[6928]{0:T(1024)S(1)}, u32[]{:S(2)}, u32[]{:S(2)}) collective-permute-start(f32[6928]{0:T(1024)S(1)} %pad_maximum_fusion.22), channel_id=1, source_target_pairs={{0,192},{64,128},{128,64},{192,0},{256,448},{320,384},{384,320},{4... | collective-permute-start | bytes 83144 | tf_op jit(solution)/shard_map/ppermute | solution.py:29
  129.0 31.8 %collective-permute-start.6 = (bf16[1,16,1,8,256]{4,1,3,2,0:T(8,128)(2,1)S(1)}, bf16[1,16,1,8,256]{4,1,3,2,0:T(8,128)(2,1)S(1)}, u32[]{:S(2)}, u32[]{:S(2)}) collective-permute-start(bf16[1,16,1,8,256]{4,1,3,2,0:T(8,128)(2,1)S(1)} %get-tuple-element.130), channel_id=1, source_target_pairs={{0,63},{1,0},{2,1},{3,2},{4,3},{5,4},{6,5},{7,6},{8,7},{9,8},{10,9... | collective-permute-start | bytes 196616 | tf_op jit(solution)/shard_map/ppermute | solution.py:19
  131.7 29.1 %collective-permute-start.7 = (bf16[1,16,1,8,256]{4,1,3,2,0:T(8,128)(2,1)S(1)}, bf16[1,16,1,8,256]{4,1,3,2,0:T(8,128)(2,1)S(1)}, u32[]{:S(2)}, u32[]{:S(2)}) collective-permute-start(bf16[1,16,1,8,256]{4,1,3,2,0:T(8,128)(2,1)S(1)} %get-tuple-element.131), channel_id=1, source_target_pairs={{0,1},{1,2},{2,3},{3,4},{4,5},{5,6},{6,7},{7,8},{8,9},{9,10},{10,1... | collective-permute-start | bytes 196616 | tf_op jit(solution)/shard_map/ppermute | solution.py:19
  137.3 6.9 %collective-permute-start.11 = (f32[6928]{0:T(1024)S(1)}, f32[6928]{0:T(1024)S(1)}, u32[]{:S(2)}, u32[]{:S(2)}) collective-permute-start(f32[6928]{0:T(1024)S(1)} %add_reduce_fusion), channel_id=1, source_target_pairs={{0,256},{64,320},{128,384},{192,448},{256,0},{320,64},{384,128},{4... | collective-permute-start | bytes 83144 | tf_op jit(solution)/shard_map/ppermute | solution.py:39
  144.2 24.5 %collective-permute-start.12 = (f32[6928]{0:T(1024)S(1)}, f32[6928]{0:T(1024)S(1)}, u32[]{:S(2)}, u32[]{:S(2)}) collective-permute-start(f32[6928]{0:T(1024)S(1)} %add.625), channel_id=1, source_target_pairs={{0,1},{1,0},{2,3},{3,2},{4,5},{5,4},{6,7},{7,6},{8,9},{9,8},{10,11... | collective-permute-start | bytes 83144 | tf_op jit(solution)/shard_map/ppermute | solution.py:29
  146.2 22.6 %collective-permute-start.13 = (f32[6928]{0:T(1024)S(1)}, f32[6928]{0:T(1024)S(1)}, u32[]{:S(2)}, u32[]{:S(2)}) collective-permute-start(f32[6928]{0:T(1024)S(1)} %add.625), channel_id=1, source_target_pairs={{0,2},{1,3},{2,0},{3,1},{4,6},{5,7},{6,4},{7,5},{8,10},{9,11},{10,... | collective-permute-start | bytes 83144 | tf_op jit(solution)/shard_map/ppermute | solution.py:29
  158.6 10.1 %collective-permute-start.14 = (f32[6928]{0:T(1024)S(1)}, f32[6928]{0:T(1024)S(1)}, u32[]{:S(2)}, u32[]{:S(2)}) collective-permute-start(f32[6928]{0:T(1024)S(1)} %add.625), channel_id=1, source_target_pairs={{0,3},{1,2},{2,1},{3,0},{4,7},{5,6},{6,5},{7,4},{8,11},{9,10},{10,... | collective-permute-start | bytes 83144 | tf_op jit(solution)/shard_map/ppermute | solution.py:29
  169.1 10.4 %collective-permute-start.15 = (f32[6928]{0:T(1024)S(1)}, f32[6928]{0:T(1024)S(1)}, u32[]{:S(2)}, u32[]{:S(2)}) collective-permute-start(f32[6928]{0:T(1024)S(1)} %get-tuple-element.38), channel_id=1, source_target_pairs={{0,4},{1,5},{2,6},{3,7},{4,0},{5,1},{6,2},{7,3},{8,12},{9,13},{10,... | collective-permute-start | bytes 83144 | tf_op jit(solution)/shard_map/ppermute | solution.py:29
  171.0 8.5 %collective-permute-start.16 = (f32[6928]{0:T(1024)S(1)}, f32[6928]{0:T(1024)S(1)}, u32[]{:S(2)}, u32[]{:S(2)}) collective-permute-start(f32[6928]{0:T(1024)S(1)} %get-tuple-element.38), channel_id=1, source_target_pairs={{0,8},{1,9},{2,10},{3,11},{4,12},{5,13},{6,14},{7,15},{8,0},{9,1},... | collective-permute-start | bytes 83144 | tf_op jit(solution)/shard_map/ppermute | solution.py:29
  173.6 7.6 %collective-permute-start.17 = (f32[6928]{0:T(1024)S(1)}, f32[6928]{0:T(1024)S(1)}, u32[]{:S(2)}, u32[]{:S(2)}) collective-permute-start(f32[6928]{0:T(1024)S(1)} %get-tuple-element.38), channel_id=1, source_target_pairs={{0,12},{1,13},{2,14},{3,15},{4,8},{5,9},{6,10},{7,11},{8,4},{9,5},... | collective-permute-start | bytes 83144 | tf_op jit(solution)/shard_map/ppermute | solution.py:29
  181.5 21.7 %collective-permute-start.18 = (f32[6928]{0:T(1024)S(1)}, f32[6928]{0:T(1024)S(1)}, u32[]{:S(2)}, u32[]{:S(2)}) collective-permute-start(f32[6928]{0:T(1024)S(1)} %get-tuple-element.36), channel_id=1, source_target_pairs={{0,16},{1,17},{2,18},{3,19},{4,20},{5,21},{6,22},{7,23},{8,24},{9,... | collective-permute-start | bytes 83144 | tf_op jit(solution)/shard_map/ppermute | solution.py:29
  193.0 10.2 %collective-permute-start.19 = (f32[6928]{0:T(1024)S(1)}, f32[6928]{0:T(1024)S(1)}, u32[]{:S(2)}, u32[]{:S(2)}) collective-permute-start(f32[6928]{0:T(1024)S(1)} %get-tuple-element.36), channel_id=1, source_target_pairs={{0,32},{1,33},{2,34},{3,35},{4,36},{5,37},{6,38},{7,39},{8,40},{9,... | collective-permute-start | bytes 83144 | tf_op jit(solution)/shard_map/ppermute | solution.py:29
  199.7 14.5 %collective-permute-start.20 = (f32[6928]{0:T(1024)S(1)}, f32[6928]{0:T(1024)S(1)}, u32[]{:S(2)}, u32[]{:S(2)}) collective-permute-start(f32[6928]{0:T(1024)S(1)} %get-tuple-element.36), channel_id=1, source_target_pairs={{0,48},{1,49},{2,50},{3,51},{4,52},{5,53},{6,54},{7,55},{8,56},{9,... | collective-permute-start | bytes 83144 | tf_op jit(solution)/shard_map/ppermute | solution.py:29

commit v2 on v0

--- a/solution.py
+++ b/solution.py
@@ -68,9 +68,8 @@
     planes = features.shape[2]
     devices_x = lax.axis_size("gx")
     length_x = planes * devices_x
-    local = jax.vmap(augment_local)(features, offsets, flip_bits)
     flip_x = flip_bits[0, 0] == 1
-    block = jnp.where(flip_x, jnp.flip(local, 2), local)
+    block = jnp.where(flip_x, jnp.flip(features, 2), features)
     effective = jnp.where(flip_x, jnp.mod(-offsets[0, 0], length_x), offsets[0, 0])
     coarse_steps = effective // planes
     remain = effective % planes
@@ -78,9 +77,10 @@
     constant = jnp.where(flip_x, devices_x - 1 + coarse_steps, coarse_steps)
     coarse = routed(block, "gx", sign, constant)
     before = shifted(coarse, "gx", 1)
-    after = shifted(coarse, "gx", -1)
+    after = shifted(coarse[:, :, 0:1], "gx", -1)
     joined = jnp.concatenate([before, coarse, after], axis=2)
-    padded = lax.dynamic_slice_in_dim(joined, planes - 1 - remain, planes + 2, axis=2)
+    window = lax.dynamic_slice_in_dim(joined, planes - 1 - remain, planes + 2, axis=2)
+    padded = jax.vmap(augment_local)(window, offsets, flip_bits)
 
     taps = len(tap_offsets)
     channels = features.shape[1]

time: 189 us -> 184 us (0.974)
  waiting for transfers between devices: 67.8 us -> 55.4 us
  starting transfers between devices: 74.7 us -> 80.3 us
    ppermute x4, waiting for transfers between devices: 12.9 us -> 0.01 us  [shifted(): return lax.ppermute(value, axis, pairs)]
    ppermute x4, starting transfers between devices: 21.2 us -> 26.7 us  [shifted(): return lax.ppermute(value, axis, pairs)]
  transfers between devices with their start and end apart: 19 -> 19, of which waited for: 14 -> 12; matrix products, arithmetic and copies ran while one was open for 8% -> 9% of each run, Pallas kernels for 0% -> 0%
where the time goes in v2:
time: 184 us; the launch traced here: 183 us
  starting transfers between devices  80.3 us (44%)
  waiting for transfers between devices  55.4 us (30%)
  matrix products  18.9 us (10%)
  local copies, waits for them, and re-layouts  13.8 us (8%)
  between operations  11.6 us (6%)
  other arithmetic  2.99 us (2%)
    ppermute x9, waiting for transfers between devices, butterfly_sum(): value = value + lax.ppermute(value, axis, pairs)  32.3 us
    ppermute x6, starting transfers between devices, routed(): value = jnp.where(swap, lax.ppermute(value, axis, pairs), value)  29.1 us
    ppermute x4, starting transfers between devices, shifted(): return lax.ppermute(value, axis, pairs)  26.7 us
    ppermute x9, starting transfers between devices, butterfly_sum(): value = value + lax.ppermute(value, axis, pairs)  24.6 us
    ppermute x6, waiting for transfers between devices, routed(): value = jnp.where(swap, lax.ppermute(value, axis, pairs), value)  23 us
    unnamed x39, local copies, waits for them, and re-layouts  9.39 us
    dot_general x27, matrix products, on_device(): jnp.einsum('oi,boxyz->bixyz', weight[tap_index], moved_grad, preferred_el...  6.57 us
    dot_general x27, matrix products, on_device(): jnp.einsum('boxyz,bixyz->oi', grad_pre, window, preferred_element_type=jn...  6.19 us
  transfers between devices with their start and end apart: 19, of which 12 were waited for; matrix products, arithmetic and copies ran while one was open for 9% of the time, Pallas kernels for 0%

profile of v2, /device:TPU:2, one launch (start us, length us, event | category | flops | bytes accessed | tf_op | source)
XLA Modules:
  0.0 182.9 jit_solution(17735264612924492396)
XLA Ops:
  0.6 1.4 fusion.381
  3.6 7.8 %collective-permute-start = (bf16[1,16,2,8,256]{4,1,3,2,0:T(8,128)(2,1)S(1)}, bf16[1,16,2,8,256]{4,1,3,2,0:T(8,128)(2,1)S(1)}, u32[]{:S(2)}, u32[]{:S(2)}) collective-permute-start(bf16[1,16,2,8,256]{4,1,3,2,0:T(8,128)(2,1)S(1)} %reverse_select_fusion), channel_id=1, source_target_pairs={{0,1},{1,0},{2,3},{3,2},{4,5},{5,4},{6,7},{7,6},{8,9},{9,8},{10,11... | collective-permute-start | bytes 393224 | tf_op jit(solution)/shard_map/ppermute | solution.py:62
  14.8 1.9 %collective-permute-start.1 = (bf16[1,16,2,8,256]{4,1,3,2,0:T(8,128)(2,1)S(1)}, bf16[1,16,2,8,256]{4,1,3,2,0:T(8,128)(2,1)S(1)}, u32[]{:S(2)}, u32[]{:S(2)}) collective-permute-start(bf16[1,16,2,8,256]{4,1,3,2,0:T(8,128)(2,1)S(1)} %broadcast_select_fusion), channel_id=1, source_target_pairs={{0,2},{1,3},{2,0},{3,1},{4,6},{5,7},{6,4},{7,5},{8,10},{9,11},{10,... | collective-permute-start | bytes 393224 | tf_op jit(solution)/shard_map/ppermute | solution.py:62
  16.9 6.3 %collective-permute-done.1 = bf16[1,16,2,8,256]{4,1,3,2,0:T(8,128)(2,1)S(1)} collective-permute-done((bf16[1,16,2,8,256]{4,1,3,2,0:T(8,128)(2,1)S(1)}, bf16[1,16,2,8,256]{4,1,3,2,0:T(8,128)(2,1)S(1)}, u32[]{:S(2)}, u32[]{:S(2)}) %collective-permute-start.1) | collective-permute-done | bytes 131104 | tf_op jit(solution)/shard_map/ppermute | solution.py:62
  23.2 1.9 %collective-permute-start.2 = (bf16[1,16,2,8,256]{4,1,3,2,0:T(8,128)(2,1)S(1)}, bf16[1,16,2,8,256]{4,1,3,2,0:T(8,128)(2,1)S(1)}, u32[]{:S(2)}, u32[]{:S(2)}) collective-permute-start(bf16[1,16,2,8,256]{4,1,3,2,0:T(8,128)(2,1)S(1)} %broadcast_select_fusion.1), channel_id=1, source_target_pairs={{0,4},{1,5},{2,6},{3,7},{4,0},{5,1},{6,2},{7,3},{8,12},{9,13},{10,... | collective-permute-start | bytes 393224 | tf_op jit(solution)/shard_map/ppermute | solution.py:62
  25.3 4.8 %collective-permute-done.2 = bf16[1,16,2,8,256]{4,1,3,2,0:T(8,128)(2,1)S(1)} collective-permute-done((bf16[1,16,2,8,256]{4,1,3,2,0:T(8,128)(2,1)S(1)}, bf16[1,16,2,8,256]{4,1,3,2,0:T(8,128)(2,1)S(1)}, u32[]{:S(2)}, u32[]{:S(2)}) %collective-permute-start.2) | collective-permute-done | bytes 131104 | tf_op jit(solution)/shard_map/ppermute | solution.py:62
  30.1 2.4 %collective-permute-start.3 = (bf16[1,16,2,8,256]{4,1,3,2,0:T(8,128)(2,1)S(1)}, bf16[1,16,2,8,256]{4,1,3,2,0:T(8,128)(2,1)S(1)}, u32[]{:S(2)}, u32[]{:S(2)}) collective-permute-start(bf16[1,16,2,8,256]{4,1,3,2,0:T(8,128)(2,1)S(1)} %broadcast_select_fusion.2), channel_id=1, source_target_pairs={{0,8},{1,9},{2,10},{3,11},{4,12},{5,13},{6,14},{7,15},{8,0},{9,1},... | collective-permute-start | bytes 393224 | tf_op jit(solution)/shard_map/ppermute | solution.py:62
  32.7 6.0 %collective-permute-done.3 = bf16[1,16,2,8,256]{4,1,3,2,0:T(8,128)(2,1)S(1)} collective-permute-done((bf16[1,16,2,8,256]{4,1,3,2,0:T(8,128)(2,1)S(1)}, bf16[1,16,2,8,256]{4,1,3,2,0:T(8,128)(2,1)S(1)}, u32[]{:S(2)}, u32[]{:S(2)}) %collective-permute-start.3) | collective-permute-done | bytes 131104 | tf_op jit(solution)/shard_map/ppermute | solution.py:62
  38.7 7.6 %collective-permute-start.4 = (bf16[1,16,2,8,256]{4,1,3,2,0:T(8,128)(2,1)S(1)}, bf16[1,16,2,8,256]{4,1,3,2,0:T(8,128)(2,1)S(1)}, u32[]{:S(2)}, u32[]{:S(2)}) collective-permute-start(bf16[1,16,2,8,256]{4,1,3,2,0:T(8,128)(2,1)S(1)} %broadcast_select_fusion.3), channel_id=1, source_target_pairs={{0,16},{1,17},{2,18},{3,19},{4,20},{5,21},{6,22},{7,23},{8,24},{9,... | collective-permute-start | bytes 393224 | tf_op jit(solution)/shard_map/ppermute | solution.py:62
  46.6 2.9 %collective-permute-done.4 = bf16[1,16,2,8,256]{4,1,3,2,0:T(8,128)(2,1)S(1)} collective-permute-done((bf16[1,16,2,8,256]{4,1,3,2,0:T(8,128)(2,1)S(1)}, bf16[1,16,2,8,256]{4,1,3,2,0:T(8,128)(2,1)S(1)}, u32[]{:S(2)}, u32[]{:S(2)}) %collective-permute-start.4) | collective-permute-done | bytes 131104 | tf_op jit(solution)/shard_map/ppermute | solution.py:62
  49.5 7.5 %collective-permute-start.5 = (bf16[1,16,2,8,256]{4,1,3,2,0:T(8,128)(2,1)S(1)}, bf16[1,16,2,8,256]{4,1,3,2,0:T(8,128)(2,1)S(1)}, u32[]{:S(2)}, u32[]{:S(2)}) collective-permute-start(bf16[1,16,2,8,256]{4,1,3,2,0:T(8,128)(2,1)S(1)} %broadcast_select_fusion.4), channel_id=1, source_target_pairs={{0,32},{1,33},{2,34},{3,35},{4,36},{5,37},{6,38},{7,39},{8,40},{9,... | collective-permute-start | bytes 393224 | tf_op jit(solution)/shard_map/ppermute | solution.py:62
  57.4 3.0 %collective-permute-done.5 = bf16[1,16,2,8,256]{4,1,3,2,0:T(8,128)(2,1)S(1)} collective-permute-done((bf16[1,16,2,8,256]{4,1,3,2,0:T(8,128)(2,1)S(1)}, bf16[1,16,2,8,256]{4,1,3,2,0:T(8,128)(2,1)S(1)}, u32[]{:S(2)}, u32[]{:S(2)}) %collective-permute-start.5) | collective-permute-done | bytes 131104 | tf_op jit(solution)/shard_map/ppermute | solution.py:62
  60.4 3.9 %collective-permute-start.6 = (bf16[1,16,2,8,256]{4,1,3,2,0:T(8,128)(2,1)S(1)}, bf16[1,16,2,8,256]{4,1,3,2,0:T(8,128)(2,1)S(1)}, u32[]{:S(2)}, u32[]{:S(2)}) collective-permute-start(bf16[1,16,2,8,256]{4,1,3,2,0:T(8,128)(2,1)S(1)} %broadcast_select_fusion.5), channel_id=1, source_target_pairs={{0,1},{1,2},{2,3},{3,4},{4,5},{5,6},{6,7},{7,8},{8,9},{9,10},{10,1... | collective-permute-start | bytes 393224 | tf_op jit(solution)/shard_map/ppermute | solution.py:19
  64.3 2.3 %collective-permute-start.7 = (bf16[1,16,1,8,256]{4,1,3,2,0:T(8,128)(2,1)S(1)}, bf16[1,16,1,8,256]{4,1,3,2,0:T(8,128)(2,1)S(1)}, u32[]{:S(2)}, u32[]{:S(2)}) collective-permute-start(bf16[1,16,1,8,256]{4,1,3,2,0:T(8,128)(2,1)S(1)} %slice.889), channel_id=1, source_target_pairs={{0,63},{1,0},{2,1},{3,2},{4,3},{5,4},{6,5},{7,6},{8,7},{9,8},{10,9... | collective-permute-start | bytes 196616 | tf_op jit(solution)/shard_map/ppermute | solution.py:19
  94.0 1.9 %collective-permute-start.10 = (f32[6928]{0:T(1024)S(1)}, f32[6928]{0:T(1024)S(1)}, u32[]{:S(2)}, u32[]{:S(2)}) collective-permute-start(f32[6928]{0:T(1024)S(1)} %pad_maximum_fusion.12), channel_id=1, source_target_pairs={{0,64},{64,0},{128,192},{192,128},{256,320},{320,256},{384,448},{4... | collective-permute-start | bytes 83144 | tf_op jit(solution)/shard_map/ppermute | solution.py:27
  95.9 18.6 %collective-permute-start.8 = (bf16[1,16,1,8,256]{4,1,3,2,0:T(8,128)(2,1)S(1)}, bf16[1,16,1,8,256]{4,1,3,2,0:T(8,128)(2,1)S(1)}, u32[]{:S(2)}, u32[]{:S(2)}) collective-permute-start(bf16[1,16,1,8,256]{4,1,3,2,0:T(8,128)(2,1)S(1)} %get-tuple-element.114), channel_id=1, source_target_pairs={{0,63},{1,0},{2,1},{3,2},{4,3},{5,4},{6,5},{7,6},{8,7},{9,8},{10,9... | collective-permute-start | bytes 196616 | tf_op jit(solution)/shard_map/ppermute | solution.py:19
  114.5 1.9 %collective-permute-start.9 = (bf16[1,16,1,8,256]{4,1,3,2,0:T(8,128)(2,1)S(1)}, bf16[1,16,1,8,256]{4,1,3,2,0:T(8,128)(2,1)S(1)}, u32[]{:S(2)}, u32[]{:S(2)}) collective-permute-start(bf16[1,16,1,8,256]{4,1,3,2,0:T(8,128)(2,1)S(1)} %get-tuple-element.115), channel_id=1, source_target_pairs={{0,1},{1,2},{2,3},{3,4},{4,5},{5,6},{6,7},{7,8},{8,9},{9,10},{10,1... | collective-permute-start | bytes 196616 | tf_op jit(solution)/shard_map/ppermute | solution.py:19
  116.5 1.9 %collective-permute-start.11 = (f32[6928]{0:T(1024)S(1)}, f32[6928]{0:T(1024)S(1)}, u32[]{:S(2)}, u32[]{:S(2)}) collective-permute-start(f32[6928]{0:T(1024)S(1)} %fusion.383), channel_id=1, source_target_pairs={{0,128},{64,192},{128,0},{192,64},{256,384},{320,448},{384,256},{4... | collective-permute-start | bytes 83144 | tf_op jit(solution)/shard_map/ppermute | solution.py:27
  119.1 3.1 %collective-permute-done.11 = f32[6928]{0:T(1024)S(1)} collective-permute-done((f32[6928]{0:T(1024)S(1)}, f32[6928]{0:T(1024)S(1)}, u32[]{:S(2)}, u32[]{:S(2)}) %collective-permute-start.11) | collective-permute-done | bytes 27744 | tf_op jit(solution)/shard_map/ppermute | solution.py:27
  122.2 2.1 %collective-permute-start.12 = (f32[6928]{0:T(1024)S(1)}, f32[6928]{0:T(1024)S(1)}, u32[]{:S(2)}, u32[]{:S(2)}) collective-permute-start(f32[6928]{0:T(1024)S(1)} %add.521), channel_id=1, source_target_pairs={{0,256},{64,320},{128,384},{192,448},{256,0},{320,64},{384,128},{4... | collective-permute-start | bytes 83144 | tf_op jit(solution)/shard_map/ppermute | solution.py:27
  131.5 9.1 %collective-permute-start.13 = (f32[6928]{0:T(1024)S(1)}, f32[6928]{0:T(1024)S(1)}, u32[]{:S(2)}, u32[]{:S(2)}) collective-permute-start(f32[6928]{0:T(1024)S(1)} %add.522), channel_id=1, source_target_pairs={{0,1},{1,0},{2,3},{3,2},{4,5},{5,4},{6,7},{7,6},{8,9},{9,8},{10,11... | collective-permute-start | bytes 83144 | tf_op jit(solution)/shard_map/ppermute | solution.py:27
  140.7 1.7 collective-permute-done.13
  142.4 1.9 %collective-permute-start.14 = (f32[6928]{0:T(1024)S(1)}, f32[6928]{0:T(1024)S(1)}, u32[]{:S(2)}, u32[]{:S(2)}) collective-permute-start(f32[6928]{0:T(1024)S(1)} %add.523), channel_id=1, source_target_pairs={{0,2},{1,3},{2,0},{3,1},{4,6},{5,7},{6,4},{7,5},{8,10},{9,11},{10,... | collective-permute-start | bytes 83144 | tf_op jit(solution)/shard_map/ppermute | solution.py:27
  144.6 5.1 %collective-permute-done.14 = f32[6928]{0:T(1024)S(1)} collective-permute-done((f32[6928]{0:T(1024)S(1)}, f32[6928]{0:T(1024)S(1)}, u32[]{:S(2)}, u32[]{:S(2)}) %collective-permute-start.14) | collective-permute-done | bytes 27744 | tf_op jit(solution)/shard_map/ppermute | solution.py:27
  149.7 1.9 %collective-permute-start.15 = (f32[6928]{0:T(1024)S(1)}, f32[6928]{0:T(1024)S(1)}, u32[]{:S(2)}, u32[]{:S(2)}) collective-permute-start(f32[6928]{0:T(1024)S(1)} %add.524), channel_id=1, source_target_pairs={{0,4},{1,5},{2,6},{3,7},{4,0},{5,1},{6,2},{7,3},{8,12},{9,13},{10,... | collective-permute-start | bytes 83144 | tf_op jit(solution)/shard_map/ppermute | solution.py:27
  151.8 3.6 %collective-permute-done.15 = f32[6928]{0:T(1024)S(1)} collective-permute-done((f32[6928]{0:T(1024)S(1)}, f32[6928]{0:T(1024)S(1)}, u32[]{:S(2)}, u32[]{:S(2)}) %collective-permute-start.15) | collective-permute-done | bytes 27744 | tf_op jit(solution)/shard_map/ppermute | solution.py:27
  155.4 1.9 %collective-permute-start.16 = (f32[6928]{0:T(1024)S(1)}, f32[6928]{0:T(1024)S(1)}, u32[]{:S(2)}, u32[]{:S(2)}) collective-permute-start(f32[6928]{0:T(1024)S(1)} %add.525), channel_id=1, source_target_pairs={{0,8},{1,9},{2,10},{3,11},{4,12},{5,13},{6,14},{7,15},{8,0},{9,1},... | collective-permute-start | bytes 83144 | tf_op jit(solution)/shard_map/ppermute | solution.py:27
  157.6 4.5 %collective-permute-done.16 = f32[6928]{0:T(1024)S(1)} collective-permute-done((f32[6928]{0:T(1024)S(1)}, f32[6928]{0:T(1024)S(1)}, u32[]{:S(2)}, u32[]{:S(2)}) %collective-permute-start.16) | collective-permute-done | bytes 27744 | tf_op jit(solution)/shard_map/ppermute | solution.py:27
  162.1 1.9 %collective-permute-start.17 = (f32[6928]{0:T(1024)S(1)}, f32[6928]{0:T(1024)S(1)}, u32[]{:S(2)}, u32[]{:S(2)}) collective-permute-start(f32[6928]{0:T(1024)S(1)} %add.526), channel_id=1, source_target_pairs={{0,16},{1,17},{2,18},{3,19},{4,20},{5,21},{6,22},{7,23},{8,24},{9,... | collective-permute-start | bytes 83144 | tf_op jit(solution)/shard_map/ppermute | solution.py:27
  164.3 7.5 %collective-permute-done.17 = f32[6928]{0:T(1024)S(1)} collective-permute-done((f32[6928]{0:T(1024)S(1)}, f32[6928]{0:T(1024)S(1)}, u32[]{:S(2)}, u32[]{:S(2)}) %collective-permute-start.17) | collective-permute-done | bytes 27744 | tf_op jit(solution)/shard_map/ppermute | solution.py:27
  171.8 1.9 %collective-permute-start.18 = (f32[6928]{0:T(1024)S(1)}, f32[6928]{0:T(1024)S(1)}, u32[]{:S(2)}, u32[]{:S(2)}) collective-permute-start(f32[6928]{0:T(1024)S(1)} %add.527), channel_id=1, source_target_pairs={{0,32},{1,33},{2,34},{3,35},{4,36},{5,37},{6,38},{7,39},{8,40},{9,... | collective-permute-start | bytes 83144 | tf_op jit(solution)/shard_map/ppermute | solution.py:27
  174.7 6.8 %collective-permute-done.18 = f32[6928]{0:T(1024)S(1)} collective-permute-done((f32[6928]{0:T(1024)S(1)}, f32[6928]{0:T(1024)S(1)}, u32[]{:S(2)}, u32[]{:S(2)}) %collective-permute-start.18) | collective-permute-done | bytes 27744 | tf_op jit(solution)/shard_map/ppermute | solution.py:27
  (184 shorter events, 34.3 us)
Async XLA Ops:
  3.6 11.1 %collective-permute-start = (bf16[1,16,2,8,256]{4,1,3,2,0:T(8,128)(2,1)S(1)}, bf16[1,16,2,8,256]{4,1,3,2,0:T(8,128)(2,1)S(1)}, u32[]{:S(2)}, u32[]{:S(2)}) collective-permute-start(bf16[1,16,2,8,256]{4,1,3,2,0:T(8,128)(2,1)S(1)} %reverse_select_fusion), channel_id=1, source_target_pairs={{0,1},{1,0},{2,3},{3,2},{4,5},{5,4},{6,7},{7,6},{8,9},{9,8},{10,11... | collective-permute-start | bytes 393224 | tf_op jit(solution)/shard_map/ppermute | solution.py:62
  11.5 0.7 copy-start.2
  14.8 8.4 %collective-permute-start.1 = (bf16[1,16,2,8,256]{4,1,3,2,0:T(8,128)(2,1)S(1)}, bf16[1,16,2,8,256]{4,1,3,2,0:T(8,128)(2,1)S(1)}, u32[]{:S(2)}, u32[]{:S(2)}) collective-permute-start(bf16[1,16,2,8,256]{4,1,3,2,0:T(8,128)(2,1)S(1)} %broadcast_select_fusion), channel_id=1, source_target_pairs={{0,2},{1,3},{2,0},{3,1},{4,6},{5,7},{6,4},{7,5},{8,10},{9,11},{10,... | collective-permute-start | bytes 393224 | tf_op jit(solution)/shard_map/ppermute | solution.py:62
  23.2 6.9 %collective-permute-start.2 = (bf16[1,16,2,8,256]{4,1,3,2,0:T(8,128)(2,1)S(1)}, bf16[1,16,2,8,256]{4,1,3,2,0:T(8,128)(2,1)S(1)}, u32[]{:S(2)}, u32[]{:S(2)}) collective-permute-start(bf16[1,16,2,8,256]{4,1,3,2,0:T(8,128)(2,1)S(1)} %broadcast_select_fusion.1), channel_id=1, source_target_pairs={{0,4},{1,5},{2,6},{3,7},{4,0},{5,1},{6,2},{7,3},{8,12},{9,13},{10,... | collective-permute-start | bytes 393224 | tf_op jit(solution)/shard_map/ppermute | solution.py:62
  30.1 8.6 %collective-permute-start.3 = (bf16[1,16,2,8,256]{4,1,3,2,0:T(8,128)(2,1)S(1)}, bf16[1,16,2,8,256]{4,1,3,2,0:T(8,128)(2,1)S(1)}, u32[]{:S(2)}, u32[]{:S(2)}) collective-permute-start(bf16[1,16,2,8,256]{4,1,3,2,0:T(8,128)(2,1)S(1)} %broadcast_select_fusion.2), channel_id=1, source_target_pairs={{0,8},{1,9},{2,10},{3,11},{4,12},{5,13},{6,14},{7,15},{8,0},{9,1},... | collective-permute-start | bytes 393224 | tf_op jit(solution)/shard_map/ppermute | solution.py:62
  38.7 10.8 %collective-permute-start.4 = (bf16[1,16,2,8,256]{4,1,3,2,0:T(8,128)(2,1)S(1)}, bf16[1,16,2,8,256]{4,1,3,2,0:T(8,128)(2,1)S(1)}, u32[]{:S(2)}, u32[]{:S(2)}) collective-permute-start(bf16[1,16,2,8,256]{4,1,3,2,0:T(8,128)(2,1)S(1)} %broadcast_select_fusion.3), channel_id=1, source_target_pairs={{0,16},{1,17},{2,18},{3,19},{4,20},{5,21},{6,22},{7,23},{8,24},{9,... | collective-permute-start | bytes 393224 | tf_op jit(solution)/shard_map/ppermute | solution.py:62
  49.5 7.5 %copy-start = (bf16[27,16,16]{0,2,1:T(8,128)(2,1)S(1)}, bf16[27,16,16]{0,2,1:T(8,128)(2,1)}, u32[]{:S(2)}) copy-start(bf16[27,16,16]{0,2,1:T(8,128)(2,1)} %param.13) | copy-start | bytes 41476
  49.5 10.9 %collective-permute-start.5 = (bf16[1,16,2,8,256]{4,1,3,2,0:T(8,128)(2,1)S(1)}, bf16[1,16,2,8,256]{4,1,3,2,0:T(8,128)(2,1)S(1)}, u32[]{:S(2)}, u32[]{:S(2)}) collective-permute-start(bf16[1,16,2,8,256]{4,1,3,2,0:T(8,128)(2,1)S(1)} %broadcast_select_fusion.4), channel_id=1, source_target_pairs={{0,32},{1,33},{2,34},{3,35},{4,36},{5,37},{6,38},{7,39},{8,40},{9,... | collective-permute-start | bytes 393224 | tf_op jit(solution)/shard_map/ppermute | solution.py:62
  60.4 17.8 %collective-permute-start.6 = (bf16[1,16,2,8,256]{4,1,3,2,0:T(8,128)(2,1)S(1)}, bf16[1,16,2,8,256]{4,1,3,2,0:T(8,128)(2,1)S(1)}, u32[]{:S(2)}, u32[]{:S(2)}) collective-permute-start(bf16[1,16,2,8,256]{4,1,3,2,0:T(8,128)(2,1)S(1)} %broadcast_select_fusion.5), channel_id=1, source_target_pairs={{0,1},{1,2},{2,3},{3,4},{4,5},{5,6},{6,7},{7,8},{8,9},{9,10},{10,1... | collective-permute-start | bytes 393224 | tf_op jit(solution)/shard_map/ppermute | solution.py:19
  64.3 13.9 %collective-permute-start.7 = (bf16[1,16,1,8,256]{4,1,3,2,0:T(8,128)(2,1)S(1)}, bf16[1,16,1,8,256]{4,1,3,2,0:T(8,128)(2,1)S(1)}, u32[]{:S(2)}, u32[]{:S(2)}) collective-permute-start(bf16[1,16,1,8,256]{4,1,3,2,0:T(8,128)(2,1)S(1)} %slice.889), channel_id=1, source_target_pairs={{0,63},{1,0},{2,1},{3,2},{4,3},{5,4},{6,5},{7,6},{8,7},{9,8},{10,9... | collective-permute-start | bytes 196616 | tf_op jit(solution)/shard_map/ppermute | solution.py:19
  85.9 0.9 copy-start.1
  86.2 0.7 copy-start.3
  94.0 22.5 %collective-permute-start.10 = (f32[6928]{0:T(1024)S(1)}, f32[6928]{0:T(1024)S(1)}, u32[]{:S(2)}, u32[]{:S(2)}) collective-permute-start(f32[6928]{0:T(1024)S(1)} %pad_maximum_fusion.12), channel_id=1, source_target_pairs={{0,64},{64,0},{128,192},{192,128},{256,320},{320,256},{384,448},{4... | collective-permute-start | bytes 83144 | tf_op jit(solution)/shard_map/ppermute | solution.py:27
  95.9 28.4 %collective-permute-start.8 = (bf16[1,16,1,8,256]{4,1,3,2,0:T(8,128)(2,1)S(1)}, bf16[1,16,1,8,256]{4,1,3,2,0:T(8,128)(2,1)S(1)}, u32[]{:S(2)}, u32[]{:S(2)}) collective-permute-start(bf16[1,16,1,8,256]{4,1,3,2,0:T(8,128)(2,1)S(1)} %get-tuple-element.114), channel_id=1, source_target_pairs={{0,63},{1,0},{2,1},{3,2},{4,3},{5,4},{6,5},{7,6},{8,7},{9,8},{10,9... | collective-permute-start | bytes 196616 | tf_op jit(solution)/shard_map/ppermute | solution.py:19
  114.5 9.8 %collective-permute-start.9 = (bf16[1,16,1,8,256]{4,1,3,2,0:T(8,128)(2,1)S(1)}, bf16[1,16,1,8,256]{4,1,3,2,0:T(8,128)(2,1)S(1)}, u32[]{:S(2)}, u32[]{:S(2)}) collective-permute-start(bf16[1,16,1,8,256]{4,1,3,2,0:T(8,128)(2,1)S(1)} %get-tuple-element.115), channel_id=1, source_target_pairs={{0,1},{1,2},{2,3},{3,4},{4,5},{5,6},{6,7},{7,8},{8,9},{9,10},{10,1... | collective-permute-start | bytes 196616 | tf_op jit(solution)/shard_map/ppermute | solution.py:19
  116.5 5.8 %collective-permute-start.11 = (f32[6928]{0:T(1024)S(1)}, f32[6928]{0:T(1024)S(1)}, u32[]{:S(2)}, u32[]{:S(2)}) collective-permute-start(f32[6928]{0:T(1024)S(1)} %fusion.383), channel_id=1, source_target_pairs={{0,128},{64,192},{128,0},{192,64},{256,384},{320,448},{384,256},{4... | collective-permute-start | bytes 83144 | tf_op jit(solution)/shard_map/ppermute | solution.py:27
  122.2 9.2 %collective-permute-start.12 = (f32[6928]{0:T(1024)S(1)}, f32[6928]{0:T(1024)S(1)}, u32[]{:S(2)}, u32[]{:S(2)}) collective-permute-start(f32[6928]{0:T(1024)S(1)} %add.521), channel_id=1, source_target_pairs={{0,256},{64,320},{128,384},{192,448},{256,0},{320,64},{384,128},{4... | collective-permute-start | bytes 83144 | tf_op jit(solution)/shard_map/ppermute | solution.py:27
  131.5 11.0 %collective-permute-start.13 = (f32[6928]{0:T(1024)S(1)}, f32[6928]{0:T(1024)S(1)}, u32[]{:S(2)}, u32[]{:S(2)}) collective-permute-start(f32[6928]{0:T(1024)S(1)} %add.522), channel_id=1, source_target_pairs={{0,1},{1,0},{2,3},{3,2},{4,5},{5,4},{6,7},{7,6},{8,9},{9,8},{10,11... | collective-permute-start | bytes 83144 | tf_op jit(solution)/shard_map/ppermute | solution.py:27
  142.4 7.3 %collective-permute-start.14 = (f32[6928]{0:T(1024)S(1)}, f32[6928]{0:T(1024)S(1)}, u32[]{:S(2)}, u32[]{:S(2)}) collective-permute-start(f32[6928]{0:T(1024)S(1)} %add.523), channel_id=1, source_target_pairs={{0,2},{1,3},{2,0},{3,1},{4,6},{5,7},{6,4},{7,5},{8,10},{9,11},{10,... | collective-permute-start | bytes 83144 | tf_op jit(solution)/shard_map/ppermute | solution.py:27
  149.7 5.8 %collective-permute-start.15 = (f32[6928]{0:T(1024)S(1)}, f32[6928]{0:T(1024)S(1)}, u32[]{:S(2)}, u32[]{:S(2)}) collective-permute-start(f32[6928]{0:T(1024)S(1)} %add.524), channel_id=1, source_target_pairs={{0,4},{1,5},{2,6},{3,7},{4,0},{5,1},{6,2},{7,3},{8,12},{9,13},{10,... | collective-permute-start | bytes 83144 | tf_op jit(solution)/shard_map/ppermute | solution.py:27
  155.4 6.7 %collective-permute-start.16 = (f32[6928]{0:T(1024)S(1)}, f32[6928]{0:T(1024)S(1)}, u32[]{:S(2)}, u32[]{:S(2)}) collective-permute-start(f32[6928]{0:T(1024)S(1)} %add.525), channel_id=1, source_target_pairs={{0,8},{1,9},{2,10},{3,11},{4,12},{5,13},{6,14},{7,15},{8,0},{9,1},... | collective-permute-start | bytes 83144 | tf_op jit(solution)/shard_map/ppermute | solution.py:27
  162.1 9.7 %collective-permute-start.17 = (f32[6928]{0:T(1024)S(1)}, f32[6928]{0:T(1024)S(1)}, u32[]{:S(2)}, u32[]{:S(2)}) collective-permute-start(f32[6928]{0:T(1024)S(1)} %add.526), channel_id=1, source_target_pairs={{0,16},{1,17},{2,18},{3,19},{4,20},{5,21},{6,22},{7,23},{8,24},{9,... | collective-permute-start | bytes 83144 | tf_op jit(solution)/shard_map/ppermute | solution.py:27
  171.8 9.7 %collective-permute-start.18 = (f32[6928]{0:T(1024)S(1)}, f32[6928]{0:T(1024)S(1)}, u32[]{:S(2)}, u32[]{:S(2)}) collective-permute-start(f32[6928]{0:T(1024)S(1)} %add.527), channel_id=1, source_target_pairs={{0,32},{1,33},{2,34},{3,35},{4,36},{5,37},{6,38},{7,39},{8,40},{9,... | collective-permute-start | bytes 83144 | tf_op jit(solution)/shard_map/ppermute | solution.py:27

commit v3 on v2

--- a/solution.py
+++ b/solution.py
@@ -49,19 +49,24 @@
     return (pre_act * normal_cdf, normal_cdf + pre_act * density)
 
 
-def routed(value, axis, sign, constant):
+def routed(pieces, axis, sign, constants):
     count = lax.axis_size(axis)
     here = lax.axis_index(axis)
     step = 1
     while step < count:
-        low = jnp.mod(sign * (here - constant), step)
-        source = here // (2 * step) * (2 * step) + here % (2 * step) // step * step + low
-        target = jnp.mod(sign * source + constant, count)
-        swap = (source // step % 2) != (target // step % 2)
         pairs = [(peer, peer ^ step) for peer in range(count)]
-        value = jnp.where(swap, lax.ppermute(value, axis, pairs), value)
+        arrived = lax.ppermute(jnp.concatenate(pieces, axis=2), axis, pairs)
+        updated = []
+        begin = 0
+        for piece, constant in zip(pieces, constants):
+            size = piece.shape[2]
+            wanted = jnp.mod(sign * (here - constant), 2 * step)
+            take = (wanted // step % 2) != (here // step % 2)
+            updated.append(jnp.where(take, arrived[:, :, begin : begin + size], piece))
+            begin += size
+        pieces = updated
         step *= 2
-    return value
+    return pieces
 
 
 def on_device(features, offsets, flip_bits, weight, conv_bias, cotangent):
@@ -75,11 +80,24 @@
     remain = effective % planes
     sign = jnp.where(flip_x, -1, 1)
     constant = jnp.where(flip_x, devices_x - 1 + coarse_steps, coarse_steps)
-    coarse = routed(block, "gx", sign, constant)
-    before = shifted(coarse, "gx", 1)
-    after = shifted(coarse[:, :, 0:1], "gx", -1)
-    joined = jnp.concatenate([before, coarse, after], axis=2)
-    window = lax.dynamic_slice_in_dim(joined, planes - 1 - remain, planes + 2, axis=2)
+    if planes == 2:
+        coarse, last_before, first_other = routed(
+            [block, block[:, :, 1:2], block[:, :, 0:1]],
+            "gx",
+            sign,
+            [constant, constant + 1, jnp.where(remain == 0, constant - 1, constant + 1)],
+        )
+        window = jnp.where(
+            remain == 0,
+            jnp.concatenate([last_before, coarse, first_other], axis=2),
+            jnp.concatenate([first_other, last_before, coarse], axis=2),
+        )
+    else:
+        (coarse,) = routed([block], "gx", sign, [constant])
+        before = shifted(coarse, "gx", 1)
+        after = shifted(coarse[:, :, 0:1], "gx", -1)
+        joined = jnp.concatenate([before, coarse, after], axis=2)
+        window = lax.dynamic_slice_in_dim(joined, planes - 1 - remain, planes + 2, axis=2)
     padded = jax.vmap(augment_local)(window, offsets, flip_bits)
 
     taps = len(tap_offsets)

time: 184 us -> 184 us (level)
  starting transfers between devices: 80.3 us -> 72.5 us
  waiting for transfers between devices: 55.4 us -> 62.3 us
    ppermute x4 -> x2, starting transfers between devices: 26.7 us -> 5.84 us  [shifted(): return lax.ppermute(value, axis, pairs)]
    ppermute x9, starting transfers between devices: 24.6 us -> 32.8 us  [butterfly_sum(): value = value + lax.ppermute(value, axis, pairs)]
    ppermute x6, waiting for transfers between devices: 23 us -> 27.9 us  [routed(): arrived = lax.ppermute(jnp.concatenate(pieces, axis=2), axis, pairs)]
    ppermute x6, starting transfers between devices: 29.1 us -> 33.9 us  [routed(): arrived = lax.ppermute(jnp.concatenate(pieces, axis=2), axis, pairs)]
    ppermute x4 -> x2, waiting for transfers between devices: 0.01 us -> 3.19 us  [shifted(): return lax.ppermute(value, axis, pairs)]
  transfers between devices with their start and end apart: 19 -> 17, of which waited for: 12 -> 14; matrix products, arithmetic and copies ran while one was open for 9% -> 9% of each run, Pallas kernels for 0% -> 0%
where the time goes in v3:
time: 184 us; the launch traced here: 183 us
  starting transfers between devices  72.5 us (39%)
  waiting for transfers between devices  62.3 us (34%)
  matrix products  18.9 us (10%)
  local copies, waits for them, and re-layouts  14.6 us (8%)
  between operations  11.9 us (6%)
  other arithmetic  3.23 us (2%)
    ppermute x6, starting transfers between devices, routed(): arrived = lax.ppermute(jnp.concatenate(pieces, axis=2), axis, pairs)  33.9 us
    ppermute x9, starting transfers between devices, butterfly_sum(): value = value + lax.ppermute(value, axis, pairs)  32.8 us
    ppermute x9, waiting for transfers between devices, butterfly_sum(): value = value + lax.ppermute(value, axis, pairs)  31.1 us
    ppermute x6, waiting for transfers between devices, routed(): arrived = lax.ppermute(jnp.concatenate(pieces, axis=2), axis, pairs)  27.9 us
    unnamed x39, local copies, waits for them, and re-layouts  10.1 us
    dot_general x27, matrix products, on_device(): jnp.einsum('oi,boxyz->bixyz', weight[tap_index], moved_grad, preferred_el...  6.58 us
    dot_general x27, matrix products, on_device(): jnp.einsum('boxyz,bixyz->oi', grad_pre, window, preferred_element_type=jn...  6.18 us
    dot_general x27, matrix products, on_device(): jnp.einsum('oi,bixyz->boxyz', weight[tap_index], window, preferred_elemen...  6.11 us
  transfers between devices with their start and end apart: 17, of which 14 were waited for; matrix products, arithmetic and copies ran while one was open for 9% of the time, Pallas kernels for 0%

profile of v3, /device:TPU:2, one launch (start us, length us, event | category | flops | bytes accessed | tf_op | source)
XLA Modules:
  0.0 183.3 jit_solution(11674353515655306053)
XLA Ops:
  0.6 1.4 fusion.380
  2.0 0.9 copy.69
  3.7 7.8 %collective-permute-start = (bf16[1,16,4,8,256]{4,1,3,2,0:T(8,128)(2,1)S(1)}, bf16[1,16,4,8,256]{4,1,3,2,0:T(8,128)(2,1)S(1)}, u32[]{:S(2)}, u32[]{:S(2)}) collective-permute-start(bf16[1,16,4,8,256]{4,1,3,2,0:T(8,128)(2,1)S(1)} %pad_maximum_fusion.10), channel_id=1, source_target_pairs={{0,1},{1,0},{2,3},{3,2},{4,5},{5,4},{6,7},{7,6},{8,9},{9,8},{10,11... | collective-permute-start | bytes 786440 | tf_op jit(solution)/shard_map/ppermute | solution.py:58
  14.9 1.0 collective-permute-done
  16.0 1.9 %collective-permute-start.1 = (bf16[1,16,4,8,256]{4,1,3,2,0:T(8,128)(2,1)S(1)}, bf16[1,16,4,8,256]{4,1,3,2,0:T(8,128)(2,1)S(1)}, u32[]{:S(2)}, u32[]{:S(2)}) collective-permute-start(bf16[1,16,4,8,256]{4,1,3,2,0:T(8,128)(2,1)S(1)} %pad_maximum_fusion.11), channel_id=1, source_target_pairs={{0,2},{1,3},{2,0},{3,1},{4,6},{5,7},{6,4},{7,5},{8,10},{9,11},{10,... | collective-permute-start | bytes 786440 | tf_op jit(solution)/shard_map/ppermute | solution.py:58
  18.1 7.6 %collective-permute-done.1 = bf16[1,16,4,8,256]{4,1,3,2,0:T(8,128)(2,1)S(1)} collective-permute-done((bf16[1,16,4,8,256]{4,1,3,2,0:T(8,128)(2,1)S(1)}, bf16[1,16,4,8,256]{4,1,3,2,0:T(8,128)(2,1)S(1)}, u32[]{:S(2)}, u32[]{:S(2)}) %collective-permute-start.1) | collective-permute-done | bytes 262176 | tf_op jit(solution)/shard_map/ppermute | solution.py:58
  25.8 2.9 %collective-permute-start.2 = (bf16[1,16,4,8,256]{4,1,3,2,0:T(8,128)(2,1)S(1)}, bf16[1,16,4,8,256]{4,1,3,2,0:T(8,128)(2,1)S(1)}, u32[]{:S(2)}, u32[]{:S(2)}) collective-permute-start(bf16[1,16,4,8,256]{4,1,3,2,0:T(8,128)(2,1)S(1)} %pad_maximum_fusion.12), channel_id=1, source_target_pairs={{0,4},{1,5},{2,6},{3,7},{4,0},{5,1},{6,2},{7,3},{8,12},{9,13},{10,... | collective-permute-start | bytes 786440 | tf_op jit(solution)/shard_map/ppermute | solution.py:58
  28.9 5.2 %collective-permute-done.2 = bf16[1,16,4,8,256]{4,1,3,2,0:T(8,128)(2,1)S(1)} collective-permute-done((bf16[1,16,4,8,256]{4,1,3,2,0:T(8,128)(2,1)S(1)}, bf16[1,16,4,8,256]{4,1,3,2,0:T(8,128)(2,1)S(1)}, u32[]{:S(2)}, u32[]{:S(2)}) %collective-permute-start.2) | collective-permute-done | bytes 262176 | tf_op jit(solution)/shard_map/ppermute | solution.py:58
  34.2 5.2 %collective-permute-start.3 = (bf16[1,16,4,8,256]{4,1,3,2,0:T(8,128)(2,1)S(1)}, bf16[1,16,4,8,256]{4,1,3,2,0:T(8,128)(2,1)S(1)}, u32[]{:S(2)}, u32[]{:S(2)}) collective-permute-start(bf16[1,16,4,8,256]{4,1,3,2,0:T(8,128)(2,1)S(1)} %pad_maximum_fusion.13), channel_id=1, source_target_pairs={{0,8},{1,9},{2,10},{3,11},{4,12},{5,13},{6,14},{7,15},{8,0},{9,1},... | collective-permute-start | bytes 786440 | tf_op jit(solution)/shard_map/ppermute | solution.py:58
  39.6 9.3 %collective-permute-done.3 = bf16[1,16,4,8,256]{4,1,3,2,0:T(8,128)(2,1)S(1)} collective-permute-done((bf16[1,16,4,8,256]{4,1,3,2,0:T(8,128)(2,1)S(1)}, bf16[1,16,4,8,256]{4,1,3,2,0:T(8,128)(2,1)S(1)}, u32[]{:S(2)}, u32[]{:S(2)}) %collective-permute-start.3) | collective-permute-done | bytes 262176 | tf_op jit(solution)/shard_map/ppermute | solution.py:58
  48.9 8.3 %collective-permute-start.4 = (bf16[1,16,4,8,256]{4,1,3,2,0:T(8,128)(2,1)S(1)}, bf16[1,16,4,8,256]{4,1,3,2,0:T(8,128)(2,1)S(1)}, u32[]{:S(2)}, u32[]{:S(2)}) collective-permute-start(bf16[1,16,4,8,256]{4,1,3,2,0:T(8,128)(2,1)S(1)} %pad_maximum_fusion.14), channel_id=1, source_target_pairs={{0,16},{1,17},{2,18},{3,19},{4,20},{5,21},{6,22},{7,23},{8,24},{9,... | collective-permute-start | bytes 786440 | tf_op jit(solution)/shard_map/ppermute | solution.py:58
  63.8 4.5 %collective-permute-done.4 = bf16[1,16,4,8,256]{4,1,3,2,0:T(8,128)(2,1)S(1)} collective-permute-done((bf16[1,16,4,8,256]{4,1,3,2,0:T(8,128)(2,1)S(1)}, bf16[1,16,4,8,256]{4,1,3,2,0:T(8,128)(2,1)S(1)}, u32[]{:S(2)}, u32[]{:S(2)}) %collective-permute-start.4) | collective-permute-done | bytes 262176 | tf_op jit(solution)/shard_map/ppermute | solution.py:58
  68.3 7.7 %collective-permute-start.5 = (bf16[1,16,4,8,256]{4,1,3,2,0:T(8,128)(2,1)S(1)}, bf16[1,16,4,8,256]{4,1,3,2,0:T(8,128)(2,1)S(1)}, u32[]{:S(2)}, u32[]{:S(2)}) collective-permute-start(bf16[1,16,4,8,256]{4,1,3,2,0:T(8,128)(2,1)S(1)} %pad_maximum_fusion.15), channel_id=1, source_target_pairs={{0,32},{1,33},{2,34},{3,35},{4,36},{5,37},{6,38},{7,39},{8,40},{9,... | collective-permute-start | bytes 786440 | tf_op jit(solution)/shard_map/ppermute | solution.py:58
  98.9 1.9 %collective-permute-start.8 = (f32[6928]{0:T(1024)S(1)}, f32[6928]{0:T(1024)S(1)}, u32[]{:S(2)}, u32[]{:S(2)}) collective-permute-start(f32[6928]{0:T(1024)S(1)} %pad_maximum_fusion.18), channel_id=1, source_target_pairs={{0,64},{64,0},{128,192},{192,128},{256,320},{320,256},{384,448},{4... | collective-permute-start | bytes 83144 | tf_op jit(solution)/shard_map/ppermute | solution.py:27
  100.8 2.4 %collective-permute-start.6 = (bf16[1,16,1,8,256]{4,1,3,2,0:T(8,128)(2,1)S(1)}, bf16[1,16,1,8,256]{4,1,3,2,0:T(8,128)(2,1)S(1)}, u32[]{:S(2)}, u32[]{:S(2)}) collective-permute-start(bf16[1,16,1,8,256]{4,1,3,2,0:T(8,128)(2,1)S(1)} %get-tuple-element.126), channel_id=1, source_target_pairs={{0,63},{1,0},{2,1},{3,2},{4,3},{5,4},{6,5},{7,6},{8,7},{9,8},{10,9... | collective-permute-start | bytes 196616 | tf_op jit(solution)/shard_map/ppermute | solution.py:19
  103.3 3.4 %collective-permute-start.7 = (bf16[1,16,1,8,256]{4,1,3,2,0:T(8,128)(2,1)S(1)}, bf16[1,16,1,8,256]{4,1,3,2,0:T(8,128)(2,1)S(1)}, u32[]{:S(2)}, u32[]{:S(2)}) collective-permute-start(bf16[1,16,1,8,256]{4,1,3,2,0:T(8,128)(2,1)S(1)} %get-tuple-element.127), channel_id=1, source_target_pairs={{0,1},{1,2},{2,3},{3,4},{4,5},{5,6},{6,7},{7,8},{8,9},{9,10},{10,1... | collective-permute-start | bytes 196616 | tf_op jit(solution)/shard_map/ppermute | solution.py:19
  106.7 3.1 %collective-permute-start.9 = (f32[6928]{0:T(1024)S(1)}, f32[6928]{0:T(1024)S(1)}, u32[]{:S(2)}, u32[]{:S(2)}) collective-permute-start(f32[6928]{0:T(1024)S(1)} %fusion.382), channel_id=1, source_target_pairs={{0,128},{64,192},{128,0},{192,64},{256,384},{320,448},{384,256},{4... | collective-permute-start | bytes 83144 | tf_op jit(solution)/shard_map/ppermute | solution.py:27
  110.5 2.0 %collective-permute-done.9 = f32[6928]{0:T(1024)S(1)} collective-permute-done((f32[6928]{0:T(1024)S(1)}, f32[6928]{0:T(1024)S(1)}, u32[]{:S(2)}, u32[]{:S(2)}) %collective-permute-start.9) | collective-permute-done | bytes 27744 | tf_op jit(solution)/shard_map/ppermute | solution.py:27
  112.5 4.8 %collective-permute-start.10 = (f32[6928]{0:T(1024)S(1)}, f32[6928]{0:T(1024)S(1)}, u32[]{:S(2)}, u32[]{:S(2)}) collective-permute-start(f32[6928]{0:T(1024)S(1)} %add.516), channel_id=1, source_target_pairs={{0,256},{64,320},{128,384},{192,448},{256,0},{320,64},{384,128},{4... | collective-permute-start | bytes 83144 | tf_op jit(solution)/shard_map/ppermute | solution.py:27
  117.3 3.2 %collective-permute-done.7 = bf16[1,16,1,8,256]{4,1,3,2,0:T(8,128)(2,1)S(1)} collective-permute-done((bf16[1,16,1,8,256]{4,1,3,2,0:T(8,128)(2,1)S(1)}, bf16[1,16,1,8,256]{4,1,3,2,0:T(8,128)(2,1)S(1)}, u32[]{:S(2)}, u32[]{:S(2)}) %collective-permute-start.7) | collective-permute-done | bytes 65568 | tf_op jit(solution)/shard_map/ppermute | solution.py:19
  127.6 13.4 %collective-permute-start.11 = (f32[6928]{0:T(1024)S(1)}, f32[6928]{0:T(1024)S(1)}, u32[]{:S(2)}, u32[]{:S(2)}) collective-permute-start(f32[6928]{0:T(1024)S(1)} %add.517), channel_id=1, source_target_pairs={{0,1},{1,0},{2,3},{3,2},{4,5},{5,4},{6,7},{7,6},{8,9},{9,8},{10,11... | collective-permute-start | bytes 83144 | tf_op jit(solution)/shard_map/ppermute | solution.py:27
  141.1 1.7 collective-permute-done.11
  142.9 1.9 %collective-permute-start.12 = (f32[6928]{0:T(1024)S(1)}, f32[6928]{0:T(1024)S(1)}, u32[]{:S(2)}, u32[]{:S(2)}) collective-permute-start(f32[6928]{0:T(1024)S(1)} %add.518), channel_id=1, source_target_pairs={{0,2},{1,3},{2,0},{3,1},{4,6},{5,7},{6,4},{7,5},{8,10},{9,11},{10,... | collective-permute-start | bytes 83144 | tf_op jit(solution)/shard_map/ppermute | solution.py:27
  145.0 5.1 %collective-permute-done.12 = f32[6928]{0:T(1024)S(1)} collective-permute-done((f32[6928]{0:T(1024)S(1)}, f32[6928]{0:T(1024)S(1)}, u32[]{:S(2)}, u32[]{:S(2)}) %collective-permute-start.12) | collective-permute-done | bytes 27744 | tf_op jit(solution)/shard_map/ppermute | solution.py:27
  150.1 1.9 %collective-permute-start.13 = (f32[6928]{0:T(1024)S(1)}, f32[6928]{0:T(1024)S(1)}, u32[]{:S(2)}, u32[]{:S(2)}) collective-permute-start(f32[6928]{0:T(1024)S(1)} %add.519), channel_id=1, source_target_pairs={{0,4},{1,5},{2,6},{3,7},{4,0},{5,1},{6,2},{7,3},{8,12},{9,13},{10,... | collective-permute-start | bytes 83144 | tf_op jit(solution)/shard_map/ppermute | solution.py:27
  152.3 3.6 %collective-permute-done.13 = f32[6928]{0:T(1024)S(1)} collective-permute-done((f32[6928]{0:T(1024)S(1)}, f32[6928]{0:T(1024)S(1)}, u32[]{:S(2)}, u32[]{:S(2)}) %collective-permute-start.13) | collective-permute-done | bytes 27744 | tf_op jit(solution)/shard_map/ppermute | solution.py:27
  155.9 1.9 %collective-permute-start.14 = (f32[6928]{0:T(1024)S(1)}, f32[6928]{0:T(1024)S(1)}, u32[]{:S(2)}, u32[]{:S(2)}) collective-permute-start(f32[6928]{0:T(1024)S(1)} %add.520), channel_id=1, source_target_pairs={{0,8},{1,9},{2,10},{3,11},{4,12},{5,13},{6,14},{7,15},{8,0},{9,1},... | collective-permute-start | bytes 83144 | tf_op jit(solution)/shard_map/ppermute | solution.py:27
  158.1 4.5 %collective-permute-done.14 = f32[6928]{0:T(1024)S(1)} collective-permute-done((f32[6928]{0:T(1024)S(1)}, f32[6928]{0:T(1024)S(1)}, u32[]{:S(2)}, u32[]{:S(2)}) %collective-permute-start.14) | collective-permute-done | bytes 27744 | tf_op jit(solution)/shard_map/ppermute | solution.py:27
  162.5 1.9 %collective-permute-start.15 = (f32[6928]{0:T(1024)S(1)}, f32[6928]{0:T(1024)S(1)}, u32[]{:S(2)}, u32[]{:S(2)}) collective-permute-start(f32[6928]{0:T(1024)S(1)} %add.521), channel_id=1, source_target_pairs={{0,16},{1,17},{2,18},{3,19},{4,20},{5,21},{6,22},{7,23},{8,24},{9,... | collective-permute-start | bytes 83144 | tf_op jit(solution)/shard_map/ppermute | solution.py:27
  164.7 7.5 %collective-permute-done.15 = f32[6928]{0:T(1024)S(1)} collective-permute-done((f32[6928]{0:T(1024)S(1)}, f32[6928]{0:T(1024)S(1)}, u32[]{:S(2)}, u32[]{:S(2)}) %collective-permute-start.15) | collective-permute-done | bytes 27744 | tf_op jit(solution)/shard_map/ppermute | solution.py:27
  172.2 1.9 %collective-permute-start.16 = (f32[6928]{0:T(1024)S(1)}, f32[6928]{0:T(1024)S(1)}, u32[]{:S(2)}, u32[]{:S(2)}) collective-permute-start(f32[6928]{0:T(1024)S(1)} %add.522), channel_id=1, source_target_pairs={{0,32},{1,33},{2,34},{3,35},{4,36},{5,37},{6,38},{7,39},{8,40},{9,... | collective-permute-start | bytes 83144 | tf_op jit(solution)/shard_map/ppermute | solution.py:27
  175.1 6.8 %collective-permute-done.16 = f32[6928]{0:T(1024)S(1)} collective-permute-done((f32[6928]{0:T(1024)S(1)}, f32[6928]{0:T(1024)S(1)}, u32[]{:S(2)}, u32[]{:S(2)}) %collective-permute-start.16) | collective-permute-done | bytes 27744 | tf_op jit(solution)/shard_map/ppermute | solution.py:27
  (192 shorter events, 34.7 us)
Async XLA Ops:
  3.7 12.2 %collective-permute-start = (bf16[1,16,4,8,256]{4,1,3,2,0:T(8,128)(2,1)S(1)}, bf16[1,16,4,8,256]{4,1,3,2,0:T(8,128)(2,1)S(1)}, u32[]{:S(2)}, u32[]{:S(2)}) collective-permute-start(bf16[1,16,4,8,256]{4,1,3,2,0:T(8,128)(2,1)S(1)} %pad_maximum_fusion.10), channel_id=1, source_target_pairs={{0,1},{1,0},{2,3},{3,2},{4,5},{5,4},{6,7},{7,6},{8,9},{9,8},{10,11... | collective-permute-start | bytes 786440 | tf_op jit(solution)/shard_map/ppermute | solution.py:58
  11.5 0.7 copy-start.2
  16.0 9.8 %collective-permute-start.1 = (bf16[1,16,4,8,256]{4,1,3,2,0:T(8,128)(2,1)S(1)}, bf16[1,16,4,8,256]{4,1,3,2,0:T(8,128)(2,1)S(1)}, u32[]{:S(2)}, u32[]{:S(2)}) collective-permute-start(bf16[1,16,4,8,256]{4,1,3,2,0:T(8,128)(2,1)S(1)} %pad_maximum_fusion.11), channel_id=1, source_target_pairs={{0,2},{1,3},{2,0},{3,1},{4,6},{5,7},{6,4},{7,5},{8,10},{9,11},{10,... | collective-permute-start | bytes 786440 | tf_op jit(solution)/shard_map/ppermute | solution.py:58
  25.8 8.3 %collective-permute-start.2 = (bf16[1,16,4,8,256]{4,1,3,2,0:T(8,128)(2,1)S(1)}, bf16[1,16,4,8,256]{4,1,3,2,0:T(8,128)(2,1)S(1)}, u32[]{:S(2)}, u32[]{:S(2)}) collective-permute-start(bf16[1,16,4,8,256]{4,1,3,2,0:T(8,128)(2,1)S(1)} %pad_maximum_fusion.12), channel_id=1, source_target_pairs={{0,4},{1,5},{2,6},{3,7},{4,0},{5,1},{6,2},{7,3},{8,12},{9,13},{10,... | collective-permute-start | bytes 786440 | tf_op jit(solution)/shard_map/ppermute | solution.py:58
  34.2 14.7 %collective-permute-start.3 = (bf16[1,16,4,8,256]{4,1,3,2,0:T(8,128)(2,1)S(1)}, bf16[1,16,4,8,256]{4,1,3,2,0:T(8,128)(2,1)S(1)}, u32[]{:S(2)}, u32[]{:S(2)}) collective-permute-start(bf16[1,16,4,8,256]{4,1,3,2,0:T(8,128)(2,1)S(1)} %pad_maximum_fusion.13), channel_id=1, source_target_pairs={{0,8},{1,9},{2,10},{3,11},{4,12},{5,13},{6,14},{7,15},{8,0},{9,1},... | collective-permute-start | bytes 786440 | tf_op jit(solution)/shard_map/ppermute | solution.py:58
  48.9 19.3 %collective-permute-start.4 = (bf16[1,16,4,8,256]{4,1,3,2,0:T(8,128)(2,1)S(1)}, bf16[1,16,4,8,256]{4,1,3,2,0:T(8,128)(2,1)S(1)}, u32[]{:S(2)}, u32[]{:S(2)}) collective-permute-start(bf16[1,16,4,8,256]{4,1,3,2,0:T(8,128)(2,1)S(1)} %pad_maximum_fusion.14), channel_id=1, source_target_pairs={{0,16},{1,17},{2,18},{3,19},{4,20},{5,21},{6,22},{7,23},{8,24},{9,... | collective-permute-start | bytes 786440 | tf_op jit(solution)/shard_map/ppermute | solution.py:58
  62.7 0.8 copy-start
  68.3 14.8 %collective-permute-start.5 = (bf16[1,16,4,8,256]{4,1,3,2,0:T(8,128)(2,1)S(1)}, bf16[1,16,4,8,256]{4,1,3,2,0:T(8,128)(2,1)S(1)}, u32[]{:S(2)}, u32[]{:S(2)}) collective-permute-start(bf16[1,16,4,8,256]{4,1,3,2,0:T(8,128)(2,1)S(1)} %pad_maximum_fusion.15), channel_id=1, source_target_pairs={{0,32},{1,33},{2,34},{3,35},{4,36},{5,37},{6,38},{7,39},{8,40},{9,... | collective-permute-start | bytes 786440 | tf_op jit(solution)/shard_map/ppermute | solution.py:58
  90.8 0.9 copy-start.1
  91.1 0.7 copy-start.3
  98.9 7.8 %collective-permute-start.8 = (f32[6928]{0:T(1024)S(1)}, f32[6928]{0:T(1024)S(1)}, u32[]{:S(2)}, u32[]{:S(2)}) collective-permute-start(f32[6928]{0:T(1024)S(1)} %pad_maximum_fusion.18), channel_id=1, source_target_pairs={{0,64},{64,0},{128,192},{192,128},{256,320},{320,256},{384,448},{4... | collective-permute-start | bytes 83144 | tf_op jit(solution)/shard_map/ppermute | solution.py:27
  100.8 16.5 %collective-permute-start.6 = (bf16[1,16,1,8,256]{4,1,3,2,0:T(8,128)(2,1)S(1)}, bf16[1,16,1,8,256]{4,1,3,2,0:T(8,128)(2,1)S(1)}, u32[]{:S(2)}, u32[]{:S(2)}) collective-permute-start(bf16[1,16,1,8,256]{4,1,3,2,0:T(8,128)(2,1)S(1)} %get-tuple-element.126), channel_id=1, source_target_pairs={{0,63},{1,0},{2,1},{3,2},{4,3},{5,4},{6,5},{7,6},{8,7},{9,8},{10,9... | collective-permute-start | bytes 196616 | tf_op jit(solution)/shard_map/ppermute | solution.py:19
  103.3 17.2 %collective-permute-start.7 = (bf16[1,16,1,8,256]{4,1,3,2,0:T(8,128)(2,1)S(1)}, bf16[1,16,1,8,256]{4,1,3,2,0:T(8,128)(2,1)S(1)}, u32[]{:S(2)}, u32[]{:S(2)}) collective-permute-start(bf16[1,16,1,8,256]{4,1,3,2,0:T(8,128)(2,1)S(1)} %get-tuple-element.127), channel_id=1, source_target_pairs={{0,1},{1,2},{2,3},{3,4},{4,5},{5,6},{6,7},{7,8},{8,9},{9,10},{10,1... | collective-permute-start | bytes 196616 | tf_op jit(solution)/shard_map/ppermute | solution.py:19
  106.7 5.8 %collective-permute-start.9 = (f32[6928]{0:T(1024)S(1)}, f32[6928]{0:T(1024)S(1)}, u32[]{:S(2)}, u32[]{:S(2)}) collective-permute-start(f32[6928]{0:T(1024)S(1)} %fusion.382), channel_id=1, source_target_pairs={{0,128},{64,192},{128,0},{192,64},{256,384},{320,448},{384,256},{4... | collective-permute-start | bytes 83144 | tf_op jit(solution)/shard_map/ppermute | solution.py:27
  112.5 15.1 %collective-permute-start.10 = (f32[6928]{0:T(1024)S(1)}, f32[6928]{0:T(1024)S(1)}, u32[]{:S(2)}, u32[]{:S(2)}) collective-permute-start(f32[6928]{0:T(1024)S(1)} %add.516), channel_id=1, source_target_pairs={{0,256},{64,320},{128,384},{192,448},{256,0},{320,64},{384,128},{4... | collective-permute-start | bytes 83144 | tf_op jit(solution)/shard_map/ppermute | solution.py:27
  127.6 15.2 %collective-permute-start.11 = (f32[6928]{0:T(1024)S(1)}, f32[6928]{0:T(1024)S(1)}, u32[]{:S(2)}, u32[]{:S(2)}) collective-permute-start(f32[6928]{0:T(1024)S(1)} %add.517), channel_id=1, source_target_pairs={{0,1},{1,0},{2,3},{3,2},{4,5},{5,4},{6,7},{7,6},{8,9},{9,8},{10,11... | collective-permute-start | bytes 83144 | tf_op jit(solution)/shard_map/ppermute | solution.py:27
  142.9 7.3 %collective-permute-start.12 = (f32[6928]{0:T(1024)S(1)}, f32[6928]{0:T(1024)S(1)}, u32[]{:S(2)}, u32[]{:S(2)}) collective-permute-start(f32[6928]{0:T(1024)S(1)} %add.518), channel_id=1, source_target_pairs={{0,2},{1,3},{2,0},{3,1},{4,6},{5,7},{6,4},{7,5},{8,10},{9,11},{10,... | collective-permute-start | bytes 83144 | tf_op jit(solution)/shard_map/ppermute | solution.py:27
  150.1 5.8 %collective-permute-start.13 = (f32[6928]{0:T(1024)S(1)}, f32[6928]{0:T(1024)S(1)}, u32[]{:S(2)}, u32[]{:S(2)}) collective-permute-start(f32[6928]{0:T(1024)S(1)} %add.519), channel_id=1, source_target_pairs={{0,4},{1,5},{2,6},{3,7},{4,0},{5,1},{6,2},{7,3},{8,12},{9,13},{10,... | collective-permute-start | bytes 83144 | tf_op jit(solution)/shard_map/ppermute | solution.py:27
  155.9 6.7 %collective-permute-start.14 = (f32[6928]{0:T(1024)S(1)}, f32[6928]{0:T(1024)S(1)}, u32[]{:S(2)}, u32[]{:S(2)}) collective-permute-start(f32[6928]{0:T(1024)S(1)} %add.520), channel_id=1, source_target_pairs={{0,8},{1,9},{2,10},{3,11},{4,12},{5,13},{6,14},{7,15},{8,0},{9,1},... | collective-permute-start | bytes 83144 | tf_op jit(solution)/shard_map/ppermute | solution.py:27
  162.5 9.7 %collective-permute-start.15 = (f32[6928]{0:T(1024)S(1)}, f32[6928]{0:T(1024)S(1)}, u32[]{:S(2)}, u32[]{:S(2)}) collective-permute-start(f32[6928]{0:T(1024)S(1)} %add.521), channel_id=1, source_target_pairs={{0,16},{1,17},{2,18},{3,19},{4,20},{5,21},{6,22},{7,23},{8,24},{9,... | collective-permute-start | bytes 83144 | tf_op jit(solution)/shard_map/ppermute | solution.py:27
  172.2 9.7 %collective-permute-start.16 = (f32[6928]{0:T(1024)S(1)}, f32[6928]{0:T(1024)S(1)}, u32[]{:S(2)}, u32[]{:S(2)}) collective-permute-start(f32[6928]{0:T(1024)S(1)} %add.522), channel_id=1, source_target_pairs={{0,32},{1,33},{2,34},{3,35},{4,36},{5,37},{6,38},{7,39},{8,40},{9,... | collective-permute-start | bytes 83144 | tf_op jit(solution)/shard_map/ppermute | solution.py:27

commit v4 on v3

--- a/solution.py
+++ b/solution.py
@@ -102,40 +102,43 @@
 
     taps = len(tap_offsets)
     channels = features.shape[1]
+    kernel = weight.reshape(3, 3, 3, channels, channels)
+    stacked_z = jnp.concatenate([jnp.roll(padded, 1 - h, axis=4) for h in range(3)], axis=1)
     total = jnp.zeros(features.shape, jnp.float32) + conv_bias[None, :, None, None, None]
-    for tap_index, (shift_x, shift_y, shift_z) in enumerate(tap_offsets):
-        window = jnp.roll(
-            padded[:, :, shift_x : shift_x + planes], (1 - shift_y, 1 - shift_z), axis=(3, 4)
-        )
-        total = total + jnp.einsum(
-            "oi,bixyz->boxyz", weight[tap_index], window, preferred_element_type=jnp.float32
-        )
+    for shift_x in range(3):
+        for shift_y in range(3):
+            window = jnp.roll(stacked_z[:, :, shift_x : shift_x + planes], 1 - shift_y, axis=3)
+            mixed = jnp.transpose(kernel[shift_x, shift_y], (1, 0, 2)).reshape(channels, -1)
+            total = total + jnp.einsum(
+                "oc,bcxyz->boxyz", mixed, window, preferred_element_type=jnp.float32
+            )
     hidden, slope = gelu_parts(total)
     grad_pre = (cotangent.astype(jnp.float32) * slope).astype(jnp.bfloat16)
     grad_before = shifted(grad_pre[:, :, planes - 1 : planes], "gx", 1)
     grad_after = shifted(grad_pre[:, :, 0:1], "gx", -1)
     grad_list = []
-    for tap_index, (shift_x, shift_y, shift_z) in enumerate(tap_offsets):
-        window = jnp.roll(
-            padded[:, :, shift_x : shift_x + planes], (1 - shift_y, 1 - shift_z), axis=(3, 4)
-        )
-        grad_list.append(
-            jnp.einsum("boxyz,bixyz->oi", grad_pre, window, preferred_element_type=jnp.float32)
-        )
+    for shift_x in range(3):
+        for shift_y in range(3):
+            window = jnp.roll(stacked_z[:, :, shift_x : shift_x + planes], 1 - shift_y, axis=3)
+            part = jnp.einsum(
+                "boxyz,bcxyz->oc", grad_pre, window, preferred_element_type=jnp.float32
+            )
+            grad_list.append(jnp.transpose(part.reshape(channels, 3, channels), (1, 0, 2)))
     grad_b = jnp.sum(grad_pre.astype(jnp.float32), axis=(0, 2, 3, 4))
-    stacked = jnp.concatenate([jnp.stack(grad_list).reshape(-1), grad_b])
+    stacked = jnp.concatenate([jnp.concatenate(grad_list, axis=0).reshape(-1), grad_b])
     summed = butterfly_sum(butterfly_sum(stacked, "dp"), "gx")
     grad_pad = jnp.concatenate([grad_before, grad_pre, grad_after], axis=2)
+    grad_z = jnp.concatenate([jnp.roll(grad_pad, h - 1, axis=4) for h in range(3)], axis=1)
     grad_in = jnp.zeros(features.shape, jnp.float32)
-    for tap_index, (shift_x, shift_y, shift_z) in enumerate(tap_offsets):
-        moved_grad = jnp.roll(
-            grad_pad[:, :, 2 - shift_x : 2 - shift_x + planes],
-            (shift_y - 1, shift_z - 1),
-            axis=(3, 4),
-        )
-        grad_in = grad_in + jnp.einsum(
-            "oi,boxyz->bixyz", weight[tap_index], moved_grad, preferred_element_type=jnp.float32
-        )
+    for shift_x in range(3):
+        for shift_y in range(3):
+            moved_grad = jnp.roll(
+                grad_z[:, :, 2 - shift_x : 2 - shift_x + planes], shift_y - 1, axis=3
+            )
+            mixed = kernel[shift_x, shift_y].reshape(-1, channels)
+            grad_in = grad_in + jnp.einsum(
+                "ci,bcxyz->bixyz", mixed, moved_grad, preferred_element_type=jnp.float32
+            )
     cell_count = (
         features.shape[0] * lax.axis_size("dp") * length_x * features.shape[3] * features.shape[4]
     )

time: 184 us -> 171 us (0.929)
  the two profiles are of different devices: /device:TPU:2 before, /device:TPU:8 now
where the time goes in v4:
time: 171 us; the launch traced here: 170 us
  starting transfers between devices  71.9 us (42%)
  waiting for transfers between devices  66.6 us (39%)
  between operations  11.4 us (7%)
  local copies, waits for them, and re-layouts  9.32 us (5%)
  matrix products  8.43 us (5%)
  other arithmetic  2.1 us (1%)
    ppermute x6, starting transfers between devices, routed(): arrived = lax.ppermute(jnp.concatenate(pieces, axis=2), axis, pairs)  33.9 us
    ppermute x6, waiting for transfers between devices, routed(): arrived = lax.ppermute(jnp.concatenate(pieces, axis=2), axis, pairs)  33.6 us
    ppermute x9, waiting for transfers between devices, butterfly_sum(): value = value + lax.ppermute(value, axis, pairs)  33 us
    ppermute x9, starting transfers between devices, butterfly_sum(): value = value + lax.ppermute(value, axis, pairs)  22.5 us
    ppermute x2, starting transfers between devices, shifted(): return lax.ppermute(value, axis, pairs)  15.6 us
    dot_general x9, matrix products, on_device(): jnp.einsum('boxyz,bcxyz->oc', grad_pre, window, preferred_element_type=jn...  4.43 us
    unnamed x13, local copies, waits for them, and re-layouts  4.4 us
  transfers between devices with their start and end apart: 17, of which 13 were waited for; matrix products, arithmetic and copies ran while one was open for 3% of the time, Pallas kernels for 0%

profile of v4, /device:TPU:8, one launch (start us, length us, event | category | flops | bytes accessed | tf_op | source)
XLA Modules:
  0.0 169.8 jit_solution(6080895174977830476)
XLA Ops:
  0.6 1.4 fusion.153
  2.0 0.9 copy.42
  3.7 3.4 %collective-permute-start = (bf16[1,16,4,8,256]{4,1,3,2,0:T(8,128)(2,1)S(1)}, bf16[1,16,4,8,256]{4,1,3,2,0:T(8,128)(2,1)S(1)}, u32[]{:S(2)}, u32[]{:S(2)}) collective-permute-start(bf16[1,16,4,8,256]{4,1,3,2,0:T(8,128)(2,1)S(1)} %pad_maximum_fusion.54), channel_id=1, source_target_pairs={{0,1},{1,0},{2,3},{3,2},{4,5},{5,4},{6,7},{7,6},{8,9},{9,8},{10,11... | collective-permute-start | bytes 786440 | tf_op jit(solution)/shard_map/ppermute | solution.py:58
  9.8 3.8 %collective-permute-done = bf16[1,16,4,8,256]{4,1,3,2,0:T(8,128)(2,1)S(1)} collective-permute-done((bf16[1,16,4,8,256]{4,1,3,2,0:T(8,128)(2,1)S(1)}, bf16[1,16,4,8,256]{4,1,3,2,0:T(8,128)(2,1)S(1)}, u32[]{:S(2)}, u32[]{:S(2)}) %collective-permute-start) | collective-permute-done | bytes 262176 | tf_op jit(solution)/shard_map/ppermute | solution.py:58
  13.8 4.9 %collective-permute-start.1 = (bf16[1,16,4,8,256]{4,1,3,2,0:T(8,128)(2,1)S(1)}, bf16[1,16,4,8,256]{4,1,3,2,0:T(8,128)(2,1)S(1)}, u32[]{:S(2)}, u32[]{:S(2)}) collective-permute-start(bf16[1,16,4,8,256]{4,1,3,2,0:T(8,128)(2,1)S(1)} %pad_maximum_fusion.55), channel_id=1, source_target_pairs={{0,2},{1,3},{2,0},{3,1},{4,6},{5,7},{6,4},{7,5},{8,10},{9,11},{10,... | collective-permute-start | bytes 786440 | tf_op jit(solution)/shard_map/ppermute | solution.py:58
  18.9 5.4 %collective-permute-done.1 = bf16[1,16,4,8,256]{4,1,3,2,0:T(8,128)(2,1)S(1)} collective-permute-done((bf16[1,16,4,8,256]{4,1,3,2,0:T(8,128)(2,1)S(1)}, bf16[1,16,4,8,256]{4,1,3,2,0:T(8,128)(2,1)S(1)}, u32[]{:S(2)}, u32[]{:S(2)}) %collective-permute-start.1) | collective-permute-done | bytes 262176 | tf_op jit(solution)/shard_map/ppermute | solution.py:58
  24.4 4.3 %collective-permute-start.2 = (bf16[1,16,4,8,256]{4,1,3,2,0:T(8,128)(2,1)S(1)}, bf16[1,16,4,8,256]{4,1,3,2,0:T(8,128)(2,1)S(1)}, u32[]{:S(2)}, u32[]{:S(2)}) collective-permute-start(bf16[1,16,4,8,256]{4,1,3,2,0:T(8,128)(2,1)S(1)} %pad_maximum_fusion.56), channel_id=1, source_target_pairs={{0,4},{1,5},{2,6},{3,7},{4,0},{5,1},{6,2},{7,3},{8,12},{9,13},{10,... | collective-permute-start | bytes 786440 | tf_op jit(solution)/shard_map/ppermute | solution.py:58
  28.9 4.3 %collective-permute-done.2 = bf16[1,16,4,8,256]{4,1,3,2,0:T(8,128)(2,1)S(1)} collective-permute-done((bf16[1,16,4,8,256]{4,1,3,2,0:T(8,128)(2,1)S(1)}, bf16[1,16,4,8,256]{4,1,3,2,0:T(8,128)(2,1)S(1)}, u32[]{:S(2)}, u32[]{:S(2)}) %collective-permute-start.2) | collective-permute-done | bytes 262176 | tf_op jit(solution)/shard_map/ppermute | solution.py:58
  33.3 6.1 %collective-permute-start.3 = (bf16[1,16,4,8,256]{4,1,3,2,0:T(8,128)(2,1)S(1)}, bf16[1,16,4,8,256]{4,1,3,2,0:T(8,128)(2,1)S(1)}, u32[]{:S(2)}, u32[]{:S(2)}) collective-permute-start(bf16[1,16,4,8,256]{4,1,3,2,0:T(8,128)(2,1)S(1)} %pad_maximum_fusion.57), channel_id=1, source_target_pairs={{0,8},{1,9},{2,10},{3,11},{4,12},{5,13},{6,14},{7,15},{8,0},{9,1},... | collective-permute-start | bytes 786440 | tf_op jit(solution)/shard_map/ppermute | solution.py:58
  39.6 9.3 %collective-permute-done.3 = bf16[1,16,4,8,256]{4,1,3,2,0:T(8,128)(2,1)S(1)} collective-permute-done((bf16[1,16,4,8,256]{4,1,3,2,0:T(8,128)(2,1)S(1)}, bf16[1,16,4,8,256]{4,1,3,2,0:T(8,128)(2,1)S(1)}, u32[]{:S(2)}, u32[]{:S(2)}) %collective-permute-start.3) | collective-permute-done | bytes 262176 | tf_op jit(solution)/shard_map/ppermute | solution.py:58
  48.9 8.3 %collective-permute-start.4 = (bf16[1,16,4,8,256]{4,1,3,2,0:T(8,128)(2,1)S(1)}, bf16[1,16,4,8,256]{4,1,3,2,0:T(8,128)(2,1)S(1)}, u32[]{:S(2)}, u32[]{:S(2)}) collective-permute-start(bf16[1,16,4,8,256]{4,1,3,2,0:T(8,128)(2,1)S(1)} %pad_maximum_fusion.58), channel_id=1, source_target_pairs={{0,16},{1,17},{2,18},{3,19},{4,20},{5,21},{6,22},{7,23},{8,24},{9,... | collective-permute-start | bytes 786440 | tf_op jit(solution)/shard_map/ppermute | solution.py:58
  57.5 10.7 %collective-permute-done.4 = bf16[1,16,4,8,256]{4,1,3,2,0:T(8,128)(2,1)S(1)} collective-permute-done((bf16[1,16,4,8,256]{4,1,3,2,0:T(8,128)(2,1)S(1)}, bf16[1,16,4,8,256]{4,1,3,2,0:T(8,128)(2,1)S(1)}, u32[]{:S(2)}, u32[]{:S(2)}) %collective-permute-start.4) | collective-permute-done | bytes 262176 | tf_op jit(solution)/shard_map/ppermute | solution.py:58
  68.3 6.8 %collective-permute-start.5 = (bf16[1,16,4,8,256]{4,1,3,2,0:T(8,128)(2,1)S(1)}, bf16[1,16,4,8,256]{4,1,3,2,0:T(8,128)(2,1)S(1)}, u32[]{:S(2)}, u32[]{:S(2)}) collective-permute-start(bf16[1,16,4,8,256]{4,1,3,2,0:T(8,128)(2,1)S(1)} %pad_maximum_fusion.59), channel_id=1, source_target_pairs={{0,32},{1,33},{2,34},{3,35},{4,36},{5,37},{6,38},{7,39},{8,40},{9,... | collective-permute-start | bytes 786440 | tf_op jit(solution)/shard_map/ppermute | solution.py:58
  92.8 1.9 %collective-permute-start.8 = (f32[6928]{0:T(1024)S(1)}, f32[6928]{0:T(1024)S(1)}, u32[]{:S(2)}, u32[]{:S(2)}) collective-permute-start(f32[6928]{0:T(1024)S(1)} %pad_maximum_fusion.61), channel_id=1, source_target_pairs={{0,64},{64,0},{128,192},{192,128},{256,320},{320,256},{384,448},{4... | collective-permute-start | bytes 83144 | tf_op jit(solution)/shard_map/ppermute | solution.py:27
  94.8 3.4 %collective-permute-start.6 = (bf16[1,16,1,8,256]{4,1,3,2,0:T(8,128)(2,1)S(1)}, bf16[1,16,1,8,256]{4,1,3,2,0:T(8,128)(2,1)S(1)}, u32[]{:S(2)}, u32[]{:S(2)}) collective-permute-start(bf16[1,16,1,8,256]{4,1,3,2,0:T(8,128)(2,1)S(1)} %get-tuple-element.80), channel_id=1, source_target_pairs={{0,1},{1,2},{2,3},{3,4},{4,5},{5,6},{6,7},{7,8},{8,9},{9,10},{10,1... | collective-permute-start | bytes 196616 | tf_op jit(solution)/shard_map/ppermute | solution.py:19
  98.2 12.2 %collective-permute-start.7 = (bf16[1,16,1,8,256]{4,1,3,2,0:T(8,128)(2,1)S(1)}, bf16[1,16,1,8,256]{4,1,3,2,0:T(8,128)(2,1)S(1)}, u32[]{:S(2)}, u32[]{:S(2)}) collective-permute-start(bf16[1,16,1,8,256]{4,1,3,2,0:T(8,128)(2,1)S(1)} %get-tuple-element.81), channel_id=1, source_target_pairs={{0,63},{1,0},{2,1},{3,2},{4,3},{5,4},{6,5},{7,6},{8,7},{9,8},{10,9... | collective-permute-start | bytes 196616 | tf_op jit(solution)/shard_map/ppermute | solution.py:19
  110.4 3.6 %collective-permute-start.9 = (f32[6928]{0:T(1024)S(1)}, f32[6928]{0:T(1024)S(1)}, u32[]{:S(2)}, u32[]{:S(2)}) collective-permute-start(f32[6928]{0:T(1024)S(1)} %fusion.173), channel_id=1, source_target_pairs={{0,128},{64,192},{128,0},{192,64},{256,384},{320,448},{384,256},{4... | collective-permute-start | bytes 83144 | tf_op jit(solution)/shard_map/ppermute | solution.py:27
  114.7 1.8 %collective-permute-done.9 = f32[6928]{0:T(1024)S(1)} collective-permute-done((f32[6928]{0:T(1024)S(1)}, f32[6928]{0:T(1024)S(1)}, u32[]{:S(2)}, u32[]{:S(2)}) %collective-permute-start.9) | collective-permute-done | bytes 27744 | tf_op jit(solution)/shard_map/ppermute | solution.py:27
  116.5 2.6 %collective-permute-start.10 = (f32[6928]{0:T(1024)S(1)}, f32[6928]{0:T(1024)S(1)}, u32[]{:S(2)}, u32[]{:S(2)}) collective-permute-start(f32[6928]{0:T(1024)S(1)} %add.372), channel_id=1, source_target_pairs={{0,256},{64,320},{128,384},{192,448},{256,0},{320,64},{384,128},{4... | collective-permute-start | bytes 83144 | tf_op jit(solution)/shard_map/ppermute | solution.py:27
  120.5 2.7 %collective-permute-done.10 = f32[6928]{0:T(1024)S(1)} collective-permute-done((f32[6928]{0:T(1024)S(1)}, f32[6928]{0:T(1024)S(1)}, u32[]{:S(2)}, u32[]{:S(2)}) %collective-permute-start.10) | collective-permute-done | bytes 27744 | tf_op jit(solution)/shard_map/ppermute | solution.py:27
  123.3 1.9 %collective-permute-start.11 = (f32[6928]{0:T(1024)S(1)}, f32[6928]{0:T(1024)S(1)}, u32[]{:S(2)}, u32[]{:S(2)}) collective-permute-start(f32[6928]{0:T(1024)S(1)} %add.373), channel_id=1, source_target_pairs={{0,1},{1,0},{2,3},{3,2},{4,5},{5,4},{6,7},{7,6},{8,9},{9,8},{10,11... | collective-permute-start | bytes 83144 | tf_op jit(solution)/shard_map/ppermute | solution.py:27
  125.4 3.6 %collective-permute-done.11 = f32[6928]{0:T(1024)S(1)} collective-permute-done((f32[6928]{0:T(1024)S(1)}, f32[6928]{0:T(1024)S(1)}, u32[]{:S(2)}, u32[]{:S(2)}) %collective-permute-start.11) | collective-permute-done | bytes 27744 | tf_op jit(solution)/shard_map/ppermute | solution.py:27
  129.0 1.9 %collective-permute-start.12 = (f32[6928]{0:T(1024)S(1)}, f32[6928]{0:T(1024)S(1)}, u32[]{:S(2)}, u32[]{:S(2)}) collective-permute-start(f32[6928]{0:T(1024)S(1)} %add.374), channel_id=1, source_target_pairs={{0,2},{1,3},{2,0},{3,1},{4,6},{5,7},{6,4},{7,5},{8,10},{9,11},{10,... | collective-permute-start | bytes 83144 | tf_op jit(solution)/shard_map/ppermute | solution.py:27
  131.2 5.1 %collective-permute-done.12 = f32[6928]{0:T(1024)S(1)} collective-permute-done((f32[6928]{0:T(1024)S(1)}, f32[6928]{0:T(1024)S(1)}, u32[]{:S(2)}, u32[]{:S(2)}) %collective-permute-start.12) | collective-permute-done | bytes 27744 | tf_op jit(solution)/shard_map/ppermute | solution.py:27
  136.3 1.9 %collective-permute-start.13 = (f32[6928]{0:T(1024)S(1)}, f32[6928]{0:T(1024)S(1)}, u32[]{:S(2)}, u32[]{:S(2)}) collective-permute-start(f32[6928]{0:T(1024)S(1)} %add.375), channel_id=1, source_target_pairs={{0,4},{1,5},{2,6},{3,7},{4,0},{5,1},{6,2},{7,3},{8,12},{9,13},{10,... | collective-permute-start | bytes 83144 | tf_op jit(solution)/shard_map/ppermute | solution.py:27
  138.5 3.6 %collective-permute-done.13 = f32[6928]{0:T(1024)S(1)} collective-permute-done((f32[6928]{0:T(1024)S(1)}, f32[6928]{0:T(1024)S(1)}, u32[]{:S(2)}, u32[]{:S(2)}) %collective-permute-start.13) | collective-permute-done | bytes 27744 | tf_op jit(solution)/shard_map/ppermute | solution.py:27
  142.1 1.9 %collective-permute-start.14 = (f32[6928]{0:T(1024)S(1)}, f32[6928]{0:T(1024)S(1)}, u32[]{:S(2)}, u32[]{:S(2)}) collective-permute-start(f32[6928]{0:T(1024)S(1)} %add.376), channel_id=1, source_target_pairs={{0,8},{1,9},{2,10},{3,11},{4,12},{5,13},{6,14},{7,15},{8,0},{9,1},... | collective-permute-start | bytes 83144 | tf_op jit(solution)/shard_map/ppermute | solution.py:27
  144.2 4.5 %collective-permute-done.14 = f32[6928]{0:T(1024)S(1)} collective-permute-done((f32[6928]{0:T(1024)S(1)}, f32[6928]{0:T(1024)S(1)}, u32[]{:S(2)}, u32[]{:S(2)}) %collective-permute-start.14) | collective-permute-done | bytes 27744 | tf_op jit(solution)/shard_map/ppermute | solution.py:27
  148.7 1.9 %collective-permute-start.15 = (f32[6928]{0:T(1024)S(1)}, f32[6928]{0:T(1024)S(1)}, u32[]{:S(2)}, u32[]{:S(2)}) collective-permute-start(f32[6928]{0:T(1024)S(1)} %add.377), channel_id=1, source_target_pairs={{0,16},{1,17},{2,18},{3,19},{4,20},{5,21},{6,22},{7,23},{8,24},{9,... | collective-permute-start | bytes 83144 | tf_op jit(solution)/shard_map/ppermute | solution.py:27
  150.9 7.5 %collective-permute-done.15 = f32[6928]{0:T(1024)S(1)} collective-permute-done((f32[6928]{0:T(1024)S(1)}, f32[6928]{0:T(1024)S(1)}, u32[]{:S(2)}, u32[]{:S(2)}) %collective-permute-start.15) | collective-permute-done | bytes 27744 | tf_op jit(solution)/shard_map/ppermute | solution.py:27
  158.4 4.9 %collective-permute-start.16 = (f32[6928]{0:T(1024)S(1)}, f32[6928]{0:T(1024)S(1)}, u32[]{:S(2)}, u32[]{:S(2)}) collective-permute-start(f32[6928]{0:T(1024)S(1)} %add.378), channel_id=1, source_target_pairs={{0,32},{1,33},{2,34},{3,35},{4,36},{5,37},{6,38},{7,39},{8,40},{9,... | collective-permute-start | bytes 83144 | tf_op jit(solution)/shard_map/ppermute | solution.py:27
  164.2 4.1 %collective-permute-done.16 = f32[6928]{0:T(1024)S(1)} collective-permute-done((f32[6928]{0:T(1024)S(1)}, f32[6928]{0:T(1024)S(1)}, u32[]{:S(2)}, u32[]{:S(2)}) %collective-permute-start.16) | collective-permute-done | bytes 27744 | tf_op jit(solution)/shard_map/ppermute | solution.py:27
  (114 shorter events, 17.5 us)
Async XLA Ops:
  0.6 6.5 %copy-start.1 = (s32[1,3]{1,0:T(1,128)S(1)}, s32[1,3]{1,0:T(1,128)}, u32[]{:S(2)}) copy-start(s32[1,3]{1,0:T(1,128)} %param.11) | copy-start | bytes 40
  3.7 9.9 %collective-permute-start = (bf16[1,16,4,8,256]{4,1,3,2,0:T(8,128)(2,1)S(1)}, bf16[1,16,4,8,256]{4,1,3,2,0:T(8,128)(2,1)S(1)}, u32[]{:S(2)}, u32[]{:S(2)}) collective-permute-start(bf16[1,16,4,8,256]{4,1,3,2,0:T(8,128)(2,1)S(1)} %pad_maximum_fusion.54), channel_id=1, source_target_pairs={{0,1},{1,0},{2,3},{3,2},{4,5},{5,4},{6,7},{7,6},{8,9},{9,8},{10,11... | collective-permute-start | bytes 786440 | tf_op jit(solution)/shard_map/ppermute | solution.py:58
  13.8 10.6 %collective-permute-start.1 = (bf16[1,16,4,8,256]{4,1,3,2,0:T(8,128)(2,1)S(1)}, bf16[1,16,4,8,256]{4,1,3,2,0:T(8,128)(2,1)S(1)}, u32[]{:S(2)}, u32[]{:S(2)}) collective-permute-start(bf16[1,16,4,8,256]{4,1,3,2,0:T(8,128)(2,1)S(1)} %pad_maximum_fusion.55), channel_id=1, source_target_pairs={{0,2},{1,3},{2,0},{3,1},{4,6},{5,7},{6,4},{7,5},{8,10},{9,11},{10,... | collective-permute-start | bytes 786440 | tf_op jit(solution)/shard_map/ppermute | solution.py:58
  24.4 8.8 %collective-permute-start.2 = (bf16[1,16,4,8,256]{4,1,3,2,0:T(8,128)(2,1)S(1)}, bf16[1,16,4,8,256]{4,1,3,2,0:T(8,128)(2,1)S(1)}, u32[]{:S(2)}, u32[]{:S(2)}) collective-permute-start(bf16[1,16,4,8,256]{4,1,3,2,0:T(8,128)(2,1)S(1)} %pad_maximum_fusion.56), channel_id=1, source_target_pairs={{0,4},{1,5},{2,6},{3,7},{4,0},{5,1},{6,2},{7,3},{8,12},{9,13},{10,... | collective-permute-start | bytes 786440 | tf_op jit(solution)/shard_map/ppermute | solution.py:58
  33.3 15.6 %collective-permute-start.3 = (bf16[1,16,4,8,256]{4,1,3,2,0:T(8,128)(2,1)S(1)}, bf16[1,16,4,8,256]{4,1,3,2,0:T(8,128)(2,1)S(1)}, u32[]{:S(2)}, u32[]{:S(2)}) collective-permute-start(bf16[1,16,4,8,256]{4,1,3,2,0:T(8,128)(2,1)S(1)} %pad_maximum_fusion.57), channel_id=1, source_target_pairs={{0,8},{1,9},{2,10},{3,11},{4,12},{5,13},{6,14},{7,15},{8,0},{9,1},... | collective-permute-start | bytes 786440 | tf_op jit(solution)/shard_map/ppermute | solution.py:58
  48.9 19.3 %collective-permute-start.4 = (bf16[1,16,4,8,256]{4,1,3,2,0:T(8,128)(2,1)S(1)}, bf16[1,16,4,8,256]{4,1,3,2,0:T(8,128)(2,1)S(1)}, u32[]{:S(2)}, u32[]{:S(2)}) collective-permute-start(bf16[1,16,4,8,256]{4,1,3,2,0:T(8,128)(2,1)S(1)} %pad_maximum_fusion.58), channel_id=1, source_target_pairs={{0,16},{1,17},{2,18},{3,19},{4,20},{5,21},{6,22},{7,23},{8,24},{9,... | collective-permute-start | bytes 786440 | tf_op jit(solution)/shard_map/ppermute | solution.py:58
  57.5 24.4 %copy-start = (bf16[27,16,16]{0,2,1:T(8,128)(2,1)S(1)}, bf16[27,16,16]{0,2,1:T(8,128)(2,1)}, u32[]{:S(2)}) copy-start(bf16[27,16,16]{0,2,1:T(8,128)(2,1)} %param.13) | copy-start | bytes 41476
  68.3 14.7 %collective-permute-start.5 = (bf16[1,16,4,8,256]{4,1,3,2,0:T(8,128)(2,1)S(1)}, bf16[1,16,4,8,256]{4,1,3,2,0:T(8,128)(2,1)S(1)}, u32[]{:S(2)}, u32[]{:S(2)}) collective-permute-start(bf16[1,16,4,8,256]{4,1,3,2,0:T(8,128)(2,1)S(1)} %pad_maximum_fusion.59), channel_id=1, source_target_pairs={{0,32},{1,33},{2,34},{3,35},{4,36},{5,37},{6,38},{7,39},{8,40},{9,... | collective-permute-start | bytes 786440 | tf_op jit(solution)/shard_map/ppermute | solution.py:58
  85.0 0.7 copy-start.2
  86.9 0.9 copy-start.3
  92.8 17.5 %collective-permute-start.8 = (f32[6928]{0:T(1024)S(1)}, f32[6928]{0:T(1024)S(1)}, u32[]{:S(2)}, u32[]{:S(2)}) collective-permute-start(f32[6928]{0:T(1024)S(1)} %pad_maximum_fusion.61), channel_id=1, source_target_pairs={{0,64},{64,0},{128,192},{192,128},{256,320},{320,256},{384,448},{4... | collective-permute-start | bytes 83144 | tf_op jit(solution)/shard_map/ppermute | solution.py:27
  94.8 24.3 %collective-permute-start.6 = (bf16[1,16,1,8,256]{4,1,3,2,0:T(8,128)(2,1)S(1)}, bf16[1,16,1,8,256]{4,1,3,2,0:T(8,128)(2,1)S(1)}, u32[]{:S(2)}, u32[]{:S(2)}) collective-permute-start(bf16[1,16,1,8,256]{4,1,3,2,0:T(8,128)(2,1)S(1)} %get-tuple-element.80), channel_id=1, source_target_pairs={{0,1},{1,2},{2,3},{3,4},{4,5},{5,6},{6,7},{7,8},{8,9},{9,10},{10,1... | collective-permute-start | bytes 196616 | tf_op jit(solution)/shard_map/ppermute | solution.py:19
  98.2 20.9 %collective-permute-start.7 = (bf16[1,16,1,8,256]{4,1,3,2,0:T(8,128)(2,1)S(1)}, bf16[1,16,1,8,256]{4,1,3,2,0:T(8,128)(2,1)S(1)}, u32[]{:S(2)}, u32[]{:S(2)}) collective-permute-start(bf16[1,16,1,8,256]{4,1,3,2,0:T(8,128)(2,1)S(1)} %get-tuple-element.81), channel_id=1, source_target_pairs={{0,63},{1,0},{2,1},{3,2},{4,3},{5,4},{6,5},{7,6},{8,7},{9,8},{10,9... | collective-permute-start | bytes 196616 | tf_op jit(solution)/shard_map/ppermute | solution.py:19
  110.4 6.1 %collective-permute-start.9 = (f32[6928]{0:T(1024)S(1)}, f32[6928]{0:T(1024)S(1)}, u32[]{:S(2)}, u32[]{:S(2)}) collective-permute-start(f32[6928]{0:T(1024)S(1)} %fusion.173), channel_id=1, source_target_pairs={{0,128},{64,192},{128,0},{192,64},{256,384},{320,448},{384,256},{4... | collective-permute-start | bytes 83144 | tf_op jit(solution)/shard_map/ppermute | solution.py:27
  116.5 6.8 %collective-permute-start.10 = (f32[6928]{0:T(1024)S(1)}, f32[6928]{0:T(1024)S(1)}, u32[]{:S(2)}, u32[]{:S(2)}) collective-permute-start(f32[6928]{0:T(1024)S(1)} %add.372), channel_id=1, source_target_pairs={{0,256},{64,320},{128,384},{192,448},{256,0},{320,64},{384,128},{4... | collective-permute-start | bytes 83144 | tf_op jit(solution)/shard_map/ppermute | solution.py:27
  123.3 5.8 %collective-permute-start.11 = (f32[6928]{0:T(1024)S(1)}, f32[6928]{0:T(1024)S(1)}, u32[]{:S(2)}, u32[]{:S(2)}) collective-permute-start(f32[6928]{0:T(1024)S(1)} %add.373), channel_id=1, source_target_pairs={{0,1},{1,0},{2,3},{3,2},{4,5},{5,4},{6,7},{7,6},{8,9},{9,8},{10,11... | collective-permute-start | bytes 83144 | tf_op jit(solution)/shard_map/ppermute | solution.py:27
  129.0 7.3 %collective-permute-start.12 = (f32[6928]{0:T(1024)S(1)}, f32[6928]{0:T(1024)S(1)}, u32[]{:S(2)}, u32[]{:S(2)}) collective-permute-start(f32[6928]{0:T(1024)S(1)} %add.374), channel_id=1, source_target_pairs={{0,2},{1,3},{2,0},{3,1},{4,6},{5,7},{6,4},{7,5},{8,10},{9,11},{10,... | collective-permute-start | bytes 83144 | tf_op jit(solution)/shard_map/ppermute | solution.py:27
  136.3 5.8 %collective-permute-start.13 = (f32[6928]{0:T(1024)S(1)}, f32[6928]{0:T(1024)S(1)}, u32[]{:S(2)}, u32[]{:S(2)}) collective-permute-start(f32[6928]{0:T(1024)S(1)} %add.375), channel_id=1, source_target_pairs={{0,4},{1,5},{2,6},{3,7},{4,0},{5,1},{6,2},{7,3},{8,12},{9,13},{10,... | collective-permute-start | bytes 83144 | tf_op jit(solution)/shard_map/ppermute | solution.py:27
  142.1 6.7 %collective-permute-start.14 = (f32[6928]{0:T(1024)S(1)}, f32[6928]{0:T(1024)S(1)}, u32[]{:S(2)}, u32[]{:S(2)}) collective-permute-start(f32[6928]{0:T(1024)S(1)} %add.376), channel_id=1, source_target_pairs={{0,8},{1,9},{2,10},{3,11},{4,12},{5,13},{6,14},{7,15},{8,0},{9,1},... | collective-permute-start | bytes 83144 | tf_op jit(solution)/shard_map/ppermute | solution.py:27
  148.7 9.7 %collective-permute-start.15 = (f32[6928]{0:T(1024)S(1)}, f32[6928]{0:T(1024)S(1)}, u32[]{:S(2)}, u32[]{:S(2)}) collective-permute-start(f32[6928]{0:T(1024)S(1)} %add.377), channel_id=1, source_target_pairs={{0,16},{1,17},{2,18},{3,19},{4,20},{5,21},{6,22},{7,23},{8,24},{9,... | collective-permute-start | bytes 83144 | tf_op jit(solution)/shard_map/ppermute | solution.py:27
  158.4 10.0 %collective-permute-start.16 = (f32[6928]{0:T(1024)S(1)}, f32[6928]{0:T(1024)S(1)}, u32[]{:S(2)}, u32[]{:S(2)}) collective-permute-start(f32[6928]{0:T(1024)S(1)} %add.378), channel_id=1, source_target_pairs={{0,32},{1,33},{2,34},{3,35},{4,36},{5,37},{6,38},{7,39},{8,40},{9,... | collective-permute-start | bytes 83144 | tf_op jit(solution)/shard_map/ppermute | solution.py:27

commit v5 on v4

--- a/solution.py
+++ b/solution.py
@@ -52,20 +52,21 @@
 def routed(pieces, axis, sign, constants):
     count = lax.axis_size(axis)
     here = lax.axis_index(axis)
-    step = 1
-    while step < count:
+    step = count // 2
+    while step >= 1:
         pairs = [(peer, peer ^ step) for peer in range(count)]
         arrived = lax.ppermute(jnp.concatenate(pieces, axis=2), axis, pairs)
         updated = []
         begin = 0
         for piece, constant in zip(pieces, constants):
             size = piece.shape[2]
-            wanted = jnp.mod(sign * (here - constant), 2 * step)
-            take = (wanted // step % 2) != (here // step % 2)
+            landed = jnp.mod(sign * (here % step) + constant, count)
+            rest = jnp.mod(sign * (here // step - landed // step), count // step)
+            take = (rest % 2) != (here // step % 2)
             updated.append(jnp.where(take, arrived[:, :, begin : begin + size], piece))
             begin += size
         pieces = updated
-        step *= 2
+        step //= 2
     return pieces
 
 

time: 171 us -> 180 us (1.053)
  the two profiles are of different devices: /device:TPU:8 before, /device:TPU:16 now
where the time goes in v5:
time: 180 us; the launch traced here: 179 us
  waiting for transfers between devices  82.4 us (46%)
  starting transfers between devices  65.1 us (36%)
  between operations  11.8 us (7%)
  local copies, waits for them, and re-layouts  9.32 us (5%)
  matrix products  8.43 us (5%)
  other arithmetic  2.08 us (1%)
    ppermute x6, waiting for transfers between devices, routed(): arrived = lax.ppermute(jnp.concatenate(pieces, axis=2), axis, pairs)  45.1 us
    ppermute x9, waiting for transfers between devices, butterfly_sum(): value = value + lax.ppermute(value, axis, pairs)  37.3 us
    ppermute x6, starting transfers between devices, routed(): arrived = lax.ppermute(jnp.concatenate(pieces, axis=2), axis, pairs)  33.3 us
    ppermute x9, starting transfers between devices, butterfly_sum(): value = value + lax.ppermute(value, axis, pairs)  17.8 us
    ppermute x2, starting transfers between devices, shifted(): return lax.ppermute(value, axis, pairs)  14 us
    dot_general x9, matrix products, on_device(): jnp.einsum('boxyz,bcxyz->oc', grad_pre, window, preferred_element_type=jn...  4.43 us
    unnamed x13, local copies, waits for them, and re-layouts  4.4 us
  transfers between devices with their start and end apart: 17, of which 13 were waited for; matrix products, arithmetic and copies ran while one was open for 3% of the time, Pallas kernels for 0%

profile of v5, /device:TPU:16, one launch (start us, length us, event | category | flops | bytes accessed | tf_op | source)
XLA Modules:
  0.0 179.1 jit_solution(3710211012175002821)
XLA Ops:
  0.6 1.4 fusion.153
  2.0 0.9 copy.42
  3.7 5.9 %collective-permute-start = (bf16[1,16,4,8,256]{4,1,3,2,0:T(8,128)(2,1)S(1)}, bf16[1,16,4,8,256]{4,1,3,2,0:T(8,128)(2,1)S(1)}, u32[]{:S(2)}, u32[]{:S(2)}) collective-permute-start(bf16[1,16,4,8,256]{4,1,3,2,0:T(8,128)(2,1)S(1)} %pad_maximum_fusion.54), channel_id=1, source_target_pairs={{0,32},{1,33},{2,34},{3,35},{4,36},{5,37},{6,38},{7,39},{8,40},{9,... | collective-permute-start | bytes 786440 | tf_op jit(solution)/shard_map/ppermute | solution.py:58
  12.5 9.6 %collective-permute-done = bf16[1,16,4,8,256]{4,1,3,2,0:T(8,128)(2,1)S(1)} collective-permute-done((bf16[1,16,4,8,256]{4,1,3,2,0:T(8,128)(2,1)S(1)}, bf16[1,16,4,8,256]{4,1,3,2,0:T(8,128)(2,1)S(1)}, u32[]{:S(2)}, u32[]{:S(2)}) %collective-permute-start) | collective-permute-done | bytes 262176 | tf_op jit(solution)/shard_map/ppermute | solution.py:58
  22.2 12.1 %collective-permute-start.1 = (bf16[1,16,4,8,256]{4,1,3,2,0:T(8,128)(2,1)S(1)}, bf16[1,16,4,8,256]{4,1,3,2,0:T(8,128)(2,1)S(1)}, u32[]{:S(2)}, u32[]{:S(2)}) collective-permute-start(bf16[1,16,4,8,256]{4,1,3,2,0:T(8,128)(2,1)S(1)} %pad_maximum_fusion.55), channel_id=1, source_target_pairs={{0,16},{1,17},{2,18},{3,19},{4,20},{5,21},{6,22},{7,23},{8,24},{9,... | collective-permute-start | bytes 786440 | tf_op jit(solution)/shard_map/ppermute | solution.py:58
  34.6 11.0 %collective-permute-done.1 = bf16[1,16,4,8,256]{4,1,3,2,0:T(8,128)(2,1)S(1)} collective-permute-done((bf16[1,16,4,8,256]{4,1,3,2,0:T(8,128)(2,1)S(1)}, bf16[1,16,4,8,256]{4,1,3,2,0:T(8,128)(2,1)S(1)}, u32[]{:S(2)}, u32[]{:S(2)}) %collective-permute-start.1) | collective-permute-done | bytes 262176 | tf_op jit(solution)/shard_map/ppermute | solution.py:58
  45.6 5.0 %collective-permute-start.2 = (bf16[1,16,4,8,256]{4,1,3,2,0:T(8,128)(2,1)S(1)}, bf16[1,16,4,8,256]{4,1,3,2,0:T(8,128)(2,1)S(1)}, u32[]{:S(2)}, u32[]{:S(2)}) collective-permute-start(bf16[1,16,4,8,256]{4,1,3,2,0:T(8,128)(2,1)S(1)} %pad_maximum_fusion.56), channel_id=1, source_target_pairs={{0,8},{1,9},{2,10},{3,11},{4,12},{5,13},{6,14},{7,15},{8,0},{9,1},... | collective-permute-start | bytes 786440 | tf_op jit(solution)/shard_map/ppermute | solution.py:58
  50.9 11.9 %collective-permute-done.2 = bf16[1,16,4,8,256]{4,1,3,2,0:T(8,128)(2,1)S(1)} collective-permute-done((bf16[1,16,4,8,256]{4,1,3,2,0:T(8,128)(2,1)S(1)}, bf16[1,16,4,8,256]{4,1,3,2,0:T(8,128)(2,1)S(1)}, u32[]{:S(2)}, u32[]{:S(2)}) %collective-permute-start.2) | collective-permute-done | bytes 262176 | tf_op jit(solution)/shard_map/ppermute | solution.py:58
  62.8 1.9 %collective-permute-start.3 = (bf16[1,16,4,8,256]{4,1,3,2,0:T(8,128)(2,1)S(1)}, bf16[1,16,4,8,256]{4,1,3,2,0:T(8,128)(2,1)S(1)}, u32[]{:S(2)}, u32[]{:S(2)}) collective-permute-start(bf16[1,16,4,8,256]{4,1,3,2,0:T(8,128)(2,1)S(1)} %pad_maximum_fusion.57), channel_id=1, source_target_pairs={{0,4},{1,5},{2,6},{3,7},{4,0},{5,1},{6,2},{7,3},{8,12},{9,13},{10,... | collective-permute-start | bytes 786440 | tf_op jit(solution)/shard_map/ppermute | solution.py:58
  65.0 7.5 %collective-permute-done.3 = bf16[1,16,4,8,256]{4,1,3,2,0:T(8,128)(2,1)S(1)} collective-permute-done((bf16[1,16,4,8,256]{4,1,3,2,0:T(8,128)(2,1)S(1)}, bf16[1,16,4,8,256]{4,1,3,2,0:T(8,128)(2,1)S(1)}, u32[]{:S(2)}, u32[]{:S(2)}) %collective-permute-start.3) | collective-permute-done | bytes 262176 | tf_op jit(solution)/shard_map/ppermute | solution.py:58
  72.6 4.9 %collective-permute-start.4 = (bf16[1,16,4,8,256]{4,1,3,2,0:T(8,128)(2,1)S(1)}, bf16[1,16,4,8,256]{4,1,3,2,0:T(8,128)(2,1)S(1)}, u32[]{:S(2)}, u32[]{:S(2)}) collective-permute-start(bf16[1,16,4,8,256]{4,1,3,2,0:T(8,128)(2,1)S(1)} %pad_maximum_fusion.58), channel_id=1, source_target_pairs={{0,2},{1,3},{2,0},{3,1},{4,6},{5,7},{6,4},{7,5},{8,10},{9,11},{10,... | collective-permute-start | bytes 786440 | tf_op jit(solution)/shard_map/ppermute | solution.py:58
  77.8 5.1 %collective-permute-done.4 = bf16[1,16,4,8,256]{4,1,3,2,0:T(8,128)(2,1)S(1)} collective-permute-done((bf16[1,16,4,8,256]{4,1,3,2,0:T(8,128)(2,1)S(1)}, bf16[1,16,4,8,256]{4,1,3,2,0:T(8,128)(2,1)S(1)}, u32[]{:S(2)}, u32[]{:S(2)}) %collective-permute-start.4) | collective-permute-done | bytes 262176 | tf_op jit(solution)/shard_map/ppermute | solution.py:58
  83.0 3.4 %collective-permute-start.5 = (bf16[1,16,4,8,256]{4,1,3,2,0:T(8,128)(2,1)S(1)}, bf16[1,16,4,8,256]{4,1,3,2,0:T(8,128)(2,1)S(1)}, u32[]{:S(2)}, u32[]{:S(2)}) collective-permute-start(bf16[1,16,4,8,256]{4,1,3,2,0:T(8,128)(2,1)S(1)} %pad_maximum_fusion.59), channel_id=1, source_target_pairs={{0,1},{1,0},{2,3},{3,2},{4,5},{5,4},{6,7},{7,6},{8,9},{9,8},{10,11... | collective-permute-start | bytes 786440 | tf_op jit(solution)/shard_map/ppermute | solution.py:58
  104.0 1.9 %collective-permute-start.8 = (f32[6928]{0:T(1024)S(1)}, f32[6928]{0:T(1024)S(1)}, u32[]{:S(2)}, u32[]{:S(2)}) collective-permute-start(f32[6928]{0:T(1024)S(1)} %pad_maximum_fusion.61), channel_id=1, source_target_pairs={{0,64},{64,0},{128,192},{192,128},{256,320},{320,256},{384,448},{4... | collective-permute-start | bytes 83144 | tf_op jit(solution)/shard_map/ppermute | solution.py:27
  106.0 2.4 %collective-permute-start.6 = (bf16[1,16,1,8,256]{4,1,3,2,0:T(8,128)(2,1)S(1)}, bf16[1,16,1,8,256]{4,1,3,2,0:T(8,128)(2,1)S(1)}, u32[]{:S(2)}, u32[]{:S(2)}) collective-permute-start(bf16[1,16,1,8,256]{4,1,3,2,0:T(8,128)(2,1)S(1)} %get-tuple-element.80), channel_id=1, source_target_pairs={{0,1},{1,2},{2,3},{3,4},{4,5},{5,6},{6,7},{7,8},{8,9},{9,10},{10,1... | collective-permute-start | bytes 196616 | tf_op jit(solution)/shard_map/ppermute | solution.py:19
  108.4 11.5 %collective-permute-start.7 = (bf16[1,16,1,8,256]{4,1,3,2,0:T(8,128)(2,1)S(1)}, bf16[1,16,1,8,256]{4,1,3,2,0:T(8,128)(2,1)S(1)}, u32[]{:S(2)}, u32[]{:S(2)}) collective-permute-start(bf16[1,16,1,8,256]{4,1,3,2,0:T(8,128)(2,1)S(1)} %get-tuple-element.81), channel_id=1, source_target_pairs={{0,63},{1,0},{2,1},{3,2},{4,3},{5,4},{6,5},{7,6},{8,7},{9,8},{10,9... | collective-permute-start | bytes 196616 | tf_op jit(solution)/shard_map/ppermute | solution.py:19
  120.0 1.9 %collective-permute-start.9 = (f32[6928]{0:T(1024)S(1)}, f32[6928]{0:T(1024)S(1)}, u32[]{:S(2)}, u32[]{:S(2)}) collective-permute-start(f32[6928]{0:T(1024)S(1)} %fusion.173), channel_id=1, source_target_pairs={{0,128},{64,192},{128,0},{192,64},{256,384},{320,448},{384,256},{4... | collective-permute-start | bytes 83144 | tf_op jit(solution)/shard_map/ppermute | solution.py:27
  122.6 3.1 %collective-permute-done.9 = f32[6928]{0:T(1024)S(1)} collective-permute-done((f32[6928]{0:T(1024)S(1)}, f32[6928]{0:T(1024)S(1)}, u32[]{:S(2)}, u32[]{:S(2)}) %collective-permute-start.9) | collective-permute-done | bytes 27744 | tf_op jit(solution)/shard_map/ppermute | solution.py:27
  125.8 1.9 %collective-permute-start.10 = (f32[6928]{0:T(1024)S(1)}, f32[6928]{0:T(1024)S(1)}, u32[]{:S(2)}, u32[]{:S(2)}) collective-permute-start(f32[6928]{0:T(1024)S(1)} %add.537), channel_id=1, source_target_pairs={{0,256},{64,320},{128,384},{192,448},{256,0},{320,64},{384,128},{4... | collective-permute-start | bytes 83144 | tf_op jit(solution)/shard_map/ppermute | solution.py:27
  129.1 3.3 %collective-permute-done.10 = f32[6928]{0:T(1024)S(1)} collective-permute-done((f32[6928]{0:T(1024)S(1)}, f32[6928]{0:T(1024)S(1)}, u32[]{:S(2)}, u32[]{:S(2)}) %collective-permute-start.10) | collective-permute-done | bytes 27744 | tf_op jit(solution)/shard_map/ppermute | solution.py:27
  132.4 1.9 %collective-permute-start.11 = (f32[6928]{0:T(1024)S(1)}, f32[6928]{0:T(1024)S(1)}, u32[]{:S(2)}, u32[]{:S(2)}) collective-permute-start(f32[6928]{0:T(1024)S(1)} %add.538), channel_id=1, source_target_pairs={{0,1},{1,0},{2,3},{3,2},{4,5},{5,4},{6,7},{7,6},{8,9},{9,8},{10,11... | collective-permute-start | bytes 83144 | tf_op jit(solution)/shard_map/ppermute | solution.py:27
  134.6 3.7 %collective-permute-done.11 = f32[6928]{0:T(1024)S(1)} collective-permute-done((f32[6928]{0:T(1024)S(1)}, f32[6928]{0:T(1024)S(1)}, u32[]{:S(2)}, u32[]{:S(2)}) %collective-permute-start.11) | collective-permute-done | bytes 27744 | tf_op jit(solution)/shard_map/ppermute | solution.py:27
  138.3 1.9 %collective-permute-start.12 = (f32[6928]{0:T(1024)S(1)}, f32[6928]{0:T(1024)S(1)}, u32[]{:S(2)}, u32[]{:S(2)}) collective-permute-start(f32[6928]{0:T(1024)S(1)} %add.539), channel_id=1, source_target_pairs={{0,2},{1,3},{2,0},{3,1},{4,6},{5,7},{6,4},{7,5},{8,10},{9,11},{10,... | collective-permute-start | bytes 83144 | tf_op jit(solution)/shard_map/ppermute | solution.py:27
  140.5 5.1 %collective-permute-done.12 = f32[6928]{0:T(1024)S(1)} collective-permute-done((f32[6928]{0:T(1024)S(1)}, f32[6928]{0:T(1024)S(1)}, u32[]{:S(2)}, u32[]{:S(2)}) %collective-permute-start.12) | collective-permute-done | bytes 27744 | tf_op jit(solution)/shard_map/ppermute | solution.py:27
  145.6 1.9 %collective-permute-start.13 = (f32[6928]{0:T(1024)S(1)}, f32[6928]{0:T(1024)S(1)}, u32[]{:S(2)}, u32[]{:S(2)}) collective-permute-start(f32[6928]{0:T(1024)S(1)} %add.540), channel_id=1, source_target_pairs={{0,4},{1,5},{2,6},{3,7},{4,0},{5,1},{6,2},{7,3},{8,12},{9,13},{10,... | collective-permute-start | bytes 83144 | tf_op jit(solution)/shard_map/ppermute | solution.py:27
  147.8 3.9 %collective-permute-done.13 = f32[6928]{0:T(1024)S(1)} collective-permute-done((f32[6928]{0:T(1024)S(1)}, f32[6928]{0:T(1024)S(1)}, u32[]{:S(2)}, u32[]{:S(2)}) %collective-permute-start.13) | collective-permute-done | bytes 27744 | tf_op jit(solution)/shard_map/ppermute | solution.py:27
  151.6 1.9 %collective-permute-start.14 = (f32[6928]{0:T(1024)S(1)}, f32[6928]{0:T(1024)S(1)}, u32[]{:S(2)}, u32[]{:S(2)}) collective-permute-start(f32[6928]{0:T(1024)S(1)} %add.541), channel_id=1, source_target_pairs={{0,8},{1,9},{2,10},{3,11},{4,12},{5,13},{6,14},{7,15},{8,0},{9,1},... | collective-permute-start | bytes 83144 | tf_op jit(solution)/shard_map/ppermute | solution.py:27
  153.8 4.5 %collective-permute-done.14 = f32[6928]{0:T(1024)S(1)} collective-permute-done((f32[6928]{0:T(1024)S(1)}, f32[6928]{0:T(1024)S(1)}, u32[]{:S(2)}, u32[]{:S(2)}) %collective-permute-start.14) | collective-permute-done | bytes 27744 | tf_op jit(solution)/shard_map/ppermute | solution.py:27
  158.3 2.5 %collective-permute-start.15 = (f32[6928]{0:T(1024)S(1)}, f32[6928]{0:T(1024)S(1)}, u32[]{:S(2)}, u32[]{:S(2)}) collective-permute-start(f32[6928]{0:T(1024)S(1)} %add.542), channel_id=1, source_target_pairs={{0,16},{1,17},{2,18},{3,19},{4,20},{5,21},{6,22},{7,23},{8,24},{9,... | collective-permute-start | bytes 83144 | tf_op jit(solution)/shard_map/ppermute | solution.py:27
  161.1 6.9 %collective-permute-done.15 = f32[6928]{0:T(1024)S(1)} collective-permute-done((f32[6928]{0:T(1024)S(1)}, f32[6928]{0:T(1024)S(1)}, u32[]{:S(2)}, u32[]{:S(2)}) %collective-permute-start.15) | collective-permute-done | bytes 27744 | tf_op jit(solution)/shard_map/ppermute | solution.py:27
  168.0 1.9 %collective-permute-start.16 = (f32[6928]{0:T(1024)S(1)}, f32[6928]{0:T(1024)S(1)}, u32[]{:S(2)}, u32[]{:S(2)}) collective-permute-start(f32[6928]{0:T(1024)S(1)} %add.543), channel_id=1, source_target_pairs={{0,32},{1,33},{2,34},{3,35},{4,36},{5,37},{6,38},{7,39},{8,40},{9,... | collective-permute-start | bytes 83144 | tf_op jit(solution)/shard_map/ppermute | solution.py:27
  170.8 6.8 %collective-permute-done.16 = f32[6928]{0:T(1024)S(1)} collective-permute-done((f32[6928]{0:T(1024)S(1)}, f32[6928]{0:T(1024)S(1)}, u32[]{:S(2)}, u32[]{:S(2)}) %collective-permute-start.16) | collective-permute-done | bytes 27744 | tf_op jit(solution)/shard_map/ppermute | solution.py:27
  (114 shorter events, 17.5 us)
Async XLA Ops:
  0.6 9.0 %copy-start.1 = (s32[1,3]{1,0:T(1,128)S(1)}, s32[1,3]{1,0:T(1,128)}, u32[]{:S(2)}) copy-start(s32[1,3]{1,0:T(1,128)} %param.11) | copy-start | bytes 40
  3.7 18.4 %collective-permute-start = (bf16[1,16,4,8,256]{4,1,3,2,0:T(8,128)(2,1)S(1)}, bf16[1,16,4,8,256]{4,1,3,2,0:T(8,128)(2,1)S(1)}, u32[]{:S(2)}, u32[]{:S(2)}) collective-permute-start(bf16[1,16,4,8,256]{4,1,3,2,0:T(8,128)(2,1)S(1)} %pad_maximum_fusion.54), channel_id=1, source_target_pairs={{0,32},{1,33},{2,34},{3,35},{4,36},{5,37},{6,38},{7,39},{8,40},{9,... | collective-permute-start | bytes 786440 | tf_op jit(solution)/shard_map/ppermute | solution.py:58
  22.2 23.3 %collective-permute-start.1 = (bf16[1,16,4,8,256]{4,1,3,2,0:T(8,128)(2,1)S(1)}, bf16[1,16,4,8,256]{4,1,3,2,0:T(8,128)(2,1)S(1)}, u32[]{:S(2)}, u32[]{:S(2)}) collective-permute-start(bf16[1,16,4,8,256]{4,1,3,2,0:T(8,128)(2,1)S(1)} %pad_maximum_fusion.55), channel_id=1, source_target_pairs={{0,16},{1,17},{2,18},{3,19},{4,20},{5,21},{6,22},{7,23},{8,24},{9,... | collective-permute-start | bytes 786440 | tf_op jit(solution)/shard_map/ppermute | solution.py:58
  45.6 17.1 %collective-permute-start.2 = (bf16[1,16,4,8,256]{4,1,3,2,0:T(8,128)(2,1)S(1)}, bf16[1,16,4,8,256]{4,1,3,2,0:T(8,128)(2,1)S(1)}, u32[]{:S(2)}, u32[]{:S(2)}) collective-permute-start(bf16[1,16,4,8,256]{4,1,3,2,0:T(8,128)(2,1)S(1)} %pad_maximum_fusion.56), channel_id=1, source_target_pairs={{0,8},{1,9},{2,10},{3,11},{4,12},{5,13},{6,14},{7,15},{8,0},{9,1},... | collective-permute-start | bytes 786440 | tf_op jit(solution)/shard_map/ppermute | solution.py:58
  62.8 9.7 %collective-permute-start.3 = (bf16[1,16,4,8,256]{4,1,3,2,0:T(8,128)(2,1)S(1)}, bf16[1,16,4,8,256]{4,1,3,2,0:T(8,128)(2,1)S(1)}, u32[]{:S(2)}, u32[]{:S(2)}) collective-permute-start(bf16[1,16,4,8,256]{4,1,3,2,0:T(8,128)(2,1)S(1)} %pad_maximum_fusion.57), channel_id=1, source_target_pairs={{0,4},{1,5},{2,6},{3,7},{4,0},{5,1},{6,2},{7,3},{8,12},{9,13},{10,... | collective-permute-start | bytes 786440 | tf_op jit(solution)/shard_map/ppermute | solution.py:58
  72.6 10.3 %collective-permute-start.4 = (bf16[1,16,4,8,256]{4,1,3,2,0:T(8,128)(2,1)S(1)}, bf16[1,16,4,8,256]{4,1,3,2,0:T(8,128)(2,1)S(1)}, u32[]{:S(2)}, u32[]{:S(2)}) collective-permute-start(bf16[1,16,4,8,256]{4,1,3,2,0:T(8,128)(2,1)S(1)} %pad_maximum_fusion.58), channel_id=1, source_target_pairs={{0,2},{1,3},{2,0},{3,1},{4,6},{5,7},{6,4},{7,5},{8,10},{9,11},{10,... | collective-permute-start | bytes 786440 | tf_op jit(solution)/shard_map/ppermute | solution.py:58
  77.8 15.3 %copy-start = (bf16[27,16,16]{0,2,1:T(8,128)(2,1)S(1)}, bf16[27,16,16]{0,2,1:T(8,128)(2,1)}, u32[]{:S(2)}) copy-start(bf16[27,16,16]{0,2,1:T(8,128)(2,1)} %param.13) | copy-start | bytes 41476
  83.0 11.2 %collective-permute-start.5 = (bf16[1,16,4,8,256]{4,1,3,2,0:T(8,128)(2,1)S(1)}, bf16[1,16,4,8,256]{4,1,3,2,0:T(8,128)(2,1)S(1)}, u32[]{:S(2)}, u32[]{:S(2)}) collective-permute-start(bf16[1,16,4,8,256]{4,1,3,2,0:T(8,128)(2,1)S(1)} %pad_maximum_fusion.59), channel_id=1, source_target_pairs={{0,1},{1,0},{2,3},{3,2},{4,5},{5,4},{6,7},{7,6},{8,9},{9,8},{10,11... | collective-permute-start | bytes 786440 | tf_op jit(solution)/shard_map/ppermute | solution.py:58
  96.2 0.7 copy-start.2
  98.1 0.9 copy-start.3
  104.0 15.9 %collective-permute-start.8 = (f32[6928]{0:T(1024)S(1)}, f32[6928]{0:T(1024)S(1)}, u32[]{:S(2)}, u32[]{:S(2)}) collective-permute-start(f32[6928]{0:T(1024)S(1)} %pad_maximum_fusion.61), channel_id=1, source_target_pairs={{0,64},{64,0},{128,192},{192,128},{256,320},{320,256},{384,448},{4... | collective-permute-start | bytes 83144 | tf_op jit(solution)/shard_map/ppermute | solution.py:27
  106.0 21.7 %collective-permute-start.6 = (bf16[1,16,1,8,256]{4,1,3,2,0:T(8,128)(2,1)S(1)}, bf16[1,16,1,8,256]{4,1,3,2,0:T(8,128)(2,1)S(1)}, u32[]{:S(2)}, u32[]{:S(2)}) collective-permute-start(bf16[1,16,1,8,256]{4,1,3,2,0:T(8,128)(2,1)S(1)} %get-tuple-element.80), channel_id=1, source_target_pairs={{0,1},{1,2},{2,3},{3,4},{4,5},{5,6},{6,7},{7,8},{8,9},{9,10},{10,1... | collective-permute-start | bytes 196616 | tf_op jit(solution)/shard_map/ppermute | solution.py:19
  108.4 19.3 %collective-permute-start.7 = (bf16[1,16,1,8,256]{4,1,3,2,0:T(8,128)(2,1)S(1)}, bf16[1,16,1,8,256]{4,1,3,2,0:T(8,128)(2,1)S(1)}, u32[]{:S(2)}, u32[]{:S(2)}) collective-permute-start(bf16[1,16,1,8,256]{4,1,3,2,0:T(8,128)(2,1)S(1)} %get-tuple-element.81), channel_id=1, source_target_pairs={{0,63},{1,0},{2,1},{3,2},{4,3},{5,4},{6,5},{7,6},{8,7},{9,8},{10,9... | collective-permute-start | bytes 196616 | tf_op jit(solution)/shard_map/ppermute | solution.py:19
  120.0 5.8 %collective-permute-start.9 = (f32[6928]{0:T(1024)S(1)}, f32[6928]{0:T(1024)S(1)}, u32[]{:S(2)}, u32[]{:S(2)}) collective-permute-start(f32[6928]{0:T(1024)S(1)} %fusion.173), channel_id=1, source_target_pairs={{0,128},{64,192},{128,0},{192,64},{256,384},{320,448},{384,256},{4... | collective-permute-start | bytes 83144 | tf_op jit(solution)/shard_map/ppermute | solution.py:27
  125.8 6.7 %collective-permute-start.10 = (f32[6928]{0:T(1024)S(1)}, f32[6928]{0:T(1024)S(1)}, u32[]{:S(2)}, u32[]{:S(2)}) collective-permute-start(f32[6928]{0:T(1024)S(1)} %add.537), channel_id=1, source_target_pairs={{0,256},{64,320},{128,384},{192,448},{256,0},{320,64},{384,128},{4... | collective-permute-start | bytes 83144 | tf_op jit(solution)/shard_map/ppermute | solution.py:27
  132.4 5.9 %collective-permute-start.11 = (f32[6928]{0:T(1024)S(1)}, f32[6928]{0:T(1024)S(1)}, u32[]{:S(2)}, u32[]{:S(2)}) collective-permute-start(f32[6928]{0:T(1024)S(1)} %add.538), channel_id=1, source_target_pairs={{0,1},{1,0},{2,3},{3,2},{4,5},{5,4},{6,7},{7,6},{8,9},{9,8},{10,11... | collective-permute-start | bytes 83144 | tf_op jit(solution)/shard_map/ppermute | solution.py:27
  138.3 7.3 %collective-permute-start.12 = (f32[6928]{0:T(1024)S(1)}, f32[6928]{0:T(1024)S(1)}, u32[]{:S(2)}, u32[]{:S(2)}) collective-permute-start(f32[6928]{0:T(1024)S(1)} %add.539), channel_id=1, source_target_pairs={{0,2},{1,3},{2,0},{3,1},{4,6},{5,7},{6,4},{7,5},{8,10},{9,11},{10,... | collective-permute-start | bytes 83144 | tf_op jit(solution)/shard_map/ppermute | solution.py:27
  145.6 6.1 %collective-permute-start.13 = (f32[6928]{0:T(1024)S(1)}, f32[6928]{0:T(1024)S(1)}, u32[]{:S(2)}, u32[]{:S(2)}) collective-permute-start(f32[6928]{0:T(1024)S(1)} %add.540), channel_id=1, source_target_pairs={{0,4},{1,5},{2,6},{3,7},{4,0},{5,1},{6,2},{7,3},{8,12},{9,13},{10,... | collective-permute-start | bytes 83144 | tf_op jit(solution)/shard_map/ppermute | solution.py:27
  151.6 6.7 %collective-permute-start.14 = (f32[6928]{0:T(1024)S(1)}, f32[6928]{0:T(1024)S(1)}, u32[]{:S(2)}, u32[]{:S(2)}) collective-permute-start(f32[6928]{0:T(1024)S(1)} %add.541), channel_id=1, source_target_pairs={{0,8},{1,9},{2,10},{3,11},{4,12},{5,13},{6,14},{7,15},{8,0},{9,1},... | collective-permute-start | bytes 83144 | tf_op jit(solution)/shard_map/ppermute | solution.py:27
  158.3 9.7 %collective-permute-start.15 = (f32[6928]{0:T(1024)S(1)}, f32[6928]{0:T(1024)S(1)}, u32[]{:S(2)}, u32[]{:S(2)}) collective-permute-start(f32[6928]{0:T(1024)S(1)} %add.542), channel_id=1, source_target_pairs={{0,16},{1,17},{2,18},{3,19},{4,20},{5,21},{6,22},{7,23},{8,24},{9,... | collective-permute-start | bytes 83144 | tf_op jit(solution)/shard_map/ppermute | solution.py:27
  168.0 9.7 %collective-permute-start.16 = (f32[6928]{0:T(1024)S(1)}, f32[6928]{0:T(1024)S(1)}, u32[]{:S(2)}, u32[]{:S(2)}) collective-permute-start(f32[6928]{0:T(1024)S(1)} %add.543), channel_id=1, source_target_pairs={{0,32},{1,33},{2,34},{3,35},{4,36},{5,37},{6,38},{7,39},{8,40},{9,... | collective-permute-start | bytes 83144 | tf_op jit(solution)/shard_map/ppermute | solution.py:27

commit v6 on v3

--- a/solution.py
+++ b/solution.py
@@ -102,39 +102,38 @@
 
     taps = len(tap_offsets)
     channels = features.shape[1]
+    kernel = weight.reshape(3, 3, 3, channels, channels)
+    rolled = [(1 - e, 1 - h) for e in range(3) for h in range(3)]
+    stacked_yz = jnp.concatenate([jnp.roll(padded, r, axis=(3, 4)) for r in rolled], axis=1)
     total = jnp.zeros(features.shape, jnp.float32) + conv_bias[None, :, None, None, None]
-    for tap_index, (shift_x, shift_y, shift_z) in enumerate(tap_offsets):
-        window = jnp.roll(
-            padded[:, :, shift_x : shift_x + planes], (1 - shift_y, 1 - shift_z), axis=(3, 4)
-        )
+    for shift_x in range(3):
+        window = stacked_yz[:, :, shift_x : shift_x + planes]
+        mixed = jnp.transpose(kernel[shift_x], (2, 0, 1, 3)).reshape(channels, -1)
         total = total + jnp.einsum(
-            "oi,bixyz->boxyz", weight[tap_index], window, preferred_element_type=jnp.float32
+            "oc,bcxyz->boxyz", mixed, window, preferred_element_type=jnp.float32
         )
     hidden, slope = gelu_parts(total)
     grad_pre = (cotangent.astype(jnp.float32) * slope).astype(jnp.bfloat16)
     grad_before = shifted(grad_pre[:, :, planes - 1 : planes], "gx", 1)
     grad_after = shifted(grad_pre[:, :, 0:1], "gx", -1)
     grad_list = []
-    for tap_index, (shift_x, shift_y, shift_z) in enumerate(tap_offsets):
-        window = jnp.roll(
-            padded[:, :, shift_x : shift_x + planes], (1 - shift_y, 1 - shift_z), axis=(3, 4)
-        )
-        grad_list.append(
-            jnp.einsum("boxyz,bixyz->oi", grad_pre, window, preferred_element_type=jnp.float32)
-        )
+    for shift_x in range(3):
+        window = stacked_yz[:, :, shift_x : shift_x + planes]
+        part = jnp.einsum("boxyz,bcxyz->oc", grad_pre, window, preferred_element_type=jnp.float32)
+        part = jnp.transpose(part.reshape(channels, 3, 3, channels), (1, 2, 0, 3))
+        grad_list.append(part.reshape(9, channels, channels))
     grad_b = jnp.sum(grad_pre.astype(jnp.float32), axis=(0, 2, 3, 4))
-    stacked = jnp.concatenate([jnp.stack(grad_list).reshape(-1), grad_b])
+    stacked = jnp.concatenate([jnp.concatenate(grad_list, axis=0).reshape(-1), grad_b])
     summed = butterfly_sum(butterfly_sum(stacked, "dp"), "gx")
     grad_pad = jnp.concatenate([grad_before, grad_pre, grad_after], axis=2)
+    rolled_back = [(e - 1, h - 1) for e in range(3) for h in range(3)]
+    grad_yz = jnp.concatenate([jnp.roll(grad_pad, r, axis=(3, 4)) for r in rolled_back], axis=1)
     grad_in = jnp.zeros(features.shape, jnp.float32)
-    for tap_index, (shift_x, shift_y, shift_z) in enumerate(tap_offsets):
-        moved_grad = jnp.roll(
-            grad_pad[:, :, 2 - shift_x : 2 - shift_x + planes],
-            (shift_y - 1, shift_z - 1),
-            axis=(3, 4),
-        )
+    for shift_x in range(3):
+        moved_grad = grad_yz[:, :, 2 - shift_x : 2 - shift_x + planes]
+        mixed = kernel[shift_x].reshape(-1, channels)
         grad_in = grad_in + jnp.einsum(
-            "oi,boxyz->bixyz", weight[tap_index], moved_grad, preferred_element_type=jnp.float32
+            "ci,bcxyz->bixyz", mixed, moved_grad, preferred_element_type=jnp.float32
         )
     cell_count = (
         features.shape[0] * lax.axis_size("dp") * length_x * features.shape[3] * features.shape[4]

time: 184 us -> 170 us (0.924)
  the two profiles are of different devices: /device:TPU:2 before, /device:TPU:8 now
where the time goes in v6:
time: 170 us; the launch traced here: 169 us
  starting transfers between devices  72.1 us (42%)
  waiting for transfers between devices  66 us (39%)
  between operations  11.5 us (7%)
  local copies, waits for them, and re-layouts  9.63 us (6%)
  matrix products  6.08 us (4%)
  other arithmetic  3.92 us (2%)
    ppermute x6, starting transfers between devices, routed(): arrived = lax.ppermute(jnp.concatenate(pieces, axis=2), axis, pairs)  33.9 us
    ppermute x9, waiting for transfers between devices, butterfly_sum(): value = value + lax.ppermute(value, axis, pairs)  33.1 us
    ppermute x6, waiting for transfers between devices, routed(): arrived = lax.ppermute(jnp.concatenate(pieces, axis=2), axis, pairs)  32.8 us
    ppermute x9, starting transfers between devices, butterfly_sum(): value = value + lax.ppermute(value, axis, pairs)  22.5 us
    ppermute x2, starting transfers between devices, shifted(): return lax.ppermute(value, axis, pairs)  15.7 us
    unnamed x14, local copies, waits for them, and re-layouts  4.43 us
    dot_general x3, matrix products, on_device(): jnp.einsum('boxyz,bcxyz->oc', grad_pre, window, preferred_element_type=jn...  4.19 us
  transfers between devices with their start and end apart: 17, of which 13 were waited for; matrix products, arithmetic and copies ran while one was open for 4% of the time, Pallas kernels for 0%

profile of v6, /device:TPU:8, one launch (start us, length us, event | category | flops | bytes accessed | tf_op | source)
XLA Modules:
  0.0 169.2 jit_solution(646703422578088535)
XLA Ops:
  3.7 3.4 %collective-permute-start = (bf16[1,16,4,8,256]{4,1,3,2,0:T(8,128)(2,1)S(1)}, bf16[1,16,4,8,256]{4,1,3,2,0:T(8,128)(2,1)S(1)}, u32[]{:S(2)}, u32[]{:S(2)}) collective-permute-start(bf16[1,16,4,8,256]{4,1,3,2,0:T(8,128)(2,1)S(1)} %pad_maximum_fusion.4), channel_id=1, source_target_pairs={{0,1},{1,0},{2,3},{3,2},{4,5},{5,4},{6,7},{7,6},{8,9},{9,8},{10,11... | collective-permute-start | bytes 786440 | tf_op jit(solution)/shard_map/ppermute | solution.py:58
  10.6 3.1 %collective-permute-done = bf16[1,16,4,8,256]{4,1,3,2,0:T(8,128)(2,1)S(1)} collective-permute-done((bf16[1,16,4,8,256]{4,1,3,2,0:T(8,128)(2,1)S(1)}, bf16[1,16,4,8,256]{4,1,3,2,0:T(8,128)(2,1)S(1)}, u32[]{:S(2)}, u32[]{:S(2)}) %collective-permute-start) | collective-permute-done | bytes 262176 | tf_op jit(solution)/shard_map/ppermute | solution.py:58
  13.7 4.9 %collective-permute-start.1 = (bf16[1,16,4,8,256]{4,1,3,2,0:T(8,128)(2,1)S(1)}, bf16[1,16,4,8,256]{4,1,3,2,0:T(8,128)(2,1)S(1)}, u32[]{:S(2)}, u32[]{:S(2)}) collective-permute-start(bf16[1,16,4,8,256]{4,1,3,2,0:T(8,128)(2,1)S(1)} %pad_maximum_fusion.5), channel_id=1, source_target_pairs={{0,2},{1,3},{2,0},{3,1},{4,6},{5,7},{6,4},{7,5},{8,10},{9,11},{10,... | collective-permute-start | bytes 786440 | tf_op jit(solution)/shard_map/ppermute | solution.py:58
  18.9 5.4 %collective-permute-done.1 = bf16[1,16,4,8,256]{4,1,3,2,0:T(8,128)(2,1)S(1)} collective-permute-done((bf16[1,16,4,8,256]{4,1,3,2,0:T(8,128)(2,1)S(1)}, bf16[1,16,4,8,256]{4,1,3,2,0:T(8,128)(2,1)S(1)}, u32[]{:S(2)}, u32[]{:S(2)}) %collective-permute-start.1) | collective-permute-done | bytes 262176 | tf_op jit(solution)/shard_map/ppermute | solution.py:58
  24.4 4.3 %collective-permute-start.2 = (bf16[1,16,4,8,256]{4,1,3,2,0:T(8,128)(2,1)S(1)}, bf16[1,16,4,8,256]{4,1,3,2,0:T(8,128)(2,1)S(1)}, u32[]{:S(2)}, u32[]{:S(2)}) collective-permute-start(bf16[1,16,4,8,256]{4,1,3,2,0:T(8,128)(2,1)S(1)} %pad_maximum_fusion.6), channel_id=1, source_target_pairs={{0,4},{1,5},{2,6},{3,7},{4,0},{5,1},{6,2},{7,3},{8,12},{9,13},{10,... | collective-permute-start | bytes 786440 | tf_op jit(solution)/shard_map/ppermute | solution.py:58
  28.9 4.3 %collective-permute-done.2 = bf16[1,16,4,8,256]{4,1,3,2,0:T(8,128)(2,1)S(1)} collective-permute-done((bf16[1,16,4,8,256]{4,1,3,2,0:T(8,128)(2,1)S(1)}, bf16[1,16,4,8,256]{4,1,3,2,0:T(8,128)(2,1)S(1)}, u32[]{:S(2)}, u32[]{:S(2)}) %collective-permute-start.2) | collective-permute-done | bytes 262176 | tf_op jit(solution)/shard_map/ppermute | solution.py:58
  33.3 6.1 %collective-permute-start.3 = (bf16[1,16,4,8,256]{4,1,3,2,0:T(8,128)(2,1)S(1)}, bf16[1,16,4,8,256]{4,1,3,2,0:T(8,128)(2,1)S(1)}, u32[]{:S(2)}, u32[]{:S(2)}) collective-permute-start(bf16[1,16,4,8,256]{4,1,3,2,0:T(8,128)(2,1)S(1)} %pad_maximum_fusion.7), channel_id=1, source_target_pairs={{0,8},{1,9},{2,10},{3,11},{4,12},{5,13},{6,14},{7,15},{8,0},{9,1},... | collective-permute-start | bytes 786440 | tf_op jit(solution)/shard_map/ppermute | solution.py:58
  39.6 9.3 %collective-permute-done.3 = bf16[1,16,4,8,256]{4,1,3,2,0:T(8,128)(2,1)S(1)} collective-permute-done((bf16[1,16,4,8,256]{4,1,3,2,0:T(8,128)(2,1)S(1)}, bf16[1,16,4,8,256]{4,1,3,2,0:T(8,128)(2,1)S(1)}, u32[]{:S(2)}, u32[]{:S(2)}) %collective-permute-start.3) | collective-permute-done | bytes 262176 | tf_op jit(solution)/shard_map/ppermute | solution.py:58
  48.9 8.3 %collective-permute-start.4 = (bf16[1,16,4,8,256]{4,1,3,2,0:T(8,128)(2,1)S(1)}, bf16[1,16,4,8,256]{4,1,3,2,0:T(8,128)(2,1)S(1)}, u32[]{:S(2)}, u32[]{:S(2)}) collective-permute-start(bf16[1,16,4,8,256]{4,1,3,2,0:T(8,128)(2,1)S(1)} %pad_maximum_fusion.8), channel_id=1, source_target_pairs={{0,16},{1,17},{2,18},{3,19},{4,20},{5,21},{6,22},{7,23},{8,24},{9,... | collective-permute-start | bytes 786440 | tf_op jit(solution)/shard_map/ppermute | solution.py:58
  57.5 10.7 %collective-permute-done.4 = bf16[1,16,4,8,256]{4,1,3,2,0:T(8,128)(2,1)S(1)} collective-permute-done((bf16[1,16,4,8,256]{4,1,3,2,0:T(8,128)(2,1)S(1)}, bf16[1,16,4,8,256]{4,1,3,2,0:T(8,128)(2,1)S(1)}, u32[]{:S(2)}, u32[]{:S(2)}) %collective-permute-start.4) | collective-permute-done | bytes 262176 | tf_op jit(solution)/shard_map/ppermute | solution.py:58
  68.3 6.8 %collective-permute-start.5 = (bf16[1,16,4,8,256]{4,1,3,2,0:T(8,128)(2,1)S(1)}, bf16[1,16,4,8,256]{4,1,3,2,0:T(8,128)(2,1)S(1)}, u32[]{:S(2)}, u32[]{:S(2)}) collective-permute-start(bf16[1,16,4,8,256]{4,1,3,2,0:T(8,128)(2,1)S(1)} %pad_maximum_fusion.9), channel_id=1, source_target_pairs={{0,32},{1,33},{2,34},{3,35},{4,36},{5,37},{6,38},{7,39},{8,40},{9,... | collective-permute-start | bytes 786440 | tf_op jit(solution)/shard_map/ppermute | solution.py:58
  89.0 1.4 fusion.68
  90.4 1.4 fusion.66
  92.0 1.9 %collective-permute-start.8 = (f32[6928]{0:T(1024)S(1)}, f32[6928]{0:T(1024)S(1)}, u32[]{:S(2)}, u32[]{:S(2)}) collective-permute-start(f32[6928]{0:T(1024)S(1)} %pad_maximum_fusion.12), channel_id=1, source_target_pairs={{0,64},{64,0},{128,192},{192,128},{256,320},{320,256},{384,448},{4... | collective-permute-start | bytes 83144 | tf_op jit(solution)/shard_map/ppermute | solution.py:27
  94.0 3.4 %collective-permute-start.6 = (bf16[1,16,1,8,256]{4,1,3,2,0:T(8,128)(2,1)S(1)}, bf16[1,16,1,8,256]{4,1,3,2,0:T(8,128)(2,1)S(1)}, u32[]{:S(2)}, u32[]{:S(2)}) collective-permute-start(bf16[1,16,1,8,256]{4,1,3,2,0:T(8,128)(2,1)S(1)} %get-tuple-element.86), channel_id=1, source_target_pairs={{0,1},{1,2},{2,3},{3,4},{4,5},{5,6},{6,7},{7,8},{8,9},{9,10},{10,1... | collective-permute-start | bytes 196616 | tf_op jit(solution)/shard_map/ppermute | solution.py:19
  97.4 12.3 %collective-permute-start.7 = (bf16[1,16,1,8,256]{4,1,3,2,0:T(8,128)(2,1)S(1)}, bf16[1,16,1,8,256]{4,1,3,2,0:T(8,128)(2,1)S(1)}, u32[]{:S(2)}, u32[]{:S(2)}) collective-permute-start(bf16[1,16,1,8,256]{4,1,3,2,0:T(8,128)(2,1)S(1)} %get-tuple-element.87), channel_id=1, source_target_pairs={{0,63},{1,0},{2,1},{3,2},{4,3},{5,4},{6,5},{7,6},{8,7},{9,8},{10,9... | collective-permute-start | bytes 196616 | tf_op jit(solution)/shard_map/ppermute | solution.py:19
  109.7 3.6 %collective-permute-start.9 = (f32[6928]{0:T(1024)S(1)}, f32[6928]{0:T(1024)S(1)}, u32[]{:S(2)}, u32[]{:S(2)}) collective-permute-start(f32[6928]{0:T(1024)S(1)} %fusion.99), channel_id=1, source_target_pairs={{0,128},{64,192},{128,0},{192,64},{256,384},{320,448},{384,256},{4... | collective-permute-start | bytes 83144 | tf_op jit(solution)/shard_map/ppermute | solution.py:27
  114.0 1.8 %collective-permute-done.9 = f32[6928]{0:T(1024)S(1)} collective-permute-done((f32[6928]{0:T(1024)S(1)}, f32[6928]{0:T(1024)S(1)}, u32[]{:S(2)}, u32[]{:S(2)}) %collective-permute-start.9) | collective-permute-done | bytes 27744 | tf_op jit(solution)/shard_map/ppermute | solution.py:27
  115.9 2.6 %collective-permute-start.10 = (f32[6928]{0:T(1024)S(1)}, f32[6928]{0:T(1024)S(1)}, u32[]{:S(2)}, u32[]{:S(2)}) collective-permute-start(f32[6928]{0:T(1024)S(1)} %add.314), channel_id=1, source_target_pairs={{0,256},{64,320},{128,384},{192,448},{256,0},{320,64},{384,128},{4... | collective-permute-start | bytes 83144 | tf_op jit(solution)/shard_map/ppermute | solution.py:27
  119.9 2.7 %collective-permute-done.10 = f32[6928]{0:T(1024)S(1)} collective-permute-done((f32[6928]{0:T(1024)S(1)}, f32[6928]{0:T(1024)S(1)}, u32[]{:S(2)}, u32[]{:S(2)}) %collective-permute-start.10) | collective-permute-done | bytes 27744 | tf_op jit(solution)/shard_map/ppermute | solution.py:27
  122.6 1.9 %collective-permute-start.11 = (f32[6928]{0:T(1024)S(1)}, f32[6928]{0:T(1024)S(1)}, u32[]{:S(2)}, u32[]{:S(2)}) collective-permute-start(f32[6928]{0:T(1024)S(1)} %add.315), channel_id=1, source_target_pairs={{0,1},{1,0},{2,3},{3,2},{4,5},{5,4},{6,7},{7,6},{8,9},{9,8},{10,11... | collective-permute-start | bytes 83144 | tf_op jit(solution)/shard_map/ppermute | solution.py:27
  124.7 3.7 %collective-permute-done.11 = f32[6928]{0:T(1024)S(1)} collective-permute-done((f32[6928]{0:T(1024)S(1)}, f32[6928]{0:T(1024)S(1)}, u32[]{:S(2)}, u32[]{:S(2)}) %collective-permute-start.11) | collective-permute-done | bytes 27744 | tf_op jit(solution)/shard_map/ppermute | solution.py:27
  128.4 1.9 %collective-permute-start.12 = (f32[6928]{0:T(1024)S(1)}, f32[6928]{0:T(1024)S(1)}, u32[]{:S(2)}, u32[]{:S(2)}) collective-permute-start(f32[6928]{0:T(1024)S(1)} %add.316), channel_id=1, source_target_pairs={{0,2},{1,3},{2,0},{3,1},{4,6},{5,7},{6,4},{7,5},{8,10},{9,11},{10,... | collective-permute-start | bytes 83144 | tf_op jit(solution)/shard_map/ppermute | solution.py:27
  130.3 5.3 %collective-permute-done.12 = f32[6928]{0:T(1024)S(1)} collective-permute-done((f32[6928]{0:T(1024)S(1)}, f32[6928]{0:T(1024)S(1)}, u32[]{:S(2)}, u32[]{:S(2)}) %collective-permute-start.12) | collective-permute-done | bytes 27744 | tf_op jit(solution)/shard_map/ppermute | solution.py:27
  135.6 1.9 %collective-permute-start.13 = (f32[6928]{0:T(1024)S(1)}, f32[6928]{0:T(1024)S(1)}, u32[]{:S(2)}, u32[]{:S(2)}) collective-permute-start(f32[6928]{0:T(1024)S(1)} %add.317), channel_id=1, source_target_pairs={{0,4},{1,5},{2,6},{3,7},{4,0},{5,1},{6,2},{7,3},{8,12},{9,13},{10,... | collective-permute-start | bytes 83144 | tf_op jit(solution)/shard_map/ppermute | solution.py:27
  137.7 3.7 %collective-permute-done.13 = f32[6928]{0:T(1024)S(1)} collective-permute-done((f32[6928]{0:T(1024)S(1)}, f32[6928]{0:T(1024)S(1)}, u32[]{:S(2)}, u32[]{:S(2)}) %collective-permute-start.13) | collective-permute-done | bytes 27744 | tf_op jit(solution)/shard_map/ppermute | solution.py:27
  141.4 1.9 %collective-permute-start.14 = (f32[6928]{0:T(1024)S(1)}, f32[6928]{0:T(1024)S(1)}, u32[]{:S(2)}, u32[]{:S(2)}) collective-permute-start(f32[6928]{0:T(1024)S(1)} %add.318), channel_id=1, source_target_pairs={{0,8},{1,9},{2,10},{3,11},{4,12},{5,13},{6,14},{7,15},{8,0},{9,1},... | collective-permute-start | bytes 83144 | tf_op jit(solution)/shard_map/ppermute | solution.py:27
  143.6 4.4 %collective-permute-done.14 = f32[6928]{0:T(1024)S(1)} collective-permute-done((f32[6928]{0:T(1024)S(1)}, f32[6928]{0:T(1024)S(1)}, u32[]{:S(2)}, u32[]{:S(2)}) %collective-permute-start.14) | collective-permute-done | bytes 27744 | tf_op jit(solution)/shard_map/ppermute | solution.py:27
  148.1 1.9 %collective-permute-start.15 = (f32[6928]{0:T(1024)S(1)}, f32[6928]{0:T(1024)S(1)}, u32[]{:S(2)}, u32[]{:S(2)}) collective-permute-start(f32[6928]{0:T(1024)S(1)} %add.319), channel_id=1, source_target_pairs={{0,16},{1,17},{2,18},{3,19},{4,20},{5,21},{6,22},{7,23},{8,24},{9,... | collective-permute-start | bytes 83144 | tf_op jit(solution)/shard_map/ppermute | solution.py:27
  150.3 7.4 %collective-permute-done.15 = f32[6928]{0:T(1024)S(1)} collective-permute-done((f32[6928]{0:T(1024)S(1)}, f32[6928]{0:T(1024)S(1)}, u32[]{:S(2)}, u32[]{:S(2)}) %collective-permute-start.15) | collective-permute-done | bytes 27744 | tf_op jit(solution)/shard_map/ppermute | solution.py:27
  157.7 4.9 %collective-permute-start.16 = (f32[6928]{0:T(1024)S(1)}, f32[6928]{0:T(1024)S(1)}, u32[]{:S(2)}, u32[]{:S(2)}) collective-permute-start(f32[6928]{0:T(1024)S(1)} %add.320), channel_id=1, source_target_pairs={{0,32},{1,33},{2,34},{3,35},{4,36},{5,37},{6,38},{7,39},{8,40},{9,... | collective-permute-start | bytes 83144 | tf_op jit(solution)/shard_map/ppermute | solution.py:27
  163.6 4.0 %collective-permute-done.16 = f32[6928]{0:T(1024)S(1)} collective-permute-done((f32[6928]{0:T(1024)S(1)}, f32[6928]{0:T(1024)S(1)}, u32[]{:S(2)}, u32[]{:S(2)}) %collective-permute-start.16) | collective-permute-done | bytes 27744 | tf_op jit(solution)/shard_map/ppermute | solution.py:27
  (107 shorter events, 16.8 us)
Async XLA Ops:
  3.7 9.9 %collective-permute-start = (bf16[1,16,4,8,256]{4,1,3,2,0:T(8,128)(2,1)S(1)}, bf16[1,16,4,8,256]{4,1,3,2,0:T(8,128)(2,1)S(1)}, u32[]{:S(2)}, u32[]{:S(2)}) collective-permute-start(bf16[1,16,4,8,256]{4,1,3,2,0:T(8,128)(2,1)S(1)} %pad_maximum_fusion.4), channel_id=1, source_target_pairs={{0,1},{1,0},{2,3},{3,2},{4,5},{5,4},{6,7},{7,6},{8,9},{9,8},{10,11... | collective-permute-start | bytes 786440 | tf_op jit(solution)/shard_map/ppermute | solution.py:58
  13.7 10.6 %collective-permute-start.1 = (bf16[1,16,4,8,256]{4,1,3,2,0:T(8,128)(2,1)S(1)}, bf16[1,16,4,8,256]{4,1,3,2,0:T(8,128)(2,1)S(1)}, u32[]{:S(2)}, u32[]{:S(2)}) collective-permute-start(bf16[1,16,4,8,256]{4,1,3,2,0:T(8,128)(2,1)S(1)} %pad_maximum_fusion.5), channel_id=1, source_target_pairs={{0,2},{1,3},{2,0},{3,1},{4,6},{5,7},{6,4},{7,5},{8,10},{9,11},{10,... | collective-permute-start | bytes 786440 | tf_op jit(solution)/shard_map/ppermute | solution.py:58
  24.4 8.8 %collective-permute-start.2 = (bf16[1,16,4,8,256]{4,1,3,2,0:T(8,128)(2,1)S(1)}, bf16[1,16,4,8,256]{4,1,3,2,0:T(8,128)(2,1)S(1)}, u32[]{:S(2)}, u32[]{:S(2)}) collective-permute-start(bf16[1,16,4,8,256]{4,1,3,2,0:T(8,128)(2,1)S(1)} %pad_maximum_fusion.6), channel_id=1, source_target_pairs={{0,4},{1,5},{2,6},{3,7},{4,0},{5,1},{6,2},{7,3},{8,12},{9,13},{10,... | collective-permute-start | bytes 786440 | tf_op jit(solution)/shard_map/ppermute | solution.py:58
  28.9 53.0 %copy-start = (bf16[27,16,16]{0,2,1:T(8,128)(2,1)S(1)}, bf16[27,16,16]{0,2,1:T(8,128)(2,1)}, u32[]{:S(2)}) copy-start(bf16[27,16,16]{0,2,1:T(8,128)(2,1)} %param.13) | copy-start | bytes 41476
  33.3 15.6 %collective-permute-start.3 = (bf16[1,16,4,8,256]{4,1,3,2,0:T(8,128)(2,1)S(1)}, bf16[1,16,4,8,256]{4,1,3,2,0:T(8,128)(2,1)S(1)}, u32[]{:S(2)}, u32[]{:S(2)}) collective-permute-start(bf16[1,16,4,8,256]{4,1,3,2,0:T(8,128)(2,1)S(1)} %pad_maximum_fusion.7), channel_id=1, source_target_pairs={{0,8},{1,9},{2,10},{3,11},{4,12},{5,13},{6,14},{7,15},{8,0},{9,1},... | collective-permute-start | bytes 786440 | tf_op jit(solution)/shard_map/ppermute | solution.py:58
  48.9 19.3 %collective-permute-start.4 = (bf16[1,16,4,8,256]{4,1,3,2,0:T(8,128)(2,1)S(1)}, bf16[1,16,4,8,256]{4,1,3,2,0:T(8,128)(2,1)S(1)}, u32[]{:S(2)}, u32[]{:S(2)}) collective-permute-start(bf16[1,16,4,8,256]{4,1,3,2,0:T(8,128)(2,1)S(1)} %pad_maximum_fusion.8), channel_id=1, source_target_pairs={{0,16},{1,17},{2,18},{3,19},{4,20},{5,21},{6,22},{7,23},{8,24},{9,... | collective-permute-start | bytes 786440 | tf_op jit(solution)/shard_map/ppermute | solution.py:58
  68.3 14.6 %collective-permute-start.5 = (bf16[1,16,4,8,256]{4,1,3,2,0:T(8,128)(2,1)S(1)}, bf16[1,16,4,8,256]{4,1,3,2,0:T(8,128)(2,1)S(1)}, u32[]{:S(2)}, u32[]{:S(2)}) collective-permute-start(bf16[1,16,4,8,256]{4,1,3,2,0:T(8,128)(2,1)S(1)} %pad_maximum_fusion.9), channel_id=1, source_target_pairs={{0,32},{1,33},{2,34},{3,35},{4,36},{5,37},{6,38},{7,39},{8,40},{9,... | collective-permute-start | bytes 786440 | tf_op jit(solution)/shard_map/ppermute | solution.py:58
  85.7 0.7 copy-start.1
  86.3 0.9 copy-start.2
  92.0 17.7 %collective-permute-start.8 = (f32[6928]{0:T(1024)S(1)}, f32[6928]{0:T(1024)S(1)}, u32[]{:S(2)}, u32[]{:S(2)}) collective-permute-start(f32[6928]{0:T(1024)S(1)} %pad_maximum_fusion.12), channel_id=1, source_target_pairs={{0,64},{64,0},{128,192},{192,128},{256,320},{320,256},{384,448},{4... | collective-permute-start | bytes 83144 | tf_op jit(solution)/shard_map/ppermute | solution.py:27
  94.0 24.4 %collective-permute-start.6 = (bf16[1,16,1,8,256]{4,1,3,2,0:T(8,128)(2,1)S(1)}, bf16[1,16,1,8,256]{4,1,3,2,0:T(8,128)(2,1)S(1)}, u32[]{:S(2)}, u32[]{:S(2)}) collective-permute-start(bf16[1,16,1,8,256]{4,1,3,2,0:T(8,128)(2,1)S(1)} %get-tuple-element.86), channel_id=1, source_target_pairs={{0,1},{1,2},{2,3},{3,4},{4,5},{5,6},{6,7},{7,8},{8,9},{9,10},{10,1... | collective-permute-start | bytes 196616 | tf_op jit(solution)/shard_map/ppermute | solution.py:19
  97.4 21.0 %collective-permute-start.7 = (bf16[1,16,1,8,256]{4,1,3,2,0:T(8,128)(2,1)S(1)}, bf16[1,16,1,8,256]{4,1,3,2,0:T(8,128)(2,1)S(1)}, u32[]{:S(2)}, u32[]{:S(2)}) collective-permute-start(bf16[1,16,1,8,256]{4,1,3,2,0:T(8,128)(2,1)S(1)} %get-tuple-element.87), channel_id=1, source_target_pairs={{0,63},{1,0},{2,1},{3,2},{4,3},{5,4},{6,5},{7,6},{8,7},{9,8},{10,9... | collective-permute-start | bytes 196616 | tf_op jit(solution)/shard_map/ppermute | solution.py:19
  109.7 6.1 %collective-permute-start.9 = (f32[6928]{0:T(1024)S(1)}, f32[6928]{0:T(1024)S(1)}, u32[]{:S(2)}, u32[]{:S(2)}) collective-permute-start(f32[6928]{0:T(1024)S(1)} %fusion.99), channel_id=1, source_target_pairs={{0,128},{64,192},{128,0},{192,64},{256,384},{320,448},{384,256},{4... | collective-permute-start | bytes 83144 | tf_op jit(solution)/shard_map/ppermute | solution.py:27
  115.9 6.8 %collective-permute-start.10 = (f32[6928]{0:T(1024)S(1)}, f32[6928]{0:T(1024)S(1)}, u32[]{:S(2)}, u32[]{:S(2)}) collective-permute-start(f32[6928]{0:T(1024)S(1)} %add.314), channel_id=1, source_target_pairs={{0,256},{64,320},{128,384},{192,448},{256,0},{320,64},{384,128},{4... | collective-permute-start | bytes 83144 | tf_op jit(solution)/shard_map/ppermute | solution.py:27
  122.6 5.8 %collective-permute-start.11 = (f32[6928]{0:T(1024)S(1)}, f32[6928]{0:T(1024)S(1)}, u32[]{:S(2)}, u32[]{:S(2)}) collective-permute-start(f32[6928]{0:T(1024)S(1)} %add.315), channel_id=1, source_target_pairs={{0,1},{1,0},{2,3},{3,2},{4,5},{5,4},{6,7},{7,6},{8,9},{9,8},{10,11... | collective-permute-start | bytes 83144 | tf_op jit(solution)/shard_map/ppermute | solution.py:27
  128.4 7.3 %collective-permute-start.12 = (f32[6928]{0:T(1024)S(1)}, f32[6928]{0:T(1024)S(1)}, u32[]{:S(2)}, u32[]{:S(2)}) collective-permute-start(f32[6928]{0:T(1024)S(1)} %add.316), channel_id=1, source_target_pairs={{0,2},{1,3},{2,0},{3,1},{4,6},{5,7},{6,4},{7,5},{8,10},{9,11},{10,... | collective-permute-start | bytes 83144 | tf_op jit(solution)/shard_map/ppermute | solution.py:27
  135.6 5.8 %collective-permute-start.13 = (f32[6928]{0:T(1024)S(1)}, f32[6928]{0:T(1024)S(1)}, u32[]{:S(2)}, u32[]{:S(2)}) collective-permute-start(f32[6928]{0:T(1024)S(1)} %add.317), channel_id=1, source_target_pairs={{0,4},{1,5},{2,6},{3,7},{4,0},{5,1},{6,2},{7,3},{8,12},{9,13},{10,... | collective-permute-start | bytes 83144 | tf_op jit(solution)/shard_map/ppermute | solution.py:27
  141.4 6.7 %collective-permute-start.14 = (f32[6928]{0:T(1024)S(1)}, f32[6928]{0:T(1024)S(1)}, u32[]{:S(2)}, u32[]{:S(2)}) collective-permute-start(f32[6928]{0:T(1024)S(1)} %add.318), channel_id=1, source_target_pairs={{0,8},{1,9},{2,10},{3,11},{4,12},{5,13},{6,14},{7,15},{8,0},{9,1},... | collective-permute-start | bytes 83144 | tf_op jit(solution)/shard_map/ppermute | solution.py:27
  148.1 9.7 %collective-permute-start.15 = (f32[6928]{0:T(1024)S(1)}, f32[6928]{0:T(1024)S(1)}, u32[]{:S(2)}, u32[]{:S(2)}) collective-permute-start(f32[6928]{0:T(1024)S(1)} %add.319), channel_id=1, source_target_pairs={{0,16},{1,17},{2,18},{3,19},{4,20},{5,21},{6,22},{7,23},{8,24},{9,... | collective-permute-start | bytes 83144 | tf_op jit(solution)/shard_map/ppermute | solution.py:27
  157.7 10.0 %collective-permute-start.16 = (f32[6928]{0:T(1024)S(1)}, f32[6928]{0:T(1024)S(1)}, u32[]{:S(2)}, u32[]{:S(2)}) collective-permute-start(f32[6928]{0:T(1024)S(1)} %add.320), channel_id=1, source_target_pairs={{0,32},{1,33},{2,34},{3,35},{4,36},{5,37},{6,38},{7,39},{8,40},{9,... | collective-permute-start | bytes 83144 | tf_op jit(solution)/shard_map/ppermute | solution.py:27

commit v7 on v6

--- a/solution.py
+++ b/solution.py
@@ -21,11 +21,11 @@
 
 def butterfly_sum(value, axis):
     count = lax.axis_size(axis)
-    step = 1
-    while step < count:
+    step = count // 2
+    while step >= 1:
         pairs = [(source, source ^ step) for source in range(count)]
         value = value + lax.ppermute(value, axis, pairs)
-        step *= 2
+        step //= 2
     return value
 
 
@@ -124,7 +124,7 @@
         grad_list.append(part.reshape(9, channels, channels))
     grad_b = jnp.sum(grad_pre.astype(jnp.float32), axis=(0, 2, 3, 4))
     stacked = jnp.concatenate([jnp.concatenate(grad_list, axis=0).reshape(-1), grad_b])
-    summed = butterfly_sum(butterfly_sum(stacked, "dp"), "gx")
+    summed = butterfly_sum(butterfly_sum(stacked, "gx"), "dp")
     grad_pad = jnp.concatenate([grad_before, grad_pre, grad_after], axis=2)
     rolled_back = [(e - 1, h - 1) for e in range(3) for h in range(3)]
     grad_yz = jnp.concatenate([jnp.roll(grad_pad, r, axis=(3, 4)) for r in rolled_back], axis=1)

time: 170 us -> 168 us (0.988)
  the two profiles are of different devices: /device:TPU:8 before, /device:TPU:1 now
where the time goes in v7:
time: 168 us
  starting transfers between devices  90.4 us (54%)
  waiting for transfers between devices  46.2 us (28%)
  between operations  11.5 us (7%)
  local copies, waits for them, and re-layouts  9.63 us (6%)
  matrix products  6.08 us (4%)
  other arithmetic  3.92 us (2%)
    ppermute x9, starting transfers between devices, butterfly_sum(): value = value + lax.ppermute(value, axis, pairs)  38.9 us
    ppermute x6, starting transfers between devices, routed(): arrived = lax.ppermute(jnp.concatenate(pieces, axis=2), axis, pairs)  38.1 us
    ppermute x6, waiting for transfers between devices, routed(): arrived = lax.ppermute(jnp.concatenate(pieces, axis=2), axis, pairs)  25.6 us
    ppermute x9, waiting for transfers between devices, butterfly_sum(): value = value + lax.ppermute(value, axis, pairs)  20.6 us
    ppermute x2, starting transfers between devices, shifted(): return lax.ppermute(value, axis, pairs)  13.4 us
    unnamed x14, local copies, waits for them, and re-layouts  4.43 us
    dot_general x3, matrix products, on_device(): jnp.einsum('boxyz,bcxyz->oc', grad_pre, window, preferred_element_type=jn...  4.19 us
  transfers between devices with their start and end apart: 17, of which 12 were waited for; matrix products, arithmetic and copies ran while one was open for 4% of the time, Pallas kernels for 0%

profile of v7, /device:TPU:1, one launch (start us, length us, event | category | flops | bytes accessed | tf_op | source)
XLA Modules:
  0.0 167.7 jit_solution(3921446578259790635)
XLA Ops:
  0.6 1.4 fusion.91
  3.7 3.9 %collective-permute-start = (bf16[1,16,4,8,256]{4,1,3,2,0:T(8,128)(2,1)S(1)}, bf16[1,16,4,8,256]{4,1,3,2,0:T(8,128)(2,1)S(1)}, u32[]{:S(2)}, u32[]{:S(2)}) collective-permute-start(bf16[1,16,4,8,256]{4,1,3,2,0:T(8,128)(2,1)S(1)} %pad_maximum_fusion.4), channel_id=1, source_target_pairs={{0,1},{1,0},{2,3},{3,2},{4,5},{5,4},{6,7},{7,6},{8,9},{9,8},{10,11... | collective-permute-start | bytes 786440 | tf_op jit(solution)/shard_map/ppermute | solution.py:58
  7.6 1.4 fusion.92
  11.5 6.8 %collective-permute-start.1 = (bf16[1,16,4,8,256]{4,1,3,2,0:T(8,128)(2,1)S(1)}, bf16[1,16,4,8,256]{4,1,3,2,0:T(8,128)(2,1)S(1)}, u32[]{:S(2)}, u32[]{:S(2)}) collective-permute-start(bf16[1,16,4,8,256]{4,1,3,2,0:T(8,128)(2,1)S(1)} %pad_maximum_fusion.5), channel_id=1, source_target_pairs={{0,2},{1,3},{2,0},{3,1},{4,6},{5,7},{6,4},{7,5},{8,10},{9,11},{10,... | collective-permute-start | bytes 786440 | tf_op jit(solution)/shard_map/ppermute | solution.py:58
  18.5 3.6 %collective-permute-done.1 = bf16[1,16,4,8,256]{4,1,3,2,0:T(8,128)(2,1)S(1)} collective-permute-done((bf16[1,16,4,8,256]{4,1,3,2,0:T(8,128)(2,1)S(1)}, bf16[1,16,4,8,256]{4,1,3,2,0:T(8,128)(2,1)S(1)}, u32[]{:S(2)}, u32[]{:S(2)}) %collective-permute-start.1) | collective-permute-done | bytes 262176 | tf_op jit(solution)/shard_map/ppermute | solution.py:58
  22.2 5.2 %collective-permute-start.2 = (bf16[1,16,4,8,256]{4,1,3,2,0:T(8,128)(2,1)S(1)}, bf16[1,16,4,8,256]{4,1,3,2,0:T(8,128)(2,1)S(1)}, u32[]{:S(2)}, u32[]{:S(2)}) collective-permute-start(bf16[1,16,4,8,256]{4,1,3,2,0:T(8,128)(2,1)S(1)} %pad_maximum_fusion.6), channel_id=1, source_target_pairs={{0,4},{1,5},{2,6},{3,7},{4,0},{5,1},{6,2},{7,3},{8,12},{9,13},{10,... | collective-permute-start | bytes 786440 | tf_op jit(solution)/shard_map/ppermute | solution.py:58
  27.6 3.5 %collective-permute-done.2 = bf16[1,16,4,8,256]{4,1,3,2,0:T(8,128)(2,1)S(1)} collective-permute-done((bf16[1,16,4,8,256]{4,1,3,2,0:T(8,128)(2,1)S(1)}, bf16[1,16,4,8,256]{4,1,3,2,0:T(8,128)(2,1)S(1)}, u32[]{:S(2)}, u32[]{:S(2)}) %collective-permute-start.2) | collective-permute-done | bytes 262176 | tf_op jit(solution)/shard_map/ppermute | solution.py:58
  31.3 6.2 %collective-permute-start.3 = (bf16[1,16,4,8,256]{4,1,3,2,0:T(8,128)(2,1)S(1)}, bf16[1,16,4,8,256]{4,1,3,2,0:T(8,128)(2,1)S(1)}, u32[]{:S(2)}, u32[]{:S(2)}) collective-permute-start(bf16[1,16,4,8,256]{4,1,3,2,0:T(8,128)(2,1)S(1)} %pad_maximum_fusion.7), channel_id=1, source_target_pairs={{0,8},{1,9},{2,10},{3,11},{4,12},{5,13},{6,14},{7,15},{8,0},{9,1},... | collective-permute-start | bytes 786440 | tf_op jit(solution)/shard_map/ppermute | solution.py:58
  37.7 10.6 %collective-permute-done.3 = bf16[1,16,4,8,256]{4,1,3,2,0:T(8,128)(2,1)S(1)} collective-permute-done((bf16[1,16,4,8,256]{4,1,3,2,0:T(8,128)(2,1)S(1)}, bf16[1,16,4,8,256]{4,1,3,2,0:T(8,128)(2,1)S(1)}, u32[]{:S(2)}, u32[]{:S(2)}) %collective-permute-start.3) | collective-permute-done | bytes 262176 | tf_op jit(solution)/shard_map/ppermute | solution.py:58
  48.4 8.4 %collective-permute-start.4 = (bf16[1,16,4,8,256]{4,1,3,2,0:T(8,128)(2,1)S(1)}, bf16[1,16,4,8,256]{4,1,3,2,0:T(8,128)(2,1)S(1)}, u32[]{:S(2)}, u32[]{:S(2)}) collective-permute-start(bf16[1,16,4,8,256]{4,1,3,2,0:T(8,128)(2,1)S(1)} %pad_maximum_fusion.8), channel_id=1, source_target_pairs={{0,16},{1,17},{2,18},{3,19},{4,20},{5,21},{6,22},{7,23},{8,24},{9,... | collective-permute-start | bytes 786440 | tf_op jit(solution)/shard_map/ppermute | solution.py:58
  57.0 7.6 %collective-permute-done.4 = bf16[1,16,4,8,256]{4,1,3,2,0:T(8,128)(2,1)S(1)} collective-permute-done((bf16[1,16,4,8,256]{4,1,3,2,0:T(8,128)(2,1)S(1)}, bf16[1,16,4,8,256]{4,1,3,2,0:T(8,128)(2,1)S(1)}, u32[]{:S(2)}, u32[]{:S(2)}) %collective-permute-start.4) | collective-permute-done | bytes 262176 | tf_op jit(solution)/shard_map/ppermute | solution.py:58
  64.6 7.5 %collective-permute-start.5 = (bf16[1,16,4,8,256]{4,1,3,2,0:T(8,128)(2,1)S(1)}, bf16[1,16,4,8,256]{4,1,3,2,0:T(8,128)(2,1)S(1)}, u32[]{:S(2)}, u32[]{:S(2)}) collective-permute-start(bf16[1,16,4,8,256]{4,1,3,2,0:T(8,128)(2,1)S(1)} %pad_maximum_fusion.9), channel_id=1, source_target_pairs={{0,32},{1,33},{2,34},{3,35},{4,36},{5,37},{6,38},{7,39},{8,40},{9,... | collective-permute-start | bytes 786440 | tf_op jit(solution)/shard_map/ppermute | solution.py:58
  84.6 1.4 fusion.70
  86.0 1.4 fusion.68
  87.4 1.4 fusion.66
  89.0 6.1 %collective-permute-start.8 = (f32[6928]{0:T(1024)S(1)}, f32[6928]{0:T(1024)S(1)}, u32[]{:S(2)}, u32[]{:S(2)}) collective-permute-start(f32[6928]{0:T(1024)S(1)} %pad_maximum_fusion.12), channel_id=1, source_target_pairs={{0,32},{1,33},{2,34},{3,35},{4,36},{5,37},{6,38},{7,39},{8,40},{9,... | collective-permute-start | bytes 83144 | tf_op jit(solution)/shard_map/ppermute | solution.py:27
  95.1 3.1 %collective-permute-start.6 = (bf16[1,16,1,8,256]{4,1,3,2,0:T(8,128)(2,1)S(1)}, bf16[1,16,1,8,256]{4,1,3,2,0:T(8,128)(2,1)S(1)}, u32[]{:S(2)}, u32[]{:S(2)}) collective-permute-start(bf16[1,16,1,8,256]{4,1,3,2,0:T(8,128)(2,1)S(1)} %get-tuple-element.86), channel_id=1, source_target_pairs={{0,1},{1,2},{2,3},{3,4},{4,5},{5,6},{6,7},{7,8},{8,9},{9,10},{10,1... | collective-permute-start | bytes 196616 | tf_op jit(solution)/shard_map/ppermute | solution.py:19
  98.2 10.3 %collective-permute-start.7 = (bf16[1,16,1,8,256]{4,1,3,2,0:T(8,128)(2,1)S(1)}, bf16[1,16,1,8,256]{4,1,3,2,0:T(8,128)(2,1)S(1)}, u32[]{:S(2)}, u32[]{:S(2)}) collective-permute-start(bf16[1,16,1,8,256]{4,1,3,2,0:T(8,128)(2,1)S(1)} %get-tuple-element.87), channel_id=1, source_target_pairs={{0,63},{1,0},{2,1},{3,2},{4,3},{5,4},{6,5},{7,6},{8,7},{9,8},{10,9... | collective-permute-start | bytes 196616 | tf_op jit(solution)/shard_map/ppermute | solution.py:19
  108.6 1.9 %collective-permute-start.9 = (f32[6928]{0:T(1024)S(1)}, f32[6928]{0:T(1024)S(1)}, u32[]{:S(2)}, u32[]{:S(2)}) collective-permute-start(f32[6928]{0:T(1024)S(1)} %fusion.99), channel_id=1, source_target_pairs={{0,16},{1,17},{2,18},{3,19},{4,20},{5,21},{6,22},{7,23},{8,24},{9,... | collective-permute-start | bytes 83144 | tf_op jit(solution)/shard_map/ppermute | solution.py:27
  111.2 5.9 %collective-permute-done.9 = f32[6928]{0:T(1024)S(1)} collective-permute-done((f32[6928]{0:T(1024)S(1)}, f32[6928]{0:T(1024)S(1)}, u32[]{:S(2)}, u32[]{:S(2)}) %collective-permute-start.9) | collective-permute-done | bytes 27744 | tf_op jit(solution)/shard_map/ppermute | solution.py:27
  117.1 1.9 %collective-permute-start.10 = (f32[6928]{0:T(1024)S(1)}, f32[6928]{0:T(1024)S(1)}, u32[]{:S(2)}, u32[]{:S(2)}) collective-permute-start(f32[6928]{0:T(1024)S(1)} %add.314), channel_id=1, source_target_pairs={{0,8},{1,9},{2,10},{3,11},{4,12},{5,13},{6,14},{7,15},{8,0},{9,1},... | collective-permute-start | bytes 83144 | tf_op jit(solution)/shard_map/ppermute | solution.py:27
  120.5 2.1 %collective-permute-done.10 = f32[6928]{0:T(1024)S(1)} collective-permute-done((f32[6928]{0:T(1024)S(1)}, f32[6928]{0:T(1024)S(1)}, u32[]{:S(2)}, u32[]{:S(2)}) %collective-permute-start.10) | collective-permute-done | bytes 27744 | tf_op jit(solution)/shard_map/ppermute | solution.py:27
  122.6 1.9 %collective-permute-start.11 = (f32[6928]{0:T(1024)S(1)}, f32[6928]{0:T(1024)S(1)}, u32[]{:S(2)}, u32[]{:S(2)}) collective-permute-start(f32[6928]{0:T(1024)S(1)} %add.315), channel_id=1, source_target_pairs={{0,4},{1,5},{2,6},{3,7},{4,0},{5,1},{6,2},{7,3},{8,12},{9,13},{10,... | collective-permute-start | bytes 83144 | tf_op jit(solution)/shard_map/ppermute | solution.py:27
  124.6 2.6 %collective-permute-done.11 = f32[6928]{0:T(1024)S(1)} collective-permute-done((f32[6928]{0:T(1024)S(1)}, f32[6928]{0:T(1024)S(1)}, u32[]{:S(2)}, u32[]{:S(2)}) %collective-permute-start.11) | collective-permute-done | bytes 27744 | tf_op jit(solution)/shard_map/ppermute | solution.py:27
  127.2 1.9 %collective-permute-start.12 = (f32[6928]{0:T(1024)S(1)}, f32[6928]{0:T(1024)S(1)}, u32[]{:S(2)}, u32[]{:S(2)}) collective-permute-start(f32[6928]{0:T(1024)S(1)} %add.316), channel_id=1, source_target_pairs={{0,2},{1,3},{2,0},{3,1},{4,6},{5,7},{6,4},{7,5},{8,10},{9,11},{10,... | collective-permute-start | bytes 83144 | tf_op jit(solution)/shard_map/ppermute | solution.py:27
  129.2 4.2 %collective-permute-done.12 = f32[6928]{0:T(1024)S(1)} collective-permute-done((f32[6928]{0:T(1024)S(1)}, f32[6928]{0:T(1024)S(1)}, u32[]{:S(2)}, u32[]{:S(2)}) %collective-permute-start.12) | collective-permute-done | bytes 27744 | tf_op jit(solution)/shard_map/ppermute | solution.py:27
  133.3 1.9 %collective-permute-start.13 = (f32[6928]{0:T(1024)S(1)}, f32[6928]{0:T(1024)S(1)}, u32[]{:S(2)}, u32[]{:S(2)}) collective-permute-start(f32[6928]{0:T(1024)S(1)} %add.317), channel_id=1, source_target_pairs={{0,1},{1,0},{2,3},{3,2},{4,5},{5,4},{6,7},{7,6},{8,9},{9,8},{10,11... | collective-permute-start | bytes 83144 | tf_op jit(solution)/shard_map/ppermute | solution.py:27
  135.4 2.5 %collective-permute-done.13 = f32[6928]{0:T(1024)S(1)} collective-permute-done((f32[6928]{0:T(1024)S(1)}, f32[6928]{0:T(1024)S(1)}, u32[]{:S(2)}, u32[]{:S(2)}) %collective-permute-start.13) | collective-permute-done | bytes 27744 | tf_op jit(solution)/shard_map/ppermute | solution.py:27
  137.9 6.7 %collective-permute-start.14 = (f32[6928]{0:T(1024)S(1)}, f32[6928]{0:T(1024)S(1)}, u32[]{:S(2)}, u32[]{:S(2)}) collective-permute-start(f32[6928]{0:T(1024)S(1)} %add.318), channel_id=1, source_target_pairs={{0,256},{64,320},{128,384},{192,448},{256,0},{320,64},{384,128},{4... | collective-permute-start | bytes 83144 | tf_op jit(solution)/shard_map/ppermute | solution.py:27
  145.9 1.9 %collective-permute-start.15 = (f32[6928]{0:T(1024)S(1)}, f32[6928]{0:T(1024)S(1)}, u32[]{:S(2)}, u32[]{:S(2)}) collective-permute-start(f32[6928]{0:T(1024)S(1)} %add.319), channel_id=1, source_target_pairs={{0,128},{64,192},{128,0},{192,64},{256,384},{320,448},{384,256},{4... | collective-permute-start | bytes 83144 | tf_op jit(solution)/shard_map/ppermute | solution.py:27
  148.1 2.4 %collective-permute-done.15 = f32[6928]{0:T(1024)S(1)} collective-permute-done((f32[6928]{0:T(1024)S(1)}, f32[6928]{0:T(1024)S(1)}, u32[]{:S(2)}, u32[]{:S(2)}) %collective-permute-start.15) | collective-permute-done | bytes 27744 | tf_op jit(solution)/shard_map/ppermute | solution.py:27
  150.5 14.7 %collective-permute-start.16 = (f32[6928]{0:T(1024)S(1)}, f32[6928]{0:T(1024)S(1)}, u32[]{:S(2)}, u32[]{:S(2)}) collective-permute-start(f32[6928]{0:T(1024)S(1)} %add.320), channel_id=1, source_target_pairs={{0,64},{64,0},{128,192},{192,128},{256,320},{320,256},{384,448},{4... | collective-permute-start | bytes 83144 | tf_op jit(solution)/shard_map/ppermute | solution.py:27
  (107 shorter events, 14.0 us)
Async XLA Ops:
  3.7 7.7 %collective-permute-start = (bf16[1,16,4,8,256]{4,1,3,2,0:T(8,128)(2,1)S(1)}, bf16[1,16,4,8,256]{4,1,3,2,0:T(8,128)(2,1)S(1)}, u32[]{:S(2)}, u32[]{:S(2)}) collective-permute-start(bf16[1,16,4,8,256]{4,1,3,2,0:T(8,128)(2,1)S(1)} %pad_maximum_fusion.4), channel_id=1, source_target_pairs={{0,1},{1,0},{2,3},{3,2},{4,5},{5,4},{6,7},{7,6},{8,9},{9,8},{10,11... | collective-permute-start | bytes 786440 | tf_op jit(solution)/shard_map/ppermute | solution.py:58
  11.5 10.6 %collective-permute-start.1 = (bf16[1,16,4,8,256]{4,1,3,2,0:T(8,128)(2,1)S(1)}, bf16[1,16,4,8,256]{4,1,3,2,0:T(8,128)(2,1)S(1)}, u32[]{:S(2)}, u32[]{:S(2)}) collective-permute-start(bf16[1,16,4,8,256]{4,1,3,2,0:T(8,128)(2,1)S(1)} %pad_maximum_fusion.5), channel_id=1, source_target_pairs={{0,2},{1,3},{2,0},{3,1},{4,6},{5,7},{6,4},{7,5},{8,10},{9,11},{10,... | collective-permute-start | bytes 786440 | tf_op jit(solution)/shard_map/ppermute | solution.py:58
  22.2 9.0 %collective-permute-start.2 = (bf16[1,16,4,8,256]{4,1,3,2,0:T(8,128)(2,1)S(1)}, bf16[1,16,4,8,256]{4,1,3,2,0:T(8,128)(2,1)S(1)}, u32[]{:S(2)}, u32[]{:S(2)}) collective-permute-start(bf16[1,16,4,8,256]{4,1,3,2,0:T(8,128)(2,1)S(1)} %pad_maximum_fusion.6), channel_id=1, source_target_pairs={{0,4},{1,5},{2,6},{3,7},{4,0},{5,1},{6,2},{7,3},{8,12},{9,13},{10,... | collective-permute-start | bytes 786440 | tf_op jit(solution)/shard_map/ppermute | solution.py:58
  27.6 51.2 %copy-start = (bf16[27,16,16]{0,2,1:T(8,128)(2,1)S(1)}, bf16[27,16,16]{0,2,1:T(8,128)(2,1)}, u32[]{:S(2)}) copy-start(bf16[27,16,16]{0,2,1:T(8,128)(2,1)} %param.13) | copy-start | bytes 41476
  31.3 17.0 %collective-permute-start.3 = (bf16[1,16,4,8,256]{4,1,3,2,0:T(8,128)(2,1)S(1)}, bf16[1,16,4,8,256]{4,1,3,2,0:T(8,128)(2,1)S(1)}, u32[]{:S(2)}, u32[]{:S(2)}) collective-permute-start(bf16[1,16,4,8,256]{4,1,3,2,0:T(8,128)(2,1)S(1)} %pad_maximum_fusion.7), channel_id=1, source_target_pairs={{0,8},{1,9},{2,10},{3,11},{4,12},{5,13},{6,14},{7,15},{8,0},{9,1},... | collective-permute-start | bytes 786440 | tf_op jit(solution)/shard_map/ppermute | solution.py:58
  48.4 16.2 %collective-permute-start.4 = (bf16[1,16,4,8,256]{4,1,3,2,0:T(8,128)(2,1)S(1)}, bf16[1,16,4,8,256]{4,1,3,2,0:T(8,128)(2,1)S(1)}, u32[]{:S(2)}, u32[]{:S(2)}) collective-permute-start(bf16[1,16,4,8,256]{4,1,3,2,0:T(8,128)(2,1)S(1)} %pad_maximum_fusion.8), channel_id=1, source_target_pairs={{0,16},{1,17},{2,18},{3,19},{4,20},{5,21},{6,22},{7,23},{8,24},{9,... | collective-permute-start | bytes 786440 | tf_op jit(solution)/shard_map/ppermute | solution.py:58
  64.6 15.2 %collective-permute-start.5 = (bf16[1,16,4,8,256]{4,1,3,2,0:T(8,128)(2,1)S(1)}, bf16[1,16,4,8,256]{4,1,3,2,0:T(8,128)(2,1)S(1)}, u32[]{:S(2)}, u32[]{:S(2)}) collective-permute-start(bf16[1,16,4,8,256]{4,1,3,2,0:T(8,128)(2,1)S(1)} %pad_maximum_fusion.9), channel_id=1, source_target_pairs={{0,32},{1,33},{2,34},{3,35},{4,36},{5,37},{6,38},{7,39},{8,40},{9,... | collective-permute-start | bytes 786440 | tf_op jit(solution)/shard_map/ppermute | solution.py:58
  82.7 0.7 copy-start.1
  83.3 0.9 copy-start.2
  89.0 19.5 %collective-permute-start.8 = (f32[6928]{0:T(1024)S(1)}, f32[6928]{0:T(1024)S(1)}, u32[]{:S(2)}, u32[]{:S(2)}) collective-permute-start(f32[6928]{0:T(1024)S(1)} %pad_maximum_fusion.12), channel_id=1, source_target_pairs={{0,32},{1,33},{2,34},{3,35},{4,36},{5,37},{6,38},{7,39},{8,40},{9,... | collective-permute-start | bytes 83144 | tf_op jit(solution)/shard_map/ppermute | solution.py:27
  95.1 23.9 %collective-permute-start.6 = (bf16[1,16,1,8,256]{4,1,3,2,0:T(8,128)(2,1)S(1)}, bf16[1,16,1,8,256]{4,1,3,2,0:T(8,128)(2,1)S(1)}, u32[]{:S(2)}, u32[]{:S(2)}) collective-permute-start(bf16[1,16,1,8,256]{4,1,3,2,0:T(8,128)(2,1)S(1)} %get-tuple-element.86), channel_id=1, source_target_pairs={{0,1},{1,2},{2,3},{3,4},{4,5},{5,6},{6,7},{7,8},{8,9},{9,10},{10,1... | collective-permute-start | bytes 196616 | tf_op jit(solution)/shard_map/ppermute | solution.py:19
  98.2 20.8 %collective-permute-start.7 = (bf16[1,16,1,8,256]{4,1,3,2,0:T(8,128)(2,1)S(1)}, bf16[1,16,1,8,256]{4,1,3,2,0:T(8,128)(2,1)S(1)}, u32[]{:S(2)}, u32[]{:S(2)}) collective-permute-start(bf16[1,16,1,8,256]{4,1,3,2,0:T(8,128)(2,1)S(1)} %get-tuple-element.87), channel_id=1, source_target_pairs={{0,63},{1,0},{2,1},{3,2},{4,3},{5,4},{6,5},{7,6},{8,7},{9,8},{10,9... | collective-permute-start | bytes 196616 | tf_op jit(solution)/shard_map/ppermute | solution.py:19
  108.6 8.5 %collective-permute-start.9 = (f32[6928]{0:T(1024)S(1)}, f32[6928]{0:T(1024)S(1)}, u32[]{:S(2)}, u32[]{:S(2)}) collective-permute-start(f32[6928]{0:T(1024)S(1)} %fusion.99), channel_id=1, source_target_pairs={{0,16},{1,17},{2,18},{3,19},{4,20},{5,21},{6,22},{7,23},{8,24},{9,... | collective-permute-start | bytes 83144 | tf_op jit(solution)/shard_map/ppermute | solution.py:27
  117.1 5.5 %collective-permute-start.10 = (f32[6928]{0:T(1024)S(1)}, f32[6928]{0:T(1024)S(1)}, u32[]{:S(2)}, u32[]{:S(2)}) collective-permute-start(f32[6928]{0:T(1024)S(1)} %add.314), channel_id=1, source_target_pairs={{0,8},{1,9},{2,10},{3,11},{4,12},{5,13},{6,14},{7,15},{8,0},{9,1},... | collective-permute-start | bytes 83144 | tf_op jit(solution)/shard_map/ppermute | solution.py:27
  122.6 4.6 %collective-permute-start.11 = (f32[6928]{0:T(1024)S(1)}, f32[6928]{0:T(1024)S(1)}, u32[]{:S(2)}, u32[]{:S(2)}) collective-permute-start(f32[6928]{0:T(1024)S(1)} %add.315), channel_id=1, source_target_pairs={{0,4},{1,5},{2,6},{3,7},{4,0},{5,1},{6,2},{7,3},{8,12},{9,13},{10,... | collective-permute-start | bytes 83144 | tf_op jit(solution)/shard_map/ppermute | solution.py:27
  127.2 6.1 %collective-permute-start.12 = (f32[6928]{0:T(1024)S(1)}, f32[6928]{0:T(1024)S(1)}, u32[]{:S(2)}, u32[]{:S(2)}) collective-permute-start(f32[6928]{0:T(1024)S(1)} %add.316), channel_id=1, source_target_pairs={{0,2},{1,3},{2,0},{3,1},{4,6},{5,7},{6,4},{7,5},{8,10},{9,11},{10,... | collective-permute-start | bytes 83144 | tf_op jit(solution)/shard_map/ppermute | solution.py:27
  133.3 4.6 %collective-permute-start.13 = (f32[6928]{0:T(1024)S(1)}, f32[6928]{0:T(1024)S(1)}, u32[]{:S(2)}, u32[]{:S(2)}) collective-permute-start(f32[6928]{0:T(1024)S(1)} %add.317), channel_id=1, source_target_pairs={{0,1},{1,0},{2,3},{3,2},{4,5},{5,4},{6,7},{7,6},{8,9},{9,8},{10,11... | collective-permute-start | bytes 83144 | tf_op jit(solution)/shard_map/ppermute | solution.py:27
  137.9 7.9 %collective-permute-start.14 = (f32[6928]{0:T(1024)S(1)}, f32[6928]{0:T(1024)S(1)}, u32[]{:S(2)}, u32[]{:S(2)}) collective-permute-start(f32[6928]{0:T(1024)S(1)} %add.318), channel_id=1, source_target_pairs={{0,256},{64,320},{128,384},{192,448},{256,0},{320,64},{384,128},{4... | collective-permute-start | bytes 83144 | tf_op jit(solution)/shard_map/ppermute | solution.py:27
  145.9 4.6 %collective-permute-start.15 = (f32[6928]{0:T(1024)S(1)}, f32[6928]{0:T(1024)S(1)}, u32[]{:S(2)}, u32[]{:S(2)}) collective-permute-start(f32[6928]{0:T(1024)S(1)} %add.319), channel_id=1, source_target_pairs={{0,128},{64,192},{128,0},{192,64},{256,384},{320,448},{384,256},{4... | collective-permute-start | bytes 83144 | tf_op jit(solution)/shard_map/ppermute | solution.py:27
  150.5 15.7 %collective-permute-start.16 = (f32[6928]{0:T(1024)S(1)}, f32[6928]{0:T(1024)S(1)}, u32[]{:S(2)}, u32[]{:S(2)}) collective-permute-start(f32[6928]{0:T(1024)S(1)} %add.320), channel_id=1, source_target_pairs={{0,64},{64,0},{128,192},{192,128},{256,320},{320,256},{384,448},{4... | collective-permute-start | bytes 83144 | tf_op jit(solution)/shard_map/ppermute | solution.py:27

commit v8 on v7

--- a/solution.py
+++ b/solution.py
@@ -17,6 +17,16 @@
     count = lax.axis_size(axis)
     pairs = [(source, (source + steps) % count) for source in range(count)]
     return lax.ppermute(value, axis, pairs)
+
+
+def halo_planes(value, axis):
+    count = lax.axis_size(axis)
+    even = lax.axis_index(axis) % 2 == 0
+    first, last = value[:, :, 0:1], value[:, :, -1:]
+    near = lax.ppermute(jnp.where(even, last, first), axis, [(s, s ^ 1) for s in range(count)])
+    pairs = [(s, (s + 1) % count if s % 2 else (s - 1) % count) for s in range(count)]
+    across = lax.ppermute(jnp.where(even, first, last), axis, pairs)
+    return jnp.where(even, across, near), jnp.where(even, near, across)
 
 
 def butterfly_sum(value, axis):
@@ -114,8 +124,7 @@
         )
     hidden, slope = gelu_parts(total)
     grad_pre = (cotangent.astype(jnp.float32) * slope).astype(jnp.bfloat16)
-    grad_before = shifted(grad_pre[:, :, planes - 1 : planes], "gx", 1)
-    grad_after = shifted(grad_pre[:, :, 0:1], "gx", -1)
+    grad_before, grad_after = halo_planes(grad_pre, "gx")
     grad_list = []
     for shift_x in range(3):
         window = stacked_yz[:, :, shift_x : shift_x + planes]

time: 168 us -> 165 us (0.982)
  starting transfers between devices: 90.4 us -> 87.6 us
where the time goes in v8:
time: 165 us; the launch traced here: 164 us
  starting transfers between devices  87.6 us (53%)
  waiting for transfers between devices  45.6 us (28%)
  between operations  11.6 us (7%)
  local copies, waits for them, and re-layouts  9.67 us (6%)
  matrix products  6.08 us (4%)
  other arithmetic  3.97 us (2%)
    ppermute x6, starting transfers between devices, routed(): arrived = lax.ppermute(jnp.concatenate(pieces, axis=2), axis, pairs)  38.1 us
    ppermute x9, starting transfers between devices, butterfly_sum(): value = value + lax.ppermute(value, axis, pairs)  37.7 us
    ppermute x6, waiting for transfers between devices, routed(): arrived = lax.ppermute(jnp.concatenate(pieces, axis=2), axis, pairs)  25.6 us
    ppermute x9, waiting for transfers between devices, butterfly_sum(): value = value + lax.ppermute(value, axis, pairs)  20 us
    ppermute x1, starting transfers between devices, halo_planes(): across = lax.ppermute(jnp.where(even, first, last), axis, pairs)  9.9 us
    unnamed x14, local copies, waits for them, and re-layouts  4.43 us
    dot_general x3, matrix products, on_device(): jnp.einsum('boxyz,bcxyz->oc', grad_pre, window, preferred_element_type=jn...  4.19 us
  transfers between devices with their start and end apart: 17, of which 12 were waited for; matrix products, arithmetic and copies ran while one was open for 4% of the time, Pallas kernels for 0%

profile of v8, /device:TPU:1, one launch (start us, length us, event | category | flops | bytes accessed | tf_op | source)
XLA Modules:
  0.0 164.5 jit_solution(10384173687243978208)
XLA Ops:
  0.6 1.4 fusion.90
  3.7 3.9 %collective-permute-start = (bf16[1,16,4,8,256]{4,1,3,2,0:T(8,128)(2,1)S(1)}, bf16[1,16,4,8,256]{4,1,3,2,0:T(8,128)(2,1)S(1)}, u32[]{:S(2)}, u32[]{:S(2)}) collective-permute-start(bf16[1,16,4,8,256]{4,1,3,2,0:T(8,128)(2,1)S(1)} %pad_maximum_fusion.4), channel_id=1, source_target_pairs={{0,1},{1,0},{2,3},{3,2},{4,5},{5,4},{6,7},{7,6},{8,9},{9,8},{10,11... | collective-permute-start | bytes 786440 | tf_op jit(solution)/shard_map/ppermute | solution.py:68
  7.7 1.4 fusion.91
  11.6 6.8 %collective-permute-start.1 = (bf16[1,16,4,8,256]{4,1,3,2,0:T(8,128)(2,1)S(1)}, bf16[1,16,4,8,256]{4,1,3,2,0:T(8,128)(2,1)S(1)}, u32[]{:S(2)}, u32[]{:S(2)}) collective-permute-start(bf16[1,16,4,8,256]{4,1,3,2,0:T(8,128)(2,1)S(1)} %pad_maximum_fusion.5), channel_id=1, source_target_pairs={{0,2},{1,3},{2,0},{3,1},{4,6},{5,7},{6,4},{7,5},{8,10},{9,11},{10,... | collective-permute-start | bytes 786440 | tf_op jit(solution)/shard_map/ppermute | solution.py:68
  18.6 3.6 %collective-permute-done.1 = bf16[1,16,4,8,256]{4,1,3,2,0:T(8,128)(2,1)S(1)} collective-permute-done((bf16[1,16,4,8,256]{4,1,3,2,0:T(8,128)(2,1)S(1)}, bf16[1,16,4,8,256]{4,1,3,2,0:T(8,128)(2,1)S(1)}, u32[]{:S(2)}, u32[]{:S(2)}) %collective-permute-start.1) | collective-permute-done | bytes 262176 | tf_op jit(solution)/shard_map/ppermute | solution.py:68
  22.2 5.2 %collective-permute-start.2 = (bf16[1,16,4,8,256]{4,1,3,2,0:T(8,128)(2,1)S(1)}, bf16[1,16,4,8,256]{4,1,3,2,0:T(8,128)(2,1)S(1)}, u32[]{:S(2)}, u32[]{:S(2)}) collective-permute-start(bf16[1,16,4,8,256]{4,1,3,2,0:T(8,128)(2,1)S(1)} %pad_maximum_fusion.6), channel_id=1, source_target_pairs={{0,4},{1,5},{2,6},{3,7},{4,0},{5,1},{6,2},{7,3},{8,12},{9,13},{10,... | collective-permute-start | bytes 786440 | tf_op jit(solution)/shard_map/ppermute | solution.py:68
  27.7 3.5 %collective-permute-done.2 = bf16[1,16,4,8,256]{4,1,3,2,0:T(8,128)(2,1)S(1)} collective-permute-done((bf16[1,16,4,8,256]{4,1,3,2,0:T(8,128)(2,1)S(1)}, bf16[1,16,4,8,256]{4,1,3,2,0:T(8,128)(2,1)S(1)}, u32[]{:S(2)}, u32[]{:S(2)}) %collective-permute-start.2) | collective-permute-done | bytes 262176 | tf_op jit(solution)/shard_map/ppermute | solution.py:68
  31.3 6.2 %collective-permute-start.3 = (bf16[1,16,4,8,256]{4,1,3,2,0:T(8,128)(2,1)S(1)}, bf16[1,16,4,8,256]{4,1,3,2,0:T(8,128)(2,1)S(1)}, u32[]{:S(2)}, u32[]{:S(2)}) collective-permute-start(bf16[1,16,4,8,256]{4,1,3,2,0:T(8,128)(2,1)S(1)} %pad_maximum_fusion.7), channel_id=1, source_target_pairs={{0,8},{1,9},{2,10},{3,11},{4,12},{5,13},{6,14},{7,15},{8,0},{9,1},... | collective-permute-start | bytes 786440 | tf_op jit(solution)/shard_map/ppermute | solution.py:68
  37.7 10.6 %collective-permute-done.3 = bf16[1,16,4,8,256]{4,1,3,2,0:T(8,128)(2,1)S(1)} collective-permute-done((bf16[1,16,4,8,256]{4,1,3,2,0:T(8,128)(2,1)S(1)}, bf16[1,16,4,8,256]{4,1,3,2,0:T(8,128)(2,1)S(1)}, u32[]{:S(2)}, u32[]{:S(2)}) %collective-permute-start.3) | collective-permute-done | bytes 262176 | tf_op jit(solution)/shard_map/ppermute | solution.py:68
  48.4 8.4 %collective-permute-start.4 = (bf16[1,16,4,8,256]{4,1,3,2,0:T(8,128)(2,1)S(1)}, bf16[1,16,4,8,256]{4,1,3,2,0:T(8,128)(2,1)S(1)}, u32[]{:S(2)}, u32[]{:S(2)}) collective-permute-start(bf16[1,16,4,8,256]{4,1,3,2,0:T(8,128)(2,1)S(1)} %pad_maximum_fusion.8), channel_id=1, source_target_pairs={{0,16},{1,17},{2,18},{3,19},{4,20},{5,21},{6,22},{7,23},{8,24},{9,... | collective-permute-start | bytes 786440 | tf_op jit(solution)/shard_map/ppermute | solution.py:68
  57.0 7.6 %collective-permute-done.4 = bf16[1,16,4,8,256]{4,1,3,2,0:T(8,128)(2,1)S(1)} collective-permute-done((bf16[1,16,4,8,256]{4,1,3,2,0:T(8,128)(2,1)S(1)}, bf16[1,16,4,8,256]{4,1,3,2,0:T(8,128)(2,1)S(1)}, u32[]{:S(2)}, u32[]{:S(2)}) %collective-permute-start.4) | collective-permute-done | bytes 262176 | tf_op jit(solution)/shard_map/ppermute | solution.py:68
  64.7 7.5 %collective-permute-start.5 = (bf16[1,16,4,8,256]{4,1,3,2,0:T(8,128)(2,1)S(1)}, bf16[1,16,4,8,256]{4,1,3,2,0:T(8,128)(2,1)S(1)}, u32[]{:S(2)}, u32[]{:S(2)}) collective-permute-start(bf16[1,16,4,8,256]{4,1,3,2,0:T(8,128)(2,1)S(1)} %pad_maximum_fusion.9), channel_id=1, source_target_pairs={{0,32},{1,33},{2,34},{3,35},{4,36},{5,37},{6,38},{7,39},{8,40},{9,... | collective-permute-start | bytes 786440 | tf_op jit(solution)/shard_map/ppermute | solution.py:68
  84.7 1.4 fusion.70
  86.1 1.4 fusion.68
  87.5 1.4 fusion.66
  89.1 6.0 %collective-permute-start.8 = (f32[6928]{0:T(1024)S(1)}, f32[6928]{0:T(1024)S(1)}, u32[]{:S(2)}, u32[]{:S(2)}) collective-permute-start(f32[6928]{0:T(1024)S(1)} %pad_maximum_fusion.12), channel_id=1, source_target_pairs={{0,32},{1,33},{2,34},{3,35},{4,36},{5,37},{6,38},{7,39},{8,40},{9,... | collective-permute-start | bytes 83144 | tf_op jit(solution)/shard_map/ppermute | solution.py:37
  95.2 9.9 %collective-permute-start.6 = (bf16[1,16,1,8,256]{4,1,3,2,0:T(8,128)(2,1)S(1)}, bf16[1,16,1,8,256]{4,1,3,2,0:T(8,128)(2,1)S(1)}, u32[]{:S(2)}, u32[]{:S(2)}) collective-permute-start(bf16[1,16,1,8,256]{4,1,3,2,0:T(8,128)(2,1)S(1)} %get-tuple-element.88), channel_id=1, source_target_pairs={{0,63},{1,2},{2,1},{3,4},{4,3},{5,6},{6,5},{7,8},{8,7},{9,10},{10,... | collective-permute-start | bytes 196616 | tf_op jit(solution)/shard_map/ppermute | solution.py:28
  105.1 1.9 %collective-permute-start.7 = (bf16[1,16,1,8,256]{4,1,3,2,0:T(8,128)(2,1)S(1)}, bf16[1,16,1,8,256]{4,1,3,2,0:T(8,128)(2,1)S(1)}, u32[]{:S(2)}, u32[]{:S(2)}) collective-permute-start(bf16[1,16,1,8,256]{4,1,3,2,0:T(8,128)(2,1)S(1)} %get-tuple-element.89), channel_id=1, source_target_pairs={{0,1},{1,0},{2,3},{3,2},{4,5},{5,4},{6,7},{7,6},{8,9},{9,8},{10,11... | collective-permute-start | bytes 196616 | tf_op jit(solution)/shard_map/ppermute | solution.py:26
  107.0 1.9 %collective-permute-start.9 = (f32[6928]{0:T(1024)S(1)}, f32[6928]{0:T(1024)S(1)}, u32[]{:S(2)}, u32[]{:S(2)}) collective-permute-start(f32[6928]{0:T(1024)S(1)} %fusion.98), channel_id=1, source_target_pairs={{0,16},{1,17},{2,18},{3,19},{4,20},{5,21},{6,22},{7,23},{8,24},{9,... | collective-permute-start | bytes 83144 | tf_op jit(solution)/shard_map/ppermute | solution.py:37
  109.7 6.2 %collective-permute-done.9 = f32[6928]{0:T(1024)S(1)} collective-permute-done((f32[6928]{0:T(1024)S(1)}, f32[6928]{0:T(1024)S(1)}, u32[]{:S(2)}, u32[]{:S(2)}) %collective-permute-start.9) | collective-permute-done | bytes 27744 | tf_op jit(solution)/shard_map/ppermute | solution.py:37
  115.9 1.9 %collective-permute-start.10 = (f32[6928]{0:T(1024)S(1)}, f32[6928]{0:T(1024)S(1)}, u32[]{:S(2)}, u32[]{:S(2)}) collective-permute-start(f32[6928]{0:T(1024)S(1)} %add.315), channel_id=1, source_target_pairs={{0,8},{1,9},{2,10},{3,11},{4,12},{5,13},{6,14},{7,15},{8,0},{9,1},... | collective-permute-start | bytes 83144 | tf_op jit(solution)/shard_map/ppermute | solution.py:37
  119.3 2.4 %collective-permute-done.10 = f32[6928]{0:T(1024)S(1)} collective-permute-done((f32[6928]{0:T(1024)S(1)}, f32[6928]{0:T(1024)S(1)}, u32[]{:S(2)}, u32[]{:S(2)}) %collective-permute-start.10) | collective-permute-done | bytes 27744 | tf_op jit(solution)/shard_map/ppermute | solution.py:37
  121.7 1.9 %collective-permute-start.11 = (f32[6928]{0:T(1024)S(1)}, f32[6928]{0:T(1024)S(1)}, u32[]{:S(2)}, u32[]{:S(2)}) collective-permute-start(f32[6928]{0:T(1024)S(1)} %add.316), channel_id=1, source_target_pairs={{0,4},{1,5},{2,6},{3,7},{4,0},{5,1},{6,2},{7,3},{8,12},{9,13},{10,... | collective-permute-start | bytes 83144 | tf_op jit(solution)/shard_map/ppermute | solution.py:37
  123.7 2.6 %collective-permute-done.11 = f32[6928]{0:T(1024)S(1)} collective-permute-done((f32[6928]{0:T(1024)S(1)}, f32[6928]{0:T(1024)S(1)}, u32[]{:S(2)}, u32[]{:S(2)}) %collective-permute-start.11) | collective-permute-done | bytes 27744 | tf_op jit(solution)/shard_map/ppermute | solution.py:37
  126.3 1.9 %collective-permute-start.12 = (f32[6928]{0:T(1024)S(1)}, f32[6928]{0:T(1024)S(1)}, u32[]{:S(2)}, u32[]{:S(2)}) collective-permute-start(f32[6928]{0:T(1024)S(1)} %add.317), channel_id=1, source_target_pairs={{0,2},{1,3},{2,0},{3,1},{4,6},{5,7},{6,4},{7,5},{8,10},{9,11},{10,... | collective-permute-start | bytes 83144 | tf_op jit(solution)/shard_map/ppermute | solution.py:37
  128.2 4.2 %collective-permute-done.12 = f32[6928]{0:T(1024)S(1)} collective-permute-done((f32[6928]{0:T(1024)S(1)}, f32[6928]{0:T(1024)S(1)}, u32[]{:S(2)}, u32[]{:S(2)}) %collective-permute-start.12) | collective-permute-done | bytes 27744 | tf_op jit(solution)/shard_map/ppermute | solution.py:37
  132.4 3.1 %collective-permute-start.13 = (f32[6928]{0:T(1024)S(1)}, f32[6928]{0:T(1024)S(1)}, u32[]{:S(2)}, u32[]{:S(2)}) collective-permute-start(f32[6928]{0:T(1024)S(1)} %add.318), channel_id=1, source_target_pairs={{0,1},{1,0},{2,3},{3,2},{4,5},{5,4},{6,7},{7,6},{8,9},{9,8},{10,11... | collective-permute-start | bytes 83144 | tf_op jit(solution)/shard_map/ppermute | solution.py:37
  135.6 1.4 collective-permute-done.13
  137.0 7.9 %collective-permute-start.14 = (f32[6928]{0:T(1024)S(1)}, f32[6928]{0:T(1024)S(1)}, u32[]{:S(2)}, u32[]{:S(2)}) collective-permute-start(f32[6928]{0:T(1024)S(1)} %add.319), channel_id=1, source_target_pairs={{0,256},{64,320},{128,384},{192,448},{256,0},{320,64},{384,128},{4... | collective-permute-start | bytes 83144 | tf_op jit(solution)/shard_map/ppermute | solution.py:37
  146.2 1.9 %collective-permute-start.15 = (f32[6928]{0:T(1024)S(1)}, f32[6928]{0:T(1024)S(1)}, u32[]{:S(2)}, u32[]{:S(2)}) collective-permute-start(f32[6928]{0:T(1024)S(1)} %add.320), channel_id=1, source_target_pairs={{0,128},{64,192},{128,0},{192,64},{256,384},{320,448},{384,256},{4... | collective-permute-start | bytes 83144 | tf_op jit(solution)/shard_map/ppermute | solution.py:37
  148.4 2.4 %collective-permute-done.15 = f32[6928]{0:T(1024)S(1)} collective-permute-done((f32[6928]{0:T(1024)S(1)}, f32[6928]{0:T(1024)S(1)}, u32[]{:S(2)}, u32[]{:S(2)}) %collective-permute-start.15) | collective-permute-done | bytes 27744 | tf_op jit(solution)/shard_map/ppermute | solution.py:37
  150.8 11.2 %collective-permute-start.16 = (f32[6928]{0:T(1024)S(1)}, f32[6928]{0:T(1024)S(1)}, u32[]{:S(2)}, u32[]{:S(2)}) collective-permute-start(f32[6928]{0:T(1024)S(1)} %add.321), channel_id=1, source_target_pairs={{0,64},{64,0},{128,192},{192,128},{256,320},{320,256},{384,448},{4... | collective-permute-start | bytes 83144 | tf_op jit(solution)/shard_map/ppermute | solution.py:37
  (108 shorter events, 14.0 us)
Async XLA Ops:
  3.7 7.7 %collective-permute-start = (bf16[1,16,4,8,256]{4,1,3,2,0:T(8,128)(2,1)S(1)}, bf16[1,16,4,8,256]{4,1,3,2,0:T(8,128)(2,1)S(1)}, u32[]{:S(2)}, u32[]{:S(2)}) collective-permute-start(bf16[1,16,4,8,256]{4,1,3,2,0:T(8,128)(2,1)S(1)} %pad_maximum_fusion.4), channel_id=1, source_target_pairs={{0,1},{1,0},{2,3},{3,2},{4,5},{5,4},{6,7},{7,6},{8,9},{9,8},{10,11... | collective-permute-start | bytes 786440 | tf_op jit(solution)/shard_map/ppermute | solution.py:68
  11.6 10.6 %collective-permute-start.1 = (bf16[1,16,4,8,256]{4,1,3,2,0:T(8,128)(2,1)S(1)}, bf16[1,16,4,8,256]{4,1,3,2,0:T(8,128)(2,1)S(1)}, u32[]{:S(2)}, u32[]{:S(2)}) collective-permute-start(bf16[1,16,4,8,256]{4,1,3,2,0:T(8,128)(2,1)S(1)} %pad_maximum_fusion.5), channel_id=1, source_target_pairs={{0,2},{1,3},{2,0},{3,1},{4,6},{5,7},{6,4},{7,5},{8,10},{9,11},{10,... | collective-permute-start | bytes 786440 | tf_op jit(solution)/shard_map/ppermute | solution.py:68
  22.2 9.0 %collective-permute-start.2 = (bf16[1,16,4,8,256]{4,1,3,2,0:T(8,128)(2,1)S(1)}, bf16[1,16,4,8,256]{4,1,3,2,0:T(8,128)(2,1)S(1)}, u32[]{:S(2)}, u32[]{:S(2)}) collective-permute-start(bf16[1,16,4,8,256]{4,1,3,2,0:T(8,128)(2,1)S(1)} %pad_maximum_fusion.6), channel_id=1, source_target_pairs={{0,4},{1,5},{2,6},{3,7},{4,0},{5,1},{6,2},{7,3},{8,12},{9,13},{10,... | collective-permute-start | bytes 786440 | tf_op jit(solution)/shard_map/ppermute | solution.py:68
  27.7 51.2 %copy-start = (bf16[27,16,16]{0,2,1:T(8,128)(2,1)S(1)}, bf16[27,16,16]{0,2,1:T(8,128)(2,1)}, u32[]{:S(2)}) copy-start(bf16[27,16,16]{0,2,1:T(8,128)(2,1)} %param.13) | copy-start | bytes 41476
  31.3 17.0 %collective-permute-start.3 = (bf16[1,16,4,8,256]{4,1,3,2,0:T(8,128)(2,1)S(1)}, bf16[1,16,4,8,256]{4,1,3,2,0:T(8,128)(2,1)S(1)}, u32[]{:S(2)}, u32[]{:S(2)}) collective-permute-start(bf16[1,16,4,8,256]{4,1,3,2,0:T(8,128)(2,1)S(1)} %pad_maximum_fusion.7), channel_id=1, source_target_pairs={{0,8},{1,9},{2,10},{3,11},{4,12},{5,13},{6,14},{7,15},{8,0},{9,1},... | collective-permute-start | bytes 786440 | tf_op jit(solution)/shard_map/ppermute | solution.py:68
  48.4 16.2 %collective-permute-start.4 = (bf16[1,16,4,8,256]{4,1,3,2,0:T(8,128)(2,1)S(1)}, bf16[1,16,4,8,256]{4,1,3,2,0:T(8,128)(2,1)S(1)}, u32[]{:S(2)}, u32[]{:S(2)}) collective-permute-start(bf16[1,16,4,8,256]{4,1,3,2,0:T(8,128)(2,1)S(1)} %pad_maximum_fusion.8), channel_id=1, source_target_pairs={{0,16},{1,17},{2,18},{3,19},{4,20},{5,21},{6,22},{7,23},{8,24},{9,... | collective-permute-start | bytes 786440 | tf_op jit(solution)/shard_map/ppermute | solution.py:68
  64.7 15.3 %collective-permute-start.5 = (bf16[1,16,4,8,256]{4,1,3,2,0:T(8,128)(2,1)S(1)}, bf16[1,16,4,8,256]{4,1,3,2,0:T(8,128)(2,1)S(1)}, u32[]{:S(2)}, u32[]{:S(2)}) collective-permute-start(bf16[1,16,4,8,256]{4,1,3,2,0:T(8,128)(2,1)S(1)} %pad_maximum_fusion.9), channel_id=1, source_target_pairs={{0,32},{1,33},{2,34},{3,35},{4,36},{5,37},{6,38},{7,39},{8,40},{9,... | collective-permute-start | bytes 786440 | tf_op jit(solution)/shard_map/ppermute | solution.py:68
  82.8 0.7 copy-start.1
  83.4 0.9 copy-start.2
  89.1 17.9 %collective-permute-start.8 = (f32[6928]{0:T(1024)S(1)}, f32[6928]{0:T(1024)S(1)}, u32[]{:S(2)}, u32[]{:S(2)}) collective-permute-start(f32[6928]{0:T(1024)S(1)} %pad_maximum_fusion.12), channel_id=1, source_target_pairs={{0,32},{1,33},{2,34},{3,35},{4,36},{5,37},{6,38},{7,39},{8,40},{9,... | collective-permute-start | bytes 83144 | tf_op jit(solution)/shard_map/ppermute | solution.py:37
  95.2 22.6 %collective-permute-start.6 = (bf16[1,16,1,8,256]{4,1,3,2,0:T(8,128)(2,1)S(1)}, bf16[1,16,1,8,256]{4,1,3,2,0:T(8,128)(2,1)S(1)}, u32[]{:S(2)}, u32[]{:S(2)}) collective-permute-start(bf16[1,16,1,8,256]{4,1,3,2,0:T(8,128)(2,1)S(1)} %get-tuple-element.88), channel_id=1, source_target_pairs={{0,63},{1,2},{2,1},{3,4},{4,3},{5,6},{6,5},{7,8},{8,7},{9,10},{10,... | collective-permute-start | bytes 196616 | tf_op jit(solution)/shard_map/ppermute | solution.py:28
  105.1 12.7 %collective-permute-start.7 = (bf16[1,16,1,8,256]{4,1,3,2,0:T(8,128)(2,1)S(1)}, bf16[1,16,1,8,256]{4,1,3,2,0:T(8,128)(2,1)S(1)}, u32[]{:S(2)}, u32[]{:S(2)}) collective-permute-start(bf16[1,16,1,8,256]{4,1,3,2,0:T(8,128)(2,1)S(1)} %get-tuple-element.89), channel_id=1, source_target_pairs={{0,1},{1,0},{2,3},{3,2},{4,5},{5,4},{6,7},{7,6},{8,9},{9,8},{10,11... | collective-permute-start | bytes 196616 | tf_op jit(solution)/shard_map/ppermute | solution.py:26
  107.0 8.8 %collective-permute-start.9 = (f32[6928]{0:T(1024)S(1)}, f32[6928]{0:T(1024)S(1)}, u32[]{:S(2)}, u32[]{:S(2)}) collective-permute-start(f32[6928]{0:T(1024)S(1)} %fusion.98), channel_id=1, source_target_pairs={{0,16},{1,17},{2,18},{3,19},{4,20},{5,21},{6,22},{7,23},{8,24},{9,... | collective-permute-start | bytes 83144 | tf_op jit(solution)/shard_map/ppermute | solution.py:37
  115.9 5.8 %collective-permute-start.10 = (f32[6928]{0:T(1024)S(1)}, f32[6928]{0:T(1024)S(1)}, u32[]{:S(2)}, u32[]{:S(2)}) collective-permute-start(f32[6928]{0:T(1024)S(1)} %add.315), channel_id=1, source_target_pairs={{0,8},{1,9},{2,10},{3,11},{4,12},{5,13},{6,14},{7,15},{8,0},{9,1},... | collective-permute-start | bytes 83144 | tf_op jit(solution)/shard_map/ppermute | solution.py:37
  121.7 4.6 %collective-permute-start.11 = (f32[6928]{0:T(1024)S(1)}, f32[6928]{0:T(1024)S(1)}, u32[]{:S(2)}, u32[]{:S(2)}) collective-permute-start(f32[6928]{0:T(1024)S(1)} %add.316), channel_id=1, source_target_pairs={{0,4},{1,5},{2,6},{3,7},{4,0},{5,1},{6,2},{7,3},{8,12},{9,13},{10,... | collective-permute-start | bytes 83144 | tf_op jit(solution)/shard_map/ppermute | solution.py:37
  126.3 6.1 %collective-permute-start.12 = (f32[6928]{0:T(1024)S(1)}, f32[6928]{0:T(1024)S(1)}, u32[]{:S(2)}, u32[]{:S(2)}) collective-permute-start(f32[6928]{0:T(1024)S(1)} %add.317), channel_id=1, source_target_pairs={{0,2},{1,3},{2,0},{3,1},{4,6},{5,7},{6,4},{7,5},{8,10},{9,11},{10,... | collective-permute-start | bytes 83144 | tf_op jit(solution)/shard_map/ppermute | solution.py:37
  132.4 4.6 %collective-permute-start.13 = (f32[6928]{0:T(1024)S(1)}, f32[6928]{0:T(1024)S(1)}, u32[]{:S(2)}, u32[]{:S(2)}) collective-permute-start(f32[6928]{0:T(1024)S(1)} %add.318), channel_id=1, source_target_pairs={{0,1},{1,0},{2,3},{3,2},{4,5},{5,4},{6,7},{7,6},{8,9},{9,8},{10,11... | collective-permute-start | bytes 83144 | tf_op jit(solution)/shard_map/ppermute | solution.py:37
  137.0 9.2 %collective-permute-start.14 = (f32[6928]{0:T(1024)S(1)}, f32[6928]{0:T(1024)S(1)}, u32[]{:S(2)}, u32[]{:S(2)}) collective-permute-start(f32[6928]{0:T(1024)S(1)} %add.319), channel_id=1, source_target_pairs={{0,256},{64,320},{128,384},{192,448},{256,0},{320,64},{384,128},{4... | collective-permute-start | bytes 83144 | tf_op jit(solution)/shard_map/ppermute | solution.py:37
  146.2 4.6 %collective-permute-start.15 = (f32[6928]{0:T(1024)S(1)}, f32[6928]{0:T(1024)S(1)}, u32[]{:S(2)}, u32[]{:S(2)}) collective-permute-start(f32[6928]{0:T(1024)S(1)} %add.320), channel_id=1, source_target_pairs={{0,128},{64,192},{128,0},{192,64},{256,384},{320,448},{384,256},{4... | collective-permute-start | bytes 83144 | tf_op jit(solution)/shard_map/ppermute | solution.py:37
  150.8 12.2 %collective-permute-start.16 = (f32[6928]{0:T(1024)S(1)}, f32[6928]{0:T(1024)S(1)}, u32[]{:S(2)}, u32[]{:S(2)}) collective-permute-start(f32[6928]{0:T(1024)S(1)} %add.321), channel_id=1, source_target_pairs={{0,64},{64,0},{128,192},{192,128},{256,320},{320,256},{384,448},{4... | collective-permute-start | bytes 83144 | tf_op jit(solution)/shard_map/ppermute | solution.py:37

commit v9 on v8

--- a/solution.py
+++ b/solution.py
@@ -17,6 +17,15 @@
     count = lax.axis_size(axis)
     pairs = [(source, (source + steps) % count) for source in range(count)]
     return lax.ppermute(value, axis, pairs)
+
+
+def neighbour_blocks(value, axis):
+    count = lax.axis_size(axis)
+    even = lax.axis_index(axis) % 2 == 0
+    near = lax.ppermute(value, axis, [(s, s ^ 1) for s in range(count)])
+    pairs = [(s, (s + 1) % count if s % 2 else (s - 1) % count) for s in range(count)]
+    across = lax.ppermute(value, axis, pairs)
+    return jnp.where(even, across, near), jnp.where(even, near, across)
 
 
 def halo_planes(value, axis):
@@ -90,24 +99,10 @@
     remain = effective % planes
     sign = jnp.where(flip_x, -1, 1)
     constant = jnp.where(flip_x, devices_x - 1 + coarse_steps, coarse_steps)
-    if planes == 2:
-        coarse, last_before, first_other = routed(
-            [block, block[:, :, 1:2], block[:, :, 0:1]],
-            "gx",
-            sign,
-            [constant, constant + 1, jnp.where(remain == 0, constant - 1, constant + 1)],
-        )
-        window = jnp.where(
-            remain == 0,
-            jnp.concatenate([last_before, coarse, first_other], axis=2),
-            jnp.concatenate([first_other, last_before, coarse], axis=2),
-        )
-    else:
-        (coarse,) = routed([block], "gx", sign, [constant])
-        before = shifted(coarse, "gx", 1)
-        after = shifted(coarse[:, :, 0:1], "gx", -1)
-        joined = jnp.concatenate([before, coarse, after], axis=2)
-        window = lax.dynamic_slice_in_dim(joined, planes - 1 - remain, planes + 2, axis=2)
+    (coarse,) = routed([block], "gx", sign, [constant])
+    before, after = neighbour_blocks(coarse, "gx")
+    joined = jnp.concatenate([before, coarse, after[:, :, 0:1]], axis=2)
+    window = lax.dynamic_slice_in_dim(joined, planes - 1 - remain, planes + 2, axis=2)
     padded = jax.vmap(augment_local)(window, offsets, flip_bits)
 
     taps = len(tap_offsets)

time: 165 us -> 164 us (level)
  waiting for transfers between devices: 45.6 us -> 35.5 us
  starting transfers between devices: 87.6 us -> 97.1 us
    ppermute x6, waiting for transfers between devices: 25.6 us -> 11.4 us  [routed(): arrived = lax.ppermute(jnp.concatenate(pieces, axis=2), axis, pairs)]
    ppermute x0 -> x2, starting transfers between devices: none -> 13.2 us  [the longest x1 11.3 us: neighbour_blocks(): across = lax.ppermute(value, axis, pairs)]
    ppermute x6, starting transfers between devices: 38.1 us -> 33.7 us  [routed(): arrived = lax.ppermute(jnp.concatenate(pieces, axis=2), axis, pairs)]
    ppermute x0 -> x2, waiting for transfers between devices: none -> 2.74 us  [the longest x1 1.51 us: neighbour_blocks(): near = lax.ppermute(value, axis, [(s, s ^ 1) for s in range(count)])]
  transfers between devices with their start and end apart: 17 -> 19, of which waited for: 12 -> 13; matrix products, arithmetic and copies ran while one was open for 4% -> 4% of each run, Pallas kernels for 0% -> 0%
where the time goes in v9:
time: 164 us; the launch traced here: 163 us
  starting transfers between devices  97.1 us (59%)
  waiting for transfers between devices  35.5 us (22%)
  between operations  10.8 us (7%)
  local copies, waits for them, and re-layouts  9.65 us (6%)
  matrix products  6.08 us (4%)
  other arithmetic  3.76 us (2%)
    ppermute x9, starting transfers between devices, butterfly_sum(): value = value + lax.ppermute(value, axis, pairs)  39.3 us
    ppermute x6, starting transfers between devices, routed(): arrived = lax.ppermute(jnp.concatenate(pieces, axis=2), axis, pairs)  33.7 us
    ppermute x9, waiting for transfers between devices, butterfly_sum(): value = value + lax.ppermute(value, axis, pairs)  21.4 us
    ppermute x6, waiting for transfers between devices, routed(): arrived = lax.ppermute(jnp.concatenate(pieces, axis=2), axis, pairs)  11.4 us
    ppermute x1, starting transfers between devices, neighbour_blocks(): across = lax.ppermute(value, axis, pairs)  11.3 us
    ppermute x1, starting transfers between devices, halo_planes(): across = lax.ppermute(jnp.where(even, first, last), axis, pairs)  8.93 us
    unnamed x14, local copies, waits for them, and re-layouts  4.43 us
    dot_general x3, matrix products, on_device(): jnp.einsum('boxyz,bcxyz->oc', grad_pre, window, preferred_element_type=jn...  4.19 us
  transfers between devices with their start and end apart: 19, of which 13 were waited for; matrix products, arithmetic and copies ran while one was open for 4% of the time, Pallas kernels for 0%

profile of v9, /device:TPU:1, one launch (start us, length us, event | category | flops | bytes accessed | tf_op | source)
XLA Modules:
  0.0 163.0 jit_solution(5446417173571378792)
XLA Ops:
  0.6 1.4 fusion.91
  3.7 3.9 %collective-permute-start = (bf16[1,16,2,8,256]{4,1,3,2,0:T(8,128)(2,1)S(1)}, bf16[1,16,2,8,256]{4,1,3,2,0:T(8,128)(2,1)S(1)}, u32[]{:S(2)}, u32[]{:S(2)}) collective-permute-start(bf16[1,16,2,8,256]{4,1,3,2,0:T(8,128)(2,1)S(1)} %reverse_select_fusion), channel_id=1, source_target_pairs={{0,1},{1,0},{2,3},{3,2},{4,5},{5,4},{6,7},{7,6},{8,9},{9,8},{10,11... | collective-permute-start | bytes 393224 | tf_op jit(solution)/shard_map/ppermute | solution.py:77
  11.1 4.4 %collective-permute-start.1 = (bf16[1,16,2,8,256]{4,1,3,2,0:T(8,128)(2,1)S(1)}, bf16[1,16,2,8,256]{4,1,3,2,0:T(8,128)(2,1)S(1)}, u32[]{:S(2)}, u32[]{:S(2)}) collective-permute-start(bf16[1,16,2,8,256]{4,1,3,2,0:T(8,128)(2,1)S(1)} %broadcast_select_fusion), channel_id=1, source_target_pairs={{0,2},{1,3},{2,0},{3,1},{4,6},{5,7},{6,4},{7,5},{8,10},{9,11},{10,... | collective-permute-start | bytes 393224 | tf_op jit(solution)/shard_map/ppermute | solution.py:77
  15.6 2.7 %collective-permute-done.1 = bf16[1,16,2,8,256]{4,1,3,2,0:T(8,128)(2,1)S(1)} collective-permute-done((bf16[1,16,2,8,256]{4,1,3,2,0:T(8,128)(2,1)S(1)}, bf16[1,16,2,8,256]{4,1,3,2,0:T(8,128)(2,1)S(1)}, u32[]{:S(2)}, u32[]{:S(2)}) %collective-permute-start.1) | collective-permute-done | bytes 131104 | tf_op jit(solution)/shard_map/ppermute | solution.py:77
  18.3 4.0 %collective-permute-start.2 = (bf16[1,16,2,8,256]{4,1,3,2,0:T(8,128)(2,1)S(1)}, bf16[1,16,2,8,256]{4,1,3,2,0:T(8,128)(2,1)S(1)}, u32[]{:S(2)}, u32[]{:S(2)}) collective-permute-start(bf16[1,16,2,8,256]{4,1,3,2,0:T(8,128)(2,1)S(1)} %broadcast_select_fusion.1), channel_id=1, source_target_pairs={{0,4},{1,5},{2,6},{3,7},{4,0},{5,1},{6,2},{7,3},{8,12},{9,13},{10,... | collective-permute-start | bytes 393224 | tf_op jit(solution)/shard_map/ppermute | solution.py:77
  22.4 2.6 %collective-permute-done.2 = bf16[1,16,2,8,256]{4,1,3,2,0:T(8,128)(2,1)S(1)} collective-permute-done((bf16[1,16,2,8,256]{4,1,3,2,0:T(8,128)(2,1)S(1)}, bf16[1,16,2,8,256]{4,1,3,2,0:T(8,128)(2,1)S(1)}, u32[]{:S(2)}, u32[]{:S(2)}) %collective-permute-start.2) | collective-permute-done | bytes 131104 | tf_op jit(solution)/shard_map/ppermute | solution.py:77
  25.0 5.5 %collective-permute-start.3 = (bf16[1,16,2,8,256]{4,1,3,2,0:T(8,128)(2,1)S(1)}, bf16[1,16,2,8,256]{4,1,3,2,0:T(8,128)(2,1)S(1)}, u32[]{:S(2)}, u32[]{:S(2)}) collective-permute-start(bf16[1,16,2,8,256]{4,1,3,2,0:T(8,128)(2,1)S(1)} %broadcast_select_fusion.2), channel_id=1, source_target_pairs={{0,8},{1,9},{2,10},{3,11},{4,12},{5,13},{6,14},{7,15},{8,0},{9,1},... | collective-permute-start | bytes 393224 | tf_op jit(solution)/shard_map/ppermute | solution.py:77
  30.6 3.7 %collective-permute-done.3 = bf16[1,16,2,8,256]{4,1,3,2,0:T(8,128)(2,1)S(1)} collective-permute-done((bf16[1,16,2,8,256]{4,1,3,2,0:T(8,128)(2,1)S(1)}, bf16[1,16,2,8,256]{4,1,3,2,0:T(8,128)(2,1)S(1)}, u32[]{:S(2)}, u32[]{:S(2)}) %collective-permute-start.3) | collective-permute-done | bytes 131104 | tf_op jit(solution)/shard_map/ppermute | solution.py:77
  34.3 8.4 %collective-permute-start.4 = (bf16[1,16,2,8,256]{4,1,3,2,0:T(8,128)(2,1)S(1)}, bf16[1,16,2,8,256]{4,1,3,2,0:T(8,128)(2,1)S(1)}, u32[]{:S(2)}, u32[]{:S(2)}) collective-permute-start(bf16[1,16,2,8,256]{4,1,3,2,0:T(8,128)(2,1)S(1)} %broadcast_select_fusion.3), channel_id=1, source_target_pairs={{0,16},{1,17},{2,18},{3,19},{4,20},{5,21},{6,22},{7,23},{8,24},{9,... | collective-permute-start | bytes 393224 | tf_op jit(solution)/shard_map/ppermute | solution.py:77
  42.8 2.4 %collective-permute-done.4 = bf16[1,16,2,8,256]{4,1,3,2,0:T(8,128)(2,1)S(1)} collective-permute-done((bf16[1,16,2,8,256]{4,1,3,2,0:T(8,128)(2,1)S(1)}, bf16[1,16,2,8,256]{4,1,3,2,0:T(8,128)(2,1)S(1)}, u32[]{:S(2)}, u32[]{:S(2)}) %collective-permute-start.4) | collective-permute-done | bytes 131104 | tf_op jit(solution)/shard_map/ppermute | solution.py:77
  45.2 7.5 %collective-permute-start.5 = (bf16[1,16,2,8,256]{4,1,3,2,0:T(8,128)(2,1)S(1)}, bf16[1,16,2,8,256]{4,1,3,2,0:T(8,128)(2,1)S(1)}, u32[]{:S(2)}, u32[]{:S(2)}) collective-permute-start(bf16[1,16,2,8,256]{4,1,3,2,0:T(8,128)(2,1)S(1)} %broadcast_select_fusion.4), channel_id=1, source_target_pairs={{0,32},{1,33},{2,34},{3,35},{4,36},{5,37},{6,38},{7,39},{8,40},{9,... | collective-permute-start | bytes 393224 | tf_op jit(solution)/shard_map/ppermute | solution.py:77
  59.3 11.3 %collective-permute-start.6 = (bf16[1,16,2,8,256]{4,1,3,2,0:T(8,128)(2,1)S(1)}, bf16[1,16,2,8,256]{4,1,3,2,0:T(8,128)(2,1)S(1)}, u32[]{:S(2)}, u32[]{:S(2)}) collective-permute-start(bf16[1,16,2,8,256]{4,1,3,2,0:T(8,128)(2,1)S(1)} %broadcast_select_fusion.5), channel_id=1, source_target_pairs={{0,63},{1,2},{2,1},{3,4},{4,3},{5,6},{6,5},{7,8},{8,7},{9,10},{10,... | collective-permute-start | bytes 393224 | tf_op jit(solution)/shard_map/ppermute | solution.py:27
  70.6 1.9 %collective-permute-start.7 = (bf16[1,16,2,8,256]{4,1,3,2,0:T(8,128)(2,1)S(1)}, bf16[1,16,2,8,256]{4,1,3,2,0:T(8,128)(2,1)S(1)}, u32[]{:S(2)}, u32[]{:S(2)}) collective-permute-start(bf16[1,16,2,8,256]{4,1,3,2,0:T(8,128)(2,1)S(1)} %broadcast_select_fusion.5), channel_id=1, source_target_pairs={{0,1},{1,0},{2,3},{3,2},{4,5},{5,4},{6,7},{7,6},{8,9},{9,8},{10,11... | collective-permute-start | bytes 393224 | tf_op jit(solution)/shard_map/ppermute | solution.py:25
  74.8 1.5 collective-permute-done.7
  83.9 1.4 fusion.68
  85.5 5.2 %collective-permute-start.10 = (f32[6928]{0:T(1024)S(1)}, f32[6928]{0:T(1024)S(1)}, u32[]{:S(2)}, u32[]{:S(2)}) collective-permute-start(f32[6928]{0:T(1024)S(1)} %pad_maximum_fusion.6), channel_id=1, source_target_pairs={{0,32},{1,33},{2,34},{3,35},{4,36},{5,37},{6,38},{7,39},{8,40},{9,... | collective-permute-start | bytes 83144 | tf_op jit(solution)/shard_map/ppermute | solution.py:46
  90.8 8.9 %collective-permute-start.8 = (bf16[1,16,1,8,256]{4,1,3,2,0:T(8,128)(2,1)S(1)}, bf16[1,16,1,8,256]{4,1,3,2,0:T(8,128)(2,1)S(1)}, u32[]{:S(2)}, u32[]{:S(2)}) collective-permute-start(bf16[1,16,1,8,256]{4,1,3,2,0:T(8,128)(2,1)S(1)} %get-tuple-element.76), channel_id=1, source_target_pairs={{0,63},{1,2},{2,1},{3,4},{4,3},{5,6},{6,5},{7,8},{8,7},{9,10},{10,... | collective-permute-start | bytes 196616 | tf_op jit(solution)/shard_map/ppermute | solution.py:37
  99.7 1.9 %collective-permute-start.9 = (bf16[1,16,1,8,256]{4,1,3,2,0:T(8,128)(2,1)S(1)}, bf16[1,16,1,8,256]{4,1,3,2,0:T(8,128)(2,1)S(1)}, u32[]{:S(2)}, u32[]{:S(2)}) collective-permute-start(bf16[1,16,1,8,256]{4,1,3,2,0:T(8,128)(2,1)S(1)} %get-tuple-element.77), channel_id=1, source_target_pairs={{0,1},{1,0},{2,3},{3,2},{4,5},{5,4},{6,7},{7,6},{8,9},{9,8},{10,11... | collective-permute-start | bytes 196616 | tf_op jit(solution)/shard_map/ppermute | solution.py:35
  101.6 1.9 %collective-permute-start.11 = (f32[6928]{0:T(1024)S(1)}, f32[6928]{0:T(1024)S(1)}, u32[]{:S(2)}, u32[]{:S(2)}) collective-permute-start(f32[6928]{0:T(1024)S(1)} %fusion.99), channel_id=1, source_target_pairs={{0,16},{1,17},{2,18},{3,19},{4,20},{5,21},{6,22},{7,23},{8,24},{9,... | collective-permute-start | bytes 83144 | tf_op jit(solution)/shard_map/ppermute | solution.py:46
  104.3 5.9 %collective-permute-done.11 = f32[6928]{0:T(1024)S(1)} collective-permute-done((f32[6928]{0:T(1024)S(1)}, f32[6928]{0:T(1024)S(1)}, u32[]{:S(2)}, u32[]{:S(2)}) %collective-permute-start.11) | collective-permute-done | bytes 27744 | tf_op jit(solution)/shard_map/ppermute | solution.py:46
  110.2 1.9 %collective-permute-start.12 = (f32[6928]{0:T(1024)S(1)}, f32[6928]{0:T(1024)S(1)}, u32[]{:S(2)}, u32[]{:S(2)}) collective-permute-start(f32[6928]{0:T(1024)S(1)} %add.195), channel_id=1, source_target_pairs={{0,8},{1,9},{2,10},{3,11},{4,12},{5,13},{6,14},{7,15},{8,0},{9,1},... | collective-permute-start | bytes 83144 | tf_op jit(solution)/shard_map/ppermute | solution.py:46
  113.6 2.1 %collective-permute-done.12 = f32[6928]{0:T(1024)S(1)} collective-permute-done((f32[6928]{0:T(1024)S(1)}, f32[6928]{0:T(1024)S(1)}, u32[]{:S(2)}, u32[]{:S(2)}) %collective-permute-start.12) | collective-permute-done | bytes 27744 | tf_op jit(solution)/shard_map/ppermute | solution.py:46
  115.7 1.9 %collective-permute-start.13 = (f32[6928]{0:T(1024)S(1)}, f32[6928]{0:T(1024)S(1)}, u32[]{:S(2)}, u32[]{:S(2)}) collective-permute-start(f32[6928]{0:T(1024)S(1)} %add.196), channel_id=1, source_target_pairs={{0,4},{1,5},{2,6},{3,7},{4,0},{5,1},{6,2},{7,3},{8,12},{9,13},{10,... | collective-permute-start | bytes 83144 | tf_op jit(solution)/shard_map/ppermute | solution.py:46
  117.7 2.6 %collective-permute-done.13 = f32[6928]{0:T(1024)S(1)} collective-permute-done((f32[6928]{0:T(1024)S(1)}, f32[6928]{0:T(1024)S(1)}, u32[]{:S(2)}, u32[]{:S(2)}) %collective-permute-start.13) | collective-permute-done | bytes 27744 | tf_op jit(solution)/shard_map/ppermute | solution.py:46
  120.3 1.9 %collective-permute-start.14 = (f32[6928]{0:T(1024)S(1)}, f32[6928]{0:T(1024)S(1)}, u32[]{:S(2)}, u32[]{:S(2)}) collective-permute-start(f32[6928]{0:T(1024)S(1)} %add.197), channel_id=1, source_target_pairs={{0,2},{1,3},{2,0},{3,1},{4,6},{5,7},{6,4},{7,5},{8,10},{9,11},{10,... | collective-permute-start | bytes 83144 | tf_op jit(solution)/shard_map/ppermute | solution.py:46
  122.2 4.2 %collective-permute-done.14 = f32[6928]{0:T(1024)S(1)} collective-permute-done((f32[6928]{0:T(1024)S(1)}, f32[6928]{0:T(1024)S(1)}, u32[]{:S(2)}, u32[]{:S(2)}) %collective-permute-start.14) | collective-permute-done | bytes 27744 | tf_op jit(solution)/shard_map/ppermute | solution.py:46
  126.4 3.9 %collective-permute-start.15 = (f32[6928]{0:T(1024)S(1)}, f32[6928]{0:T(1024)S(1)}, u32[]{:S(2)}, u32[]{:S(2)}) collective-permute-start(f32[6928]{0:T(1024)S(1)} %add.198), channel_id=1, source_target_pairs={{0,1},{1,0},{2,3},{3,2},{4,5},{5,4},{6,7},{7,6},{8,9},{9,8},{10,11... | collective-permute-start | bytes 83144 | tf_op jit(solution)/shard_map/ppermute | solution.py:46
  131.6 1.9 %collective-permute-start.16 = (f32[6928]{0:T(1024)S(1)}, f32[6928]{0:T(1024)S(1)}, u32[]{:S(2)}, u32[]{:S(2)}) collective-permute-start(f32[6928]{0:T(1024)S(1)} %add.199), channel_id=1, source_target_pairs={{0,256},{64,320},{128,384},{192,448},{256,0},{320,64},{384,128},{4... | collective-permute-start | bytes 83144 | tf_op jit(solution)/shard_map/ppermute | solution.py:46
  133.8 3.3 %collective-permute-done.16 = f32[6928]{0:T(1024)S(1)} collective-permute-done((f32[6928]{0:T(1024)S(1)}, f32[6928]{0:T(1024)S(1)}, u32[]{:S(2)}, u32[]{:S(2)}) %collective-permute-start.16) | collective-permute-done | bytes 27744 | tf_op jit(solution)/shard_map/ppermute | solution.py:46
  137.1 1.9 %collective-permute-start.17 = (f32[6928]{0:T(1024)S(1)}, f32[6928]{0:T(1024)S(1)}, u32[]{:S(2)}, u32[]{:S(2)}) collective-permute-start(f32[6928]{0:T(1024)S(1)} %add.200), channel_id=1, source_target_pairs={{0,128},{64,192},{128,0},{192,64},{256,384},{320,448},{384,256},{4... | collective-permute-start | bytes 83144 | tf_op jit(solution)/shard_map/ppermute | solution.py:46
  139.3 2.4 %collective-permute-done.17 = f32[6928]{0:T(1024)S(1)} collective-permute-done((f32[6928]{0:T(1024)S(1)}, f32[6928]{0:T(1024)S(1)}, u32[]{:S(2)}, u32[]{:S(2)}) %collective-permute-start.17) | collective-permute-done | bytes 27744 | tf_op jit(solution)/shard_map/ppermute | solution.py:46
  141.7 18.7 %collective-permute-start.18 = (f32[6928]{0:T(1024)S(1)}, f32[6928]{0:T(1024)S(1)}, u32[]{:S(2)}, u32[]{:S(2)}) collective-permute-start(f32[6928]{0:T(1024)S(1)} %add.201), channel_id=1, source_target_pairs={{0,64},{64,0},{128,192},{192,128},{256,320},{320,256},{384,448},{4... | collective-permute-start | bytes 83144 | tf_op jit(solution)/shard_map/ppermute | solution.py:46
  (101 shorter events, 19.0 us)
Async XLA Ops:
  0.6 71.9 %copy-start = (bf16[27,16,16]{0,2,1:T(8,128)(2,1)S(1)}, bf16[27,16,16]{0,2,1:T(8,128)(2,1)}, u32[]{:S(2)}) copy-start(bf16[27,16,16]{0,2,1:T(8,128)(2,1)} %param.13) | copy-start | bytes 41476
  3.7 7.3 %collective-permute-start = (bf16[1,16,2,8,256]{4,1,3,2,0:T(8,128)(2,1)S(1)}, bf16[1,16,2,8,256]{4,1,3,2,0:T(8,128)(2,1)S(1)}, u32[]{:S(2)}, u32[]{:S(2)}) collective-permute-start(bf16[1,16,2,8,256]{4,1,3,2,0:T(8,128)(2,1)S(1)} %reverse_select_fusion), channel_id=1, source_target_pairs={{0,1},{1,0},{2,3},{3,2},{4,5},{5,4},{6,7},{7,6},{8,9},{9,8},{10,11... | collective-permute-start | bytes 393224 | tf_op jit(solution)/shard_map/ppermute | solution.py:77
  11.1 7.2 %collective-permute-start.1 = (bf16[1,16,2,8,256]{4,1,3,2,0:T(8,128)(2,1)S(1)}, bf16[1,16,2,8,256]{4,1,3,2,0:T(8,128)(2,1)S(1)}, u32[]{:S(2)}, u32[]{:S(2)}) collective-permute-start(bf16[1,16,2,8,256]{4,1,3,2,0:T(8,128)(2,1)S(1)} %broadcast_select_fusion), channel_id=1, source_target_pairs={{0,2},{1,3},{2,0},{3,1},{4,6},{5,7},{6,4},{7,5},{8,10},{9,11},{10,... | collective-permute-start | bytes 393224 | tf_op jit(solution)/shard_map/ppermute | solution.py:77
  18.3 6.6 %collective-permute-start.2 = (bf16[1,16,2,8,256]{4,1,3,2,0:T(8,128)(2,1)S(1)}, bf16[1,16,2,8,256]{4,1,3,2,0:T(8,128)(2,1)S(1)}, u32[]{:S(2)}, u32[]{:S(2)}) collective-permute-start(bf16[1,16,2,8,256]{4,1,3,2,0:T(8,128)(2,1)S(1)} %broadcast_select_fusion.1), channel_id=1, source_target_pairs={{0,4},{1,5},{2,6},{3,7},{4,0},{5,1},{6,2},{7,3},{8,12},{9,13},{10,... | collective-permute-start | bytes 393224 | tf_op jit(solution)/shard_map/ppermute | solution.py:77
  25.0 9.3 %collective-permute-start.3 = (bf16[1,16,2,8,256]{4,1,3,2,0:T(8,128)(2,1)S(1)}, bf16[1,16,2,8,256]{4,1,3,2,0:T(8,128)(2,1)S(1)}, u32[]{:S(2)}, u32[]{:S(2)}) collective-permute-start(bf16[1,16,2,8,256]{4,1,3,2,0:T(8,128)(2,1)S(1)} %broadcast_select_fusion.2), channel_id=1, source_target_pairs={{0,8},{1,9},{2,10},{3,11},{4,12},{5,13},{6,14},{7,15},{8,0},{9,1},... | collective-permute-start | bytes 393224 | tf_op jit(solution)/shard_map/ppermute | solution.py:77
  34.3 10.9 %collective-permute-start.4 = (bf16[1,16,2,8,256]{4,1,3,2,0:T(8,128)(2,1)S(1)}, bf16[1,16,2,8,256]{4,1,3,2,0:T(8,128)(2,1)S(1)}, u32[]{:S(2)}, u32[]{:S(2)}) collective-permute-start(bf16[1,16,2,8,256]{4,1,3,2,0:T(8,128)(2,1)S(1)} %broadcast_select_fusion.3), channel_id=1, source_target_pairs={{0,16},{1,17},{2,18},{3,19},{4,20},{5,21},{6,22},{7,23},{8,24},{9,... | collective-permute-start | bytes 393224 | tf_op jit(solution)/shard_map/ppermute | solution.py:77
  45.2 14.1 %collective-permute-start.5 = (bf16[1,16,2,8,256]{4,1,3,2,0:T(8,128)(2,1)S(1)}, bf16[1,16,2,8,256]{4,1,3,2,0:T(8,128)(2,1)S(1)}, u32[]{:S(2)}, u32[]{:S(2)}) collective-permute-start(bf16[1,16,2,8,256]{4,1,3,2,0:T(8,128)(2,1)S(1)} %broadcast_select_fusion.4), channel_id=1, source_target_pairs={{0,32},{1,33},{2,34},{3,35},{4,36},{5,37},{6,38},{7,39},{8,40},{9,... | collective-permute-start | bytes 393224 | tf_op jit(solution)/shard_map/ppermute | solution.py:77
  59.3 15.5 %collective-permute-start.6 = (bf16[1,16,2,8,256]{4,1,3,2,0:T(8,128)(2,1)S(1)}, bf16[1,16,2,8,256]{4,1,3,2,0:T(8,128)(2,1)S(1)}, u32[]{:S(2)}, u32[]{:S(2)}) collective-permute-start(bf16[1,16,2,8,256]{4,1,3,2,0:T(8,128)(2,1)S(1)} %broadcast_select_fusion.5), channel_id=1, source_target_pairs={{0,63},{1,2},{2,1},{3,4},{4,3},{5,6},{6,5},{7,8},{8,7},{9,10},{10,... | collective-permute-start | bytes 393224 | tf_op jit(solution)/shard_map/ppermute | solution.py:27
  70.6 5.7 %collective-permute-start.7 = (bf16[1,16,2,8,256]{4,1,3,2,0:T(8,128)(2,1)S(1)}, bf16[1,16,2,8,256]{4,1,3,2,0:T(8,128)(2,1)S(1)}, u32[]{:S(2)}, u32[]{:S(2)}) collective-permute-start(bf16[1,16,2,8,256]{4,1,3,2,0:T(8,128)(2,1)S(1)} %broadcast_select_fusion.5), channel_id=1, source_target_pairs={{0,1},{1,0},{2,3},{3,2},{4,5},{5,4},{6,7},{7,6},{8,9},{9,8},{10,11... | collective-permute-start | bytes 393224 | tf_op jit(solution)/shard_map/ppermute | solution.py:25
  79.2 0.7 copy-start.1
  79.8 0.9 copy-start.2
  85.5 16.1 %collective-permute-start.10 = (f32[6928]{0:T(1024)S(1)}, f32[6928]{0:T(1024)S(1)}, u32[]{:S(2)}, u32[]{:S(2)}) collective-permute-start(f32[6928]{0:T(1024)S(1)} %pad_maximum_fusion.6), channel_id=1, source_target_pairs={{0,32},{1,33},{2,34},{3,35},{4,36},{5,37},{6,38},{7,39},{8,40},{9,... | collective-permute-start | bytes 83144 | tf_op jit(solution)/shard_map/ppermute | solution.py:46
  90.8 21.3 %collective-permute-start.8 = (bf16[1,16,1,8,256]{4,1,3,2,0:T(8,128)(2,1)S(1)}, bf16[1,16,1,8,256]{4,1,3,2,0:T(8,128)(2,1)S(1)}, u32[]{:S(2)}, u32[]{:S(2)}) collective-permute-start(bf16[1,16,1,8,256]{4,1,3,2,0:T(8,128)(2,1)S(1)} %get-tuple-element.76), channel_id=1, source_target_pairs={{0,63},{1,2},{2,1},{3,4},{4,3},{5,6},{6,5},{7,8},{8,7},{9,10},{10,... | collective-permute-start | bytes 196616 | tf_op jit(solution)/shard_map/ppermute | solution.py:37
  99.7 12.4 %collective-permute-start.9 = (bf16[1,16,1,8,256]{4,1,3,2,0:T(8,128)(2,1)S(1)}, bf16[1,16,1,8,256]{4,1,3,2,0:T(8,128)(2,1)S(1)}, u32[]{:S(2)}, u32[]{:S(2)}) collective-permute-start(bf16[1,16,1,8,256]{4,1,3,2,0:T(8,128)(2,1)S(1)} %get-tuple-element.77), channel_id=1, source_target_pairs={{0,1},{1,0},{2,3},{3,2},{4,5},{5,4},{6,7},{7,6},{8,9},{9,8},{10,11... | collective-permute-start | bytes 196616 | tf_op jit(solution)/shard_map/ppermute | solution.py:35
  101.6 8.5 %collective-permute-start.11 = (f32[6928]{0:T(1024)S(1)}, f32[6928]{0:T(1024)S(1)}, u32[]{:S(2)}, u32[]{:S(2)}) collective-permute-start(f32[6928]{0:T(1024)S(1)} %fusion.99), channel_id=1, source_target_pairs={{0,16},{1,17},{2,18},{3,19},{4,20},{5,21},{6,22},{7,23},{8,24},{9,... | collective-permute-start | bytes 83144 | tf_op jit(solution)/shard_map/ppermute | solution.py:46
  110.2 5.5 %collective-permute-start.12 = (f32[6928]{0:T(1024)S(1)}, f32[6928]{0:T(1024)S(1)}, u32[]{:S(2)}, u32[]{:S(2)}) collective-permute-start(f32[6928]{0:T(1024)S(1)} %add.195), channel_id=1, source_target_pairs={{0,8},{1,9},{2,10},{3,11},{4,12},{5,13},{6,14},{7,15},{8,0},{9,1},... | collective-permute-start | bytes 83144 | tf_op jit(solution)/shard_map/ppermute | solution.py:46
  115.7 4.6 %collective-permute-start.13 = (f32[6928]{0:T(1024)S(1)}, f32[6928]{0:T(1024)S(1)}, u32[]{:S(2)}, u32[]{:S(2)}) collective-permute-start(f32[6928]{0:T(1024)S(1)} %add.196), channel_id=1, source_target_pairs={{0,4},{1,5},{2,6},{3,7},{4,0},{5,1},{6,2},{7,3},{8,12},{9,13},{10,... | collective-permute-start | bytes 83144 | tf_op jit(solution)/shard_map/ppermute | solution.py:46
  120.3 6.1 %collective-permute-start.14 = (f32[6928]{0:T(1024)S(1)}, f32[6928]{0:T(1024)S(1)}, u32[]{:S(2)}, u32[]{:S(2)}) collective-permute-start(f32[6928]{0:T(1024)S(1)} %add.197), channel_id=1, source_target_pairs={{0,2},{1,3},{2,0},{3,1},{4,6},{5,7},{6,4},{7,5},{8,10},{9,11},{10,... | collective-permute-start | bytes 83144 | tf_op jit(solution)/shard_map/ppermute | solution.py:46
  126.4 5.2 %collective-permute-start.15 = (f32[6928]{0:T(1024)S(1)}, f32[6928]{0:T(1024)S(1)}, u32[]{:S(2)}, u32[]{:S(2)}) collective-permute-start(f32[6928]{0:T(1024)S(1)} %add.198), channel_id=1, source_target_pairs={{0,1},{1,0},{2,3},{3,2},{4,5},{5,4},{6,7},{7,6},{8,9},{9,8},{10,11... | collective-permute-start | bytes 83144 | tf_op jit(solution)/shard_map/ppermute | solution.py:46
  131.6 5.5 %collective-permute-start.16 = (f32[6928]{0:T(1024)S(1)}, f32[6928]{0:T(1024)S(1)}, u32[]{:S(2)}, u32[]{:S(2)}) collective-permute-start(f32[6928]{0:T(1024)S(1)} %add.199), channel_id=1, source_target_pairs={{0,256},{64,320},{128,384},{192,448},{256,0},{320,64},{384,128},{4... | collective-permute-start | bytes 83144 | tf_op jit(solution)/shard_map/ppermute | solution.py:46
  137.1 4.6 %collective-permute-start.17 = (f32[6928]{0:T(1024)S(1)}, f32[6928]{0:T(1024)S(1)}, u32[]{:S(2)}, u32[]{:S(2)}) collective-permute-start(f32[6928]{0:T(1024)S(1)} %add.200), channel_id=1, source_target_pairs={{0,128},{64,192},{128,0},{192,64},{256,384},{320,448},{384,256},{4... | collective-permute-start | bytes 83144 | tf_op jit(solution)/shard_map/ppermute | solution.py:46
  141.7 19.8 %collective-permute-start.18 = (f32[6928]{0:T(1024)S(1)}, f32[6928]{0:T(1024)S(1)}, u32[]{:S(2)}, u32[]{:S(2)}) collective-permute-start(f32[6928]{0:T(1024)S(1)} %add.201), channel_id=1, source_target_pairs={{0,64},{64,0},{128,192},{192,128},{256,320},{320,256},{384,448},{4... | collective-permute-start | bytes 83144 | tf_op jit(solution)/shard_map/ppermute | solution.py:46

commit v10 on v9

--- a/solution.py
+++ b/solution.py
@@ -93,13 +93,13 @@
     devices_x = lax.axis_size("gx")
     length_x = planes * devices_x
     flip_x = flip_bits[0, 0] == 1
-    block = jnp.where(flip_x, jnp.flip(features, 2), features)
     effective = jnp.where(flip_x, jnp.mod(-offsets[0, 0], length_x), offsets[0, 0])
     coarse_steps = effective // planes
     remain = effective % planes
     sign = jnp.where(flip_x, -1, 1)
     constant = jnp.where(flip_x, devices_x - 1 + coarse_steps, coarse_steps)
-    (coarse,) = routed([block], "gx", sign, [constant])
+    (raw,) = routed([features], "gx", sign, [constant])
+    coarse = jnp.where(flip_x, jnp.flip(raw, 2), raw)
     before, after = neighbour_blocks(coarse, "gx")
     joined = jnp.concatenate([before, coarse, after[:, :, 0:1]], axis=2)
     window = lax.dynamic_slice_in_dim(joined, planes - 1 - remain, planes + 2, axis=2)

time: 164 us -> 164 us (level)
  starting transfers between devices: 97.1 us -> 95.3 us
    ppermute x9, starting transfers between devices: 39.3 us -> 37.4 us  [butterfly_sum(): value = value + lax.ppermute(value, axis, pairs)]
  transfers between devices with their start and end apart: 19 -> 19, of which waited for: 13 -> 13; matrix products, arithmetic and copies ran while one was open for 4% -> 5% of each run, Pallas kernels for 0% -> 0%
where the time goes in v10:
time: 164 us; the launch traced here: 162 us
  starting transfers between devices  95.3 us (58%)
  waiting for transfers between devices  35.5 us (22%)
  between operations  10.8 us (7%)
  local copies, waits for them, and re-layouts  9.66 us (6%)
  matrix products  6.08 us (4%)
  other arithmetic  4.67 us (3%)
    ppermute x9, starting transfers between devices, butterfly_sum(): value = value + lax.ppermute(value, axis, pairs)  37.4 us
    ppermute x6, starting transfers between devices, routed(): arrived = lax.ppermute(jnp.concatenate(pieces, axis=2), axis, pairs)  34 us
    ppermute x9, waiting for transfers between devices, butterfly_sum(): value = value + lax.ppermute(value, axis, pairs)  21.6 us
    ppermute x6, waiting for transfers between devices, routed(): arrived = lax.ppermute(jnp.concatenate(pieces, axis=2), axis, pairs)  11.2 us
    ppermute x1, starting transfers between devices, neighbour_blocks(): across = lax.ppermute(value, axis, pairs)  10.8 us
    ppermute x1, starting transfers between devices, halo_planes(): across = lax.ppermute(jnp.where(even, first, last), axis, pairs)  9.3 us
    unnamed x14, local copies, waits for them, and re-layouts  4.46 us
    dot_general x3, matrix products, on_device(): jnp.einsum('boxyz,bcxyz->oc', grad_pre, window, preferred_element_type=jn...  4.19 us
  transfers between devices with their start and end apart: 19, of which 13 were waited for; matrix products, arithmetic and copies ran while one was open for 5% of the time, Pallas kernels for 0%

profile of v10, /device:TPU:1, one launch (start us, length us, event | category | flops | bytes accessed | tf_op | source)
XLA Modules:
  0.0 162.1 jit_solution(17473121999888865675)
XLA Ops:
  1.6 3.9 %collective-permute-start = (bf16[1,16,2,8,256]{4,1,3,2,0:T(8,128)(2,1)S(1)}, bf16[1,16,2,8,256]{4,1,3,2,0:T(8,128)(2,1)S(1)}, u32[]{:S(2)}, u32[]{:S(2)}) collective-permute-start(bf16[1,16,2,8,256]{4,1,3,2,0:T(8,128)(2,1)S(1)} %copy.24), channel_id=1, source_target_pairs={{0,1},{1,0},{2,3},{3,2},{4,5},{5,4},{6,7},{7,6},{8,9},{9,8},{10,11... | collective-permute-start | bytes 393224 | tf_op jit(solution)/shard_map/ppermute | solution.py:77
  11.9 4.4 %collective-permute-start.1 = (bf16[1,16,2,8,256]{4,1,3,2,0:T(8,128)(2,1)S(1)}, bf16[1,16,2,8,256]{4,1,3,2,0:T(8,128)(2,1)S(1)}, u32[]{:S(2)}, u32[]{:S(2)}) collective-permute-start(bf16[1,16,2,8,256]{4,1,3,2,0:T(8,128)(2,1)S(1)} %broadcast_select_fusion), channel_id=1, source_target_pairs={{0,2},{1,3},{2,0},{3,1},{4,6},{5,7},{6,4},{7,5},{8,10},{9,11},{10,... | collective-permute-start | bytes 393224 | tf_op jit(solution)/shard_map/ppermute | solution.py:77
  16.3 2.8 %collective-permute-done.1 = bf16[1,16,2,8,256]{4,1,3,2,0:T(8,128)(2,1)S(1)} collective-permute-done((bf16[1,16,2,8,256]{4,1,3,2,0:T(8,128)(2,1)S(1)}, bf16[1,16,2,8,256]{4,1,3,2,0:T(8,128)(2,1)S(1)}, u32[]{:S(2)}, u32[]{:S(2)}) %collective-permute-start.1) | collective-permute-done | bytes 131104 | tf_op jit(solution)/shard_map/ppermute | solution.py:77
  19.1 4.0 %collective-permute-start.2 = (bf16[1,16,2,8,256]{4,1,3,2,0:T(8,128)(2,1)S(1)}, bf16[1,16,2,8,256]{4,1,3,2,0:T(8,128)(2,1)S(1)}, u32[]{:S(2)}, u32[]{:S(2)}) collective-permute-start(bf16[1,16,2,8,256]{4,1,3,2,0:T(8,128)(2,1)S(1)} %broadcast_select_fusion.1), channel_id=1, source_target_pairs={{0,4},{1,5},{2,6},{3,7},{4,0},{5,1},{6,2},{7,3},{8,12},{9,13},{10,... | collective-permute-start | bytes 393224 | tf_op jit(solution)/shard_map/ppermute | solution.py:77
  23.2 2.3 %collective-permute-done.2 = bf16[1,16,2,8,256]{4,1,3,2,0:T(8,128)(2,1)S(1)} collective-permute-done((bf16[1,16,2,8,256]{4,1,3,2,0:T(8,128)(2,1)S(1)}, bf16[1,16,2,8,256]{4,1,3,2,0:T(8,128)(2,1)S(1)}, u32[]{:S(2)}, u32[]{:S(2)}) %collective-permute-start.2) | collective-permute-done | bytes 131104 | tf_op jit(solution)/shard_map/ppermute | solution.py:77
  25.5 5.8 %collective-permute-start.3 = (bf16[1,16,2,8,256]{4,1,3,2,0:T(8,128)(2,1)S(1)}, bf16[1,16,2,8,256]{4,1,3,2,0:T(8,128)(2,1)S(1)}, u32[]{:S(2)}, u32[]{:S(2)}) collective-permute-start(bf16[1,16,2,8,256]{4,1,3,2,0:T(8,128)(2,1)S(1)} %broadcast_select_fusion.2), channel_id=1, source_target_pairs={{0,8},{1,9},{2,10},{3,11},{4,12},{5,13},{6,14},{7,15},{8,0},{9,1},... | collective-permute-start | bytes 393224 | tf_op jit(solution)/shard_map/ppermute | solution.py:77
  31.4 3.7 %collective-permute-done.3 = bf16[1,16,2,8,256]{4,1,3,2,0:T(8,128)(2,1)S(1)} collective-permute-done((bf16[1,16,2,8,256]{4,1,3,2,0:T(8,128)(2,1)S(1)}, bf16[1,16,2,8,256]{4,1,3,2,0:T(8,128)(2,1)S(1)}, u32[]{:S(2)}, u32[]{:S(2)}) %collective-permute-start.3) | collective-permute-done | bytes 131104 | tf_op jit(solution)/shard_map/ppermute | solution.py:77
  35.1 8.4 %collective-permute-start.4 = (bf16[1,16,2,8,256]{4,1,3,2,0:T(8,128)(2,1)S(1)}, bf16[1,16,2,8,256]{4,1,3,2,0:T(8,128)(2,1)S(1)}, u32[]{:S(2)}, u32[]{:S(2)}) collective-permute-start(bf16[1,16,2,8,256]{4,1,3,2,0:T(8,128)(2,1)S(1)} %broadcast_select_fusion.3), channel_id=1, source_target_pairs={{0,16},{1,17},{2,18},{3,19},{4,20},{5,21},{6,22},{7,23},{8,24},{9,... | collective-permute-start | bytes 393224 | tf_op jit(solution)/shard_map/ppermute | solution.py:77
  43.6 2.5 %collective-permute-done.4 = bf16[1,16,2,8,256]{4,1,3,2,0:T(8,128)(2,1)S(1)} collective-permute-done((bf16[1,16,2,8,256]{4,1,3,2,0:T(8,128)(2,1)S(1)}, bf16[1,16,2,8,256]{4,1,3,2,0:T(8,128)(2,1)S(1)}, u32[]{:S(2)}, u32[]{:S(2)}) %collective-permute-start.4) | collective-permute-done | bytes 131104 | tf_op jit(solution)/shard_map/ppermute | solution.py:77
  46.1 7.5 %collective-permute-start.5 = (bf16[1,16,2,8,256]{4,1,3,2,0:T(8,128)(2,1)S(1)}, bf16[1,16,2,8,256]{4,1,3,2,0:T(8,128)(2,1)S(1)}, u32[]{:S(2)}, u32[]{:S(2)}) collective-permute-start(bf16[1,16,2,8,256]{4,1,3,2,0:T(8,128)(2,1)S(1)} %broadcast_select_fusion.4), channel_id=1, source_target_pairs={{0,32},{1,33},{2,34},{3,35},{4,36},{5,37},{6,38},{7,39},{8,40},{9,... | collective-permute-start | bytes 393224 | tf_op jit(solution)/shard_map/ppermute | solution.py:77
  60.2 10.8 %collective-permute-start.6 = (bf16[1,16,2,8,256]{4,1,3,2,0:T(8,128)(2,1)S(1)}, bf16[1,16,2,8,256]{4,1,3,2,0:T(8,128)(2,1)S(1)}, u32[]{:S(2)}, u32[]{:S(2)}) collective-permute-start(bf16[1,16,2,8,256]{4,1,3,2,0:T(8,128)(2,1)S(1)} %reverse_select_fusion), channel_id=1, source_target_pairs={{0,63},{1,2},{2,1},{3,4},{4,3},{5,6},{6,5},{7,8},{8,7},{9,10},{10,... | collective-permute-start | bytes 393224 | tf_op jit(solution)/shard_map/ppermute | solution.py:27
  71.0 1.9 %collective-permute-start.7 = (bf16[1,16,2,8,256]{4,1,3,2,0:T(8,128)(2,1)S(1)}, bf16[1,16,2,8,256]{4,1,3,2,0:T(8,128)(2,1)S(1)}, u32[]{:S(2)}, u32[]{:S(2)}) collective-permute-start(bf16[1,16,2,8,256]{4,1,3,2,0:T(8,128)(2,1)S(1)} %reverse_select_fusion), channel_id=1, source_target_pairs={{0,1},{1,0},{2,3},{3,2},{4,5},{5,4},{6,7},{7,6},{8,9},{9,8},{10,11... | collective-permute-start | bytes 393224 | tf_op jit(solution)/shard_map/ppermute | solution.py:25
  74.0 2.1 %collective-permute-done.6 = bf16[1,16,2,8,256]{4,1,3,2,0:T(8,128)(2,1)S(1)} collective-permute-done((bf16[1,16,2,8,256]{4,1,3,2,0:T(8,128)(2,1)S(1)}, bf16[1,16,2,8,256]{4,1,3,2,0:T(8,128)(2,1)S(1)}, u32[]{:S(2)}, u32[]{:S(2)}) %collective-permute-start.6) | collective-permute-done | bytes 131104 | tf_op jit(solution)/shard_map/ppermute | solution.py:27
  83.0 1.4 fusion.70
  84.4 1.4 fusion.68
  86.0 4.8 %collective-permute-start.10 = (f32[6928]{0:T(1024)S(1)}, f32[6928]{0:T(1024)S(1)}, u32[]{:S(2)}, u32[]{:S(2)}) collective-permute-start(f32[6928]{0:T(1024)S(1)} %pad_maximum_fusion.6), channel_id=1, source_target_pairs={{0,32},{1,33},{2,34},{3,35},{4,36},{5,37},{6,38},{7,39},{8,40},{9,... | collective-permute-start | bytes 83144 | tf_op jit(solution)/shard_map/ppermute | solution.py:46
  90.8 9.3 %collective-permute-start.8 = (bf16[1,16,1,8,256]{4,1,3,2,0:T(8,128)(2,1)S(1)}, bf16[1,16,1,8,256]{4,1,3,2,0:T(8,128)(2,1)S(1)}, u32[]{:S(2)}, u32[]{:S(2)}) collective-permute-start(bf16[1,16,1,8,256]{4,1,3,2,0:T(8,128)(2,1)S(1)} %get-tuple-element.76), channel_id=1, source_target_pairs={{0,63},{1,2},{2,1},{3,4},{4,3},{5,6},{6,5},{7,8},{8,7},{9,10},{10,... | collective-permute-start | bytes 196616 | tf_op jit(solution)/shard_map/ppermute | solution.py:37
  100.2 1.9 %collective-permute-start.9 = (bf16[1,16,1,8,256]{4,1,3,2,0:T(8,128)(2,1)S(1)}, bf16[1,16,1,8,256]{4,1,3,2,0:T(8,128)(2,1)S(1)}, u32[]{:S(2)}, u32[]{:S(2)}) collective-permute-start(bf16[1,16,1,8,256]{4,1,3,2,0:T(8,128)(2,1)S(1)} %get-tuple-element.77), channel_id=1, source_target_pairs={{0,1},{1,0},{2,3},{3,2},{4,5},{5,4},{6,7},{7,6},{8,9},{9,8},{10,11... | collective-permute-start | bytes 196616 | tf_op jit(solution)/shard_map/ppermute | solution.py:35
  102.1 1.9 %collective-permute-start.11 = (f32[6928]{0:T(1024)S(1)}, f32[6928]{0:T(1024)S(1)}, u32[]{:S(2)}, u32[]{:S(2)}) collective-permute-start(f32[6928]{0:T(1024)S(1)} %fusion.99), channel_id=1, source_target_pairs={{0,16},{1,17},{2,18},{3,19},{4,20},{5,21},{6,22},{7,23},{8,24},{9,... | collective-permute-start | bytes 83144 | tf_op jit(solution)/shard_map/ppermute | solution.py:46
  104.7 5.9 %collective-permute-done.11 = f32[6928]{0:T(1024)S(1)} collective-permute-done((f32[6928]{0:T(1024)S(1)}, f32[6928]{0:T(1024)S(1)}, u32[]{:S(2)}, u32[]{:S(2)}) %collective-permute-start.11) | collective-permute-done | bytes 27744 | tf_op jit(solution)/shard_map/ppermute | solution.py:46
  110.6 1.9 %collective-permute-start.12 = (f32[6928]{0:T(1024)S(1)}, f32[6928]{0:T(1024)S(1)}, u32[]{:S(2)}, u32[]{:S(2)}) collective-permute-start(f32[6928]{0:T(1024)S(1)} %add.195), channel_id=1, source_target_pairs={{0,8},{1,9},{2,10},{3,11},{4,12},{5,13},{6,14},{7,15},{8,0},{9,1},... | collective-permute-start | bytes 83144 | tf_op jit(solution)/shard_map/ppermute | solution.py:46
  114.1 2.1 %collective-permute-done.12 = f32[6928]{0:T(1024)S(1)} collective-permute-done((f32[6928]{0:T(1024)S(1)}, f32[6928]{0:T(1024)S(1)}, u32[]{:S(2)}, u32[]{:S(2)}) %collective-permute-start.12) | collective-permute-done | bytes 27744 | tf_op jit(solution)/shard_map/ppermute | solution.py:46
  116.1 1.9 %collective-permute-start.13 = (f32[6928]{0:T(1024)S(1)}, f32[6928]{0:T(1024)S(1)}, u32[]{:S(2)}, u32[]{:S(2)}) collective-permute-start(f32[6928]{0:T(1024)S(1)} %add.196), channel_id=1, source_target_pairs={{0,4},{1,5},{2,6},{3,7},{4,0},{5,1},{6,2},{7,3},{8,12},{9,13},{10,... | collective-permute-start | bytes 83144 | tf_op jit(solution)/shard_map/ppermute | solution.py:46
  118.2 2.6 %collective-permute-done.13 = f32[6928]{0:T(1024)S(1)} collective-permute-done((f32[6928]{0:T(1024)S(1)}, f32[6928]{0:T(1024)S(1)}, u32[]{:S(2)}, u32[]{:S(2)}) %collective-permute-start.13) | collective-permute-done | bytes 27744 | tf_op jit(solution)/shard_map/ppermute | solution.py:46
  120.8 1.9 %collective-permute-start.14 = (f32[6928]{0:T(1024)S(1)}, f32[6928]{0:T(1024)S(1)}, u32[]{:S(2)}, u32[]{:S(2)}) collective-permute-start(f32[6928]{0:T(1024)S(1)} %add.197), channel_id=1, source_target_pairs={{0,2},{1,3},{2,0},{3,1},{4,6},{5,7},{6,4},{7,5},{8,10},{9,11},{10,... | collective-permute-start | bytes 83144 | tf_op jit(solution)/shard_map/ppermute | solution.py:46
  122.7 4.2 %collective-permute-done.14 = f32[6928]{0:T(1024)S(1)} collective-permute-done((f32[6928]{0:T(1024)S(1)}, f32[6928]{0:T(1024)S(1)}, u32[]{:S(2)}, u32[]{:S(2)}) %collective-permute-start.14) | collective-permute-done | bytes 27744 | tf_op jit(solution)/shard_map/ppermute | solution.py:46
  126.9 3.7 %collective-permute-start.15 = (f32[6928]{0:T(1024)S(1)}, f32[6928]{0:T(1024)S(1)}, u32[]{:S(2)}, u32[]{:S(2)}) collective-permute-start(f32[6928]{0:T(1024)S(1)} %add.198), channel_id=1, source_target_pairs={{0,1},{1,0},{2,3},{3,2},{4,5},{5,4},{6,7},{7,6},{8,9},{9,8},{10,11... | collective-permute-start | bytes 83144 | tf_op jit(solution)/shard_map/ppermute | solution.py:46
  131.8 1.9 %collective-permute-start.16 = (f32[6928]{0:T(1024)S(1)}, f32[6928]{0:T(1024)S(1)}, u32[]{:S(2)}, u32[]{:S(2)}) collective-permute-start(f32[6928]{0:T(1024)S(1)} %add.199), channel_id=1, source_target_pairs={{0,256},{64,320},{128,384},{192,448},{256,0},{320,64},{384,128},{4... | collective-permute-start | bytes 83144 | tf_op jit(solution)/shard_map/ppermute | solution.py:46
  134.0 3.5 %collective-permute-done.16 = f32[6928]{0:T(1024)S(1)} collective-permute-done((f32[6928]{0:T(1024)S(1)}, f32[6928]{0:T(1024)S(1)}, u32[]{:S(2)}, u32[]{:S(2)}) %collective-permute-start.16) | collective-permute-done | bytes 27744 | tf_op jit(solution)/shard_map/ppermute | solution.py:46
  137.5 1.9 %collective-permute-start.17 = (f32[6928]{0:T(1024)S(1)}, f32[6928]{0:T(1024)S(1)}, u32[]{:S(2)}, u32[]{:S(2)}) collective-permute-start(f32[6928]{0:T(1024)S(1)} %add.200), channel_id=1, source_target_pairs={{0,128},{64,192},{128,0},{192,64},{256,384},{320,448},{384,256},{4... | collective-permute-start | bytes 83144 | tf_op jit(solution)/shard_map/ppermute | solution.py:46
  139.7 2.4 %collective-permute-done.17 = f32[6928]{0:T(1024)S(1)} collective-permute-done((f32[6928]{0:T(1024)S(1)}, f32[6928]{0:T(1024)S(1)}, u32[]{:S(2)}, u32[]{:S(2)}) %collective-permute-start.17) | collective-permute-done | bytes 27744 | tf_op jit(solution)/shard_map/ppermute | solution.py:46
  142.1 17.4 %collective-permute-start.18 = (f32[6928]{0:T(1024)S(1)}, f32[6928]{0:T(1024)S(1)}, u32[]{:S(2)}, u32[]{:S(2)}) collective-permute-start(f32[6928]{0:T(1024)S(1)} %add.201), channel_id=1, source_target_pairs={{0,64},{64,0},{128,192},{192,128},{256,320},{320,256},{384,448},{4... | collective-permute-start | bytes 83144 | tf_op jit(solution)/shard_map/ppermute | solution.py:46
  (101 shorter events, 19.3 us)
Async XLA Ops:
  0.6 72.3 %copy-start = (bf16[27,16,16]{0,2,1:T(8,128)(2,1)S(1)}, bf16[27,16,16]{0,2,1:T(8,128)(2,1)}, u32[]{:S(2)}) copy-start(bf16[27,16,16]{0,2,1:T(8,128)(2,1)} %param.13) | copy-start | bytes 41476
  1.6 9.3 %collective-permute-start = (bf16[1,16,2,8,256]{4,1,3,2,0:T(8,128)(2,1)S(1)}, bf16[1,16,2,8,256]{4,1,3,2,0:T(8,128)(2,1)S(1)}, u32[]{:S(2)}, u32[]{:S(2)}) collective-permute-start(bf16[1,16,2,8,256]{4,1,3,2,0:T(8,128)(2,1)S(1)} %copy.24), channel_id=1, source_target_pairs={{0,1},{1,0},{2,3},{3,2},{4,5},{5,4},{6,7},{7,6},{8,9},{9,8},{10,11... | collective-permute-start | bytes 393224 | tf_op jit(solution)/shard_map/ppermute | solution.py:77
  11.9 7.2 %collective-permute-start.1 = (bf16[1,16,2,8,256]{4,1,3,2,0:T(8,128)(2,1)S(1)}, bf16[1,16,2,8,256]{4,1,3,2,0:T(8,128)(2,1)S(1)}, u32[]{:S(2)}, u32[]{:S(2)}) collective-permute-start(bf16[1,16,2,8,256]{4,1,3,2,0:T(8,128)(2,1)S(1)} %broadcast_select_fusion), channel_id=1, source_target_pairs={{0,2},{1,3},{2,0},{3,1},{4,6},{5,7},{6,4},{7,5},{8,10},{9,11},{10,... | collective-permute-start | bytes 393224 | tf_op jit(solution)/shard_map/ppermute | solution.py:77
  19.1 6.4 %collective-permute-start.2 = (bf16[1,16,2,8,256]{4,1,3,2,0:T(8,128)(2,1)S(1)}, bf16[1,16,2,8,256]{4,1,3,2,0:T(8,128)(2,1)S(1)}, u32[]{:S(2)}, u32[]{:S(2)}) collective-permute-start(bf16[1,16,2,8,256]{4,1,3,2,0:T(8,128)(2,1)S(1)} %broadcast_select_fusion.1), channel_id=1, source_target_pairs={{0,4},{1,5},{2,6},{3,7},{4,0},{5,1},{6,2},{7,3},{8,12},{9,13},{10,... | collective-permute-start | bytes 393224 | tf_op jit(solution)/shard_map/ppermute | solution.py:77
  25.5 9.6 %collective-permute-start.3 = (bf16[1,16,2,8,256]{4,1,3,2,0:T(8,128)(2,1)S(1)}, bf16[1,16,2,8,256]{4,1,3,2,0:T(8,128)(2,1)S(1)}, u32[]{:S(2)}, u32[]{:S(2)}) collective-permute-start(bf16[1,16,2,8,256]{4,1,3,2,0:T(8,128)(2,1)S(1)} %broadcast_select_fusion.2), channel_id=1, source_target_pairs={{0,8},{1,9},{2,10},{3,11},{4,12},{5,13},{6,14},{7,15},{8,0},{9,1},... | collective-permute-start | bytes 393224 | tf_op jit(solution)/shard_map/ppermute | solution.py:77
  35.1 11.0 %collective-permute-start.4 = (bf16[1,16,2,8,256]{4,1,3,2,0:T(8,128)(2,1)S(1)}, bf16[1,16,2,8,256]{4,1,3,2,0:T(8,128)(2,1)S(1)}, u32[]{:S(2)}, u32[]{:S(2)}) collective-permute-start(bf16[1,16,2,8,256]{4,1,3,2,0:T(8,128)(2,1)S(1)} %broadcast_select_fusion.3), channel_id=1, source_target_pairs={{0,16},{1,17},{2,18},{3,19},{4,20},{5,21},{6,22},{7,23},{8,24},{9,... | collective-permute-start | bytes 393224 | tf_op jit(solution)/shard_map/ppermute | solution.py:77
  46.1 14.1 %collective-permute-start.5 = (bf16[1,16,2,8,256]{4,1,3,2,0:T(8,128)(2,1)S(1)}, bf16[1,16,2,8,256]{4,1,3,2,0:T(8,128)(2,1)S(1)}, u32[]{:S(2)}, u32[]{:S(2)}) collective-permute-start(bf16[1,16,2,8,256]{4,1,3,2,0:T(8,128)(2,1)S(1)} %broadcast_select_fusion.4), channel_id=1, source_target_pairs={{0,32},{1,33},{2,34},{3,35},{4,36},{5,37},{6,38},{7,39},{8,40},{9,... | collective-permute-start | bytes 393224 | tf_op jit(solution)/shard_map/ppermute | solution.py:77
  60.2 15.9 %collective-permute-start.6 = (bf16[1,16,2,8,256]{4,1,3,2,0:T(8,128)(2,1)S(1)}, bf16[1,16,2,8,256]{4,1,3,2,0:T(8,128)(2,1)S(1)}, u32[]{:S(2)}, u32[]{:S(2)}) collective-permute-start(bf16[1,16,2,8,256]{4,1,3,2,0:T(8,128)(2,1)S(1)} %reverse_select_fusion), channel_id=1, source_target_pairs={{0,63},{1,2},{2,1},{3,4},{4,3},{5,6},{6,5},{7,8},{8,7},{9,10},{10,... | collective-permute-start | bytes 393224 | tf_op jit(solution)/shard_map/ppermute | solution.py:27
  71.0 5.7 %collective-permute-start.7 = (bf16[1,16,2,8,256]{4,1,3,2,0:T(8,128)(2,1)S(1)}, bf16[1,16,2,8,256]{4,1,3,2,0:T(8,128)(2,1)S(1)}, u32[]{:S(2)}, u32[]{:S(2)}) collective-permute-start(bf16[1,16,2,8,256]{4,1,3,2,0:T(8,128)(2,1)S(1)} %reverse_select_fusion), channel_id=1, source_target_pairs={{0,1},{1,0},{2,3},{3,2},{4,5},{5,4},{6,7},{7,6},{8,9},{9,8},{10,11... | collective-permute-start | bytes 393224 | tf_op jit(solution)/shard_map/ppermute | solution.py:25
  79.6 0.7 copy-start.1
  80.3 0.9 copy-start.2
  86.0 16.1 %collective-permute-start.10 = (f32[6928]{0:T(1024)S(1)}, f32[6928]{0:T(1024)S(1)}, u32[]{:S(2)}, u32[]{:S(2)}) collective-permute-start(f32[6928]{0:T(1024)S(1)} %pad_maximum_fusion.6), channel_id=1, source_target_pairs={{0,32},{1,33},{2,34},{3,35},{4,36},{5,37},{6,38},{7,39},{8,40},{9,... | collective-permute-start | bytes 83144 | tf_op jit(solution)/shard_map/ppermute | solution.py:46
  90.8 21.7 %collective-permute-start.8 = (bf16[1,16,1,8,256]{4,1,3,2,0:T(8,128)(2,1)S(1)}, bf16[1,16,1,8,256]{4,1,3,2,0:T(8,128)(2,1)S(1)}, u32[]{:S(2)}, u32[]{:S(2)}) collective-permute-start(bf16[1,16,1,8,256]{4,1,3,2,0:T(8,128)(2,1)S(1)} %get-tuple-element.76), channel_id=1, source_target_pairs={{0,63},{1,2},{2,1},{3,4},{4,3},{5,6},{6,5},{7,8},{8,7},{9,10},{10,... | collective-permute-start | bytes 196616 | tf_op jit(solution)/shard_map/ppermute | solution.py:37
  100.2 12.4 %collective-permute-start.9 = (bf16[1,16,1,8,256]{4,1,3,2,0:T(8,128)(2,1)S(1)}, bf16[1,16,1,8,256]{4,1,3,2,0:T(8,128)(2,1)S(1)}, u32[]{:S(2)}, u32[]{:S(2)}) collective-permute-start(bf16[1,16,1,8,256]{4,1,3,2,0:T(8,128)(2,1)S(1)} %get-tuple-element.77), channel_id=1, source_target_pairs={{0,1},{1,0},{2,3},{3,2},{4,5},{5,4},{6,7},{7,6},{8,9},{9,8},{10,11... | collective-permute-start | bytes 196616 | tf_op jit(solution)/shard_map/ppermute | solution.py:35
  102.1 8.5 %collective-permute-start.11 = (f32[6928]{0:T(1024)S(1)}, f32[6928]{0:T(1024)S(1)}, u32[]{:S(2)}, u32[]{:S(2)}) collective-permute-start(f32[6928]{0:T(1024)S(1)} %fusion.99), channel_id=1, source_target_pairs={{0,16},{1,17},{2,18},{3,19},{4,20},{5,21},{6,22},{7,23},{8,24},{9,... | collective-permute-start | bytes 83144 | tf_op jit(solution)/shard_map/ppermute | solution.py:46
  110.6 5.5 %collective-permute-start.12 = (f32[6928]{0:T(1024)S(1)}, f32[6928]{0:T(1024)S(1)}, u32[]{:S(2)}, u32[]{:S(2)}) collective-permute-start(f32[6928]{0:T(1024)S(1)} %add.195), channel_id=1, source_target_pairs={{0,8},{1,9},{2,10},{3,11},{4,12},{5,13},{6,14},{7,15},{8,0},{9,1},... | collective-permute-start | bytes 83144 | tf_op jit(solution)/shard_map/ppermute | solution.py:46
  116.1 4.6 %collective-permute-start.13 = (f32[6928]{0:T(1024)S(1)}, f32[6928]{0:T(1024)S(1)}, u32[]{:S(2)}, u32[]{:S(2)}) collective-permute-start(f32[6928]{0:T(1024)S(1)} %add.196), channel_id=1, source_target_pairs={{0,4},{1,5},{2,6},{3,7},{4,0},{5,1},{6,2},{7,3},{8,12},{9,13},{10,... | collective-permute-start | bytes 83144 | tf_op jit(solution)/shard_map/ppermute | solution.py:46
  120.8 6.1 %collective-permute-start.14 = (f32[6928]{0:T(1024)S(1)}, f32[6928]{0:T(1024)S(1)}, u32[]{:S(2)}, u32[]{:S(2)}) collective-permute-start(f32[6928]{0:T(1024)S(1)} %add.197), channel_id=1, source_target_pairs={{0,2},{1,3},{2,0},{3,1},{4,6},{5,7},{6,4},{7,5},{8,10},{9,11},{10,... | collective-permute-start | bytes 83144 | tf_op jit(solution)/shard_map/ppermute | solution.py:46
  126.9 4.9 %collective-permute-start.15 = (f32[6928]{0:T(1024)S(1)}, f32[6928]{0:T(1024)S(1)}, u32[]{:S(2)}, u32[]{:S(2)}) collective-permute-start(f32[6928]{0:T(1024)S(1)} %add.198), channel_id=1, source_target_pairs={{0,1},{1,0},{2,3},{3,2},{4,5},{5,4},{6,7},{7,6},{8,9},{9,8},{10,11... | collective-permute-start | bytes 83144 | tf_op jit(solution)/shard_map/ppermute | solution.py:46
  131.8 5.7 %collective-permute-start.16 = (f32[6928]{0:T(1024)S(1)}, f32[6928]{0:T(1024)S(1)}, u32[]{:S(2)}, u32[]{:S(2)}) collective-permute-start(f32[6928]{0:T(1024)S(1)} %add.199), channel_id=1, source_target_pairs={{0,256},{64,320},{128,384},{192,448},{256,0},{320,64},{384,128},{4... | collective-permute-start | bytes 83144 | tf_op jit(solution)/shard_map/ppermute | solution.py:46
  137.5 4.6 %collective-permute-start.17 = (f32[6928]{0:T(1024)S(1)}, f32[6928]{0:T(1024)S(1)}, u32[]{:S(2)}, u32[]{:S(2)}) collective-permute-start(f32[6928]{0:T(1024)S(1)} %add.200), channel_id=1, source_target_pairs={{0,128},{64,192},{128,0},{192,64},{256,384},{320,448},{384,256},{4... | collective-permute-start | bytes 83144 | tf_op jit(solution)/shard_map/ppermute | solution.py:46
  142.1 18.5 %collective-permute-start.18 = (f32[6928]{0:T(1024)S(1)}, f32[6928]{0:T(1024)S(1)}, u32[]{:S(2)}, u32[]{:S(2)}) collective-permute-start(f32[6928]{0:T(1024)S(1)} %add.201), channel_id=1, source_target_pairs={{0,64},{64,0},{128,192},{192,128},{256,320},{320,256},{384,448},{4... | collective-permute-start | bytes 83144 | tf_op jit(solution)/shard_map/ppermute | solution.py:46

commit v11 on v10

--- a/solution.py
+++ b/solution.py
@@ -123,8 +123,8 @@
     grad_list = []
     for shift_x in range(3):
         window = stacked_yz[:, :, shift_x : shift_x + planes]
-        part = jnp.einsum("boxyz,bcxyz->oc", grad_pre, window, preferred_element_type=jnp.float32)
-        part = jnp.transpose(part.reshape(channels, 3, 3, channels), (1, 2, 0, 3))
+        part = jnp.einsum("bcxyz,boxyz->co", window, grad_pre, preferred_element_type=jnp.float32)
+        part = jnp.transpose(part.reshape(3, 3, channels, channels), (0, 1, 3, 2))
         grad_list.append(part.reshape(9, channels, channels))
     grad_b = jnp.sum(grad_pre.astype(jnp.float32), axis=(0, 2, 3, 4))
     stacked = jnp.concatenate([jnp.concatenate(grad_list, axis=0).reshape(-1), grad_b])

time: 164 us -> 161 us (0.982)
  matrix products: 6.08 us -> 3.2 us
    dot_general x3, matrix products: 4.19 us -> 1.31 us  [on_device(): jnp.einsum('bcxyz,boxyz->co', window, grad_pre, preferred_element_type=jn...]
where the time goes in v11:
time: 161 us; the launch traced here: 159 us
  starting transfers between devices  95.3 us (59%)
  waiting for transfers between devices  35.5 us (22%)
  between operations  10.8 us (7%)
  local copies, waits for them, and re-layouts  9.88 us (6%)
  other arithmetic  4.65 us (3%)
  matrix products  3.2 us (2%)
    ppermute x9, starting transfers between devices, butterfly_sum(): value = value + lax.ppermute(value, axis, pairs)  37.4 us
    ppermute x6, starting transfers between devices, routed(): arrived = lax.ppermute(jnp.concatenate(pieces, axis=2), axis, pairs)  34 us
    ppermute x9, waiting for transfers between devices, butterfly_sum(): value = value + lax.ppermute(value, axis, pairs)  21.6 us
    ppermute x6, waiting for transfers between devices, routed(): arrived = lax.ppermute(jnp.concatenate(pieces, axis=2), axis, pairs)  11.2 us
    ppermute x1, starting transfers between devices, neighbour_blocks(): across = lax.ppermute(value, axis, pairs)  10.8 us
    ppermute x1, starting transfers between devices, halo_planes(): across = lax.ppermute(jnp.where(even, first, last), axis, pairs)  9.3 us
    unnamed x14, local copies, waits for them, and re-layouts  4.46 us
  transfers between devices with their start and end apart: 19, of which 13 were waited for; matrix products, arithmetic and copies ran while one was open for 5% of the time, Pallas kernels for 0%

profile of v11, /device:TPU:1, one launch (start us, length us, event | category | flops | bytes accessed | tf_op | source)
XLA Modules:
  0.0 159.4 jit_solution(4103470206704660741)
XLA Ops:
  1.6 3.9 %collective-permute-start = (bf16[1,16,2,8,256]{4,1,3,2,0:T(8,128)(2,1)S(1)}, bf16[1,16,2,8,256]{4,1,3,2,0:T(8,128)(2,1)S(1)}, u32[]{:S(2)}, u32[]{:S(2)}) collective-permute-start(bf16[1,16,2,8,256]{4,1,3,2,0:T(8,128)(2,1)S(1)} %copy.24), channel_id=1, source_target_pairs={{0,1},{1,0},{2,3},{3,2},{4,5},{5,4},{6,7},{7,6},{8,9},{9,8},{10,11... | collective-permute-start | bytes 393224 | tf_op jit(solution)/shard_map/ppermute | solution.py:77
  5.6 1.4 fusion.92
  8.2 1.4 fusion.91
  11.9 4.4 %collective-permute-start.1 = (bf16[1,16,2,8,256]{4,1,3,2,0:T(8,128)(2,1)S(1)}, bf16[1,16,2,8,256]{4,1,3,2,0:T(8,128)(2,1)S(1)}, u32[]{:S(2)}, u32[]{:S(2)}) collective-permute-start(bf16[1,16,2,8,256]{4,1,3,2,0:T(8,128)(2,1)S(1)} %broadcast_select_fusion), channel_id=1, source_target_pairs={{0,2},{1,3},{2,0},{3,1},{4,6},{5,7},{6,4},{7,5},{8,10},{9,11},{10,... | collective-permute-start | bytes 393224 | tf_op jit(solution)/shard_map/ppermute | solution.py:77
  16.3 2.8 %collective-permute-done.1 = bf16[1,16,2,8,256]{4,1,3,2,0:T(8,128)(2,1)S(1)} collective-permute-done((bf16[1,16,2,8,256]{4,1,3,2,0:T(8,128)(2,1)S(1)}, bf16[1,16,2,8,256]{4,1,3,2,0:T(8,128)(2,1)S(1)}, u32[]{:S(2)}, u32[]{:S(2)}) %collective-permute-start.1) | collective-permute-done | bytes 131104 | tf_op jit(solution)/shard_map/ppermute | solution.py:77
  19.1 4.0 %collective-permute-start.2 = (bf16[1,16,2,8,256]{4,1,3,2,0:T(8,128)(2,1)S(1)}, bf16[1,16,2,8,256]{4,1,3,2,0:T(8,128)(2,1)S(1)}, u32[]{:S(2)}, u32[]{:S(2)}) collective-permute-start(bf16[1,16,2,8,256]{4,1,3,2,0:T(8,128)(2,1)S(1)} %broadcast_select_fusion.1), channel_id=1, source_target_pairs={{0,4},{1,5},{2,6},{3,7},{4,0},{5,1},{6,2},{7,3},{8,12},{9,13},{10,... | collective-permute-start | bytes 393224 | tf_op jit(solution)/shard_map/ppermute | solution.py:77
  23.2 2.3 %collective-permute-done.2 = bf16[1,16,2,8,256]{4,1,3,2,0:T(8,128)(2,1)S(1)} collective-permute-done((bf16[1,16,2,8,256]{4,1,3,2,0:T(8,128)(2,1)S(1)}, bf16[1,16,2,8,256]{4,1,3,2,0:T(8,128)(2,1)S(1)}, u32[]{:S(2)}, u32[]{:S(2)}) %collective-permute-start.2) | collective-permute-done | bytes 131104 | tf_op jit(solution)/shard_map/ppermute | solution.py:77
  25.5 5.8 %collective-permute-start.3 = (bf16[1,16,2,8,256]{4,1,3,2,0:T(8,128)(2,1)S(1)}, bf16[1,16,2,8,256]{4,1,3,2,0:T(8,128)(2,1)S(1)}, u32[]{:S(2)}, u32[]{:S(2)}) collective-permute-start(bf16[1,16,2,8,256]{4,1,3,2,0:T(8,128)(2,1)S(1)} %broadcast_select_fusion.2), channel_id=1, source_target_pairs={{0,8},{1,9},{2,10},{3,11},{4,12},{5,13},{6,14},{7,15},{8,0},{9,1},... | collective-permute-start | bytes 393224 | tf_op jit(solution)/shard_map/ppermute | solution.py:77
  31.4 3.7 %collective-permute-done.3 = bf16[1,16,2,8,256]{4,1,3,2,0:T(8,128)(2,1)S(1)} collective-permute-done((bf16[1,16,2,8,256]{4,1,3,2,0:T(8,128)(2,1)S(1)}, bf16[1,16,2,8,256]{4,1,3,2,0:T(8,128)(2,1)S(1)}, u32[]{:S(2)}, u32[]{:S(2)}) %collective-permute-start.3) | collective-permute-done | bytes 131104 | tf_op jit(solution)/shard_map/ppermute | solution.py:77
  35.1 8.4 %collective-permute-start.4 = (bf16[1,16,2,8,256]{4,1,3,2,0:T(8,128)(2,1)S(1)}, bf16[1,16,2,8,256]{4,1,3,2,0:T(8,128)(2,1)S(1)}, u32[]{:S(2)}, u32[]{:S(2)}) collective-permute-start(bf16[1,16,2,8,256]{4,1,3,2,0:T(8,128)(2,1)S(1)} %broadcast_select_fusion.3), channel_id=1, source_target_pairs={{0,16},{1,17},{2,18},{3,19},{4,20},{5,21},{6,22},{7,23},{8,24},{9,... | collective-permute-start | bytes 393224 | tf_op jit(solution)/shard_map/ppermute | solution.py:77
  43.6 2.5 %collective-permute-done.4 = bf16[1,16,2,8,256]{4,1,3,2,0:T(8,128)(2,1)S(1)} collective-permute-done((bf16[1,16,2,8,256]{4,1,3,2,0:T(8,128)(2,1)S(1)}, bf16[1,16,2,8,256]{4,1,3,2,0:T(8,128)(2,1)S(1)}, u32[]{:S(2)}, u32[]{:S(2)}) %collective-permute-start.4) | collective-permute-done | bytes 131104 | tf_op jit(solution)/shard_map/ppermute | solution.py:77
  46.1 7.5 %collective-permute-start.5 = (bf16[1,16,2,8,256]{4,1,3,2,0:T(8,128)(2,1)S(1)}, bf16[1,16,2,8,256]{4,1,3,2,0:T(8,128)(2,1)S(1)}, u32[]{:S(2)}, u32[]{:S(2)}) collective-permute-start(bf16[1,16,2,8,256]{4,1,3,2,0:T(8,128)(2,1)S(1)} %broadcast_select_fusion.4), channel_id=1, source_target_pairs={{0,32},{1,33},{2,34},{3,35},{4,36},{5,37},{6,38},{7,39},{8,40},{9,... | collective-permute-start | bytes 393224 | tf_op jit(solution)/shard_map/ppermute | solution.py:77
  60.2 10.8 %collective-permute-start.6 = (bf16[1,16,2,8,256]{4,1,3,2,0:T(8,128)(2,1)S(1)}, bf16[1,16,2,8,256]{4,1,3,2,0:T(8,128)(2,1)S(1)}, u32[]{:S(2)}, u32[]{:S(2)}) collective-permute-start(bf16[1,16,2,8,256]{4,1,3,2,0:T(8,128)(2,1)S(1)} %reverse_select_fusion), channel_id=1, source_target_pairs={{0,63},{1,2},{2,1},{3,4},{4,3},{5,6},{6,5},{7,8},{8,7},{9,10},{10,... | collective-permute-start | bytes 393224 | tf_op jit(solution)/shard_map/ppermute | solution.py:27
  71.0 1.9 %collective-permute-start.7 = (bf16[1,16,2,8,256]{4,1,3,2,0:T(8,128)(2,1)S(1)}, bf16[1,16,2,8,256]{4,1,3,2,0:T(8,128)(2,1)S(1)}, u32[]{:S(2)}, u32[]{:S(2)}) collective-permute-start(bf16[1,16,2,8,256]{4,1,3,2,0:T(8,128)(2,1)S(1)} %reverse_select_fusion), channel_id=1, source_target_pairs={{0,1},{1,0},{2,3},{3,2},{4,5},{5,4},{6,7},{7,6},{8,9},{9,8},{10,11... | collective-permute-start | bytes 393224 | tf_op jit(solution)/shard_map/ppermute | solution.py:25
  74.0 2.1 %collective-permute-done.6 = bf16[1,16,2,8,256]{4,1,3,2,0:T(8,128)(2,1)S(1)} collective-permute-done((bf16[1,16,2,8,256]{4,1,3,2,0:T(8,128)(2,1)S(1)}, bf16[1,16,2,8,256]{4,1,3,2,0:T(8,128)(2,1)S(1)}, u32[]{:S(2)}, u32[]{:S(2)}) %collective-permute-start.6) | collective-permute-done | bytes 131104 | tf_op jit(solution)/shard_map/ppermute | solution.py:27
  83.4 4.8 %collective-permute-start.10 = (f32[6928]{0:T(1024)S(1)}, f32[6928]{0:T(1024)S(1)}, u32[]{:S(2)}, u32[]{:S(2)}) collective-permute-start(f32[6928]{0:T(1024)S(1)} %pad_maximum_fusion.6), channel_id=1, source_target_pairs={{0,32},{1,33},{2,34},{3,35},{4,36},{5,37},{6,38},{7,39},{8,40},{9,... | collective-permute-start | bytes 83144 | tf_op jit(solution)/shard_map/ppermute | solution.py:46
  88.2 9.3 %collective-permute-start.8 = (bf16[1,16,1,8,256]{4,1,3,2,0:T(8,128)(2,1)S(1)}, bf16[1,16,1,8,256]{4,1,3,2,0:T(8,128)(2,1)S(1)}, u32[]{:S(2)}, u32[]{:S(2)}) collective-permute-start(bf16[1,16,1,8,256]{4,1,3,2,0:T(8,128)(2,1)S(1)} %get-tuple-element.76), channel_id=1, source_target_pairs={{0,63},{1,2},{2,1},{3,4},{4,3},{5,6},{6,5},{7,8},{8,7},{9,10},{10,... | collective-permute-start | bytes 196616 | tf_op jit(solution)/shard_map/ppermute | solution.py:37
  97.5 1.9 %collective-permute-start.9 = (bf16[1,16,1,8,256]{4,1,3,2,0:T(8,128)(2,1)S(1)}, bf16[1,16,1,8,256]{4,1,3,2,0:T(8,128)(2,1)S(1)}, u32[]{:S(2)}, u32[]{:S(2)}) collective-permute-start(bf16[1,16,1,8,256]{4,1,3,2,0:T(8,128)(2,1)S(1)} %get-tuple-element.77), channel_id=1, source_target_pairs={{0,1},{1,0},{2,3},{3,2},{4,5},{5,4},{6,7},{7,6},{8,9},{9,8},{10,11... | collective-permute-start | bytes 196616 | tf_op jit(solution)/shard_map/ppermute | solution.py:35
  99.5 1.9 %collective-permute-start.11 = (f32[6928]{0:T(1024)S(1)}, f32[6928]{0:T(1024)S(1)}, u32[]{:S(2)}, u32[]{:S(2)}) collective-permute-start(f32[6928]{0:T(1024)S(1)} %fusion.99), channel_id=1, source_target_pairs={{0,16},{1,17},{2,18},{3,19},{4,20},{5,21},{6,22},{7,23},{8,24},{9,... | collective-permute-start | bytes 83144 | tf_op jit(solution)/shard_map/ppermute | solution.py:46
  102.1 5.9 %collective-permute-done.11 = f32[6928]{0:T(1024)S(1)} collective-permute-done((f32[6928]{0:T(1024)S(1)}, f32[6928]{0:T(1024)S(1)}, u32[]{:S(2)}, u32[]{:S(2)}) %collective-permute-start.11) | collective-permute-done | bytes 27744 | tf_op jit(solution)/shard_map/ppermute | solution.py:46
  108.0 1.9 %collective-permute-start.12 = (f32[6928]{0:T(1024)S(1)}, f32[6928]{0:T(1024)S(1)}, u32[]{:S(2)}, u32[]{:S(2)}) collective-permute-start(f32[6928]{0:T(1024)S(1)} %add.195), channel_id=1, source_target_pairs={{0,8},{1,9},{2,10},{3,11},{4,12},{5,13},{6,14},{7,15},{8,0},{9,1},... | collective-permute-start | bytes 83144 | tf_op jit(solution)/shard_map/ppermute | solution.py:46
  111.4 2.1 %collective-permute-done.12 = f32[6928]{0:T(1024)S(1)} collective-permute-done((f32[6928]{0:T(1024)S(1)}, f32[6928]{0:T(1024)S(1)}, u32[]{:S(2)}, u32[]{:S(2)}) %collective-permute-start.12) | collective-permute-done | bytes 27744 | tf_op jit(solution)/shard_map/ppermute | solution.py:46
  113.5 1.9 %collective-permute-start.13 = (f32[6928]{0:T(1024)S(1)}, f32[6928]{0:T(1024)S(1)}, u32[]{:S(2)}, u32[]{:S(2)}) collective-permute-start(f32[6928]{0:T(1024)S(1)} %add.196), channel_id=1, source_target_pairs={{0,4},{1,5},{2,6},{3,7},{4,0},{5,1},{6,2},{7,3},{8,12},{9,13},{10,... | collective-permute-start | bytes 83144 | tf_op jit(solution)/shard_map/ppermute | solution.py:46
  115.5 2.6 %collective-permute-done.13 = f32[6928]{0:T(1024)S(1)} collective-permute-done((f32[6928]{0:T(1024)S(1)}, f32[6928]{0:T(1024)S(1)}, u32[]{:S(2)}, u32[]{:S(2)}) %collective-permute-start.13) | collective-permute-done | bytes 27744 | tf_op jit(solution)/shard_map/ppermute | solution.py:46
  118.1 1.9 %collective-permute-start.14 = (f32[6928]{0:T(1024)S(1)}, f32[6928]{0:T(1024)S(1)}, u32[]{:S(2)}, u32[]{:S(2)}) collective-permute-start(f32[6928]{0:T(1024)S(1)} %add.197), channel_id=1, source_target_pairs={{0,2},{1,3},{2,0},{3,1},{4,6},{5,7},{6,4},{7,5},{8,10},{9,11},{10,... | collective-permute-start | bytes 83144 | tf_op jit(solution)/shard_map/ppermute | solution.py:46
  120.1 4.2 %collective-permute-done.14 = f32[6928]{0:T(1024)S(1)} collective-permute-done((f32[6928]{0:T(1024)S(1)}, f32[6928]{0:T(1024)S(1)}, u32[]{:S(2)}, u32[]{:S(2)}) %collective-permute-start.14) | collective-permute-done | bytes 27744 | tf_op jit(solution)/shard_map/ppermute | solution.py:46
  124.2 3.7 %collective-permute-start.15 = (f32[6928]{0:T(1024)S(1)}, f32[6928]{0:T(1024)S(1)}, u32[]{:S(2)}, u32[]{:S(2)}) collective-permute-start(f32[6928]{0:T(1024)S(1)} %add.198), channel_id=1, source_target_pairs={{0,1},{1,0},{2,3},{3,2},{4,5},{5,4},{6,7},{7,6},{8,9},{9,8},{10,11... | collective-permute-start | bytes 83144 | tf_op jit(solution)/shard_map/ppermute | solution.py:46
  129.1 1.9 %collective-permute-start.16 = (f32[6928]{0:T(1024)S(1)}, f32[6928]{0:T(1024)S(1)}, u32[]{:S(2)}, u32[]{:S(2)}) collective-permute-start(f32[6928]{0:T(1024)S(1)} %add.199), channel_id=1, source_target_pairs={{0,256},{64,320},{128,384},{192,448},{256,0},{320,64},{384,128},{4... | collective-permute-start | bytes 83144 | tf_op jit(solution)/shard_map/ppermute | solution.py:46
  131.4 3.5 %collective-permute-done.16 = f32[6928]{0:T(1024)S(1)} collective-permute-done((f32[6928]{0:T(1024)S(1)}, f32[6928]{0:T(1024)S(1)}, u32[]{:S(2)}, u32[]{:S(2)}) %collective-permute-start.16) | collective-permute-done | bytes 27744 | tf_op jit(solution)/shard_map/ppermute | solution.py:46
  134.9 1.9 %collective-permute-start.17 = (f32[6928]{0:T(1024)S(1)}, f32[6928]{0:T(1024)S(1)}, u32[]{:S(2)}, u32[]{:S(2)}) collective-permute-start(f32[6928]{0:T(1024)S(1)} %add.200), channel_id=1, source_target_pairs={{0,128},{64,192},{128,0},{192,64},{256,384},{320,448},{384,256},{4... | collective-permute-start | bytes 83144 | tf_op jit(solution)/shard_map/ppermute | solution.py:46
  137.1 2.4 %collective-permute-done.17 = f32[6928]{0:T(1024)S(1)} collective-permute-done((f32[6928]{0:T(1024)S(1)}, f32[6928]{0:T(1024)S(1)}, u32[]{:S(2)}, u32[]{:S(2)}) %collective-permute-start.17) | collective-permute-done | bytes 27744 | tf_op jit(solution)/shard_map/ppermute | solution.py:46
  139.5 17.4 %collective-permute-start.18 = (f32[6928]{0:T(1024)S(1)}, f32[6928]{0:T(1024)S(1)}, u32[]{:S(2)}, u32[]{:S(2)}) collective-permute-start(f32[6928]{0:T(1024)S(1)} %add.201), channel_id=1, source_target_pairs={{0,64},{64,0},{128,192},{192,128},{256,320},{320,256},{384,448},{4... | collective-permute-start | bytes 83144 | tf_op jit(solution)/shard_map/ppermute | solution.py:46
  (104 shorter events, 16.7 us)
Async XLA Ops:
  0.6 72.3 %copy-start = (bf16[27,16,16]{0,2,1:T(8,128)(2,1)S(1)}, bf16[27,16,16]{0,2,1:T(8,128)(2,1)}, u32[]{:S(2)}) copy-start(bf16[27,16,16]{0,2,1:T(8,128)(2,1)} %param.13) | copy-start | bytes 41476
  1.6 9.3 %collective-permute-start = (bf16[1,16,2,8,256]{4,1,3,2,0:T(8,128)(2,1)S(1)}, bf16[1,16,2,8,256]{4,1,3,2,0:T(8,128)(2,1)S(1)}, u32[]{:S(2)}, u32[]{:S(2)}) collective-permute-start(bf16[1,16,2,8,256]{4,1,3,2,0:T(8,128)(2,1)S(1)} %copy.24), channel_id=1, source_target_pairs={{0,1},{1,0},{2,3},{3,2},{4,5},{5,4},{6,7},{7,6},{8,9},{9,8},{10,11... | collective-permute-start | bytes 393224 | tf_op jit(solution)/shard_map/ppermute | solution.py:77
  11.9 7.2 %collective-permute-start.1 = (bf16[1,16,2,8,256]{4,1,3,2,0:T(8,128)(2,1)S(1)}, bf16[1,16,2,8,256]{4,1,3,2,0:T(8,128)(2,1)S(1)}, u32[]{:S(2)}, u32[]{:S(2)}) collective-permute-start(bf16[1,16,2,8,256]{4,1,3,2,0:T(8,128)(2,1)S(1)} %broadcast_select_fusion), channel_id=1, source_target_pairs={{0,2},{1,3},{2,0},{3,1},{4,6},{5,7},{6,4},{7,5},{8,10},{9,11},{10,... | collective-permute-start | bytes 393224 | tf_op jit(solution)/shard_map/ppermute | solution.py:77
  19.1 6.4 %collective-permute-start.2 = (bf16[1,16,2,8,256]{4,1,3,2,0:T(8,128)(2,1)S(1)}, bf16[1,16,2,8,256]{4,1,3,2,0:T(8,128)(2,1)S(1)}, u32[]{:S(2)}, u32[]{:S(2)}) collective-permute-start(bf16[1,16,2,8,256]{4,1,3,2,0:T(8,128)(2,1)S(1)} %broadcast_select_fusion.1), channel_id=1, source_target_pairs={{0,4},{1,5},{2,6},{3,7},{4,0},{5,1},{6,2},{7,3},{8,12},{9,13},{10,... | collective-permute-start | bytes 393224 | tf_op jit(solution)/shard_map/ppermute | solution.py:77
  25.5 9.6 %collective-permute-start.3 = (bf16[1,16,2,8,256]{4,1,3,2,0:T(8,128)(2,1)S(1)}, bf16[1,16,2,8,256]{4,1,3,2,0:T(8,128)(2,1)S(1)}, u32[]{:S(2)}, u32[]{:S(2)}) collective-permute-start(bf16[1,16,2,8,256]{4,1,3,2,0:T(8,128)(2,1)S(1)} %broadcast_select_fusion.2), channel_id=1, source_target_pairs={{0,8},{1,9},{2,10},{3,11},{4,12},{5,13},{6,14},{7,15},{8,0},{9,1},... | collective-permute-start | bytes 393224 | tf_op jit(solution)/shard_map/ppermute | solution.py:77
  35.1 11.0 %collective-permute-start.4 = (bf16[1,16,2,8,256]{4,1,3,2,0:T(8,128)(2,1)S(1)}, bf16[1,16,2,8,256]{4,1,3,2,0:T(8,128)(2,1)S(1)}, u32[]{:S(2)}, u32[]{:S(2)}) collective-permute-start(bf16[1,16,2,8,256]{4,1,3,2,0:T(8,128)(2,1)S(1)} %broadcast_select_fusion.3), channel_id=1, source_target_pairs={{0,16},{1,17},{2,18},{3,19},{4,20},{5,21},{6,22},{7,23},{8,24},{9,... | collective-permute-start | bytes 393224 | tf_op jit(solution)/shard_map/ppermute | solution.py:77
  46.1 14.1 %collective-permute-start.5 = (bf16[1,16,2,8,256]{4,1,3,2,0:T(8,128)(2,1)S(1)}, bf16[1,16,2,8,256]{4,1,3,2,0:T(8,128)(2,1)S(1)}, u32[]{:S(2)}, u32[]{:S(2)}) collective-permute-start(bf16[1,16,2,8,256]{4,1,3,2,0:T(8,128)(2,1)S(1)} %broadcast_select_fusion.4), channel_id=1, source_target_pairs={{0,32},{1,33},{2,34},{3,35},{4,36},{5,37},{6,38},{7,39},{8,40},{9,... | collective-permute-start | bytes 393224 | tf_op jit(solution)/shard_map/ppermute | solution.py:77
  60.2 15.9 %collective-permute-start.6 = (bf16[1,16,2,8,256]{4,1,3,2,0:T(8,128)(2,1)S(1)}, bf16[1,16,2,8,256]{4,1,3,2,0:T(8,128)(2,1)S(1)}, u32[]{:S(2)}, u32[]{:S(2)}) collective-permute-start(bf16[1,16,2,8,256]{4,1,3,2,0:T(8,128)(2,1)S(1)} %reverse_select_fusion), channel_id=1, source_target_pairs={{0,63},{1,2},{2,1},{3,4},{4,3},{5,6},{6,5},{7,8},{8,7},{9,10},{10,... | collective-permute-start | bytes 393224 | tf_op jit(solution)/shard_map/ppermute | solution.py:27
  71.0 5.7 %collective-permute-start.7 = (bf16[1,16,2,8,256]{4,1,3,2,0:T(8,128)(2,1)S(1)}, bf16[1,16,2,8,256]{4,1,3,2,0:T(8,128)(2,1)S(1)}, u32[]{:S(2)}, u32[]{:S(2)}) collective-permute-start(bf16[1,16,2,8,256]{4,1,3,2,0:T(8,128)(2,1)S(1)} %reverse_select_fusion), channel_id=1, source_target_pairs={{0,1},{1,0},{2,3},{3,2},{4,5},{5,4},{6,7},{7,6},{8,9},{9,8},{10,11... | collective-permute-start | bytes 393224 | tf_op jit(solution)/shard_map/ppermute | solution.py:25
  79.6 0.7 copy-start.1
  80.3 0.9 copy-start.2
  83.4 16.1 %collective-permute-start.10 = (f32[6928]{0:T(1024)S(1)}, f32[6928]{0:T(1024)S(1)}, u32[]{:S(2)}, u32[]{:S(2)}) collective-permute-start(f32[6928]{0:T(1024)S(1)} %pad_maximum_fusion.6), channel_id=1, source_target_pairs={{0,32},{1,33},{2,34},{3,35},{4,36},{5,37},{6,38},{7,39},{8,40},{9,... | collective-permute-start | bytes 83144 | tf_op jit(solution)/shard_map/ppermute | solution.py:46
  88.2 21.7 %collective-permute-start.8 = (bf16[1,16,1,8,256]{4,1,3,2,0:T(8,128)(2,1)S(1)}, bf16[1,16,1,8,256]{4,1,3,2,0:T(8,128)(2,1)S(1)}, u32[]{:S(2)}, u32[]{:S(2)}) collective-permute-start(bf16[1,16,1,8,256]{4,1,3,2,0:T(8,128)(2,1)S(1)} %get-tuple-element.76), channel_id=1, source_target_pairs={{0,63},{1,2},{2,1},{3,4},{4,3},{5,6},{6,5},{7,8},{8,7},{9,10},{10,... | collective-permute-start | bytes 196616 | tf_op jit(solution)/shard_map/ppermute | solution.py:37
  97.5 12.4 %collective-permute-start.9 = (bf16[1,16,1,8,256]{4,1,3,2,0:T(8,128)(2,1)S(1)}, bf16[1,16,1,8,256]{4,1,3,2,0:T(8,128)(2,1)S(1)}, u32[]{:S(2)}, u32[]{:S(2)}) collective-permute-start(bf16[1,16,1,8,256]{4,1,3,2,0:T(8,128)(2,1)S(1)} %get-tuple-element.77), channel_id=1, source_target_pairs={{0,1},{1,0},{2,3},{3,2},{4,5},{5,4},{6,7},{7,6},{8,9},{9,8},{10,11... | collective-permute-start | bytes 196616 | tf_op jit(solution)/shard_map/ppermute | solution.py:35
  99.5 8.5 %collective-permute-start.11 = (f32[6928]{0:T(1024)S(1)}, f32[6928]{0:T(1024)S(1)}, u32[]{:S(2)}, u32[]{:S(2)}) collective-permute-start(f32[6928]{0:T(1024)S(1)} %fusion.99), channel_id=1, source_target_pairs={{0,16},{1,17},{2,18},{3,19},{4,20},{5,21},{6,22},{7,23},{8,24},{9,... | collective-permute-start | bytes 83144 | tf_op jit(solution)/shard_map/ppermute | solution.py:46
  108.0 5.5 %collective-permute-start.12 = (f32[6928]{0:T(1024)S(1)}, f32[6928]{0:T(1024)S(1)}, u32[]{:S(2)}, u32[]{:S(2)}) collective-permute-start(f32[6928]{0:T(1024)S(1)} %add.195), channel_id=1, source_target_pairs={{0,8},{1,9},{2,10},{3,11},{4,12},{5,13},{6,14},{7,15},{8,0},{9,1},... | collective-permute-start | bytes 83144 | tf_op jit(solution)/shard_map/ppermute | solution.py:46
  113.5 4.6 %collective-permute-start.13 = (f32[6928]{0:T(1024)S(1)}, f32[6928]{0:T(1024)S(1)}, u32[]{:S(2)}, u32[]{:S(2)}) collective-permute-start(f32[6928]{0:T(1024)S(1)} %add.196), channel_id=1, source_target_pairs={{0,4},{1,5},{2,6},{3,7},{4,0},{5,1},{6,2},{7,3},{8,12},{9,13},{10,... | collective-permute-start | bytes 83144 | tf_op jit(solution)/shard_map/ppermute | solution.py:46
  118.1 6.1 %collective-permute-start.14 = (f32[6928]{0:T(1024)S(1)}, f32[6928]{0:T(1024)S(1)}, u32[]{:S(2)}, u32[]{:S(2)}) collective-permute-start(f32[6928]{0:T(1024)S(1)} %add.197), channel_id=1, source_target_pairs={{0,2},{1,3},{2,0},{3,1},{4,6},{5,7},{6,4},{7,5},{8,10},{9,11},{10,... | collective-permute-start | bytes 83144 | tf_op jit(solution)/shard_map/ppermute | solution.py:46
  124.2 4.9 %collective-permute-start.15 = (f32[6928]{0:T(1024)S(1)}, f32[6928]{0:T(1024)S(1)}, u32[]{:S(2)}, u32[]{:S(2)}) collective-permute-start(f32[6928]{0:T(1024)S(1)} %add.198), channel_id=1, source_target_pairs={{0,1},{1,0},{2,3},{3,2},{4,5},{5,4},{6,7},{7,6},{8,9},{9,8},{10,11... | collective-permute-start | bytes 83144 | tf_op jit(solution)/shard_map/ppermute | solution.py:46
  129.1 5.7 %collective-permute-start.16 = (f32[6928]{0:T(1024)S(1)}, f32[6928]{0:T(1024)S(1)}, u32[]{:S(2)}, u32[]{:S(2)}) collective-permute-start(f32[6928]{0:T(1024)S(1)} %add.199), channel_id=1, source_target_pairs={{0,256},{64,320},{128,384},{192,448},{256,0},{320,64},{384,128},{4... | collective-permute-start | bytes 83144 | tf_op jit(solution)/shard_map/ppermute | solution.py:46
  134.9 4.6 %collective-permute-start.17 = (f32[6928]{0:T(1024)S(1)}, f32[6928]{0:T(1024)S(1)}, u32[]{:S(2)}, u32[]{:S(2)}) collective-permute-start(f32[6928]{0:T(1024)S(1)} %add.200), channel_id=1, source_target_pairs={{0,128},{64,192},{128,0},{192,64},{256,384},{320,448},{384,256},{4... | collective-permute-start | bytes 83144 | tf_op jit(solution)/shard_map/ppermute | solution.py:46
  139.5 18.5 %collective-permute-start.18 = (f32[6928]{0:T(1024)S(1)}, f32[6928]{0:T(1024)S(1)}, u32[]{:S(2)}, u32[]{:S(2)}) collective-permute-start(f32[6928]{0:T(1024)S(1)} %add.201), channel_id=1, source_target_pairs={{0,64},{64,0},{128,192},{192,128},{256,320},{320,256},{384,448},{4... | collective-permute-start | bytes 83144 | tf_op jit(solution)/shard_map/ppermute | solution.py:46

commit v12 on v11

--- a/solution.py
+++ b/solution.py
@@ -115,7 +115,7 @@
         window = stacked_yz[:, :, shift_x : shift_x + planes]
         mixed = jnp.transpose(kernel[shift_x], (2, 0, 1, 3)).reshape(channels, -1)
         total = total + jnp.einsum(
-            "oc,bcxyz->boxyz", mixed, window, preferred_element_type=jnp.float32
+            "bcxyz,oc->boxyz", window, mixed, preferred_element_type=jnp.float32
         )
     hidden, slope = gelu_parts(total)
     grad_pre = (cotangent.astype(jnp.float32) * slope).astype(jnp.bfloat16)

time: 161 us -> 161 us (level)
  no operation moved by 1% of the time
where the time goes in v12:
time: 161 us; the launch traced here: 159 us
  starting transfers between devices  95.3 us (59%)
  waiting for transfers between devices  35.5 us (22%)
  between operations  10.8 us (7%)
  local copies, waits for them, and re-layouts  9.55 us (6%)
  other arithmetic  4.7 us (3%)
  matrix products  3.19 us (2%)
    ppermute x9, starting transfers between devices, butterfly_sum(): value = value + lax.ppermute(value, axis, pairs)  37.4 us
    ppermute x6, starting transfers between devices, routed(): arrived = lax.ppermute(jnp.concatenate(pieces, axis=2), axis, pairs)  34 us
    ppermute x9, waiting for transfers between devices, butterfly_sum(): value = value + lax.ppermute(value, axis, pairs)  21.6 us
    ppermute x6, waiting for transfers between devices, routed(): arrived = lax.ppermute(jnp.concatenate(pieces, axis=2), axis, pairs)  11.2 us
    ppermute x1, starting transfers between devices, neighbour_blocks(): across = lax.ppermute(value, axis, pairs)  10.8 us
    ppermute x1, starting transfers between devices, halo_planes(): across = lax.ppermute(jnp.where(even, first, last), axis, pairs)  9.28 us
    unnamed x14, local copies, waits for them, and re-layouts  4.12 us
  transfers between devices with their start and end apart: 19, of which 13 were waited for; matrix products, arithmetic and copies ran while one was open for 5% of the time, Pallas kernels for 0%

profile of v12, /device:TPU:1, one launch (start us, length us, event | category | flops | bytes accessed | tf_op | source)
XLA Modules:
  0.0 159.1 jit_solution(5454436588705961742)
XLA Ops:
  1.6 3.9 %collective-permute-start = (bf16[1,16,2,8,256]{4,1,3,2,0:T(8,128)(2,1)S(1)}, bf16[1,16,2,8,256]{4,1,3,2,0:T(8,128)(2,1)S(1)}, u32[]{:S(2)}, u32[]{:S(2)}) collective-permute-start(bf16[1,16,2,8,256]{4,1,3,2,0:T(8,128)(2,1)S(1)} %copy.24), channel_id=1, source_target_pairs={{0,1},{1,0},{2,3},{3,2},{4,5},{5,4},{6,7},{7,6},{8,9},{9,8},{10,11... | collective-permute-start | bytes 393224 | tf_op jit(solution)/shard_map/ppermute | solution.py:77
  5.6 1.4 fusion.85
  8.2 1.4 fusion.84
  11.9 4.4 %collective-permute-start.1 = (bf16[1,16,2,8,256]{4,1,3,2,0:T(8,128)(2,1)S(1)}, bf16[1,16,2,8,256]{4,1,3,2,0:T(8,128)(2,1)S(1)}, u32[]{:S(2)}, u32[]{:S(2)}) collective-permute-start(bf16[1,16,2,8,256]{4,1,3,2,0:T(8,128)(2,1)S(1)} %broadcast_select_fusion), channel_id=1, source_target_pairs={{0,2},{1,3},{2,0},{3,1},{4,6},{5,7},{6,4},{7,5},{8,10},{9,11},{10,... | collective-permute-start | bytes 393224 | tf_op jit(solution)/shard_map/ppermute | solution.py:77
  16.3 2.8 %collective-permute-done.1 = bf16[1,16,2,8,256]{4,1,3,2,0:T(8,128)(2,1)S(1)} collective-permute-done((bf16[1,16,2,8,256]{4,1,3,2,0:T(8,128)(2,1)S(1)}, bf16[1,16,2,8,256]{4,1,3,2,0:T(8,128)(2,1)S(1)}, u32[]{:S(2)}, u32[]{:S(2)}) %collective-permute-start.1) | collective-permute-done | bytes 131104 | tf_op jit(solution)/shard_map/ppermute | solution.py:77
  19.1 4.0 %collective-permute-start.2 = (bf16[1,16,2,8,256]{4,1,3,2,0:T(8,128)(2,1)S(1)}, bf16[1,16,2,8,256]{4,1,3,2,0:T(8,128)(2,1)S(1)}, u32[]{:S(2)}, u32[]{:S(2)}) collective-permute-start(bf16[1,16,2,8,256]{4,1,3,2,0:T(8,128)(2,1)S(1)} %broadcast_select_fusion.1), channel_id=1, source_target_pairs={{0,4},{1,5},{2,6},{3,7},{4,0},{5,1},{6,2},{7,3},{8,12},{9,13},{10,... | collective-permute-start | bytes 393224 | tf_op jit(solution)/shard_map/ppermute | solution.py:77
  23.2 2.3 %collective-permute-done.2 = bf16[1,16,2,8,256]{4,1,3,2,0:T(8,128)(2,1)S(1)} collective-permute-done((bf16[1,16,2,8,256]{4,1,3,2,0:T(8,128)(2,1)S(1)}, bf16[1,16,2,8,256]{4,1,3,2,0:T(8,128)(2,1)S(1)}, u32[]{:S(2)}, u32[]{:S(2)}) %collective-permute-start.2) | collective-permute-done | bytes 131104 | tf_op jit(solution)/shard_map/ppermute | solution.py:77
  25.5 5.8 %collective-permute-start.3 = (bf16[1,16,2,8,256]{4,1,3,2,0:T(8,128)(2,1)S(1)}, bf16[1,16,2,8,256]{4,1,3,2,0:T(8,128)(2,1)S(1)}, u32[]{:S(2)}, u32[]{:S(2)}) collective-permute-start(bf16[1,16,2,8,256]{4,1,3,2,0:T(8,128)(2,1)S(1)} %broadcast_select_fusion.2), channel_id=1, source_target_pairs={{0,8},{1,9},{2,10},{3,11},{4,12},{5,13},{6,14},{7,15},{8,0},{9,1},... | collective-permute-start | bytes 393224 | tf_op jit(solution)/shard_map/ppermute | solution.py:77
  31.4 3.7 %collective-permute-done.3 = bf16[1,16,2,8,256]{4,1,3,2,0:T(8,128)(2,1)S(1)} collective-permute-done((bf16[1,16,2,8,256]{4,1,3,2,0:T(8,128)(2,1)S(1)}, bf16[1,16,2,8,256]{4,1,3,2,0:T(8,128)(2,1)S(1)}, u32[]{:S(2)}, u32[]{:S(2)}) %collective-permute-start.3) | collective-permute-done | bytes 131104 | tf_op jit(solution)/shard_map/ppermute | solution.py:77
  35.1 8.4 %collective-permute-start.4 = (bf16[1,16,2,8,256]{4,1,3,2,0:T(8,128)(2,1)S(1)}, bf16[1,16,2,8,256]{4,1,3,2,0:T(8,128)(2,1)S(1)}, u32[]{:S(2)}, u32[]{:S(2)}) collective-permute-start(bf16[1,16,2,8,256]{4,1,3,2,0:T(8,128)(2,1)S(1)} %broadcast_select_fusion.3), channel_id=1, source_target_pairs={{0,16},{1,17},{2,18},{3,19},{4,20},{5,21},{6,22},{7,23},{8,24},{9,... | collective-permute-start | bytes 393224 | tf_op jit(solution)/shard_map/ppermute | solution.py:77
  43.6 2.5 %collective-permute-done.4 = bf16[1,16,2,8,256]{4,1,3,2,0:T(8,128)(2,1)S(1)} collective-permute-done((bf16[1,16,2,8,256]{4,1,3,2,0:T(8,128)(2,1)S(1)}, bf16[1,16,2,8,256]{4,1,3,2,0:T(8,128)(2,1)S(1)}, u32[]{:S(2)}, u32[]{:S(2)}) %collective-permute-start.4) | collective-permute-done | bytes 131104 | tf_op jit(solution)/shard_map/ppermute | solution.py:77
  46.1 7.5 %collective-permute-start.5 = (bf16[1,16,2,8,256]{4,1,3,2,0:T(8,128)(2,1)S(1)}, bf16[1,16,2,8,256]{4,1,3,2,0:T(8,128)(2,1)S(1)}, u32[]{:S(2)}, u32[]{:S(2)}) collective-permute-start(bf16[1,16,2,8,256]{4,1,3,2,0:T(8,128)(2,1)S(1)} %broadcast_select_fusion.4), channel_id=1, source_target_pairs={{0,32},{1,33},{2,34},{3,35},{4,36},{5,37},{6,38},{7,39},{8,40},{9,... | collective-permute-start | bytes 393224 | tf_op jit(solution)/shard_map/ppermute | solution.py:77
  60.2 10.8 %collective-permute-start.6 = (bf16[1,16,2,8,256]{4,1,3,2,0:T(8,128)(2,1)S(1)}, bf16[1,16,2,8,256]{4,1,3,2,0:T(8,128)(2,1)S(1)}, u32[]{:S(2)}, u32[]{:S(2)}) collective-permute-start(bf16[1,16,2,8,256]{4,1,3,2,0:T(8,128)(2,1)S(1)} %reverse_select_fusion), channel_id=1, source_target_pairs={{0,63},{1,2},{2,1},{3,4},{4,3},{5,6},{6,5},{7,8},{8,7},{9,10},{10,... | collective-permute-start | bytes 393224 | tf_op jit(solution)/shard_map/ppermute | solution.py:27
  71.0 1.9 %collective-permute-start.7 = (bf16[1,16,2,8,256]{4,1,3,2,0:T(8,128)(2,1)S(1)}, bf16[1,16,2,8,256]{4,1,3,2,0:T(8,128)(2,1)S(1)}, u32[]{:S(2)}, u32[]{:S(2)}) collective-permute-start(bf16[1,16,2,8,256]{4,1,3,2,0:T(8,128)(2,1)S(1)} %reverse_select_fusion), channel_id=1, source_target_pairs={{0,1},{1,0},{2,3},{3,2},{4,5},{5,4},{6,7},{7,6},{8,9},{9,8},{10,11... | collective-permute-start | bytes 393224 | tf_op jit(solution)/shard_map/ppermute | solution.py:25
  74.0 2.1 %collective-permute-done.6 = bf16[1,16,2,8,256]{4,1,3,2,0:T(8,128)(2,1)S(1)} collective-permute-done((bf16[1,16,2,8,256]{4,1,3,2,0:T(8,128)(2,1)S(1)}, bf16[1,16,2,8,256]{4,1,3,2,0:T(8,128)(2,1)S(1)}, u32[]{:S(2)}, u32[]{:S(2)}) %collective-permute-start.6) | collective-permute-done | bytes 131104 | tf_op jit(solution)/shard_map/ppermute | solution.py:27
  83.0 4.8 %collective-permute-start.10 = (f32[6928]{0:T(1024)S(1)}, f32[6928]{0:T(1024)S(1)}, u32[]{:S(2)}, u32[]{:S(2)}) collective-permute-start(f32[6928]{0:T(1024)S(1)} %pad_maximum_fusion.6), channel_id=1, source_target_pairs={{0,32},{1,33},{2,34},{3,35},{4,36},{5,37},{6,38},{7,39},{8,40},{9,... | collective-permute-start | bytes 83144 | tf_op jit(solution)/shard_map/ppermute | solution.py:46
  87.9 9.3 %collective-permute-start.8 = (bf16[1,16,1,8,256]{4,1,3,2,0:T(8,128)(2,1)S(1)}, bf16[1,16,1,8,256]{4,1,3,2,0:T(8,128)(2,1)S(1)}, u32[]{:S(2)}, u32[]{:S(2)}) collective-permute-start(bf16[1,16,1,8,256]{4,1,3,2,0:T(8,128)(2,1)S(1)} %get-tuple-element.75), channel_id=1, source_target_pairs={{0,63},{1,2},{2,1},{3,4},{4,3},{5,6},{6,5},{7,8},{8,7},{9,10},{10,... | collective-permute-start | bytes 196616 | tf_op jit(solution)/shard_map/ppermute | solution.py:37
  97.2 1.9 %collective-permute-start.9 = (bf16[1,16,1,8,256]{4,1,3,2,0:T(8,128)(2,1)S(1)}, bf16[1,16,1,8,256]{4,1,3,2,0:T(8,128)(2,1)S(1)}, u32[]{:S(2)}, u32[]{:S(2)}) collective-permute-start(bf16[1,16,1,8,256]{4,1,3,2,0:T(8,128)(2,1)S(1)} %get-tuple-element.76), channel_id=1, source_target_pairs={{0,1},{1,0},{2,3},{3,2},{4,5},{5,4},{6,7},{7,6},{8,9},{9,8},{10,11... | collective-permute-start | bytes 196616 | tf_op jit(solution)/shard_map/ppermute | solution.py:35
  99.1 1.9 %collective-permute-start.11 = (f32[6928]{0:T(1024)S(1)}, f32[6928]{0:T(1024)S(1)}, u32[]{:S(2)}, u32[]{:S(2)}) collective-permute-start(f32[6928]{0:T(1024)S(1)} %fusion.92), channel_id=1, source_target_pairs={{0,16},{1,17},{2,18},{3,19},{4,20},{5,21},{6,22},{7,23},{8,24},{9,... | collective-permute-start | bytes 83144 | tf_op jit(solution)/shard_map/ppermute | solution.py:46
  101.8 5.8 %collective-permute-done.11 = f32[6928]{0:T(1024)S(1)} collective-permute-done((f32[6928]{0:T(1024)S(1)}, f32[6928]{0:T(1024)S(1)}, u32[]{:S(2)}, u32[]{:S(2)}) %collective-permute-start.11) | collective-permute-done | bytes 27744 | tf_op jit(solution)/shard_map/ppermute | solution.py:46
  107.7 1.9 %collective-permute-start.12 = (f32[6928]{0:T(1024)S(1)}, f32[6928]{0:T(1024)S(1)}, u32[]{:S(2)}, u32[]{:S(2)}) collective-permute-start(f32[6928]{0:T(1024)S(1)} %add.203), channel_id=1, source_target_pairs={{0,8},{1,9},{2,10},{3,11},{4,12},{5,13},{6,14},{7,15},{8,0},{9,1},... | collective-permute-start | bytes 83144 | tf_op jit(solution)/shard_map/ppermute | solution.py:46
  111.1 2.1 %collective-permute-done.12 = f32[6928]{0:T(1024)S(1)} collective-permute-done((f32[6928]{0:T(1024)S(1)}, f32[6928]{0:T(1024)S(1)}, u32[]{:S(2)}, u32[]{:S(2)}) %collective-permute-start.12) | collective-permute-done | bytes 27744 | tf_op jit(solution)/shard_map/ppermute | solution.py:46
  113.2 1.9 %collective-permute-start.13 = (f32[6928]{0:T(1024)S(1)}, f32[6928]{0:T(1024)S(1)}, u32[]{:S(2)}, u32[]{:S(2)}) collective-permute-start(f32[6928]{0:T(1024)S(1)} %add.204), channel_id=1, source_target_pairs={{0,4},{1,5},{2,6},{3,7},{4,0},{5,1},{6,2},{7,3},{8,12},{9,13},{10,... | collective-permute-start | bytes 83144 | tf_op jit(solution)/shard_map/ppermute | solution.py:46
  115.2 2.6 %collective-permute-done.13 = f32[6928]{0:T(1024)S(1)} collective-permute-done((f32[6928]{0:T(1024)S(1)}, f32[6928]{0:T(1024)S(1)}, u32[]{:S(2)}, u32[]{:S(2)}) %collective-permute-start.13) | collective-permute-done | bytes 27744 | tf_op jit(solution)/shard_map/ppermute | solution.py:46
  117.8 1.9 %collective-permute-start.14 = (f32[6928]{0:T(1024)S(1)}, f32[6928]{0:T(1024)S(1)}, u32[]{:S(2)}, u32[]{:S(2)}) collective-permute-start(f32[6928]{0:T(1024)S(1)} %add.205), channel_id=1, source_target_pairs={{0,2},{1,3},{2,0},{3,1},{4,6},{5,7},{6,4},{7,5},{8,10},{9,11},{10,... | collective-permute-start | bytes 83144 | tf_op jit(solution)/shard_map/ppermute | solution.py:46
  119.7 4.2 %collective-permute-done.14 = f32[6928]{0:T(1024)S(1)} collective-permute-done((f32[6928]{0:T(1024)S(1)}, f32[6928]{0:T(1024)S(1)}, u32[]{:S(2)}, u32[]{:S(2)}) %collective-permute-start.14) | collective-permute-done | bytes 27744 | tf_op jit(solution)/shard_map/ppermute | solution.py:46
  123.9 3.7 %collective-permute-start.15 = (f32[6928]{0:T(1024)S(1)}, f32[6928]{0:T(1024)S(1)}, u32[]{:S(2)}, u32[]{:S(2)}) collective-permute-start(f32[6928]{0:T(1024)S(1)} %add.206), channel_id=1, source_target_pairs={{0,1},{1,0},{2,3},{3,2},{4,5},{5,4},{6,7},{7,6},{8,9},{9,8},{10,11... | collective-permute-start | bytes 83144 | tf_op jit(solution)/shard_map/ppermute | solution.py:46
  128.8 1.9 %collective-permute-start.16 = (f32[6928]{0:T(1024)S(1)}, f32[6928]{0:T(1024)S(1)}, u32[]{:S(2)}, u32[]{:S(2)}) collective-permute-start(f32[6928]{0:T(1024)S(1)} %add.207), channel_id=1, source_target_pairs={{0,256},{64,320},{128,384},{192,448},{256,0},{320,64},{384,128},{4... | collective-permute-start | bytes 83144 | tf_op jit(solution)/shard_map/ppermute | solution.py:46
  131.0 3.5 %collective-permute-done.16 = f32[6928]{0:T(1024)S(1)} collective-permute-done((f32[6928]{0:T(1024)S(1)}, f32[6928]{0:T(1024)S(1)}, u32[]{:S(2)}, u32[]{:S(2)}) %collective-permute-start.16) | collective-permute-done | bytes 27744 | tf_op jit(solution)/shard_map/ppermute | solution.py:46
  134.5 1.9 %collective-permute-start.17 = (f32[6928]{0:T(1024)S(1)}, f32[6928]{0:T(1024)S(1)}, u32[]{:S(2)}, u32[]{:S(2)}) collective-permute-start(f32[6928]{0:T(1024)S(1)} %add.208), channel_id=1, source_target_pairs={{0,128},{64,192},{128,0},{192,64},{256,384},{320,448},{384,256},{4... | collective-permute-start | bytes 83144 | tf_op jit(solution)/shard_map/ppermute | solution.py:46
  136.8 2.4 %collective-permute-done.17 = f32[6928]{0:T(1024)S(1)} collective-permute-done((f32[6928]{0:T(1024)S(1)}, f32[6928]{0:T(1024)S(1)}, u32[]{:S(2)}, u32[]{:S(2)}) %collective-permute-start.17) | collective-permute-done | bytes 27744 | tf_op jit(solution)/shard_map/ppermute | solution.py:46
  139.1 17.4 %collective-permute-start.18 = (f32[6928]{0:T(1024)S(1)}, f32[6928]{0:T(1024)S(1)}, u32[]{:S(2)}, u32[]{:S(2)}) collective-permute-start(f32[6928]{0:T(1024)S(1)} %add.209), channel_id=1, source_target_pairs={{0,64},{64,0},{128,192},{192,128},{256,320},{320,256},{384,448},{4... | collective-permute-start | bytes 83144 | tf_op jit(solution)/shard_map/ppermute | solution.py:46
  (105 shorter events, 16.4 us)
Async XLA Ops:
  0.6 72.3 %copy-start = (bf16[27,16,16]{0,2,1:T(8,128)(2,1)S(1)}, bf16[27,16,16]{0,2,1:T(8,128)(2,1)}, u32[]{:S(2)}) copy-start(bf16[27,16,16]{0,2,1:T(8,128)(2,1)} %param.13) | copy-start | bytes 41476
  1.6 9.3 %collective-permute-start = (bf16[1,16,2,8,256]{4,1,3,2,0:T(8,128)(2,1)S(1)}, bf16[1,16,2,8,256]{4,1,3,2,0:T(8,128)(2,1)S(1)}, u32[]{:S(2)}, u32[]{:S(2)}) collective-permute-start(bf16[1,16,2,8,256]{4,1,3,2,0:T(8,128)(2,1)S(1)} %copy.24), channel_id=1, source_target_pairs={{0,1},{1,0},{2,3},{3,2},{4,5},{5,4},{6,7},{7,6},{8,9},{9,8},{10,11... | collective-permute-start | bytes 393224 | tf_op jit(solution)/shard_map/ppermute | solution.py:77
  11.9 7.2 %collective-permute-start.1 = (bf16[1,16,2,8,256]{4,1,3,2,0:T(8,128)(2,1)S(1)}, bf16[1,16,2,8,256]{4,1,3,2,0:T(8,128)(2,1)S(1)}, u32[]{:S(2)}, u32[]{:S(2)}) collective-permute-start(bf16[1,16,2,8,256]{4,1,3,2,0:T(8,128)(2,1)S(1)} %broadcast_select_fusion), channel_id=1, source_target_pairs={{0,2},{1,3},{2,0},{3,1},{4,6},{5,7},{6,4},{7,5},{8,10},{9,11},{10,... | collective-permute-start | bytes 393224 | tf_op jit(solution)/shard_map/ppermute | solution.py:77
  19.1 6.4 %collective-permute-start.2 = (bf16[1,16,2,8,256]{4,1,3,2,0:T(8,128)(2,1)S(1)}, bf16[1,16,2,8,256]{4,1,3,2,0:T(8,128)(2,1)S(1)}, u32[]{:S(2)}, u32[]{:S(2)}) collective-permute-start(bf16[1,16,2,8,256]{4,1,3,2,0:T(8,128)(2,1)S(1)} %broadcast_select_fusion.1), channel_id=1, source_target_pairs={{0,4},{1,5},{2,6},{3,7},{4,0},{5,1},{6,2},{7,3},{8,12},{9,13},{10,... | collective-permute-start | bytes 393224 | tf_op jit(solution)/shard_map/ppermute | solution.py:77
  25.5 9.6 %collective-permute-start.3 = (bf16[1,16,2,8,256]{4,1,3,2,0:T(8,128)(2,1)S(1)}, bf16[1,16,2,8,256]{4,1,3,2,0:T(8,128)(2,1)S(1)}, u32[]{:S(2)}, u32[]{:S(2)}) collective-permute-start(bf16[1,16,2,8,256]{4,1,3,2,0:T(8,128)(2,1)S(1)} %broadcast_select_fusion.2), channel_id=1, source_target_pairs={{0,8},{1,9},{2,10},{3,11},{4,12},{5,13},{6,14},{7,15},{8,0},{9,1},... | collective-permute-start | bytes 393224 | tf_op jit(solution)/shard_map/ppermute | solution.py:77
  35.1 11.0 %collective-permute-start.4 = (bf16[1,16,2,8,256]{4,1,3,2,0:T(8,128)(2,1)S(1)}, bf16[1,16,2,8,256]{4,1,3,2,0:T(8,128)(2,1)S(1)}, u32[]{:S(2)}, u32[]{:S(2)}) collective-permute-start(bf16[1,16,2,8,256]{4,1,3,2,0:T(8,128)(2,1)S(1)} %broadcast_select_fusion.3), channel_id=1, source_target_pairs={{0,16},{1,17},{2,18},{3,19},{4,20},{5,21},{6,22},{7,23},{8,24},{9,... | collective-permute-start | bytes 393224 | tf_op jit(solution)/shard_map/ppermute | solution.py:77
  46.1 14.1 %collective-permute-start.5 = (bf16[1,16,2,8,256]{4,1,3,2,0:T(8,128)(2,1)S(1)}, bf16[1,16,2,8,256]{4,1,3,2,0:T(8,128)(2,1)S(1)}, u32[]{:S(2)}, u32[]{:S(2)}) collective-permute-start(bf16[1,16,2,8,256]{4,1,3,2,0:T(8,128)(2,1)S(1)} %broadcast_select_fusion.4), channel_id=1, source_target_pairs={{0,32},{1,33},{2,34},{3,35},{4,36},{5,37},{6,38},{7,39},{8,40},{9,... | collective-permute-start | bytes 393224 | tf_op jit(solution)/shard_map/ppermute | solution.py:77
  60.2 15.9 %collective-permute-start.6 = (bf16[1,16,2,8,256]{4,1,3,2,0:T(8,128)(2,1)S(1)}, bf16[1,16,2,8,256]{4,1,3,2,0:T(8,128)(2,1)S(1)}, u32[]{:S(2)}, u32[]{:S(2)}) collective-permute-start(bf16[1,16,2,8,256]{4,1,3,2,0:T(8,128)(2,1)S(1)} %reverse_select_fusion), channel_id=1, source_target_pairs={{0,63},{1,2},{2,1},{3,4},{4,3},{5,6},{6,5},{7,8},{8,7},{9,10},{10,... | collective-permute-start | bytes 393224 | tf_op jit(solution)/shard_map/ppermute | solution.py:27
  71.0 5.7 %collective-permute-start.7 = (bf16[1,16,2,8,256]{4,1,3,2,0:T(8,128)(2,1)S(1)}, bf16[1,16,2,8,256]{4,1,3,2,0:T(8,128)(2,1)S(1)}, u32[]{:S(2)}, u32[]{:S(2)}) collective-permute-start(bf16[1,16,2,8,256]{4,1,3,2,0:T(8,128)(2,1)S(1)} %reverse_select_fusion), channel_id=1, source_target_pairs={{0,1},{1,0},{2,3},{3,2},{4,5},{5,4},{6,7},{7,6},{8,9},{9,8},{10,11... | collective-permute-start | bytes 393224 | tf_op jit(solution)/shard_map/ppermute | solution.py:25
  80.0 0.9 copy-start.1
  80.0 0.9 copy-start.2
  83.0 16.1 %collective-permute-start.10 = (f32[6928]{0:T(1024)S(1)}, f32[6928]{0:T(1024)S(1)}, u32[]{:S(2)}, u32[]{:S(2)}) collective-permute-start(f32[6928]{0:T(1024)S(1)} %pad_maximum_fusion.6), channel_id=1, source_target_pairs={{0,32},{1,33},{2,34},{3,35},{4,36},{5,37},{6,38},{7,39},{8,40},{9,... | collective-permute-start | bytes 83144 | tf_op jit(solution)/shard_map/ppermute | solution.py:46
  87.9 21.7 %collective-permute-start.8 = (bf16[1,16,1,8,256]{4,1,3,2,0:T(8,128)(2,1)S(1)}, bf16[1,16,1,8,256]{4,1,3,2,0:T(8,128)(2,1)S(1)}, u32[]{:S(2)}, u32[]{:S(2)}) collective-permute-start(bf16[1,16,1,8,256]{4,1,3,2,0:T(8,128)(2,1)S(1)} %get-tuple-element.75), channel_id=1, source_target_pairs={{0,63},{1,2},{2,1},{3,4},{4,3},{5,6},{6,5},{7,8},{8,7},{9,10},{10,... | collective-permute-start | bytes 196616 | tf_op jit(solution)/shard_map/ppermute | solution.py:37
  97.2 12.4 %collective-permute-start.9 = (bf16[1,16,1,8,256]{4,1,3,2,0:T(8,128)(2,1)S(1)}, bf16[1,16,1,8,256]{4,1,3,2,0:T(8,128)(2,1)S(1)}, u32[]{:S(2)}, u32[]{:S(2)}) collective-permute-start(bf16[1,16,1,8,256]{4,1,3,2,0:T(8,128)(2,1)S(1)} %get-tuple-element.76), channel_id=1, source_target_pairs={{0,1},{1,0},{2,3},{3,2},{4,5},{5,4},{6,7},{7,6},{8,9},{9,8},{10,11... | collective-permute-start | bytes 196616 | tf_op jit(solution)/shard_map/ppermute | solution.py:35
  99.1 8.5 %collective-permute-start.11 = (f32[6928]{0:T(1024)S(1)}, f32[6928]{0:T(1024)S(1)}, u32[]{:S(2)}, u32[]{:S(2)}) collective-permute-start(f32[6928]{0:T(1024)S(1)} %fusion.92), channel_id=1, source_target_pairs={{0,16},{1,17},{2,18},{3,19},{4,20},{5,21},{6,22},{7,23},{8,24},{9,... | collective-permute-start | bytes 83144 | tf_op jit(solution)/shard_map/ppermute | solution.py:46
  107.7 5.5 %collective-permute-start.12 = (f32[6928]{0:T(1024)S(1)}, f32[6928]{0:T(1024)S(1)}, u32[]{:S(2)}, u32[]{:S(2)}) collective-permute-start(f32[6928]{0:T(1024)S(1)} %add.203), channel_id=1, source_target_pairs={{0,8},{1,9},{2,10},{3,11},{4,12},{5,13},{6,14},{7,15},{8,0},{9,1},... | collective-permute-start | bytes 83144 | tf_op jit(solution)/shard_map/ppermute | solution.py:46
  113.2 4.6 %collective-permute-start.13 = (f32[6928]{0:T(1024)S(1)}, f32[6928]{0:T(1024)S(1)}, u32[]{:S(2)}, u32[]{:S(2)}) collective-permute-start(f32[6928]{0:T(1024)S(1)} %add.204), channel_id=1, source_target_pairs={{0,4},{1,5},{2,6},{3,7},{4,0},{5,1},{6,2},{7,3},{8,12},{9,13},{10,... | collective-permute-start | bytes 83144 | tf_op jit(solution)/shard_map/ppermute | solution.py:46
  117.8 6.1 %collective-permute-start.14 = (f32[6928]{0:T(1024)S(1)}, f32[6928]{0:T(1024)S(1)}, u32[]{:S(2)}, u32[]{:S(2)}) collective-permute-start(f32[6928]{0:T(1024)S(1)} %add.205), channel_id=1, source_target_pairs={{0,2},{1,3},{2,0},{3,1},{4,6},{5,7},{6,4},{7,5},{8,10},{9,11},{10,... | collective-permute-start | bytes 83144 | tf_op jit(solution)/shard_map/ppermute | solution.py:46
  123.9 4.9 %collective-permute-start.15 = (f32[6928]{0:T(1024)S(1)}, f32[6928]{0:T(1024)S(1)}, u32[]{:S(2)}, u32[]{:S(2)}) collective-permute-start(f32[6928]{0:T(1024)S(1)} %add.206), channel_id=1, source_target_pairs={{0,1},{1,0},{2,3},{3,2},{4,5},{5,4},{6,7},{7,6},{8,9},{9,8},{10,11... | collective-permute-start | bytes 83144 | tf_op jit(solution)/shard_map/ppermute | solution.py:46
  128.8 5.7 %collective-permute-start.16 = (f32[6928]{0:T(1024)S(1)}, f32[6928]{0:T(1024)S(1)}, u32[]{:S(2)}, u32[]{:S(2)}) collective-permute-start(f32[6928]{0:T(1024)S(1)} %add.207), channel_id=1, source_target_pairs={{0,256},{64,320},{128,384},{192,448},{256,0},{320,64},{384,128},{4... | collective-permute-start | bytes 83144 | tf_op jit(solution)/shard_map/ppermute | solution.py:46
  134.5 4.6 %collective-permute-start.17 = (f32[6928]{0:T(1024)S(1)}, f32[6928]{0:T(1024)S(1)}, u32[]{:S(2)}, u32[]{:S(2)}) collective-permute-start(f32[6928]{0:T(1024)S(1)} %add.208), channel_id=1, source_target_pairs={{0,128},{64,192},{128,0},{192,64},{256,384},{320,448},{384,256},{4... | collective-permute-start | bytes 83144 | tf_op jit(solution)/shard_map/ppermute | solution.py:46
  139.1 18.5 %collective-permute-start.18 = (f32[6928]{0:T(1024)S(1)}, f32[6928]{0:T(1024)S(1)}, u32[]{:S(2)}, u32[]{:S(2)}) collective-permute-start(f32[6928]{0:T(1024)S(1)} %add.209), channel_id=1, source_target_pairs={{0,64},{64,0},{128,192},{192,128},{256,320},{320,256},{384,448},{4... | collective-permute-start | bytes 83144 | tf_op jit(solution)/shard_map/ppermute | solution.py:46

commit v13 on v12

--- a/solution.py
+++ b/solution.py
@@ -128,7 +128,7 @@
         grad_list.append(part.reshape(9, channels, channels))
     grad_b = jnp.sum(grad_pre.astype(jnp.float32), axis=(0, 2, 3, 4))
     stacked = jnp.concatenate([jnp.concatenate(grad_list, axis=0).reshape(-1), grad_b])
-    summed = butterfly_sum(butterfly_sum(stacked, "gx"), "dp")
+    summed = butterfly_sum(butterfly_sum(stacked, "dp"), "gx")
     grad_pad = jnp.concatenate([grad_before, grad_pre, grad_after], axis=2)
     rolled_back = [(e - 1, h - 1) for e in range(3) for h in range(3)]
     grad_yz = jnp.concatenate([jnp.roll(grad_pad, r, axis=(3, 4)) for r in rolled_back], axis=1)

time: 161 us -> 163 us (1.012)
  the two profiles are of different devices: /device:TPU:1 before, /device:TPU:26 now
where the time goes in v13:
time: 163 us; the launch traced here: 162 us
  starting transfers between devices  84.7 us (52%)
  waiting for transfers between devices  48.9 us (30%)
  between operations  10.9 us (7%)
  local copies, waits for them, and re-layouts  9.55 us (6%)
  other arithmetic  4.7 us (3%)
  matrix products  3.21 us (2%)
    ppermute x9, waiting for transfers between devices, butterfly_sum(): value = value + lax.ppermute(value, axis, pairs)  33.9 us
    ppermute x6, starting transfers between devices, routed(): arrived = lax.ppermute(jnp.concatenate(pieces, axis=2), axis, pairs)  32.9 us
    ppermute x9, starting transfers between devices, butterfly_sum(): value = value + lax.ppermute(value, axis, pairs)  20.3 us
    ppermute x1, starting transfers between devices, neighbour_blocks(): near = lax.ppermute(value, axis, [(s, s ^ 1) for s in range(count)])  14.1 us
    ppermute x6, waiting for transfers between devices, routed(): arrived = lax.ppermute(jnp.concatenate(pieces, axis=2), axis, pairs)  13.1 us
    ppermute x1, starting transfers between devices, halo_planes(): lax.ppermute(jnp.where(even, last, first), axis, [(s, s ^ 1) for s in ran...  11.4 us
    unnamed x14, local copies, waits for them, and re-layouts  4.12 us
    ppermute x1, starting transfers between devices, neighbour_blocks(): across = lax.ppermute(value, axis, pairs)  4.06 us
  transfers between devices with their start and end apart: 19, of which 12 were waited for; matrix products, arithmetic and copies ran while one was open for 5% of the time, Pallas kernels for 0%

profile of v13, /device:TPU:26, one launch (start us, length us, event | category | flops | bytes accessed | tf_op | source)
XLA Modules:
  0.0 161.9 jit_solution(11728570207604549867)
XLA Ops:
  1.6 2.4 %collective-permute-start = (bf16[1,16,2,8,256]{4,1,3,2,0:T(8,128)(2,1)S(1)}, bf16[1,16,2,8,256]{4,1,3,2,0:T(8,128)(2,1)S(1)}, u32[]{:S(2)}, u32[]{:S(2)}) collective-permute-start(bf16[1,16,2,8,256]{4,1,3,2,0:T(8,128)(2,1)S(1)} %copy.24), channel_id=1, source_target_pairs={{0,1},{1,0},{2,3},{3,2},{4,5},{5,4},{6,7},{7,6},{8,9},{9,8},{10,11... | collective-permute-start | bytes 393224 | tf_op jit(solution)/shard_map/ppermute | solution.py:77
  6.7 1.4 fusion.84
  10.4 4.3 %collective-permute-start.1 = (bf16[1,16,2,8,256]{4,1,3,2,0:T(8,128)(2,1)S(1)}, bf16[1,16,2,8,256]{4,1,3,2,0:T(8,128)(2,1)S(1)}, u32[]{:S(2)}, u32[]{:S(2)}) collective-permute-start(bf16[1,16,2,8,256]{4,1,3,2,0:T(8,128)(2,1)S(1)} %broadcast_select_fusion), channel_id=1, source_target_pairs={{0,2},{1,3},{2,0},{3,1},{4,6},{5,7},{6,4},{7,5},{8,10},{9,11},{10,... | collective-permute-start | bytes 393224 | tf_op jit(solution)/shard_map/ppermute | solution.py:77
  14.8 3.9 %collective-permute-done.1 = bf16[1,16,2,8,256]{4,1,3,2,0:T(8,128)(2,1)S(1)} collective-permute-done((bf16[1,16,2,8,256]{4,1,3,2,0:T(8,128)(2,1)S(1)}, bf16[1,16,2,8,256]{4,1,3,2,0:T(8,128)(2,1)S(1)}, u32[]{:S(2)}, u32[]{:S(2)}) %collective-permute-start.1) | collective-permute-done | bytes 131104 | tf_op jit(solution)/shard_map/ppermute | solution.py:77
  18.8 4.3 %collective-permute-start.2 = (bf16[1,16,2,8,256]{4,1,3,2,0:T(8,128)(2,1)S(1)}, bf16[1,16,2,8,256]{4,1,3,2,0:T(8,128)(2,1)S(1)}, u32[]{:S(2)}, u32[]{:S(2)}) collective-permute-start(bf16[1,16,2,8,256]{4,1,3,2,0:T(8,128)(2,1)S(1)} %broadcast_select_fusion.1), channel_id=1, source_target_pairs={{0,4},{1,5},{2,6},{3,7},{4,0},{5,1},{6,2},{7,3},{8,12},{9,13},{10,... | collective-permute-start | bytes 393224 | tf_op jit(solution)/shard_map/ppermute | solution.py:77
  23.1 2.9 %collective-permute-done.2 = bf16[1,16,2,8,256]{4,1,3,2,0:T(8,128)(2,1)S(1)} collective-permute-done((bf16[1,16,2,8,256]{4,1,3,2,0:T(8,128)(2,1)S(1)}, bf16[1,16,2,8,256]{4,1,3,2,0:T(8,128)(2,1)S(1)}, u32[]{:S(2)}, u32[]{:S(2)}) %collective-permute-start.2) | collective-permute-done | bytes 131104 | tf_op jit(solution)/shard_map/ppermute | solution.py:77
  26.0 6.1 %collective-permute-start.3 = (bf16[1,16,2,8,256]{4,1,3,2,0:T(8,128)(2,1)S(1)}, bf16[1,16,2,8,256]{4,1,3,2,0:T(8,128)(2,1)S(1)}, u32[]{:S(2)}, u32[]{:S(2)}) collective-permute-start(bf16[1,16,2,8,256]{4,1,3,2,0:T(8,128)(2,1)S(1)} %broadcast_select_fusion.2), channel_id=1, source_target_pairs={{0,8},{1,9},{2,10},{3,11},{4,12},{5,13},{6,14},{7,15},{8,0},{9,1},... | collective-permute-start | bytes 393224 | tf_op jit(solution)/shard_map/ppermute | solution.py:77
  32.2 2.9 %collective-permute-done.3 = bf16[1,16,2,8,256]{4,1,3,2,0:T(8,128)(2,1)S(1)} collective-permute-done((bf16[1,16,2,8,256]{4,1,3,2,0:T(8,128)(2,1)S(1)}, bf16[1,16,2,8,256]{4,1,3,2,0:T(8,128)(2,1)S(1)}, u32[]{:S(2)}, u32[]{:S(2)}) %collective-permute-start.3) | collective-permute-done | bytes 131104 | tf_op jit(solution)/shard_map/ppermute | solution.py:77
  35.1 10.7 %collective-permute-start.4 = (bf16[1,16,2,8,256]{4,1,3,2,0:T(8,128)(2,1)S(1)}, bf16[1,16,2,8,256]{4,1,3,2,0:T(8,128)(2,1)S(1)}, u32[]{:S(2)}, u32[]{:S(2)}) collective-permute-start(bf16[1,16,2,8,256]{4,1,3,2,0:T(8,128)(2,1)S(1)} %broadcast_select_fusion.3), channel_id=1, source_target_pairs={{0,16},{1,17},{2,18},{3,19},{4,20},{5,21},{6,22},{7,23},{8,24},{9,... | collective-permute-start | bytes 393224 | tf_op jit(solution)/shard_map/ppermute | solution.py:77
  45.9 3.4 %collective-permute-done.4 = bf16[1,16,2,8,256]{4,1,3,2,0:T(8,128)(2,1)S(1)} collective-permute-done((bf16[1,16,2,8,256]{4,1,3,2,0:T(8,128)(2,1)S(1)}, bf16[1,16,2,8,256]{4,1,3,2,0:T(8,128)(2,1)S(1)}, u32[]{:S(2)}, u32[]{:S(2)}) %collective-permute-start.4) | collective-permute-done | bytes 131104 | tf_op jit(solution)/shard_map/ppermute | solution.py:77
  49.3 5.0 %collective-permute-start.5 = (bf16[1,16,2,8,256]{4,1,3,2,0:T(8,128)(2,1)S(1)}, bf16[1,16,2,8,256]{4,1,3,2,0:T(8,128)(2,1)S(1)}, u32[]{:S(2)}, u32[]{:S(2)}) collective-permute-start(bf16[1,16,2,8,256]{4,1,3,2,0:T(8,128)(2,1)S(1)} %broadcast_select_fusion.4), channel_id=1, source_target_pairs={{0,32},{1,33},{2,34},{3,35},{4,36},{5,37},{6,38},{7,39},{8,40},{9,... | collective-permute-start | bytes 393224 | tf_op jit(solution)/shard_map/ppermute | solution.py:77
  61.0 4.1 %collective-permute-start.6 = (bf16[1,16,2,8,256]{4,1,3,2,0:T(8,128)(2,1)S(1)}, bf16[1,16,2,8,256]{4,1,3,2,0:T(8,128)(2,1)S(1)}, u32[]{:S(2)}, u32[]{:S(2)}) collective-permute-start(bf16[1,16,2,8,256]{4,1,3,2,0:T(8,128)(2,1)S(1)} %reverse_select_fusion), channel_id=1, source_target_pairs={{0,63},{1,2},{2,1},{3,4},{4,3},{5,6},{6,5},{7,8},{8,7},{9,10},{10,... | collective-permute-start | bytes 393224 | tf_op jit(solution)/shard_map/ppermute | solution.py:27
  65.1 14.1 %collective-permute-start.7 = (bf16[1,16,2,8,256]{4,1,3,2,0:T(8,128)(2,1)S(1)}, bf16[1,16,2,8,256]{4,1,3,2,0:T(8,128)(2,1)S(1)}, u32[]{:S(2)}, u32[]{:S(2)}) collective-permute-start(bf16[1,16,2,8,256]{4,1,3,2,0:T(8,128)(2,1)S(1)} %reverse_select_fusion), channel_id=1, source_target_pairs={{0,1},{1,0},{2,3},{3,2},{4,5},{5,4},{6,7},{7,6},{8,9},{9,8},{10,11... | collective-permute-start | bytes 393224 | tf_op jit(solution)/shard_map/ppermute | solution.py:25
  80.3 1.9 %collective-permute-done.7 = bf16[1,16,2,8,256]{4,1,3,2,0:T(8,128)(2,1)S(1)} collective-permute-done((bf16[1,16,2,8,256]{4,1,3,2,0:T(8,128)(2,1)S(1)}, bf16[1,16,2,8,256]{4,1,3,2,0:T(8,128)(2,1)S(1)}, u32[]{:S(2)}, u32[]{:S(2)}) %collective-permute-start.7) | collective-permute-done | bytes 131104 | tf_op jit(solution)/shard_map/ppermute | solution.py:25
  88.5 4.6 %collective-permute-start.10 = (f32[6928]{0:T(1024)S(1)}, f32[6928]{0:T(1024)S(1)}, u32[]{:S(2)}, u32[]{:S(2)}) collective-permute-start(f32[6928]{0:T(1024)S(1)} %pad_maximum_fusion.6), channel_id=1, source_target_pairs={{0,256},{64,320},{128,384},{192,448},{256,0},{320,64},{384,128},{4... | collective-permute-start | bytes 83144 | tf_op jit(solution)/shard_map/ppermute | solution.py:46
  93.1 1.9 %collective-permute-start.8 = (bf16[1,16,1,8,256]{4,1,3,2,0:T(8,128)(2,1)S(1)}, bf16[1,16,1,8,256]{4,1,3,2,0:T(8,128)(2,1)S(1)}, u32[]{:S(2)}, u32[]{:S(2)}) collective-permute-start(bf16[1,16,1,8,256]{4,1,3,2,0:T(8,128)(2,1)S(1)} %get-tuple-element.75), channel_id=1, source_target_pairs={{0,63},{1,2},{2,1},{3,4},{4,3},{5,6},{6,5},{7,8},{8,7},{9,10},{10,... | collective-permute-start | bytes 196616 | tf_op jit(solution)/shard_map/ppermute | solution.py:37
  95.0 11.4 %collective-permute-start.9 = (bf16[1,16,1,8,256]{4,1,3,2,0:T(8,128)(2,1)S(1)}, bf16[1,16,1,8,256]{4,1,3,2,0:T(8,128)(2,1)S(1)}, u32[]{:S(2)}, u32[]{:S(2)}) collective-permute-start(bf16[1,16,1,8,256]{4,1,3,2,0:T(8,128)(2,1)S(1)} %get-tuple-element.76), channel_id=1, source_target_pairs={{0,1},{1,0},{2,3},{3,2},{4,5},{5,4},{6,7},{7,6},{8,9},{9,8},{10,11... | collective-permute-start | bytes 196616 | tf_op jit(solution)/shard_map/ppermute | solution.py:35
  106.4 1.9 %collective-permute-start.11 = (f32[6928]{0:T(1024)S(1)}, f32[6928]{0:T(1024)S(1)}, u32[]{:S(2)}, u32[]{:S(2)}) collective-permute-start(f32[6928]{0:T(1024)S(1)} %fusion.92), channel_id=1, source_target_pairs={{0,128},{64,192},{128,0},{192,64},{256,384},{320,448},{384,256},{4... | collective-permute-start | bytes 83144 | tf_op jit(solution)/shard_map/ppermute | solution.py:46
  109.1 3.1 %collective-permute-done.11 = f32[6928]{0:T(1024)S(1)} collective-permute-done((f32[6928]{0:T(1024)S(1)}, f32[6928]{0:T(1024)S(1)}, u32[]{:S(2)}, u32[]{:S(2)}) %collective-permute-start.11) | collective-permute-done | bytes 27744 | tf_op jit(solution)/shard_map/ppermute | solution.py:46
  112.2 1.9 %collective-permute-start.12 = (f32[6928]{0:T(1024)S(1)}, f32[6928]{0:T(1024)S(1)}, u32[]{:S(2)}, u32[]{:S(2)}) collective-permute-start(f32[6928]{0:T(1024)S(1)} %add.203), channel_id=1, source_target_pairs={{0,64},{64,0},{128,192},{192,128},{256,320},{320,256},{384,448},{4... | collective-permute-start | bytes 83144 | tf_op jit(solution)/shard_map/ppermute | solution.py:46
  115.7 2.3 %collective-permute-start.13 = (f32[6928]{0:T(1024)S(1)}, f32[6928]{0:T(1024)S(1)}, u32[]{:S(2)}, u32[]{:S(2)}) collective-permute-start(f32[6928]{0:T(1024)S(1)} %add.204), channel_id=1, source_target_pairs={{0,32},{1,33},{2,34},{3,35},{4,36},{5,37},{6,38},{7,39},{8,40},{9,... | collective-permute-start | bytes 83144 | tf_op jit(solution)/shard_map/ppermute | solution.py:46
  118.1 7.2 %collective-permute-done.13 = f32[6928]{0:T(1024)S(1)} collective-permute-done((f32[6928]{0:T(1024)S(1)}, f32[6928]{0:T(1024)S(1)}, u32[]{:S(2)}, u32[]{:S(2)}) %collective-permute-start.13) | collective-permute-done | bytes 27744 | tf_op jit(solution)/shard_map/ppermute | solution.py:46
  125.3 1.9 %collective-permute-start.14 = (f32[6928]{0:T(1024)S(1)}, f32[6928]{0:T(1024)S(1)}, u32[]{:S(2)}, u32[]{:S(2)}) collective-permute-start(f32[6928]{0:T(1024)S(1)} %add.205), channel_id=1, source_target_pairs={{0,16},{1,17},{2,18},{3,19},{4,20},{5,21},{6,22},{7,23},{8,24},{9,... | collective-permute-start | bytes 83144 | tf_op jit(solution)/shard_map/ppermute | solution.py:46
  127.3 7.7 %collective-permute-done.14 = f32[6928]{0:T(1024)S(1)} collective-permute-done((f32[6928]{0:T(1024)S(1)}, f32[6928]{0:T(1024)S(1)}, u32[]{:S(2)}, u32[]{:S(2)}) %collective-permute-start.14) | collective-permute-done | bytes 27744 | tf_op jit(solution)/shard_map/ppermute | solution.py:46
  135.0 1.9 %collective-permute-start.15 = (f32[6928]{0:T(1024)S(1)}, f32[6928]{0:T(1024)S(1)}, u32[]{:S(2)}, u32[]{:S(2)}) collective-permute-start(f32[6928]{0:T(1024)S(1)} %add.206), channel_id=1, source_target_pairs={{0,8},{1,9},{2,10},{3,11},{4,12},{5,13},{6,14},{7,15},{8,0},{9,1},... | collective-permute-start | bytes 83144 | tf_op jit(solution)/shard_map/ppermute | solution.py:46
  137.1 4.6 %collective-permute-done.15 = f32[6928]{0:T(1024)S(1)} collective-permute-done((f32[6928]{0:T(1024)S(1)}, f32[6928]{0:T(1024)S(1)}, u32[]{:S(2)}, u32[]{:S(2)}) %collective-permute-start.15) | collective-permute-done | bytes 27744 | tf_op jit(solution)/shard_map/ppermute | solution.py:46
  141.7 1.9 %collective-permute-start.16 = (f32[6928]{0:T(1024)S(1)}, f32[6928]{0:T(1024)S(1)}, u32[]{:S(2)}, u32[]{:S(2)}) collective-permute-start(f32[6928]{0:T(1024)S(1)} %add.207), channel_id=1, source_target_pairs={{0,4},{1,5},{2,6},{3,7},{4,0},{5,1},{6,2},{7,3},{8,12},{9,13},{10,... | collective-permute-start | bytes 83144 | tf_op jit(solution)/shard_map/ppermute | solution.py:46
  143.9 3.5 %collective-permute-done.16 = f32[6928]{0:T(1024)S(1)} collective-permute-done((f32[6928]{0:T(1024)S(1)}, f32[6928]{0:T(1024)S(1)}, u32[]{:S(2)}, u32[]{:S(2)}) %collective-permute-start.16) | collective-permute-done | bytes 27744 | tf_op jit(solution)/shard_map/ppermute | solution.py:46
  147.4 1.9 %collective-permute-start.17 = (f32[6928]{0:T(1024)S(1)}, f32[6928]{0:T(1024)S(1)}, u32[]{:S(2)}, u32[]{:S(2)}) collective-permute-start(f32[6928]{0:T(1024)S(1)} %add.208), channel_id=1, source_target_pairs={{0,2},{1,3},{2,0},{3,1},{4,6},{5,7},{6,4},{7,5},{8,10},{9,11},{10,... | collective-permute-start | bytes 83144 | tf_op jit(solution)/shard_map/ppermute | solution.py:46
  149.7 5.0 %collective-permute-done.17 = f32[6928]{0:T(1024)S(1)} collective-permute-done((f32[6928]{0:T(1024)S(1)}, f32[6928]{0:T(1024)S(1)}, u32[]{:S(2)}, u32[]{:S(2)}) %collective-permute-start.17) | collective-permute-done | bytes 27744 | tf_op jit(solution)/shard_map/ppermute | solution.py:46
  154.7 1.9 %collective-permute-start.18 = (f32[6928]{0:T(1024)S(1)}, f32[6928]{0:T(1024)S(1)}, u32[]{:S(2)}, u32[]{:S(2)}) collective-permute-start(f32[6928]{0:T(1024)S(1)} %add.209), channel_id=1, source_target_pairs={{0,1},{1,0},{2,3},{3,2},{4,5},{5,4},{6,7},{7,6},{8,9},{9,8},{10,11... | collective-permute-start | bytes 83144 | tf_op jit(solution)/shard_map/ppermute | solution.py:46
  157.6 2.8 %collective-permute-done.18 = f32[6928]{0:T(1024)S(1)} collective-permute-done((f32[6928]{0:T(1024)S(1)}, f32[6928]{0:T(1024)S(1)}, u32[]{:S(2)}, u32[]{:S(2)}) %collective-permute-start.18) | collective-permute-done | bytes 27744 | tf_op jit(solution)/shard_map/ppermute | solution.py:46
  (105 shorter events, 16.1 us)
Async XLA Ops:
  0.6 78.6 %copy-start = (bf16[27,16,16]{0,2,1:T(8,128)(2,1)S(1)}, bf16[27,16,16]{0,2,1:T(8,128)(2,1)}, u32[]{:S(2)}) copy-start(bf16[27,16,16]{0,2,1:T(8,128)(2,1)} %param.13) | copy-start | bytes 41476
  1.6 7.8 %collective-permute-start = (bf16[1,16,2,8,256]{4,1,3,2,0:T(8,128)(2,1)S(1)}, bf16[1,16,2,8,256]{4,1,3,2,0:T(8,128)(2,1)S(1)}, u32[]{:S(2)}, u32[]{:S(2)}) collective-permute-start(bf16[1,16,2,8,256]{4,1,3,2,0:T(8,128)(2,1)S(1)} %copy.24), channel_id=1, source_target_pairs={{0,1},{1,0},{2,3},{3,2},{4,5},{5,4},{6,7},{7,6},{8,9},{9,8},{10,11... | collective-permute-start | bytes 393224 | tf_op jit(solution)/shard_map/ppermute | solution.py:77
  10.4 8.4 %collective-permute-start.1 = (bf16[1,16,2,8,256]{4,1,3,2,0:T(8,128)(2,1)S(1)}, bf16[1,16,2,8,256]{4,1,3,2,0:T(8,128)(2,1)S(1)}, u32[]{:S(2)}, u32[]{:S(2)}) collective-permute-start(bf16[1,16,2,8,256]{4,1,3,2,0:T(8,128)(2,1)S(1)} %broadcast_select_fusion), channel_id=1, source_target_pairs={{0,2},{1,3},{2,0},{3,1},{4,6},{5,7},{6,4},{7,5},{8,10},{9,11},{10,... | collective-permute-start | bytes 393224 | tf_op jit(solution)/shard_map/ppermute | solution.py:77
  18.8 7.2 %collective-permute-start.2 = (bf16[1,16,2,8,256]{4,1,3,2,0:T(8,128)(2,1)S(1)}, bf16[1,16,2,8,256]{4,1,3,2,0:T(8,128)(2,1)S(1)}, u32[]{:S(2)}, u32[]{:S(2)}) collective-permute-start(bf16[1,16,2,8,256]{4,1,3,2,0:T(8,128)(2,1)S(1)} %broadcast_select_fusion.1), channel_id=1, source_target_pairs={{0,4},{1,5},{2,6},{3,7},{4,0},{5,1},{6,2},{7,3},{8,12},{9,13},{10,... | collective-permute-start | bytes 393224 | tf_op jit(solution)/shard_map/ppermute | solution.py:77
  26.0 9.0 %collective-permute-start.3 = (bf16[1,16,2,8,256]{4,1,3,2,0:T(8,128)(2,1)S(1)}, bf16[1,16,2,8,256]{4,1,3,2,0:T(8,128)(2,1)S(1)}, u32[]{:S(2)}, u32[]{:S(2)}) collective-permute-start(bf16[1,16,2,8,256]{4,1,3,2,0:T(8,128)(2,1)S(1)} %broadcast_select_fusion.2), channel_id=1, source_target_pairs={{0,8},{1,9},{2,10},{3,11},{4,12},{5,13},{6,14},{7,15},{8,0},{9,1},... | collective-permute-start | bytes 393224 | tf_op jit(solution)/shard_map/ppermute | solution.py:77
  35.1 14.2 %collective-permute-start.4 = (bf16[1,16,2,8,256]{4,1,3,2,0:T(8,128)(2,1)S(1)}, bf16[1,16,2,8,256]{4,1,3,2,0:T(8,128)(2,1)S(1)}, u32[]{:S(2)}, u32[]{:S(2)}) collective-permute-start(bf16[1,16,2,8,256]{4,1,3,2,0:T(8,128)(2,1)S(1)} %broadcast_select_fusion.3), channel_id=1, source_target_pairs={{0,16},{1,17},{2,18},{3,19},{4,20},{5,21},{6,22},{7,23},{8,24},{9,... | collective-permute-start | bytes 393224 | tf_op jit(solution)/shard_map/ppermute | solution.py:77
  49.3 11.7 %collective-permute-start.5 = (bf16[1,16,2,8,256]{4,1,3,2,0:T(8,128)(2,1)S(1)}, bf16[1,16,2,8,256]{4,1,3,2,0:T(8,128)(2,1)S(1)}, u32[]{:S(2)}, u32[]{:S(2)}) collective-permute-start(bf16[1,16,2,8,256]{4,1,3,2,0:T(8,128)(2,1)S(1)} %broadcast_select_fusion.4), channel_id=1, source_target_pairs={{0,32},{1,33},{2,34},{3,35},{4,36},{5,37},{6,38},{7,39},{8,40},{9,... | collective-permute-start | bytes 393224 | tf_op jit(solution)/shard_map/ppermute | solution.py:77
  61.0 19.3 %collective-permute-start.6 = (bf16[1,16,2,8,256]{4,1,3,2,0:T(8,128)(2,1)S(1)}, bf16[1,16,2,8,256]{4,1,3,2,0:T(8,128)(2,1)S(1)}, u32[]{:S(2)}, u32[]{:S(2)}) collective-permute-start(bf16[1,16,2,8,256]{4,1,3,2,0:T(8,128)(2,1)S(1)} %reverse_select_fusion), channel_id=1, source_target_pairs={{0,63},{1,2},{2,1},{3,4},{4,3},{5,6},{6,5},{7,8},{8,7},{9,10},{10,... | collective-permute-start | bytes 393224 | tf_op jit(solution)/shard_map/ppermute | solution.py:27
  65.1 17.1 %collective-permute-start.7 = (bf16[1,16,2,8,256]{4,1,3,2,0:T(8,128)(2,1)S(1)}, bf16[1,16,2,8,256]{4,1,3,2,0:T(8,128)(2,1)S(1)}, u32[]{:S(2)}, u32[]{:S(2)}) collective-permute-start(bf16[1,16,2,8,256]{4,1,3,2,0:T(8,128)(2,1)S(1)} %reverse_select_fusion), channel_id=1, source_target_pairs={{0,1},{1,0},{2,3},{3,2},{4,5},{5,4},{6,7},{7,6},{8,9},{9,8},{10,11... | collective-permute-start | bytes 393224 | tf_op jit(solution)/shard_map/ppermute | solution.py:25
  85.4 0.9 copy-start.1
  85.4 0.9 copy-start.2
  88.5 17.9 %collective-permute-start.10 = (f32[6928]{0:T(1024)S(1)}, f32[6928]{0:T(1024)S(1)}, u32[]{:S(2)}, u32[]{:S(2)}) collective-permute-start(f32[6928]{0:T(1024)S(1)} %pad_maximum_fusion.6), channel_id=1, source_target_pairs={{0,256},{64,320},{128,384},{192,448},{256,0},{320,64},{384,128},{4... | collective-permute-start | bytes 83144 | tf_op jit(solution)/shard_map/ppermute | solution.py:46
  93.1 21.0 %collective-permute-start.8 = (bf16[1,16,1,8,256]{4,1,3,2,0:T(8,128)(2,1)S(1)}, bf16[1,16,1,8,256]{4,1,3,2,0:T(8,128)(2,1)S(1)}, u32[]{:S(2)}, u32[]{:S(2)}) collective-permute-start(bf16[1,16,1,8,256]{4,1,3,2,0:T(8,128)(2,1)S(1)} %get-tuple-element.75), channel_id=1, source_target_pairs={{0,63},{1,2},{2,1},{3,4},{4,3},{5,6},{6,5},{7,8},{8,7},{9,10},{10,... | collective-permute-start | bytes 196616 | tf_op jit(solution)/shard_map/ppermute | solution.py:37
  95.0 19.1 %collective-permute-start.9 = (bf16[1,16,1,8,256]{4,1,3,2,0:T(8,128)(2,1)S(1)}, bf16[1,16,1,8,256]{4,1,3,2,0:T(8,128)(2,1)S(1)}, u32[]{:S(2)}, u32[]{:S(2)}) collective-permute-start(bf16[1,16,1,8,256]{4,1,3,2,0:T(8,128)(2,1)S(1)} %get-tuple-element.76), channel_id=1, source_target_pairs={{0,1},{1,0},{2,3},{3,2},{4,5},{5,4},{6,7},{7,6},{8,9},{9,8},{10,11... | collective-permute-start | bytes 196616 | tf_op jit(solution)/shard_map/ppermute | solution.py:35
  106.4 5.8 %collective-permute-start.11 = (f32[6928]{0:T(1024)S(1)}, f32[6928]{0:T(1024)S(1)}, u32[]{:S(2)}, u32[]{:S(2)}) collective-permute-start(f32[6928]{0:T(1024)S(1)} %fusion.92), channel_id=1, source_target_pairs={{0,128},{64,192},{128,0},{192,64},{256,384},{320,448},{384,256},{4... | collective-permute-start | bytes 83144 | tf_op jit(solution)/shard_map/ppermute | solution.py:46
  112.2 3.4 %collective-permute-start.12 = (f32[6928]{0:T(1024)S(1)}, f32[6928]{0:T(1024)S(1)}, u32[]{:S(2)}, u32[]{:S(2)}) collective-permute-start(f32[6928]{0:T(1024)S(1)} %add.203), channel_id=1, source_target_pairs={{0,64},{64,0},{128,192},{192,128},{256,320},{320,256},{384,448},{4... | collective-permute-start | bytes 83144 | tf_op jit(solution)/shard_map/ppermute | solution.py:46
  115.7 9.7 %collective-permute-start.13 = (f32[6928]{0:T(1024)S(1)}, f32[6928]{0:T(1024)S(1)}, u32[]{:S(2)}, u32[]{:S(2)}) collective-permute-start(f32[6928]{0:T(1024)S(1)} %add.204), channel_id=1, source_target_pairs={{0,32},{1,33},{2,34},{3,35},{4,36},{5,37},{6,38},{7,39},{8,40},{9,... | collective-permute-start | bytes 83144 | tf_op jit(solution)/shard_map/ppermute | solution.py:46
  125.3 9.7 %collective-permute-start.14 = (f32[6928]{0:T(1024)S(1)}, f32[6928]{0:T(1024)S(1)}, u32[]{:S(2)}, u32[]{:S(2)}) collective-permute-start(f32[6928]{0:T(1024)S(1)} %add.205), channel_id=1, source_target_pairs={{0,16},{1,17},{2,18},{3,19},{4,20},{5,21},{6,22},{7,23},{8,24},{9,... | collective-permute-start | bytes 83144 | tf_op jit(solution)/shard_map/ppermute | solution.py:46
  135.0 6.7 %collective-permute-start.15 = (f32[6928]{0:T(1024)S(1)}, f32[6928]{0:T(1024)S(1)}, u32[]{:S(2)}, u32[]{:S(2)}) collective-permute-start(f32[6928]{0:T(1024)S(1)} %add.206), channel_id=1, source_target_pairs={{0,8},{1,9},{2,10},{3,11},{4,12},{5,13},{6,14},{7,15},{8,0},{9,1},... | collective-permute-start | bytes 83144 | tf_op jit(solution)/shard_map/ppermute | solution.py:46
  141.7 5.8 %collective-permute-start.16 = (f32[6928]{0:T(1024)S(1)}, f32[6928]{0:T(1024)S(1)}, u32[]{:S(2)}, u32[]{:S(2)}) collective-permute-start(f32[6928]{0:T(1024)S(1)} %add.207), channel_id=1, source_target_pairs={{0,4},{1,5},{2,6},{3,7},{4,0},{5,1},{6,2},{7,3},{8,12},{9,13},{10,... | collective-permute-start | bytes 83144 | tf_op jit(solution)/shard_map/ppermute | solution.py:46
  147.4 7.3 %collective-permute-start.17 = (f32[6928]{0:T(1024)S(1)}, f32[6928]{0:T(1024)S(1)}, u32[]{:S(2)}, u32[]{:S(2)}) collective-permute-start(f32[6928]{0:T(1024)S(1)} %add.208), channel_id=1, source_target_pairs={{0,2},{1,3},{2,0},{3,1},{4,6},{5,7},{6,4},{7,5},{8,10},{9,11},{10,... | collective-permute-start | bytes 83144 | tf_op jit(solution)/shard_map/ppermute | solution.py:46
  154.7 5.8 %collective-permute-start.18 = (f32[6928]{0:T(1024)S(1)}, f32[6928]{0:T(1024)S(1)}, u32[]{:S(2)}, u32[]{:S(2)}) collective-permute-start(f32[6928]{0:T(1024)S(1)} %add.209), channel_id=1, source_target_pairs={{0,1},{1,0},{2,3},{3,2},{4,5},{5,4},{6,7},{7,6},{8,9},{9,8},{10,11... | collective-permute-start | bytes 83144 | tf_op jit(solution)/shard_map/ppermute | solution.py:46
